TPU v7x, 256 devices: a whole 4x4x8 slice. The times are simulated.
256 devices in a mesh: tm: 32 (over y, x, core), tensor: 8 (over z).
Axes of the slice: x: 4, y: 4, z: 8, core: 2. Of those that a mesh axis runs over, the one named last changes fastest.
Arguments:
- features: bfloat16 [32768, 1536], P(('tm', 'tensor')), may hold values from -4 to 4
- frame_mask: int32 [32768], P('tm'), may hold values 0 or 1
- total_length: int32 [1], replicated, may hold values from 24576 to 32768
- norm_gain: float32 [1536], replicated, may hold values from 0.1 to 1.9
- value_weight: bfloat16 [1536, 1536], P(None, 'tensor'), may hold values from -0.15625 to 0.15625
- gate_weight: bfloat16 [1536, 1536], P(None, 'tensor'), may hold values from -0.15625 to 0.15625
- depth_kernel: float32 [31, 1536], P(None, 'tensor'), may hold values from -1 to 1
- batch_gain: float32 [1536], P('tensor'), may hold values from 0.1 to 1.9
- batch_bias: float32 [1536], P('tensor'), may hold values from -2 to 2
- out_weight: bfloat16 [1536, 1536], P('tensor'), may hold values from -0.15625 to 0.15625
- feed_gain: float32 [1536], replicated, may hold values from 0.1 to 1.9
- up_weight: bfloat16 [1536, 6144], P('tm', 'tensor'), may hold values from -0.15625 to 0.15625
- down_weight: bfloat16 [6144, 1536], P('tensor', 'tm'), may hold values from -0.078125 to 0.078125
Outputs:
- encoded: bfloat16 [32768, 1536], P(('tm', 'tensor'))
All inputs are finite; a program needn't handle non-finite values. No bound on the sum of `frame_mask` on one device may be relied on, other than what follows from the above.
Results may differ from a plain program's by a relative error of at most 0.0074.
Values may be sent and summed in bfloat16 or wider, within the bound.
No kernel may reach another device: no remote copies, remote signals or barrier semaphores. Data moves between devices by JAX's collectives and lax.ppermute only.
A program may use at most 64 MiB of HBM per device.

v0:
```python
import jax
import jax.numpy as jnp
from jax import lax
from jax.sharding import PartitionSpec as P

KERNEL = 31


def extended(array, sides, width):
    for axis, dim in sides:
        devices, length = (lax.axis_size(axis), array.shape[dim])
        up = [(i, (i + 1) % devices) for i in range(devices - 1)]
        down = [(j, i) for i, j in up]
        last = lax.slice_in_dim(array, length - width, length, axis=dim)
        initial = lax.slice_in_dim(array, 0, width, axis=dim)
        before = lax.ppermute(last, axis, up)
        after = lax.ppermute(initial, axis, down)
        array = jnp.concatenate([before, array, after], axis=dim)
    return array


def layer_norm(rows, gain):
    values = rows.astype(jnp.float32)
    centre = jnp.mean(values, axis=-1, keepdims=True)
    spread = jnp.mean(jnp.square(values - centre), axis=-1, keepdims=True)
    return (values - centre) * lax.rsqrt(spread + 1e-05) * gain


def shards(
    features,
    frame_mask,
    total_length,
    norm_gain,
    value_weight,
    gate_weight,
    depth_kernel,
    batch_gain,
    batch_bias,
    out_weight,
    feed_gain,
    up_weight,
    down_weight,
):
    own_rows = features.shape[0]
    block = own_rows * lax.axis_size("tensor")
    positions = lax.axis_index("tm") * block + jnp.arange(block, dtype=jnp.int32)
    valid = ((frame_mask > 0) & (positions < total_length[0])).astype(jnp.float32)
    normed = layer_norm(features, norm_gain).astype(jnp.bfloat16)
    piece = lax.all_gather(normed, "tensor", axis=0, tiled=True)
    value = jnp.dot(piece, value_weight, preferred_element_type=jnp.float32)
    gate = jnp.dot(piece, gate_weight, preferred_element_type=jnp.float32)
    glu = (value * jax.nn.sigmoid(gate) * valid[:, None]).astype(jnp.bfloat16)
    padded = extended(glu, (("tm", 0),), KERNEL // 2)
    conv = jnp.zeros(glu.shape, jnp.float32)
    for tap in range(KERNEL):
        conv = conv + padded[tap : tap + block].astype(jnp.float32) * depth_kernel[tap]
    count_local = jnp.sum(valid)
    first_sum = jnp.sum(conv * valid[:, None], axis=0)
    total, count = lax.psum((first_sum, count_local), "tm")
    mean = total / count
    centred = conv - mean
    spread = lax.psum(jnp.sum(jnp.square(centred) * valid[:, None], axis=0), "tm")
    var = spread / count
    scaled = centred * lax.rsqrt(var + 1e-05) * batch_gain + batch_bias
    swished = (scaled * jax.nn.sigmoid(scaled)).astype(jnp.bfloat16)
    conv_out = lax.psum_scatter(
        jnp.dot(swished, out_weight, preferred_element_type=jnp.float32),
        "tensor",
        scatter_dimension=0,
        tiled=True,
    )
    mid = (features.astype(jnp.float32) + conv_out).astype(jnp.bfloat16)
    feed_normed = layer_norm(mid, feed_gain).astype(jnp.bfloat16)
    feed_block = lax.all_gather(feed_normed, "tensor", axis=0, tiled=True)
    up_whole = lax.all_gather(up_weight, "tm", axis=0, tiled=True)
    pre = jnp.dot(feed_block, up_whole, preferred_element_type=jnp.float32)
    hidden = (pre * jax.nn.sigmoid(pre)).astype(jnp.bfloat16)
    down_whole = lax.all_gather(down_weight, "tm", axis=1, tiled=True)
    partial_out = jnp.dot(hidden, down_whole, preferred_element_type=jnp.float32)
    feed_out = lax.psum_scatter(partial_out, "tensor", scatter_dimension=0, tiled=True)
    return (mid.astype(jnp.float32) + 0.5 * feed_out).astype(jnp.bfloat16)


def solution(mesh):
    placed = (
        P(("tm", "tensor"), None),
        P("tm"),
        P(),
        P(),
        P(None, "tensor"),
        P(None, "tensor"),
        P(None, "tensor"),
        P("tensor"),
        P("tensor"),
        P("tensor", None),
        P(),
        P("tm", "tensor"),
        P("tensor", "tm"),
    )
    return jax.shard_map(
        shards, mesh=mesh, in_specs=placed, out_specs=P(("tm", "tensor"), None), check_vma=False
    )
```

profile of v0, /device:TPU:2, one launch (start us, length us, event | category | flops | bytes accessed | tf_op | source)
XLA Modules:
  0.0 449.9 jit_solution(13662535378616291768)
XLA Ops:
  7.4 1.2 convert_reduce_fusion.1
  8.6 1.2 fusion.14
  9.8 2.0 fusion.16
  12.6 1.4 fusion.58
  14.0 1.0 fusion.61
  15.0 45.0 %all-gather.5.cloned.1.call-done = bf16[1024,1536]{1,0:T(8,128)(2,1)} async-done(((bf16[128,1536]{1,0:T(8,128)(2,1)}), bf16[1024,1536]{1,0:T(8,128)(2,1)}) %all-gather.5.cloned.1.call-update) | async-done | bytes 3145744 | tf_op jit(solution)/shard_map/all_gather | solution.py:49
  60.0 3.4 fusion.5
  63.4 1.2 fusion.6
  64.7 1.9 collective-permute-start
  66.6 3.6 collective-permute-start.1
  70.3 1.0 fusion.62
  71.3 0.7 collective-permute-done.1
  72.0 5.6 %multiply_reduce_fusion.1 = (f32[192]{0:T(256)S(1)}, f32[1024,192]{0,1:T(8,128)S(1)}) fusion(f32[1024]{0:T(1024)S(1)} %get-tuple-element.10, f32[192]{0:T(256)S(1)} %bitcast.70, bf16[15,192]{0,1:T(8,128)(2,1)S(1)} %collective-permute-done.1, bf16[1024,192]{0,1:T(8,128)(2,1)S(1)} %fusion.6, f32[192]{0:T(256)S(1)} %bitcast.71, f32[192]{0:T(256)S(1)} %bitcast.42, ...), kind=kLoop, calls=%fused_computation.58 | loop fusion | flops 36175680 | bytes 1219840 | tf_op jit(solution)/shard_map/reduce_sum | solution.py:58
  77.6 60.7 %all-reduce = (f32[192]{0:T(256)S(1)}, f32[]{:T(128)}) all-reduce(f32[192]{0:T(256)S(1)} %get-tuple-element.11, f32[]{:T(128)} %get-tuple-element.9), channel_id=1, replica_groups=mesh['tm'=32,'tensor'=8] {'tm'}, use_global_device_ids=true, to_apply=%region_3.0 | all-reduce | flops 193 | bytes 1544 | tf_op jit(solution)/shard_map/psum | solution.py:59
  139.2 62.7 %psum.23 = f32[192]{0:T(256)S(1)} all-reduce(f32[192]{0:T(256)S(1)} %multiply_reduce_fusion), channel_id=1, replica_groups=mesh['tm'=32,'tensor'=8] {'tm'}, use_global_device_ids=true, to_apply=%region_7.0 | all-reduce | flops 192 | bytes 1536 | tf_op jit(solution)/shard_map/psum | solution.py:62
  202.5 3.9 fusion.19
  207.7 72.8 %reduce-scatter.3.cloned.1.call-done = f32[128,1536]{1,0:T(8,128)} async-done(((f32[1024,1536]{1,0:T(8,128)}), f32[128,1536]{1,0:T(8,128)}) %reduce-scatter.3.cloned.1.call-update) | async-done | bytes 786448 | tf_op jit(solution)/shard_map/reduce_scatter | solution.py:66
  280.5 1.3 convert_reduce_fusion
  282.1 1.0 fusion.13
  283.4 24.6 %all-gather.11.cloned.1.call-done = bf16[768,1536]{0,1:T(8,128)(2,1)} async-done(((bf16[768,48]{0,1:T(8,128)(2,1)}), bf16[768,1536]{0,1:T(8,128)(2,1)}) %all-gather.11.cloned.1.call-update) | async-done | bytes 2359312 | tf_op jit(solution)/shard_map/all_gather | solution.py:78
  308.1 46.5 %all-gather.7.cloned.1.call-done = bf16[1024,1536]{1,0:T(8,128)(2,1)} async-done(((bf16[128,1536]{1,0:T(8,128)(2,1)}), bf16[1024,1536]{1,0:T(8,128)(2,1)}) %all-gather.7.cloned.1.call-update) | async-done | bytes 3145744 | tf_op jit(solution)/shard_map/all_gather | solution.py:74
  354.5 12.1 %fusion = f32[1024,1536]{1,0:T(8,128)} fusion(bf16[768,1536]{0,1:T(8,128)(2,1)} %all-gather.11.cloned.1.call-done, bf16[1024,1536]{1,0:T(8,128)(2,1)} %all-gather.7.cloned.1.call-done, bf16[1536,768]{1,0:T(8,128)(2,1)} %all-gather.9.cloned.1.call-done), kind=kOutput, calls=%fused_computation.29 | convolution fusion | flops 4835770368 | bytes 14155776 | tf_op jit(solution)/shard_map/dot_general | solution.py:79
  366.6 73.8 %reduce-scatter.5.cloned.1.call-done = f32[128,1536]{1,0:T(8,128)} async-done(((f32[1024,1536]{1,0:T(8,128)}), f32[128,1536]{1,0:T(8,128)}) %reduce-scatter.5.cloned.1.call-update) | async-done | bytes 786448 | tf_op jit(solution)/shard_map/reduce_scatter | solution.py:80
  440.3 2.0 fusion.18
  (37 shorter events, 3.5 us)
Async XLA Ops:
  7.4 195.1 %copy-start = (bf16[192,1536]{1,0:T(8,128)(2,1)S(1)}, bf16[192,1536]{1,0:T(8,128)(2,1)}, u32[]{:S(2)}) copy-start(bf16[192,1536]{1,0:T(8,128)(2,1)} %param.22) | copy-start | bytes 1769476
  7.4 52.6 %all-gather.5.cloned.1.call-start = ((), (), s32[]{:S(2)}) async-start(), calls=%async_computation.2 | async-start | bytes 3538944 | tf_op jit(solution)/shard_map/all_gather | solution.py:49
  11.9 268.6 %reduce-scatter.3.cloned.1.call-start = ((), (), s32[]{:S(2)}) async-start(), calls=%async_computation.3 | async-start | bytes 7077888 | tf_op jit(solution)/shard_map/reduce_scatter | solution.py:66
  15.0 48.4 %copy-start.6 = (bf16[1536,192]{0,1:T(8,128)(2,1)S(1)}, bf16[1536,192]{0,1:T(8,128)(2,1)}, u32[]{:S(2)}) copy-start(bf16[1536,192]{0,1:T(8,128)(2,1)} %param.17) | copy-start | bytes 1769476
  60.0 3.4 copy-start.5
  63.4 139.1 %copy-start.3 = (f32[192]{0:T(256)S(1)}, f32[192]{0:T(256)}, u32[]{:S(2)}) copy-start(f32[192]{0:T(256)} %param.21) | copy-start | bytes 2308
  63.4 139.1 %copy-start.4 = (f32[192]{0:T(256)S(1)}, f32[192]{0:T(256)}, u32[]{:S(2)}) copy-start(f32[192]{0:T(256)} %param.20) | copy-start | bytes 2308
  64.7 6.6 %collective-permute-start = (bf16[15,192]{0,1:T(8,128)(2,1)S(1)}, bf16[15,192]{0,1:T(8,128)(2,1)S(1)}, u32[]{:S(2)}, u32[]{:S(2)}) collective-permute-start(bf16[15,192]{0,1:T(8,128)(2,1)S(1)} %get-tuple-element.13), channel_id=1, source_target_pairs={{0,8},{8,16},{16,24},{24,32},{32,40},{40,48},{48,56},{56,64},{64,7... | collective-permute-start | bytes 17288 | tf_op jit(solution)/shard_map/ppermute | solution.py:16
  66.6 5.4 %collective-permute-start.1 = (bf16[15,192]{0,1:T(8,128)(2,1)S(1)}, bf16[15,192]{0,1:T(8,128)(2,1)S(1)}, u32[]{:S(2)}, u32[]{:S(2)}) collective-permute-start(bf16[15,192]{0,1:T(8,128)(2,1)S(1)} %get-tuple-element.14), channel_id=1, source_target_pairs={{8,0},{16,8},{24,16},{32,24},{40,32},{48,40},{56,48},{64,56},{72,6... | collective-permute-start | bytes 17288 | tf_op jit(solution)/shard_map/ppermute | solution.py:17
  206.4 74.1 %copy-start.1 = (bf16[128,1536]{1,0:T(8,128)(2,1)S(1)}, bf16[128,1536]{1,0:T(8,128)(2,1)}, u32[]{:S(2)}) copy-start(bf16[128,1536]{1,0:T(8,128)(2,1)} %param.13) | copy-start | bytes 1179652
  206.4 75.7 %copy-start.2 = (f32[1536]{0:T(1024)S(1)}, f32[1536]{0:T(1024)}, u32[]{:S(2)}) copy-start(f32[1536]{0:T(1024)} %param.23) | copy-start | bytes 18436
  206.4 77.0 %all-gather.9.cloned.1.call-start = ((), (), s32[]{:S(2)}) async-start(), calls=%async_computation.5 | async-start | bytes 2433024 | tf_op jit(solution)/shard_map/all_gather | solution.py:75
  207.0 101.0 %all-gather.11.cloned.1.call-start = ((), (), s32[]{:S(2)}) async-start(), calls=%async_computation.6 | async-start | bytes 2433024 | tf_op jit(solution)/shard_map/all_gather | solution.py:78
  207.6 146.9 %all-gather.7.cloned.1.call-start = ((), (), s32[]{:S(2)}) async-start(), calls=%async_computation.4 | async-start | bytes 3538944 | tf_op jit(solution)/shard_map/all_gather | solution.py:74
  283.1 157.2 %reduce-scatter.5.cloned.1.call-start = ((), (), s32[]{:S(2)}) async-start(), calls=%async_computation.7 | async-start | bytes 7077888 | tf_op jit(solution)/shard_map/reduce_scatter | solution.py:80
Sparse Core Ops, SparseCore 0:
  12.0 47.9 all-gather.4
  206.6 73.8 reduce-scatter.2
Sparse Core Ops, SparseCore 1:
  209.5 47.5 all-gather.8
  259.4 48.6 all-gather.10
  309.7 44.7 all-gather.6
  366.7 73.6 reduce-scatter.4
where the time goes:
time: 451 us; the launch traced here: 450 us
  waiting for transfers between devices  265 us (59%)
  blocking collectives  123 us (27%)
  matrix products  20.5 us (5%)
  other arithmetic  17.6 us (4%)
  between operations  15.9 us (4%)
  starting transfers between devices  5.96 us (1%)
    reduce_scatter x1, waiting for transfers between devices, shards(): lax.psum_scatter(partial_out, 'tensor', scatter_dimension=0, tiled=True)  73.8 us
    reduce_scatter x1, waiting for transfers between devices, shards(): lax.psum_scatter(jnp.dot(swished, out_weight, preferred_element_type=jnp....  72.8 us
    psum x1, blocking collectives, shards(): lax.psum(jnp.sum(jnp.square(centred) * valid[:, None], axis=0), 'tm')  62.7 us
    psum x1, blocking collectives, shards(): total, count = lax.psum((first_sum, count_local), 'tm')  60.7 us
    all_gather x1, waiting for transfers between devices, shards(): feed_block = lax.all_gather(feed_normed, 'tensor', axis=0, tiled=True)  46.5 us
    all_gather x1, waiting for transfers between devices, shards(): piece = lax.all_gather(normed, 'tensor', axis=0, tiled=True)  45 us
    all_gather x1, waiting for transfers between devices, shards(): down_whole = lax.all_gather(down_weight, 'tm', axis=1, tiled=True)  24.6 us
    dot_general x1, matrix products, shards(): jnp.dot(hidden, down_whole, preferred_element_type=jnp.float32)  12.1 us
  transfers between devices with their start and end apart: 8, of which 6 were waited for; matrix products, arithmetic and copies ran while one was open for 1% of the time, Pallas kernels for 0%

commit v1 on v0

--- a/solution.py
+++ b/solution.py
@@ -26,6 +26,32 @@
     return (values - centre) * lax.rsqrt(spread + 1e-05) * gain
 
 
+def merge_moments(low, high):
+    n_a, mean_a, m2_a = low[0], low[1], low[2]
+    n_b, mean_b, m2_b = high[0], high[1], high[2]
+    n = n_a + n_b
+    share = jnp.where(n > 0, n_b / jnp.maximum(n, 1.0), 0.0)
+    delta = mean_b - mean_a
+    mean = mean_a + delta * share
+    m2 = m2_a + m2_b + jnp.square(delta) * n_a * share
+    return jnp.stack([n, mean, m2])
+
+
+def moments_over(stats, axis):
+    size = lax.axis_size(axis)
+    me = lax.axis_index(axis)
+    step = 1
+    while step < size:
+        pairs = [(i, i ^ step) for i in range(size)]
+        other = lax.ppermute(stats, axis, pairs)
+        mine_low = (me & step) == 0
+        low = jnp.where(mine_low, stats, other)
+        high = jnp.where(mine_low, other, stats)
+        stats = merge_moments(low, high)
+        step *= 2
+    return stats
+
+
 def shards(
     features,
     frame_mask,
@@ -47,6 +73,8 @@
     valid = ((frame_mask > 0) & (positions < total_length[0])).astype(jnp.float32)
     normed = layer_norm(features, norm_gain).astype(jnp.bfloat16)
     piece = lax.all_gather(normed, "tensor", axis=0, tiled=True)
+    up_whole = lax.all_gather(up_weight, "tm", axis=0, tiled=True)
+    down_whole = lax.all_gather(down_weight, "tm", axis=1, tiled=True)
     value = jnp.dot(piece, value_weight, preferred_element_type=jnp.float32)
     gate = jnp.dot(piece, gate_weight, preferred_element_type=jnp.float32)
     glu = (value * jax.nn.sigmoid(gate) * valid[:, None]).astype(jnp.bfloat16)
@@ -55,29 +83,30 @@
     for tap in range(KERNEL):
         conv = conv + padded[tap : tap + block].astype(jnp.float32) * depth_kernel[tap]
     count_local = jnp.sum(valid)
-    first_sum = jnp.sum(conv * valid[:, None], axis=0)
-    total, count = lax.psum((first_sum, count_local), "tm")
-    mean = total / count
+    local_sum = jnp.sum(conv * valid[:, None], axis=0)
+    local_mean = jnp.where(count_local > 0, local_sum / jnp.maximum(count_local, 1.0), 0.0)
+    local_m2 = jnp.sum(jnp.square(conv - local_mean) * valid[:, None], axis=0)
+    stats = jnp.stack([jnp.broadcast_to(count_local, local_sum.shape), local_mean, local_m2])
+    stats = moments_over(stats, "tm")
+    count, mean, m2 = stats[0], stats[1], stats[2]
     centred = conv - mean
-    spread = lax.psum(jnp.sum(jnp.square(centred) * valid[:, None], axis=0), "tm")
-    var = spread / count
+    var = m2 / count
     scaled = centred * lax.rsqrt(var + 1e-05) * batch_gain + batch_bias
     swished = (scaled * jax.nn.sigmoid(scaled)).astype(jnp.bfloat16)
+    conv_part = jnp.dot(swished, out_weight, preferred_element_type=jnp.float32)
+    conv_part, up_whole, down_whole = lax.optimization_barrier((conv_part, up_whole, down_whole))
     conv_out = lax.psum_scatter(
-        jnp.dot(swished, out_weight, preferred_element_type=jnp.float32),
-        "tensor",
-        scatter_dimension=0,
-        tiled=True,
-    )
+        conv_part.astype(jnp.bfloat16), "tensor", scatter_dimension=0, tiled=True
+    ).astype(jnp.float32)
     mid = (features.astype(jnp.float32) + conv_out).astype(jnp.bfloat16)
     feed_normed = layer_norm(mid, feed_gain).astype(jnp.bfloat16)
     feed_block = lax.all_gather(feed_normed, "tensor", axis=0, tiled=True)
-    up_whole = lax.all_gather(up_weight, "tm", axis=0, tiled=True)
     pre = jnp.dot(feed_block, up_whole, preferred_element_type=jnp.float32)
     hidden = (pre * jax.nn.sigmoid(pre)).astype(jnp.bfloat16)
-    down_whole = lax.all_gather(down_weight, "tm", axis=1, tiled=True)
     partial_out = jnp.dot(hidden, down_whole, preferred_element_type=jnp.float32)
-    feed_out = lax.psum_scatter(partial_out, "tensor", scatter_dimension=0, tiled=True)
+    feed_out = lax.psum_scatter(
+        partial_out.astype(jnp.bfloat16), "tensor", scatter_dimension=0, tiled=True
+    ).astype(jnp.float32)
     return (mid.astype(jnp.float32) + 0.5 * feed_out).astype(jnp.bfloat16)
 
 

time: 451 us -> 322 us (0.71)
  blocking collectives: 123 us -> 0 us
  waiting for transfers between devices: 265 us -> 253 us
  starting transfers between devices: 5.96 us -> 15.9 us
    psum x2 -> x0, blocking collectives: 123 us -> none  [the longest x1 62.7 us: shards(): lax.psum(jnp.sum(jnp.square(centred) * valid[:, None], axis=0), 'tm')]
    reduce_scatter x2, waiting for transfers between devices: 147 us -> 94.4 us  [the longest x1 48.8 us: shards(): lax.psum_scatter(conv_part.astype(jnp.bfloat16), 'tensor', scatter_dimens...]
    all_gather x1, waiting for transfers between devices: 24.6 us -> 51.2 us  [shards(): down_whole = lax.all_gather(down_weight, 'tm', axis=1, tiled=True)]
    ppermute x0 -> x5, starting transfers between devices: none -> 10.1 us  [moments_over(): other = lax.ppermute(stats, axis, pairs)]
    ppermute x0 -> x5, waiting for transfers between devices: none -> 9.85 us  [moments_over(): other = lax.ppermute(stats, axis, pairs)]
    all_gather x1, waiting for transfers between devices: 0.02 us -> 7.71 us  [shards(): up_whole = lax.all_gather(up_weight, 'tm', axis=0, tiled=True)]
  transfers between devices with their start and end apart: 8 -> 13, of which waited for: 6 -> 11; matrix products, arithmetic and copies ran while one was open for 1% -> 6% of each run, Pallas kernels for 0% -> 0%
where the time goes in v1:
time: 322 us
  waiting for transfers between devices  253 us (79%)
  matrix products  18.5 us (6%)
  other arithmetic  16.4 us (5%)
  starting transfers between devices  15.9 us (5%)
  between operations  15.7 us (5%)
    all_gather x1, waiting for transfers between devices, shards(): down_whole = lax.all_gather(down_weight, 'tm', axis=1, tiled=True)  51.2 us
    reduce_scatter x1, waiting for transfers between devices, shards(): lax.psum_scatter(conv_part.astype(jnp.bfloat16), 'tensor', scatter_dimens...  48.8 us
    reduce_scatter x1, waiting for transfers between devices, shards(): lax.psum_scatter(partial_out.astype(jnp.bfloat16), 'tensor', scatter_dime...  45.6 us
    all_gather x1, waiting for transfers between devices, shards(): feed_block = lax.all_gather(feed_normed, 'tensor', axis=0, tiled=True)  44.4 us
    all_gather x1, waiting for transfers between devices, shards(): piece = lax.all_gather(normed, 'tensor', axis=0, tiled=True)  43.5 us
    dot_general x1, matrix products, shards(): jnp.dot(hidden, down_whole, preferred_element_type=jnp.float32)  11.1 us
    ppermute x5, starting transfers between devices, moments_over(): other = lax.ppermute(stats, axis, pairs)  10.1 us
    ppermute x5, waiting for transfers between devices, moments_over(): other = lax.ppermute(stats, axis, pairs)  9.85 us
  transfers between devices with their start and end apart: 13, of which 11 were waited for; matrix products, arithmetic and copies ran while one was open for 6% of the time, Pallas kernels for 0%

profile of v1, /device:TPU:2, one launch (start us, length us, event | category | flops | bytes accessed | tf_op | source)
XLA Modules:
  0.0 321.7 jit_solution(17575117318898476684)
XLA Ops:
  7.7 1.2 fusion.13
  9.0 2.0 fusion.15
  14.3 1.4 fusion.63
  15.6 43.5 %all-gather.5.cloned.1.call-done = bf16[1024,1536]{1,0:T(8,128)(2,1)} async-done(((bf16[128,1536]{1,0:T(8,128)(2,1)}), bf16[1024,1536]{1,0:T(8,128)(2,1)}) %all-gather.5.cloned.1.call-update) | async-done | bytes 3145744 | tf_op jit(solution)/shard_map/all_gather | solution.py:75
  59.1 3.4 %fusion.4 = f32[1024,192]{0,1:T(8,128)S(1)} fusion(bf16[1024,1536]{1,0:T(8,128)(2,1)} %all-gather.5.cloned.1.call-done, bf16[1536,192]{0,1:T(8,128)(2,1)} %param.18), kind=kOutput, calls=%fused_computation.36 | convolution fusion | flops 604569600 | bytes 4521984 | tf_op jit(solution)/shard_map/dot_general | solution.py:79
  63.9 1.9 collective-permute-start
  65.8 3.6 %collective-permute-start.1 = (bf16[15,192]{0,1:T(8,128)(2,1)S(1)}, bf16[15,192]{0,1:T(8,128)(2,1)S(1)}, u32[]{:S(2)}, u32[]{:S(2)}) collective-permute-start(bf16[15,192]{0,1:T(8,128)(2,1)S(1)} %get-tuple-element.32), channel_id=1, source_target_pairs={{8,0},{16,8},{24,16},{32,24},{40,32},{48,40},{56,48},{64,56},{72,6... | collective-permute-start | bytes 17288 | tf_op jit(solution)/shard_map/ppermute | solution.py:17
  72.4 5.6 %multiply_reduce_fusion.1 = (f32[192]{0:T(256)S(1)}, f32[1024,192]{0,1:T(8,128)S(1)}) fusion(f32[1024]{0:T(1024)S(1)} %get-tuple-element.28, f32[192]{0:T(256)S(1)} %bitcast.79, bf16[15,192]{0,1:T(8,128)(2,1)S(1)} %collective-permute-done.1, bf16[1024,192]{0,1:T(8,128)(2,1)S(1)} %fusion.5, f32[192]{0:T(256)S(1)} %bitcast.80, f32[192]{0:T(256)S(1)} %bitcast.51, ...), kind=kLoop, calls=%fused_computation.58 | loop fusion | flops 36175680 | bytes 1219840 | tf_op jit(solution)/shard_map/reduce_sum | solution.py:86
  80.3 3.1 collective-permute-done.3
  83.5 4.3 %collective-permute-start.4 = (f32[3,192]{1,0:T(4,128)S(1)}, f32[3,192]{1,0:T(4,128)S(1)}, u32[]{:S(2)}, u32[]{:S(2)}) collective-permute-start(f32[3,192]{1,0:T(4,128)S(1)} %pad_maximum_fusion.4), channel_id=1, source_target_pairs={{0,32},{8,40},{16,48},{24,56},{32,0},{40,8},{48,16},{56,24},{64,96... | collective-permute-start | bytes 6920 | tf_op jit(solution)/shard_map/ppermute | solution.py:46
  87.7 1.6 collective-permute-done.4
  89.4 1.6 collective-permute-start.5
  91.0 2.1 collective-permute-done.5
  93.2 3.2 collective-permute-start.6
  96.4 2.3 collective-permute-done.6
  98.7 2.9 fusion.18
  101.6 7.7 %all-gather.7.cloned.1.call-done = bf16[1536,768]{1,0:T(8,128)(2,1)} async-done(((bf16[48,768]{1,0:T(8,128)(2,1)}), bf16[1536,768]{1,0:T(8,128)(2,1)}) %all-gather.7.cloned.1.call-update) | async-done | bytes 2359312 | tf_op jit(solution)/shard_map/all_gather | solution.py:76
  109.3 51.2 %all-gather.9.cloned.1.call-done = bf16[768,1536]{0,1:T(8,128)(2,1)} async-done(((bf16[768,48]{0,1:T(8,128)(2,1)}), bf16[768,1536]{0,1:T(8,128)(2,1)}) %all-gather.9.cloned.1.call-update) | async-done | bytes 2359312 | tf_op jit(solution)/shard_map/all_gather | solution.py:77
  160.6 48.8 %reduce-scatter.3.cloned.1.call-done = bf16[128,1536]{1,0:T(8,128)(2,1)} async-done(((bf16[1024,1536]{1,0:T(8,128)(2,1)}), bf16[128,1536]{1,0:T(8,128)(2,1)}) %reduce-scatter.3.cloned.1.call-update) | async-done | bytes 393232 | tf_op jit(solution)/shard_map/reduce_scatter | solution.py:98
  209.3 1.2 convert_reduce_fusion
  211.9 44.4 %all-gather.11.cloned.1.call-done = bf16[1024,1536]{1,0:T(8,128)(2,1)} async-done(((bf16[128,1536]{1,0:T(8,128)(2,1)}), bf16[1024,1536]{1,0:T(8,128)(2,1)}) %all-gather.11.cloned.1.call-update) | async-done | bytes 3145744 | tf_op jit(solution)/shard_map/all_gather | solution.py:103
  256.4 11.1 %convolution_convert_fusion = bf16[1024,1536]{1,0:T(8,128)(2,1)} fusion(bf16[768,1536]{0,1:T(8,128)(2,1)} %all-gather.9.cloned.1.call-done, bf16[1024,1536]{1,0:T(8,128)(2,1)} %all-gather.11.cloned.1.call-done, bf16[1536,768]{1,0:T(8,128)(2,1)} %all-gather.7.cloned.1.call-done), kind=kOutput, calls=%fused_computation | convolution fusion | flops 4837343232 | bytes 11010048 | tf_op jit(solution)/shard_map/dot_general | solution.py:106
  267.4 45.6 %reduce-scatter.5.cloned.1.call-done = bf16[128,1536]{1,0:T(8,128)(2,1)} async-done(((bf16[1024,1536]{1,0:T(8,128)(2,1)}), bf16[128,1536]{1,0:T(8,128)(2,1)}) %reduce-scatter.5.cloned.1.call-update) | async-done | bytes 393232 | tf_op jit(solution)/shard_map/reduce_scatter | solution.py:107
  313.0 1.9 fusion.17
  (65 shorter events, 10.6 us)
Async XLA Ops:
  6.5 92.2 %copy-start = (bf16[192,1536]{1,0:T(8,128)(2,1)S(1)}, bf16[192,1536]{1,0:T(8,128)(2,1)}, u32[]{:S(2)}) copy-start(bf16[192,1536]{1,0:T(8,128)(2,1)} %param.22) | copy-start | bytes 1769476
  6.5 52.6 %all-gather.5.cloned.1.call-start = ((), (), s32[]{:S(2)}) async-start(), calls=%async_computation.2 | async-start | bytes 3538944 | tf_op jit(solution)/shard_map/all_gather | solution.py:75
  11.1 98.3 %all-gather.7.cloned.1.call-start = ((), (), s32[]{:S(2)}) async-start(), calls=%async_computation.3 | async-start | bytes 2433024 | tf_op jit(solution)/shard_map/all_gather | solution.py:76
  11.8 148.7 %all-gather.9.cloned.1.call-start = ((), (), s32[]{:S(2)}) async-start(), calls=%async_computation.4 | async-start | bytes 2433024 | tf_op jit(solution)/shard_map/all_gather | solution.py:77
  12.5 196.8 %reduce-scatter.3.cloned.1.call-start = ((), (), s32[]{:S(2)}) async-start(), calls=%async_computation.5 | async-start | bytes 3538944 | tf_op jit(solution)/shard_map/reduce_scatter | solution.py:98
  15.6 46.9 %copy-start.4 = (bf16[1536,192]{0,1:T(8,128)(2,1)S(1)}, bf16[1536,192]{0,1:T(8,128)(2,1)}, u32[]{:S(2)}) copy-start(bf16[1536,192]{0,1:T(8,128)(2,1)} %param.17) | copy-start | bytes 1769476
  59.1 3.4 %copy-start.3 = (bf16[1024,1536]{1,0:T(8,128)(2,1)S(1)}, bf16[1024,1536]{1,0:T(8,128)(2,1)}, u32[]{:S(2)}) copy-start(bf16[1024,1536]{1,0:T(8,128)(2,1)} %all-gather.5.cloned.1.call-done) | copy-start | bytes 9437188
  62.6 36.1 %copy-start.5 = (f32[192]{0:T(256)S(1)}, f32[192]{0:T(256)}, u32[]{:S(2)}) copy-start(f32[192]{0:T(256)} %param.21) | copy-start | bytes 2308
  62.6 36.1 %copy-start.6 = (f32[192]{0:T(256)S(1)}, f32[192]{0:T(256)}, u32[]{:S(2)}) copy-start(f32[192]{0:T(256)} %param.20) | copy-start | bytes 2308
  63.9 8.5 %collective-permute-start = (bf16[15,192]{0,1:T(8,128)(2,1)S(1)}, bf16[15,192]{0,1:T(8,128)(2,1)S(1)}, u32[]{:S(2)}, u32[]{:S(2)}) collective-permute-start(bf16[15,192]{0,1:T(8,128)(2,1)S(1)} %get-tuple-element.31), channel_id=1, source_target_pairs={{0,8},{8,16},{16,24},{24,32},{32,40},{40,48},{48,56},{56,64},{64,7... | collective-permute-start | bytes 17288 | tf_op jit(solution)/shard_map/ppermute | solution.py:16
  65.8 6.6 %collective-permute-start.1 = (bf16[15,192]{0,1:T(8,128)(2,1)S(1)}, bf16[15,192]{0,1:T(8,128)(2,1)S(1)}, u32[]{:S(2)}, u32[]{:S(2)}) collective-permute-start(bf16[15,192]{0,1:T(8,128)(2,1)S(1)} %get-tuple-element.32), channel_id=1, source_target_pairs={{8,0},{16,8},{24,16},{32,24},{40,32},{48,40},{56,48},{64,56},{72,6... | collective-permute-start | bytes 17288 | tf_op jit(solution)/shard_map/ppermute | solution.py:17
  78.3 1.2 collective-permute-start.2
  79.7 3.7 %collective-permute-start.3 = (f32[3,192]{1,0:T(4,128)S(1)}, f32[3,192]{1,0:T(4,128)S(1)}, u32[]{:S(2)}, u32[]{:S(2)}) collective-permute-start(f32[3,192]{1,0:T(4,128)S(1)} %pad_maximum_fusion.3), channel_id=1, source_target_pairs={{0,16},{8,24},{16,0},{24,8},{32,48},{40,56},{48,32},{56,40},{64,80... | collective-permute-start | bytes 6920 | tf_op jit(solution)/shard_map/ppermute | solution.py:46
  83.5 5.9 %collective-permute-start.4 = (f32[3,192]{1,0:T(4,128)S(1)}, f32[3,192]{1,0:T(4,128)S(1)}, u32[]{:S(2)}, u32[]{:S(2)}) collective-permute-start(f32[3,192]{1,0:T(4,128)S(1)} %pad_maximum_fusion.4), channel_id=1, source_target_pairs={{0,32},{8,40},{16,48},{24,56},{32,0},{40,8},{48,16},{56,24},{64,96... | collective-permute-start | bytes 6920 | tf_op jit(solution)/shard_map/ppermute | solution.py:46
  89.4 3.7 %collective-permute-start.5 = (f32[3,192]{1,0:T(4,128)S(1)}, f32[3,192]{1,0:T(4,128)S(1)}, u32[]{:S(2)}, u32[]{:S(2)}) collective-permute-start(f32[3,192]{1,0:T(4,128)S(1)} %pad_maximum_fusion.5), channel_id=1, source_target_pairs={{0,64},{8,72},{16,80},{24,88},{32,96},{40,104},{48,112},{56,120},{... | collective-permute-start | bytes 6920 | tf_op jit(solution)/shard_map/ppermute | solution.py:46
  93.2 5.5 %collective-permute-start.6 = (f32[3,192]{1,0:T(4,128)S(1)}, f32[3,192]{1,0:T(4,128)S(1)}, u32[]{:S(2)}, u32[]{:S(2)}) collective-permute-start(f32[3,192]{1,0:T(4,128)S(1)} %pad_maximum_fusion.6), channel_id=1, source_target_pairs={{0,128},{8,136},{16,144},{24,152},{32,160},{40,168},{48,176},{56,1... | collective-permute-start | bytes 6920 | tf_op jit(solution)/shard_map/ppermute | solution.py:46
  101.6 107.8 %copy-start.1 = (bf16[128,1536]{1,0:T(8,128)(2,1)S(1)}, bf16[128,1536]{1,0:T(8,128)(2,1)}, u32[]{:S(2)}) copy-start(bf16[128,1536]{1,0:T(8,128)(2,1)} %param.13) | copy-start | bytes 1179652
  101.6 109.2 %copy-start.2 = (f32[1536]{0:T(1024)S(1)}, f32[1536]{0:T(1024)}, u32[]{:S(2)}) copy-start(f32[1536]{0:T(1024)} %param.23) | copy-start | bytes 18436
  160.5 95.9 %all-gather.11.cloned.1.call-start = ((), (), s32[]{:S(2)}) async-start(), calls=%async_computation.6 | async-start | bytes 3538944 | tf_op jit(solution)/shard_map/all_gather | solution.py:103
  211.9 101.1 %reduce-scatter.5.cloned.1.call-start = ((), (), s32[]{:S(2)}) async-start(), calls=%async_computation.7 | async-start | bytes 3538944 | tf_op jit(solution)/shard_map/reduce_scatter | solution.py:107
Sparse Core Ops, SparseCore 0:
  11.2 47.9 all-gather.4
  61.7 47.5 all-gather.6
  111.8 48.5 all-gather.8
  162.9 46.4 reduce-scatter.2
  212.0 44.3 all-gather.10
  267.6 45.4 reduce-scatter.4

commit v2 on v1

--- a/solution.py
+++ b/solution.py
@@ -52,6 +52,51 @@
     return stats
 
 
+def gather_torus(pieces, axis):
+    size = lax.axis_size(axis)
+    cores, xs = 2, 4
+    ys = size // (cores * xs)
+
+    def coords(i):
+        return i // (cores * xs), (i // cores) % xs, i % cores
+
+    def index(y, x, c):
+        return (y * xs + x) * cores + c
+
+    me = lax.axis_index(axis)
+    my_c = me % cores
+    my_x = (me // cores) % xs
+    my_y = me // (cores * xs)
+
+    def shifted(value, move):
+        pairs = []
+        for i in range(size):
+            y, x, c = coords(i)
+            pairs.append((i, index(*move(y, x, c))))
+        return lax.ppermute(value, axis, pairs)
+
+    def ordered(own, received, mine, count):
+        slots = [own] + received
+        picks = []
+        for j in range(count):
+            k = (mine - j) % count
+            picked = slots[0]
+            for t in range(1, count):
+                picked = jnp.where(k == t, slots[t], picked)
+            picks.append(picked)
+        return picks
+
+    out = []
+    for piece in pieces:
+        other = shifted(piece, lambda y, x, c: (y, x, 1 - c))
+        pair = jnp.concatenate(ordered(piece, [other], my_c, cores), axis=0)
+        got = [shifted(pair, lambda y, x, c, d=d: (y, (x + d) % xs, c)) for d in range(1, xs)]
+        row = jnp.concatenate(ordered(pair, got, my_x, xs), axis=0)
+        got = [shifted(row, lambda y, x, c, d=d: ((y + d) % ys, x, c)) for d in range(1, ys)]
+        out.append(jnp.concatenate(ordered(row, got, my_y, ys), axis=0))
+    return out
+
+
 def shards(
     features,
     frame_mask,
@@ -73,8 +118,7 @@
     valid = ((frame_mask > 0) & (positions < total_length[0])).astype(jnp.float32)
     normed = layer_norm(features, norm_gain).astype(jnp.bfloat16)
     piece = lax.all_gather(normed, "tensor", axis=0, tiled=True)
-    up_whole = lax.all_gather(up_weight, "tm", axis=0, tiled=True)
-    down_whole = lax.all_gather(down_weight, "tm", axis=1, tiled=True)
+    up_whole, down_t = gather_torus([up_weight, down_weight.T], "tm")
     value = jnp.dot(piece, value_weight, preferred_element_type=jnp.float32)
     gate = jnp.dot(piece, gate_weight, preferred_element_type=jnp.float32)
     glu = (value * jax.nn.sigmoid(gate) * valid[:, None]).astype(jnp.bfloat16)
@@ -94,7 +138,7 @@
     scaled = centred * lax.rsqrt(var + 1e-05) * batch_gain + batch_bias
     swished = (scaled * jax.nn.sigmoid(scaled)).astype(jnp.bfloat16)
     conv_part = jnp.dot(swished, out_weight, preferred_element_type=jnp.float32)
-    conv_part, up_whole, down_whole = lax.optimization_barrier((conv_part, up_whole, down_whole))
+    conv_part, up_whole, down_t = lax.optimization_barrier((conv_part, up_whole, down_t))
     conv_out = lax.psum_scatter(
         conv_part.astype(jnp.bfloat16), "tensor", scatter_dimension=0, tiled=True
     ).astype(jnp.float32)
@@ -103,7 +147,9 @@
     feed_block = lax.all_gather(feed_normed, "tensor", axis=0, tiled=True)
     pre = jnp.dot(feed_block, up_whole, preferred_element_type=jnp.float32)
     hidden = (pre * jax.nn.sigmoid(pre)).astype(jnp.bfloat16)
-    partial_out = jnp.dot(hidden, down_whole, preferred_element_type=jnp.float32)
+    partial_out = lax.dot_general(
+        hidden, down_t, (((1,), (1,)), ((), ())), preferred_element_type=jnp.float32
+    )
     feed_out = lax.psum_scatter(
         partial_out.astype(jnp.bfloat16), "tensor", scatter_dimension=0, tiled=True
     ).astype(jnp.float32)

time: 322 us -> 282 us (0.88)
  waiting for transfers between devices: 253 us -> 186 us
  starting transfers between devices: 15.9 us -> 30.4 us
  other arithmetic: 16.4 us -> 26.2 us
    all_gather x2 -> x0, waiting for transfers between devices: 58.9 us -> none  [the longest x1 51.2 us: shards(): down_whole = lax.all_gather(down_weight, 'tm', axis=1, tiled=True)]
    all_gather x1, waiting for transfers between devices: 43.5 us -> 17.4 us  [shards(): piece = lax.all_gather(normed, 'tensor', axis=0, tiled=True)]
    ppermute x0 -> x14, waiting for transfers between devices: none -> 21.5 us  [shifted(): return lax.ppermute(value, axis, pairs)]
    ppermute x0 -> x14, starting transfers between devices: none -> 19.2 us  [shifted(): return lax.ppermute(value, axis, pairs)]
    select_n x0 -> x9, other arithmetic: none -> 5.62 us  [ordered(): picked = jnp.where(k == t, slots[t], picked)]
    concatenate x0 -> x6, other arithmetic: none -> 4.93 us  [the longest x2 3.16 us: gather_torus(): out.append(jnp.concatenate(ordered(row, got, my_y, ys), axis=0))]
    ppermute x5, starting transfers between devices: 10.1 us -> 5.56 us  [moments_over(): other = lax.ppermute(stats, axis, pairs)]
  transfers between devices with their start and end apart: 13 -> 25, of which waited for: 11 -> 13; matrix products, arithmetic and copies ran while one was open for 6% -> 9% of each run, Pallas kernels for 0% -> 0%
where the time goes in v2:
time: 282 us; the launch traced here: 281 us
  waiting for transfers between devices  186 us (66%)
  starting transfers between devices  30.4 us (11%)
  other arithmetic  26.2 us (9%)
  matrix products  18.4 us (7%)
  between operations  15.7 us (6%)
  local copies, waits for them, and re-layouts  4.64 us (2%)
    reduce_scatter x1, waiting for transfers between devices, shards(): lax.psum_scatter(conv_part.astype(jnp.bfloat16), 'tensor', scatter_dimens...  48.1 us
    reduce_scatter x1, waiting for transfers between devices, shards(): lax.psum_scatter(partial_out.astype(jnp.bfloat16), 'tensor', scatter_dime...  45.6 us
    all_gather x1, waiting for transfers between devices, shards(): feed_block = lax.all_gather(feed_normed, 'tensor', axis=0, tiled=True)  44.3 us
    ppermute x14, waiting for transfers between devices, shifted(): return lax.ppermute(value, axis, pairs)  21.5 us
    ppermute x14, starting transfers between devices, shifted(): return lax.ppermute(value, axis, pairs)  19.2 us
    all_gather x1, waiting for transfers between devices, shards(): piece = lax.all_gather(normed, 'tensor', axis=0, tiled=True)  17.4 us
    dot_general x1, matrix products, shards(): lax.dot_general(hidden, down_t, (((1,), (1,)), ((), ())), preferred_eleme...  11 us
    ppermute x5, waiting for transfers between devices, moments_over(): other = lax.ppermute(stats, axis, pairs)  9.01 us
  transfers between devices with their start and end apart: 25, of which 13 were waited for; matrix products, arithmetic and copies ran while one was open for 9% of the time, Pallas kernels for 0%

profile of v2, /device:TPU:2, one launch (start us, length us, event | category | flops | bytes accessed | tf_op | source)
XLA Modules:
  0.0 281.4 jit_solution(7204642507625720212)
XLA Ops:
  9.0 2.0 fusion.15
  18.2 2.8 %collective-permute-start.9 = (bf16[96,768]{1,0:T(8,128)(2,1)S(1)}, bf16[96,768]{1,0:T(8,128)(2,1)S(1)}, u32[]{:S(2)}, u32[]{:S(2)}) collective-permute-start(bf16[96,768]{1,0:T(8,128)(2,1)S(1)} %pad_maximum_fusion.6), channel_id=1, source_target_pairs={{0,32},{8,40},{16,48},{24,56},{32,0},{40,8},{48,16},{56,24},{64,96... | collective-permute-start | bytes 442376 | tf_op jit(solution)/shard_map/ppermute | solution.py:76
  24.4 1.7 collective-permute-start.17
  26.1 1.9 collective-permute-start.16
  30.7 2.9 %collective-permute-start.12 = (bf16[384,768]{1,0:T(8,128)(2,1)}, bf16[384,768]{1,0:T(8,128)(2,1)S(1)}, u32[]{:S(2)}, u32[]{:S(2)}) collective-permute-start(bf16[384,768]{1,0:T(8,128)(2,1)} %pad_maximum_fusion.2), channel_id=1, source_target_pairs={{0,128},{8,136},{16,144},{24,152},{32,160},{40,168},{48,176},{56,1... | collective-permute-start | bytes 1769480 | tf_op jit(solution)/shard_map/ppermute | solution.py:76
  37.5 2.9 %collective-permute-start.19 = (bf16[384,768]{1,0:T(8,128)(2,1)}, bf16[384,768]{1,0:T(8,128)(2,1)}, u32[]{:S(2)}, u32[]{:S(2)}) collective-permute-start(bf16[384,768]{1,0:T(8,128)(2,1)} %pad_maximum_fusion.3), channel_id=1, source_target_pairs={{0,128},{8,136},{16,144},{24,152},{32,160},{40,168},{48,176},{56,1... | collective-permute-start | bytes 1769480 | tf_op jit(solution)/shard_map/ppermute | solution.py:76
  41.8 17.4 %all-gather.3.cloned.1.call-done = bf16[1024,1536]{1,0:T(8,128)(2,1)} async-done(((bf16[128,1536]{1,0:T(8,128)(2,1)}), bf16[1024,1536]{1,0:T(8,128)(2,1)}) %all-gather.3.cloned.1.call-update) | async-done | bytes 3145744 | tf_op jit(solution)/shard_map/all_gather | solution.py:120
  59.2 3.4 %fusion.4 = f32[1024,192]{0,1:T(8,128)S(1)} fusion(bf16[1024,1536]{1,0:T(8,128)(2,1)} %all-gather.3.cloned.1.call-done, bf16[1536,192]{0,1:T(8,128)(2,1)} %param.18), kind=kOutput, calls=%fused_computation.38 | convolution fusion | flops 604569600 | bytes 4521984 | tf_op jit(solution)/shard_map/dot_general | solution.py:123
  64.1 9.3 %collective-permute-done.20 = bf16[384,768]{1,0:T(8,128)(2,1)S(1)} collective-permute-done((bf16[384,768]{1,0:T(8,128)(2,1)}, bf16[384,768]{1,0:T(8,128)(2,1)S(1)}, u32[]{:S(2)}, u32[]{:S(2)}) %collective-permute-start.20) | collective-permute-done | bytes 589856 | tf_op jit(solution)/shard_map/ppermute | solution.py:76
  73.9 10.3 %collective-permute-done.19 = bf16[384,768]{1,0:T(8,128)(2,1)} collective-permute-done((bf16[384,768]{1,0:T(8,128)(2,1)}, bf16[384,768]{1,0:T(8,128)(2,1)}, u32[]{:S(2)}, u32[]{:S(2)}) %collective-permute-start.19) | collective-permute-done | bytes 589856 | tf_op jit(solution)/shard_map/ppermute | solution.py:76
  84.2 1.9 collective-permute-start
  86.1 3.6 %collective-permute-start.1 = (bf16[15,192]{0,1:T(8,128)(2,1)S(1)}, bf16[15,192]{0,1:T(8,128)(2,1)S(1)}, u32[]{:S(2)}, u32[]{:S(2)}) collective-permute-start(bf16[15,192]{0,1:T(8,128)(2,1)S(1)} %get-tuple-element.46), channel_id=1, source_target_pairs={{8,0},{16,8},{24,16},{32,24},{40,32},{48,40},{56,48},{64,56},{72,6... | collective-permute-start | bytes 17288 | tf_op jit(solution)/shard_map/ppermute | solution.py:17
  89.8 1.7 select_select_fusion.3
  91.8 5.6 %multiply_reduce_fusion.1 = (f32[192]{0:T(256)S(1)}, f32[1024,192]{0,1:T(8,128)S(1)}) fusion(f32[1024]{0:T(1024)S(1)} %get-tuple-element.28, f32[192]{0:T(256)S(1)} %bitcast.83, bf16[15,192]{0,1:T(8,128)(2,1)S(1)} %collective-permute-done.1, bf16[1024,192]{0,1:T(8,128)(2,1)S(1)} %fusion.5, f32[192]{0:T(256)S(1)} %bitcast.84, f32[192]{0:T(256)S(1)} %bitcast.55, ...), kind=kLoop, calls=%fused_computation.60 | loop fusion | flops 36175680 | bytes 1219840 | tf_op jit(solution)/shard_map/reduce_sum | solution.py:130
  103.9 1.9 collective-permute-start.4
  106.2 2.9 %collective-permute-done.4 = f32[3,192]{1,0:T(4,128)S(1)} collective-permute-done((f32[3,192]{1,0:T(4,128)S(1)}, f32[3,192]{1,0:T(4,128)S(1)}, u32[]{:S(2)}, u32[]{:S(2)}) %collective-permute-start.4) | collective-permute-done | bytes 2336 | tf_op jit(solution)/shard_map/ppermute | solution.py:46
  111.2 1.7 collective-permute-done.5
  115.5 2.9 %collective-permute-done.6 = f32[3,192]{1,0:T(4,128)S(1)} collective-permute-done((f32[3,192]{1,0:T(4,128)S(1)}, f32[3,192]{1,0:T(4,128)S(1)}, u32[]{:S(2)}, u32[]{:S(2)}) %collective-permute-start.6) | collective-permute-done | bytes 2336 | tf_op jit(solution)/shard_map/ppermute | solution.py:46
  118.5 2.8 %fusion.18 = bf16[1024,1536]{1,0:T(8,128)(2,1)} fusion(bf16[192,1536]{1,0:T(8,128)(2,1)S(1)} %copy-done, f32[1024,192]{0,1:T(8,128)S(1)} %get-tuple-element.30, f32[192]{0:T(256)S(1)} %copy-done.35, f32[192]{0:T(256)S(1)} %copy-done.36, f32[192]{0:T(256)S(1)} %bitcast.86, f32[192]{0:T(256)S(1)} %bitcast.85), kind=kOutput, calls=%fused_computation.72 | convolution fusion | flops 605749248 | bytes 4525056 | tf_op jit(solution)/shard_map/dot_general | solution.py:140
  121.4 48.1 %reduce-scatter.3.cloned.1.call-done = bf16[128,1536]{1,0:T(8,128)(2,1)} async-done(((bf16[1024,1536]{1,0:T(8,128)(2,1)}), bf16[128,1536]{1,0:T(8,128)(2,1)}) %reduce-scatter.3.cloned.1.call-update) | async-done | bytes 393232 | tf_op jit(solution)/shard_map/reduce_scatter | solution.py:142
  172.1 44.3 %all-gather.5.cloned.1.call-done = bf16[1024,1536]{1,0:T(8,128)(2,1)} async-done(((bf16[128,1536]{1,0:T(8,128)(2,1)}), bf16[1024,1536]{1,0:T(8,128)(2,1)}) %all-gather.5.cloned.1.call-update) | async-done | bytes 3145744 | tf_op jit(solution)/shard_map/all_gather | solution.py:147
  216.4 11.0 %convolution_convert_fusion = bf16[1024,1536]{1,0:T(8,128)(2,1)} fusion(bf16[1536,768]{1,0:T(8,128)(2,1)} %pad_maximum_fusion.1, bf16[1024,1536]{1,0:T(8,128)(2,1)} %all-gather.5.cloned.1.call-done, bf16[1536,768]{1,0:T(8,128)(2,1)} %pad_maximum_fusion), kind=kOutput, calls=%fused_computation | convolution fusion | flops 4837343232 | bytes 11010048 | tf_op jit(solution)/shard_map/dot_general | solution.py:150
  227.4 45.6 %reduce-scatter.5.cloned.1.call-done = bf16[128,1536]{1,0:T(8,128)(2,1)} async-done(((bf16[1024,1536]{1,0:T(8,128)(2,1)}), bf16[128,1536]{1,0:T(8,128)(2,1)}) %reduce-scatter.5.cloned.1.call-update) | async-done | bytes 393232 | tf_op jit(solution)/shard_map/reduce_scatter | solution.py:153
  273.0 1.9 fusion.17
  (162 shorter events, 35.2 us)
Async XLA Ops:
  6.5 52.6 %all-gather.3.cloned.1.call-start = ((), (), s32[]{:S(2)}) async-start(), calls=%async_computation.2 | async-start | bytes 3538944 | tf_op jit(solution)/shard_map/all_gather | solution.py:120
  11.1 158.4 %reduce-scatter.3.cloned.1.call-start = ((), (), s32[]{:S(2)}) async-start(), calls=%async_computation.3 | async-start | bytes 3538944 | tf_op jit(solution)/shard_map/reduce_scatter | solution.py:142
  11.1 4.5 %collective-permute-start.14 = (bf16[48,768]{1,0:T(8,128)(2,1)}, bf16[48,768]{1,0:T(8,128)(2,1)S(1)}, u32[]{:S(2)}, u32[]{:S(2)}) collective-permute-start(bf16[48,768]{1,0:T(8,128)(2,1)} %bitcast.49), channel_id=1, source_target_pairs={{0,8},{8,0},{16,24},{24,16},{32,40},{40,32},{48,56},{56,48},{64,72... | collective-permute-start | bytes 221192 | tf_op jit(solution)/shard_map/ppermute | solution.py:76
  11.2 4.4 %collective-permute-start.7 = (bf16[48,768]{1,0:T(8,128)(2,1)}, bf16[48,768]{1,0:T(8,128)(2,1)S(1)}, u32[]{:S(2)}, u32[]{:S(2)}) collective-permute-start(bf16[48,768]{1,0:T(8,128)(2,1)} %param.24), channel_id=1, source_target_pairs={{0,8},{8,0},{16,24},{24,16},{32,40},{40,32},{48,56},{56,48},{64,72... | collective-permute-start | bytes 221192 | tf_op jit(solution)/shard_map/ppermute | solution.py:76
  16.6 11.3 %collective-permute-start.10 = (bf16[96,768]{1,0:T(8,128)(2,1)S(1)}, bf16[96,768]{1,0:T(8,128)(2,1)S(1)}, u32[]{:S(2)}, u32[]{:S(2)}) collective-permute-start(bf16[96,768]{1,0:T(8,128)(2,1)S(1)} %pad_maximum_fusion.6), channel_id=1, source_target_pairs={{0,16},{8,24},{16,32},{24,40},{32,48},{40,56},{48,0},{56,8},{64,80... | collective-permute-start | bytes 442376 | tf_op jit(solution)/shard_map/ppermute | solution.py:76
  18.2 11.2 %collective-permute-start.9 = (bf16[96,768]{1,0:T(8,128)(2,1)S(1)}, bf16[96,768]{1,0:T(8,128)(2,1)S(1)}, u32[]{:S(2)}, u32[]{:S(2)}) collective-permute-start(bf16[96,768]{1,0:T(8,128)(2,1)S(1)} %pad_maximum_fusion.6), channel_id=1, source_target_pairs={{0,32},{8,40},{16,48},{24,56},{32,0},{40,8},{48,16},{56,24},{64,96... | collective-permute-start | bytes 442376 | tf_op jit(solution)/shard_map/ppermute | solution.py:76
  21.1 8.4 %collective-permute-start.8 = (bf16[96,768]{1,0:T(8,128)(2,1)S(1)}, bf16[96,768]{1,0:T(8,128)(2,1)S(1)}, u32[]{:S(2)}, u32[]{:S(2)}) collective-permute-start(bf16[96,768]{1,0:T(8,128)(2,1)S(1)} %pad_maximum_fusion.6), channel_id=1, source_target_pairs={{0,48},{8,56},{16,0},{24,8},{32,16},{40,24},{48,32},{56,40},{64,11... | collective-permute-start | bytes 442376 | tf_op jit(solution)/shard_map/ppermute | solution.py:76
  24.4 9.2 %collective-permute-start.17 = (bf16[96,768]{1,0:T(8,128)(2,1)S(1)}, bf16[96,768]{1,0:T(8,128)(2,1)S(1)}, u32[]{:S(2)}, u32[]{:S(2)}) collective-permute-start(bf16[96,768]{1,0:T(8,128)(2,1)S(1)} %pad_maximum_fusion.7), channel_id=1, source_target_pairs={{0,16},{8,24},{16,32},{24,40},{32,48},{40,56},{48,0},{56,8},{64,80... | collective-permute-start | bytes 442376 | tf_op jit(solution)/shard_map/ppermute | solution.py:76
  26.1 7.9 %collective-permute-start.16 = (bf16[96,768]{1,0:T(8,128)(2,1)S(1)}, bf16[96,768]{1,0:T(8,128)(2,1)S(1)}, u32[]{:S(2)}, u32[]{:S(2)}) collective-permute-start(bf16[96,768]{1,0:T(8,128)(2,1)S(1)} %pad_maximum_fusion.7), channel_id=1, source_target_pairs={{0,32},{8,40},{16,48},{24,56},{32,0},{40,8},{48,16},{56,24},{64,96... | collective-permute-start | bytes 442376 | tf_op jit(solution)/shard_map/ppermute | solution.py:76
  28.0 7.5 %collective-permute-start.15 = (bf16[96,768]{1,0:T(8,128)(2,1)S(1)}, bf16[96,768]{1,0:T(8,128)(2,1)S(1)}, u32[]{:S(2)}, u32[]{:S(2)}) collective-permute-start(bf16[96,768]{1,0:T(8,128)(2,1)S(1)} %pad_maximum_fusion.7), channel_id=1, source_target_pairs={{0,48},{8,56},{16,0},{24,8},{32,16},{40,24},{48,32},{56,40},{64,11... | collective-permute-start | bytes 442376 | tf_op jit(solution)/shard_map/ppermute | solution.py:76
  30.5 68.7 %collective-permute-start.13 = (bf16[384,768]{1,0:T(8,128)(2,1)}, bf16[384,768]{1,0:T(8,128)(2,1)S(1)}, u32[]{:S(2)}, u32[]{:S(2)}) collective-permute-start(bf16[384,768]{1,0:T(8,128)(2,1)} %pad_maximum_fusion.2), channel_id=1, source_target_pairs={{0,64},{8,72},{16,80},{24,88},{32,96},{40,104},{48,112},{56,120},{... | collective-permute-start | bytes 1769480 | tf_op jit(solution)/shard_map/ppermute | solution.py:76
  30.7 68.5 %collective-permute-start.12 = (bf16[384,768]{1,0:T(8,128)(2,1)}, bf16[384,768]{1,0:T(8,128)(2,1)S(1)}, u32[]{:S(2)}, u32[]{:S(2)}) collective-permute-start(bf16[384,768]{1,0:T(8,128)(2,1)} %pad_maximum_fusion.2), channel_id=1, source_target_pairs={{0,128},{8,136},{16,144},{24,152},{32,160},{40,168},{48,176},{56,1... | collective-permute-start | bytes 1769480 | tf_op jit(solution)/shard_map/ppermute | solution.py:76
  36.6 36.8 %collective-permute-start.20 = (bf16[384,768]{1,0:T(8,128)(2,1)}, bf16[384,768]{1,0:T(8,128)(2,1)S(1)}, u32[]{:S(2)}, u32[]{:S(2)}) collective-permute-start(bf16[384,768]{1,0:T(8,128)(2,1)} %pad_maximum_fusion.3), channel_id=1, source_target_pairs={{0,64},{8,72},{16,80},{24,88},{32,96},{40,104},{48,112},{56,120},{... | collective-permute-start | bytes 1769480 | tf_op jit(solution)/shard_map/ppermute | solution.py:76
  37.5 46.7 %collective-permute-start.19 = (bf16[384,768]{1,0:T(8,128)(2,1)}, bf16[384,768]{1,0:T(8,128)(2,1)}, u32[]{:S(2)}, u32[]{:S(2)}) collective-permute-start(bf16[384,768]{1,0:T(8,128)(2,1)} %pad_maximum_fusion.3), channel_id=1, source_target_pairs={{0,128},{8,136},{16,144},{24,152},{32,160},{40,168},{48,176},{56,1... | collective-permute-start | bytes 1769480 | tf_op jit(solution)/shard_map/ppermute | solution.py:76
  40.4 45.7 %collective-permute-start.18 = (bf16[384,768]{1,0:T(8,128)(2,1)}, bf16[384,768]{1,0:T(8,128)(2,1)}, u32[]{:S(2)}, u32[]{:S(2)}) collective-permute-start(bf16[384,768]{1,0:T(8,128)(2,1)} %pad_maximum_fusion.3), channel_id=1, source_target_pairs={{0,192},{8,200},{16,208},{24,216},{32,224},{40,232},{48,240},{56,2... | collective-permute-start | bytes 1769480 | tf_op jit(solution)/shard_map/ppermute | solution.py:76
  73.4 25.8 %collective-permute-start.11 = (bf16[384,768]{1,0:T(8,128)(2,1)}, bf16[384,768]{1,0:T(8,128)(2,1)S(1)}, u32[]{:S(2)}, u32[]{:S(2)}) collective-permute-start(bf16[384,768]{1,0:T(8,128)(2,1)} %pad_maximum_fusion.2), channel_id=1, source_target_pairs={{0,192},{8,200},{16,208},{24,216},{32,224},{40,232},{48,240},{56,2... | collective-permute-start | bytes 1769480 | tf_op jit(solution)/shard_map/ppermute | solution.py:76
  84.2 7.3 %collective-permute-start = (bf16[15,192]{0,1:T(8,128)(2,1)S(1)}, bf16[15,192]{0,1:T(8,128)(2,1)S(1)}, u32[]{:S(2)}, u32[]{:S(2)}) collective-permute-start(bf16[15,192]{0,1:T(8,128)(2,1)S(1)} %get-tuple-element.45), channel_id=1, source_target_pairs={{0,8},{8,16},{16,24},{24,32},{32,40},{40,48},{48,56},{56,64},{64,7... | collective-permute-start | bytes 17288 | tf_op jit(solution)/shard_map/ppermute | solution.py:16
  86.1 5.4 %collective-permute-start.1 = (bf16[15,192]{0,1:T(8,128)(2,1)S(1)}, bf16[15,192]{0,1:T(8,128)(2,1)S(1)}, u32[]{:S(2)}, u32[]{:S(2)}) collective-permute-start(bf16[15,192]{0,1:T(8,128)(2,1)S(1)} %get-tuple-element.46), channel_id=1, source_target_pairs={{8,0},{16,8},{24,16},{32,24},{40,32},{48,40},{56,48},{64,56},{72,6... | collective-permute-start | bytes 17288 | tf_op jit(solution)/shard_map/ppermute | solution.py:17
  100.1 3.7 %collective-permute-start.3 = (f32[3,192]{1,0:T(4,128)S(1)}, f32[3,192]{1,0:T(4,128)S(1)}, u32[]{:S(2)}, u32[]{:S(2)}) collective-permute-start(f32[3,192]{1,0:T(4,128)S(1)} %pad_maximum_fusion.9), channel_id=1, source_target_pairs={{0,16},{8,24},{16,0},{24,8},{32,48},{40,56},{48,32},{56,40},{64,80... | collective-permute-start | bytes 6920 | tf_op jit(solution)/shard_map/ppermute | solution.py:46
  103.9 5.2 %collective-permute-start.4 = (f32[3,192]{1,0:T(4,128)S(1)}, f32[3,192]{1,0:T(4,128)S(1)}, u32[]{:S(2)}, u32[]{:S(2)}) collective-permute-start(f32[3,192]{1,0:T(4,128)S(1)} %pad_maximum_fusion.10), channel_id=1, source_target_pairs={{0,32},{8,40},{16,48},{24,56},{32,0},{40,8},{48,16},{56,24},{64,96... | collective-permute-start | bytes 6920 | tf_op jit(solution)/shard_map/ppermute | solution.py:46
  109.2 3.7 %collective-permute-start.5 = (f32[3,192]{1,0:T(4,128)S(1)}, f32[3,192]{1,0:T(4,128)S(1)}, u32[]{:S(2)}, u32[]{:S(2)}) collective-permute-start(f32[3,192]{1,0:T(4,128)S(1)} %pad_maximum_fusion.11), channel_id=1, source_target_pairs={{0,64},{8,72},{16,80},{24,88},{32,96},{40,104},{48,112},{56,120},{... | collective-permute-start | bytes 6920 | tf_op jit(solution)/shard_map/ppermute | solution.py:46
  112.9 5.4 %collective-permute-start.6 = (f32[3,192]{1,0:T(4,128)S(1)}, f32[3,192]{1,0:T(4,128)S(1)}, u32[]{:S(2)}, u32[]{:S(2)}) collective-permute-start(f32[3,192]{1,0:T(4,128)S(1)} %pad_maximum_fusion.12), channel_id=1, source_target_pairs={{0,128},{8,136},{16,144},{24,152},{32,160},{40,168},{48,176},{56,1... | collective-permute-start | bytes 6920 | tf_op jit(solution)/shard_map/ppermute | solution.py:46
  121.3 95.0 %all-gather.5.cloned.1.call-start = ((), (), s32[]{:S(2)}) async-start(), calls=%async_computation.4 | async-start | bytes 3538944 | tf_op jit(solution)/shard_map/all_gather | solution.py:147
  172.0 101.0 %reduce-scatter.5.cloned.1.call-start = ((), (), s32[]{:S(2)}) async-start(), calls=%async_computation.5 | async-start | bytes 3538944 | tf_op jit(solution)/shard_map/reduce_scatter | solution.py:153
  (38 other events, 1031.3 us)
Sparse Core Ops, SparseCore 0:
  11.2 47.9 all-gather.2
  121.4 47.9 reduce-scatter.2
  172.1 44.1 all-gather.4
  227.5 45.4 reduce-scatter.4

commit v3 on v2

--- a/solution.py
+++ b/solution.py
@@ -118,6 +118,7 @@
     valid = ((frame_mask > 0) & (positions < total_length[0])).astype(jnp.float32)
     normed = layer_norm(features, norm_gain).astype(jnp.bfloat16)
     piece = lax.all_gather(normed, "tensor", axis=0, tiled=True)
+    out_whole = lax.all_gather(out_weight, "tensor", axis=0, tiled=True)
     up_whole, down_t = gather_torus([up_weight, down_weight.T], "tm")
     value = jnp.dot(piece, value_weight, preferred_element_type=jnp.float32)
     gate = jnp.dot(piece, gate_weight, preferred_element_type=jnp.float32)
@@ -137,12 +138,10 @@
     var = m2 / count
     scaled = centred * lax.rsqrt(var + 1e-05) * batch_gain + batch_bias
     swished = (scaled * jax.nn.sigmoid(scaled)).astype(jnp.bfloat16)
-    conv_part = jnp.dot(swished, out_weight, preferred_element_type=jnp.float32)
-    conv_part, up_whole, down_t = lax.optimization_barrier((conv_part, up_whole, down_t))
-    conv_out = lax.psum_scatter(
-        conv_part.astype(jnp.bfloat16), "tensor", scatter_dimension=0, tiled=True
-    ).astype(jnp.float32)
+    own_swished = lax.all_to_all(swished, "tensor", 0, 1, tiled=True)
+    conv_out = jnp.dot(own_swished, out_whole, preferred_element_type=jnp.float32)
     mid = (features.astype(jnp.float32) + conv_out).astype(jnp.bfloat16)
+    mid, up_whole, down_t = lax.optimization_barrier((mid, up_whole, down_t))
     feed_normed = layer_norm(mid, feed_gain).astype(jnp.bfloat16)
     feed_block = lax.all_gather(feed_normed, "tensor", axis=0, tiled=True)
     pre = jnp.dot(feed_block, up_whole, preferred_element_type=jnp.float32)

time: 282 us -> 253 us (0.90)
  waiting for transfers between devices: 186 us -> 149 us
  starting transfers between devices: 30.4 us -> 38.9 us
    reduce_scatter x1 -> x0, waiting for transfers between devices: 48.1 us -> none  [shards(): lax.psum_scatter(conv_part.astype(jnp.bfloat16), 'tensor', scatter_dimens...]
    all_gather x1, waiting for transfers between devices: 17.4 us -> 28.1 us  [shards(): piece = lax.all_gather(normed, 'tensor', axis=0, tiled=True)]
    all_to_all x0 -> x1, waiting for transfers between devices: none -> 8.43 us  [shards(): own_swished = lax.all_to_all(swished, 'tensor', 0, 1, tiled=True)]
    ppermute x5, waiting for transfers between devices: 9.01 us -> 3.97 us  [moments_over(): other = lax.ppermute(stats, axis, pairs)]
    all_to_all x0 -> x1, starting transfers between devices: none -> 4.25 us  [shards(): own_swished = lax.all_to_all(swished, 'tensor', 0, 1, tiled=True)]
    ppermute x5, starting transfers between devices: 5.56 us -> 8.84 us  [moments_over(): other = lax.ppermute(stats, axis, pairs)]
    all_gather x1, waiting for transfers between devices: 44.3 us -> 41.4 us  [shards(): feed_block = lax.all_gather(feed_normed, 'tensor', axis=0, tiled=True)]
  transfers between devices with their start and end apart: 25 -> 26, of which waited for: 13 -> 11; matrix products, arithmetic and copies ran while one was open for 9% -> 10% of each run, Pallas kernels for 0% -> 0%
where the time goes in v3:
time: 253 us; the launch traced here: 252 us
  waiting for transfers between devices  149 us (59%)
  starting transfers between devices  38.9 us (15%)
  other arithmetic  26.3 us (10%)
  matrix products  18.8 us (7%)
  between operations  16.1 us (6%)
  local copies, waits for them, and re-layouts  3.37 us (1%)
    reduce_scatter x1, waiting for transfers between devices, shards(): lax.psum_scatter(partial_out.astype(jnp.bfloat16), 'tensor', scatter_dime...  45.6 us
    all_gather x1, waiting for transfers between devices, shards(): feed_block = lax.all_gather(feed_normed, 'tensor', axis=0, tiled=True)  41.4 us
    all_gather x1, waiting for transfers between devices, shards(): piece = lax.all_gather(normed, 'tensor', axis=0, tiled=True)  28.1 us
    ppermute x14, starting transfers between devices, shifted(): return lax.ppermute(value, axis, pairs)  20 us
    ppermute x14, waiting for transfers between devices, shifted(): return lax.ppermute(value, axis, pairs)  19.8 us
    dot_general x1, matrix products, shards(): lax.dot_general(hidden, down_t, (((1,), (1,)), ((), ())), preferred_eleme...  11 us
    ppermute x5, starting transfers between devices, moments_over(): other = lax.ppermute(stats, axis, pairs)  8.84 us
    all_to_all x1, waiting for transfers between devices, shards(): own_swished = lax.all_to_all(swished, 'tensor', 0, 1, tiled=True)  8.43 us
  transfers between devices with their start and end apart: 26, of which 11 were waited for; matrix products, arithmetic and copies ran while one was open for 10% of the time, Pallas kernels for 0%

profile of v3, /device:TPU:2, one launch (start us, length us, event | category | flops | bytes accessed | tf_op | source)
XLA Modules:
  0.0 252.3 jit_solution(13386784746913609993)
XLA Ops:
  9.1 2.0 fusion.16
  13.9 2.3 collective-permute-start.15
  17.0 1.8 collective-permute-start.17
  26.7 3.8 %collective-permute-start.18 = (bf16[384,768]{1,0:T(8,128)(2,1)}, bf16[384,768]{1,0:T(8,128)(2,1)S(1)}, u32[]{:S(2)}, u32[]{:S(2)}) collective-permute-start(bf16[384,768]{1,0:T(8,128)(2,1)} %pad_maximum_fusion.3), channel_id=1, source_target_pairs={{0,192},{8,200},{16,208},{24,216},{32,224},{40,232},{48,240},{56,2... | collective-permute-start | bytes 1769480 | tf_op jit(solution)/shard_map/ppermute | solution.py:76
  31.1 28.1 %all-gather.4.cloned.1.call-done = bf16[1024,1536]{1,0:T(8,128)(2,1)} async-done(((bf16[128,1536]{1,0:T(8,128)(2,1)}), bf16[1024,1536]{1,0:T(8,128)(2,1)}) %all-gather.4.cloned.1.call-update) | async-done | bytes 3145744 | tf_op jit(solution)/shard_map/all_gather | solution.py:120
  59.2 3.3 %fusion.5 = f32[1024,192]{0,1:T(8,128)S(1)} fusion(bf16[1024,1536]{1,0:T(8,128)(2,1)} %all-gather.4.cloned.1.call-done, bf16[1536,192]{0,1:T(8,128)(2,1)S(1)} %copy-done), kind=kOutput, calls=%fused_computation.40 | convolution fusion | flops 604569600 | bytes 4521984 | tf_op jit(solution)/shard_map/dot_general | solution.py:124
  65.6 1.9 collective-permute-start
  67.6 3.8 %collective-permute-start.1 = (bf16[15,192]{0,1:T(8,128)(2,1)S(1)}, bf16[15,192]{0,1:T(8,128)(2,1)S(1)}, u32[]{:S(2)}, u32[]{:S(2)}) collective-permute-start(bf16[15,192]{0,1:T(8,128)(2,1)S(1)} %get-tuple-element.44), channel_id=1, source_target_pairs={{8,0},{16,8},{24,16},{32,24},{40,32},{48,40},{56,48},{64,56},{72,6... | collective-permute-start | bytes 17288 | tf_op jit(solution)/shard_map/ppermute | solution.py:17
  73.2 5.6 %multiply_reduce_fusion.1 = (f32[192]{0:T(256)S(1)}, f32[1024,192]{0,1:T(8,128)S(1)}) fusion(f32[1024]{0:T(1024)S(1)} %get-tuple-element.26, f32[192]{0:T(256)S(1)} %bitcast.92, bf16[15,192]{0,1:T(8,128)(2,1)S(1)} %collective-permute-done.1, bf16[1024,192]{0,1:T(8,128)(2,1)S(1)} %fusion.6, f32[192]{0:T(256)S(1)} %bitcast.93, f32[192]{0:T(256)S(1)} %bitcast.64, ...), kind=kLoop, calls=%fused_computation.60 | loop fusion | flops 36175680 | bytes 1219840 | tf_op jit(solution)/shard_map/reduce_sum | solution.py:131
  79.2 2.0 collective-permute-start.2
  82.8 2.3 collective-permute-start.11
  85.8 2.7 %collective-permute-start.12 = (bf16[384,768]{1,0:T(8,128)(2,1)S(1)}, bf16[384,768]{1,0:T(8,128)(2,1)S(1)}, u32[]{:S(2)}, u32[]{:S(2)}) collective-permute-start(bf16[384,768]{1,0:T(8,128)(2,1)S(1)} %pad_maximum_fusion.2), channel_id=1, source_target_pairs={{0,128},{8,136},{16,144},{24,152},{32,160},{40,168},{48,176},{56,1... | collective-permute-start | bytes 1769480 | tf_op jit(solution)/shard_map/ppermute | solution.py:76
  88.8 2.9 %collective-permute-start.4 = (f32[3,192]{1,0:T(4,128)S(1)}, f32[3,192]{1,0:T(4,128)S(1)}, u32[]{:S(2)}, u32[]{:S(2)}) collective-permute-start(f32[3,192]{1,0:T(4,128)S(1)} %pad_maximum_fusion.10), channel_id=1, source_target_pairs={{0,32},{8,40},{16,48},{24,56},{32,0},{40,8},{48,16},{56,24},{64,96... | collective-permute-start | bytes 6920 | tf_op jit(solution)/shard_map/ppermute | solution.py:46
  95.1 15.3 %collective-permute-done.11 = bf16[384,768]{1,0:T(8,128)(2,1)S(1)} collective-permute-done((bf16[384,768]{1,0:T(8,128)(2,1)S(1)}, bf16[384,768]{1,0:T(8,128)(2,1)S(1)}, u32[]{:S(2)}, u32[]{:S(2)}) %collective-permute-start.11) | collective-permute-done | bytes 589856 | tf_op jit(solution)/shard_map/ppermute | solution.py:76
  110.4 4.4 %collective-permute-done.13 = bf16[384,768]{1,0:T(8,128)(2,1)S(1)} collective-permute-done((bf16[384,768]{1,0:T(8,128)(2,1)S(1)}, bf16[384,768]{1,0:T(8,128)(2,1)S(1)}, u32[]{:S(2)}, u32[]{:S(2)}) %collective-permute-start.13) | collective-permute-done | bytes 589856 | tf_op jit(solution)/shard_map/ppermute | solution.py:76
  116.2 2.2 collective-permute-start.6
  122.9 4.3 %all-to-all-start = ((bf16[8,128,192]{1,2,0:T(8,128)(2,1)}), bf16[8,128,192]{1,2,0:T(8,128)(2,1)}, u32[]{:S(2)}, u32[]{:S(2)}) async-start(bf16[8,128,192]{1,2,0:T(8,128)(2,1)} %copy_bitcast_fusion), calls=%async_computation | async-start | bytes 786432 | tf_op jit(solution)/shard_map/all_to_all | solution.py:141
  127.2 2.8 %pad_maximum_fusion.1 = bf16[1536,768]{1,0:T(8,128)(2,1)} fusion(bf16[384,768]{1,0:T(8,128)(2,1)} %get-tuple-element.30, bf16[384,768]{1,0:T(8,128)(2,1)S(1)} %get-tuple-element.32, bf16[384,768]{1,0:T(8,128)(2,1)S(1)} %get-tuple-element.31, bf16[384,768]{1,0:T(8,128)(2,1)S(1)} %copy-done.3), kind=kLoop, calls=%fused_computation.5 | loop fusion | flops 9437184 | bytes 4718592 | tf_op jit(solution)/shard_map/concatenate | solution.py:96
  132.6 8.4 %all-to-all-done = bf16[8,128,192]{1,2,0:T(8,128)(2,1)} async-done(((bf16[8,128,192]{1,2,0:T(8,128)(2,1)}), bf16[8,128,192]{1,2,0:T(8,128)(2,1)}, u32[]{:S(2)}, u32[]{:S(2)}) %all-to-all-start) | async-done | bytes 393248 | tf_op jit(solution)/shard_map/all_to_all | solution.py:141
  141.1 3.3 %fusion = bf16[128,1536]{1,0:T(8,128)(2,1)S(1)} fusion(bf16[128,1536]{0,1:T(8,128)(2,1)} %bitcast.37, bf16[1536,1536]{1,0:T(8,128)(2,1)} %all-gather.6.cloned.1.call-done, bf16[128,1536]{1,0:T(8,128)(2,1)S(1)} %copy-done.1), kind=kOutput, calls=%fused_computation.3 | convolution fusion | flops 604569600 | bytes 5898240 | tf_op jit(solution)/shard_map/dot_general | solution.py:142
  145.9 41.4 %all-gather.8.cloned.1.call-done = bf16[1024,1536]{1,0:T(8,128)(2,1)} async-done(((bf16[128,1536]{1,0:T(8,128)(2,1)}), bf16[1024,1536]{1,0:T(8,128)(2,1)}) %all-gather.8.cloned.1.call-update) | async-done | bytes 3145744 | tf_op jit(solution)/shard_map/all_gather | solution.py:146
  187.3 11.0 %convolution_convert_fusion = bf16[1024,1536]{1,0:T(8,128)(2,1)} fusion(bf16[1536,768]{1,0:T(8,128)(2,1)} %pad_maximum_fusion.1, bf16[1024,1536]{1,0:T(8,128)(2,1)} %all-gather.8.cloned.1.call-done, bf16[1536,768]{1,0:T(8,128)(2,1)} %pad_maximum_fusion), kind=kOutput, calls=%fused_computation | convolution fusion | flops 4837343232 | bytes 11010048 | tf_op jit(solution)/shard_map/dot_general | solution.py:149
  198.4 45.6 %reduce-scatter.2.cloned.1.call-done = bf16[128,1536]{1,0:T(8,128)(2,1)} async-done(((bf16[1024,1536]{1,0:T(8,128)(2,1)}), bf16[128,1536]{1,0:T(8,128)(2,1)}) %reduce-scatter.2.cloned.1.call-update) | async-done | bytes 393232 | tf_op jit(solution)/shard_map/reduce_scatter | solution.py:152
  244.0 1.9 fusion.17
  (195 shorter events, 33.0 us)
Async XLA Ops:
  6.5 52.6 %all-gather.4.cloned.1.call-start = ((), (), s32[]{:S(2)}) async-start(), calls=%async_computation.2 | async-start | bytes 3538944 | tf_op jit(solution)/shard_map/all_gather | solution.py:120
  11.1 130.0 %all-gather.6.cloned.1.call-start = ((), (), s32[]{:S(2)}) async-start(), calls=%async_computation.3 | async-start | bytes 5308416 | tf_op jit(solution)/shard_map/all_gather | solution.py:121
  13.9 10.2 %collective-permute-start.15 = (bf16[96,768]{1,0:T(8,128)(2,1)S(1)}, bf16[96,768]{1,0:T(8,128)(2,1)S(1)}, u32[]{:S(2)}, u32[]{:S(2)}) collective-permute-start(bf16[96,768]{1,0:T(8,128)(2,1)S(1)} %pad_maximum_fusion.7), channel_id=1, source_target_pairs={{0,48},{8,56},{16,0},{24,8},{32,16},{40,24},{48,32},{56,40},{64,11... | collective-permute-start | bytes 442376 | tf_op jit(solution)/shard_map/ppermute | solution.py:76
  16.3 9.3 %collective-permute-start.16 = (bf16[96,768]{1,0:T(8,128)(2,1)S(1)}, bf16[96,768]{1,0:T(8,128)(2,1)S(1)}, u32[]{:S(2)}, u32[]{:S(2)}) collective-permute-start(bf16[96,768]{1,0:T(8,128)(2,1)S(1)} %pad_maximum_fusion.7), channel_id=1, source_target_pairs={{0,32},{8,40},{16,48},{24,56},{32,0},{40,8},{48,16},{56,24},{64,96... | collective-permute-start | bytes 442376 | tf_op jit(solution)/shard_map/ppermute | solution.py:76
  17.0 8.6 %collective-permute-start.17 = (bf16[96,768]{1,0:T(8,128)(2,1)S(1)}, bf16[96,768]{1,0:T(8,128)(2,1)S(1)}, u32[]{:S(2)}, u32[]{:S(2)}) collective-permute-start(bf16[96,768]{1,0:T(8,128)(2,1)S(1)} %pad_maximum_fusion.7), channel_id=1, source_target_pairs={{0,16},{8,24},{16,32},{24,40},{32,48},{40,56},{48,0},{56,8},{64,80... | collective-permute-start | bytes 442376 | tf_op jit(solution)/shard_map/ppermute | solution.py:76
  22.0 42.0 %collective-permute-start.10 = (bf16[96,768]{1,0:T(8,128)(2,1)S(1)}, bf16[96,768]{1,0:T(8,128)(2,1)S(1)}, u32[]{:S(2)}, u32[]{:S(2)}) collective-permute-start(bf16[96,768]{1,0:T(8,128)(2,1)S(1)} %pad_maximum_fusion.6), channel_id=1, source_target_pairs={{0,16},{8,24},{16,32},{24,40},{32,48},{40,56},{48,0},{56,8},{64,80... | collective-permute-start | bytes 442376 | tf_op jit(solution)/shard_map/ppermute | solution.py:76
  23.7 41.9 %collective-permute-start.8 = (bf16[96,768]{1,0:T(8,128)(2,1)S(1)}, bf16[96,768]{1,0:T(8,128)(2,1)S(1)}, u32[]{:S(2)}, u32[]{:S(2)}) collective-permute-start(bf16[96,768]{1,0:T(8,128)(2,1)S(1)} %pad_maximum_fusion.6), channel_id=1, source_target_pairs={{0,48},{8,56},{16,0},{24,8},{32,16},{40,24},{48,32},{56,40},{64,11... | collective-permute-start | bytes 442376 | tf_op jit(solution)/shard_map/ppermute | solution.py:76
  24.1 43.4 %collective-permute-start.9 = (bf16[96,768]{1,0:T(8,128)(2,1)S(1)}, bf16[96,768]{1,0:T(8,128)(2,1)S(1)}, u32[]{:S(2)}, u32[]{:S(2)}) collective-permute-start(bf16[96,768]{1,0:T(8,128)(2,1)S(1)} %pad_maximum_fusion.6), channel_id=1, source_target_pairs={{0,32},{8,40},{16,48},{24,56},{32,0},{40,8},{48,16},{56,24},{64,96... | collective-permute-start | bytes 442376 | tf_op jit(solution)/shard_map/ppermute | solution.py:76
  26.7 62.0 %collective-permute-start.18 = (bf16[384,768]{1,0:T(8,128)(2,1)}, bf16[384,768]{1,0:T(8,128)(2,1)S(1)}, u32[]{:S(2)}, u32[]{:S(2)}) collective-permute-start(bf16[384,768]{1,0:T(8,128)(2,1)} %pad_maximum_fusion.3), channel_id=1, source_target_pairs={{0,192},{8,200},{16,208},{24,216},{32,224},{40,232},{48,240},{56,2... | collective-permute-start | bytes 1769480 | tf_op jit(solution)/shard_map/ppermute | solution.py:76
  30.4 58.3 %collective-permute-start.19 = (bf16[384,768]{1,0:T(8,128)(2,1)}, bf16[384,768]{1,0:T(8,128)(2,1)S(1)}, u32[]{:S(2)}, u32[]{:S(2)}) collective-permute-start(bf16[384,768]{1,0:T(8,128)(2,1)} %pad_maximum_fusion.3), channel_id=1, source_target_pairs={{0,128},{8,136},{16,144},{24,152},{32,160},{40,168},{48,176},{56,1... | collective-permute-start | bytes 1769480 | tf_op jit(solution)/shard_map/ppermute | solution.py:76
  64.1 27.6 %collective-permute-start.20 = (bf16[384,768]{1,0:T(8,128)(2,1)}, bf16[384,768]{1,0:T(8,128)(2,1)S(1)}, u32[]{:S(2)}, u32[]{:S(2)}) collective-permute-start(bf16[384,768]{1,0:T(8,128)(2,1)} %pad_maximum_fusion.3), channel_id=1, source_target_pairs={{0,64},{8,72},{16,80},{24,88},{32,96},{40,104},{48,112},{56,120},{... | collective-permute-start | bytes 1769480 | tf_op jit(solution)/shard_map/ppermute | solution.py:76
  65.6 5.9 %collective-permute-start = (bf16[15,192]{0,1:T(8,128)(2,1)S(1)}, bf16[15,192]{0,1:T(8,128)(2,1)S(1)}, u32[]{:S(2)}, u32[]{:S(2)}) collective-permute-start(bf16[15,192]{0,1:T(8,128)(2,1)S(1)} %get-tuple-element.43), channel_id=1, source_target_pairs={{0,8},{8,16},{16,24},{24,32},{32,40},{40,48},{48,56},{56,64},{64,7... | collective-permute-start | bytes 17288 | tf_op jit(solution)/shard_map/ppermute | solution.py:16
  67.6 5.4 %collective-permute-start.1 = (bf16[15,192]{0,1:T(8,128)(2,1)S(1)}, bf16[15,192]{0,1:T(8,128)(2,1)S(1)}, u32[]{:S(2)}, u32[]{:S(2)}) collective-permute-start(bf16[15,192]{0,1:T(8,128)(2,1)S(1)} %get-tuple-element.44), channel_id=1, source_target_pairs={{8,0},{16,8},{24,16},{32,24},{40,32},{48,40},{56,48},{64,56},{72,6... | collective-permute-start | bytes 17288 | tf_op jit(solution)/shard_map/ppermute | solution.py:17
  79.2 2.9 %collective-permute-start.2 = (f32[3,192]{1,0:T(4,128)S(1)}, f32[3,192]{1,0:T(4,128)S(1)}, u32[]{:S(2)}, u32[]{:S(2)}) collective-permute-start(f32[3,192]{1,0:T(4,128)S(1)} %pad_maximum_fusion.8), channel_id=1, source_target_pairs={{0,8},{8,0},{16,24},{24,16},{32,40},{40,32},{48,56},{56,48},{64,72... | collective-permute-start | bytes 6920 | tf_op jit(solution)/shard_map/ppermute | solution.py:46
  82.2 3.7 %collective-permute-start.3 = (f32[3,192]{1,0:T(4,128)S(1)}, f32[3,192]{1,0:T(4,128)S(1)}, u32[]{:S(2)}, u32[]{:S(2)}) collective-permute-start(f32[3,192]{1,0:T(4,128)S(1)} %pad_maximum_fusion.9), channel_id=1, source_target_pairs={{0,16},{8,24},{16,0},{24,8},{32,48},{40,56},{48,32},{56,40},{64,80... | collective-permute-start | bytes 6920 | tf_op jit(solution)/shard_map/ppermute | solution.py:46
  82.8 27.6 %collective-permute-start.11 = (bf16[384,768]{1,0:T(8,128)(2,1)S(1)}, bf16[384,768]{1,0:T(8,128)(2,1)S(1)}, u32[]{:S(2)}, u32[]{:S(2)}) collective-permute-start(bf16[384,768]{1,0:T(8,128)(2,1)S(1)} %pad_maximum_fusion.2), channel_id=1, source_target_pairs={{0,192},{8,200},{16,208},{24,216},{32,224},{40,232},{48,240},{56,2... | collective-permute-start | bytes 1769480 | tf_op jit(solution)/shard_map/ppermute | solution.py:76
  85.8 24.6 %collective-permute-start.12 = (bf16[384,768]{1,0:T(8,128)(2,1)S(1)}, bf16[384,768]{1,0:T(8,128)(2,1)S(1)}, u32[]{:S(2)}, u32[]{:S(2)}) collective-permute-start(bf16[384,768]{1,0:T(8,128)(2,1)S(1)} %pad_maximum_fusion.2), channel_id=1, source_target_pairs={{0,128},{8,136},{16,144},{24,152},{32,160},{40,168},{48,176},{56,1... | collective-permute-start | bytes 1769480 | tf_op jit(solution)/shard_map/ppermute | solution.py:76
  88.7 26.2 %collective-permute-start.13 = (bf16[384,768]{1,0:T(8,128)(2,1)S(1)}, bf16[384,768]{1,0:T(8,128)(2,1)S(1)}, u32[]{:S(2)}, u32[]{:S(2)}) collective-permute-start(bf16[384,768]{1,0:T(8,128)(2,1)S(1)} %pad_maximum_fusion.2), channel_id=1, source_target_pairs={{0,64},{8,72},{16,80},{24,88},{32,96},{40,104},{48,112},{56,120},{... | collective-permute-start | bytes 1769480 | tf_op jit(solution)/shard_map/ppermute | solution.py:76
  88.8 5.2 %collective-permute-start.4 = (f32[3,192]{1,0:T(4,128)S(1)}, f32[3,192]{1,0:T(4,128)S(1)}, u32[]{:S(2)}, u32[]{:S(2)}) collective-permute-start(f32[3,192]{1,0:T(4,128)S(1)} %pad_maximum_fusion.10), channel_id=1, source_target_pairs={{0,32},{8,40},{16,48},{24,56},{32,0},{40,8},{48,16},{56,24},{64,96... | collective-permute-start | bytes 6920 | tf_op jit(solution)/shard_map/ppermute | solution.py:46
  94.0 22.1 %collective-permute-start.5 = (f32[3,192]{1,0:T(4,128)S(1)}, f32[3,192]{1,0:T(4,128)S(1)}, u32[]{:S(2)}, u32[]{:S(2)}) collective-permute-start(f32[3,192]{1,0:T(4,128)S(1)} %pad_maximum_fusion.11), channel_id=1, source_target_pairs={{0,64},{8,72},{16,80},{24,88},{32,96},{40,104},{48,112},{56,120},{... | collective-permute-start | bytes 6920 | tf_op jit(solution)/shard_map/ppermute | solution.py:46
  116.2 5.4 %collective-permute-start.6 = (f32[3,192]{1,0:T(4,128)S(1)}, f32[3,192]{1,0:T(4,128)S(1)}, u32[]{:S(2)}, u32[]{:S(2)}) collective-permute-start(f32[3,192]{1,0:T(4,128)S(1)} %pad_maximum_fusion.12), channel_id=1, source_target_pairs={{0,128},{8,136},{16,144},{24,152},{32,160},{40,168},{48,176},{56,1... | collective-permute-start | bytes 6920 | tf_op jit(solution)/shard_map/ppermute | solution.py:46
  122.9 18.2 %all-to-all-start = ((bf16[8,128,192]{1,2,0:T(8,128)(2,1)}), bf16[8,128,192]{1,2,0:T(8,128)(2,1)}, u32[]{:S(2)}, u32[]{:S(2)}) async-start(bf16[8,128,192]{1,2,0:T(8,128)(2,1)} %copy_bitcast_fusion), calls=%async_computation | async-start | bytes 786432 | tf_op jit(solution)/shard_map/all_to_all | solution.py:141
  127.1 60.2 %all-gather.8.cloned.1.call-start = ((), (), s32[]{:S(2)}) async-start(), calls=%async_computation.4 | async-start | bytes 3538944 | tf_op jit(solution)/shard_map/all_gather | solution.py:146
  145.8 98.1 %reduce-scatter.2.cloned.1.call-start = ((), (), s32[]{:S(2)}) async-start(), calls=%async_computation.5 | async-start | bytes 3538944 | tf_op jit(solution)/shard_map/reduce_scatter | solution.py:152
  (54 other events, 522.9 us)
Sparse Core Ops, SparseCore 0:
  11.2 47.9 all-gather.3
  61.0 58.3 all-gather.5
  146.0 41.3 all-gather.7
  198.5 45.4 reduce-scatter.1

commit v4 on v3

--- a/solution.py
+++ b/solution.py
@@ -52,7 +52,7 @@
     return stats
 
 
-def gather_torus(pieces, axis):
+def gather_torus(up_piece, down_piece, axis, tie):
     size = lax.axis_size(axis)
     cores, xs = 2, 4
     ys = size // (cores * xs)
@@ -86,15 +86,20 @@
             picks.append(picked)
         return picks
 
-    out = []
-    for piece in pieces:
-        other = shifted(piece, lambda y, x, c: (y, x, 1 - c))
-        pair = jnp.concatenate(ordered(piece, [other], my_c, cores), axis=0)
-        got = [shifted(pair, lambda y, x, c, d=d: (y, (x + d) % xs, c)) for d in range(1, xs)]
-        row = jnp.concatenate(ordered(pair, got, my_x, xs), axis=0)
-        got = [shifted(row, lambda y, x, c, d=d: ((y + d) % ys, x, c)) for d in range(1, ys)]
-        out.append(jnp.concatenate(ordered(row, got, my_y, ys), axis=0))
-    return out
+    partner = lambda y, x, c: (y, x, 1 - c)
+    other_up, other_down = shifted((up_piece, down_piece), partner)
+    pair_up = jnp.concatenate(ordered(up_piece, [other_up], my_c, cores), axis=0)
+    pair_down = jnp.concatenate(ordered(down_piece, [other_down], my_c, cores), axis=0)
+    pair = jnp.where(my_c == 0, pair_up, pair_down)
+    got = [shifted(pair, lambda y, x, c, d=d: (y, (x + d) % xs, c)) for d in range(1, xs)]
+    row = jnp.concatenate(ordered(pair, got, my_x, xs), axis=0)
+    got = [shifted(row, lambda y, x, c, d=d: ((y + d) % ys, x, c)) for d in range(1, ys)]
+    whole = jnp.concatenate(ordered(row, got, my_y, ys), axis=0)
+    whole, tie = lax.optimization_barrier((whole, tie))
+    swapped = shifted(whole, partner)
+    up_whole = jnp.where(my_c == 0, whole, swapped)
+    down_whole = jnp.where(my_c == 0, swapped, whole)
+    return up_whole, down_whole, tie
 
 
 def shards(
@@ -119,10 +124,10 @@
     normed = layer_norm(features, norm_gain).astype(jnp.bfloat16)
     piece = lax.all_gather(normed, "tensor", axis=0, tiled=True)
     out_whole = lax.all_gather(out_weight, "tensor", axis=0, tiled=True)
-    up_whole, down_t = gather_torus([up_weight, down_weight.T], "tm")
     value = jnp.dot(piece, value_weight, preferred_element_type=jnp.float32)
     gate = jnp.dot(piece, gate_weight, preferred_element_type=jnp.float32)
     glu = (value * jax.nn.sigmoid(gate) * valid[:, None]).astype(jnp.bfloat16)
+    up_whole, down_t, glu = gather_torus(up_weight, down_weight.T, "tm", glu)
     padded = extended(glu, (("tm", 0),), KERNEL // 2)
     conv = jnp.zeros(glu.shape, jnp.float32)
     for tap in range(KERNEL):

time: 253 us -> 242 us (0.957)
  starting transfers between devices: 38.9 us -> 31.8 us
  other arithmetic: 26.3 us -> 23 us
  waiting for transfers between devices: 149 us -> 146 us
    all_gather x1, waiting for transfers between devices: 28.1 us -> 2.2 us  [shards(): piece = lax.all_gather(normed, 'tensor', axis=0, tiled=True)]
    ppermute x14 -> x9, starting transfers between devices: 20 us -> 10.1 us  [shifted(): return lax.ppermute(value, axis, pairs)]
    ppermute x5, waiting for transfers between devices: 3.97 us -> 11.4 us  [moments_over(): other = lax.ppermute(stats, axis, pairs)]
    ppermute x14 -> x9, waiting for transfers between devices: 19.8 us -> 26.4 us  [shifted(): return lax.ppermute(value, axis, pairs)]
    all_to_all x1, waiting for transfers between devices: 8.43 us -> 13.6 us  [shards(): own_swished = lax.all_to_all(swished, 'tensor', 0, 1, tiled=True)]
    select_n x0 -> x2, other arithmetic: none -> 4.32 us  [the longest x1 4.28 us: gather_torus(): down_whole = jnp.where(my_c == 0, swapped, whole)]
    concatenate x4 -> x1, other arithmetic: 4.37 us -> 0.15 us  [gather_torus(): whole = jnp.concatenate(ordered(row, got, my_y, ys), axis=0)]
    all_to_all x1, starting transfers between devices: 4.25 us -> 7.78 us  [shards(): own_swished = lax.all_to_all(swished, 'tensor', 0, 1, tiled=True)]
  transfers between devices with their start and end apart: 26 -> 21, of which waited for: 11 -> 16; matrix products, arithmetic and copies ran while one was open for 10% -> 10% of each run, Pallas kernels for 0% -> 0%
where the time goes in v4:
time: 242 us; the launch traced here: 241 us
  waiting for transfers between devices  146 us (60%)
  starting transfers between devices  31.8 us (13%)
  other arithmetic  23 us (10%)
  matrix products  18.7 us (8%)
  between operations  16.1 us (7%)
  local copies, waits for them, and re-layouts  5.56 us (2%)
    reduce_scatter x1, waiting for transfers between devices, shards(): lax.psum_scatter(partial_out.astype(jnp.bfloat16), 'tensor', scatter_dime...  45.6 us
    all_gather x1, waiting for transfers between devices, shards(): feed_block = lax.all_gather(feed_normed, 'tensor', axis=0, tiled=True)  43.6 us
    ppermute x9, waiting for transfers between devices, shifted(): return lax.ppermute(value, axis, pairs)  26.4 us
    all_to_all x1, waiting for transfers between devices, shards(): own_swished = lax.all_to_all(swished, 'tensor', 0, 1, tiled=True)  13.6 us
    ppermute x5, waiting for transfers between devices, moments_over(): other = lax.ppermute(stats, axis, pairs)  11.4 us
    dot_general x1, matrix products, shards(): lax.dot_general(hidden, down_t, (((1,), (1,)), ((), ())), preferred_eleme...  11 us
    ppermute x9, starting transfers between devices, shifted(): return lax.ppermute(value, axis, pairs)  10.1 us
    ppermute x5, starting transfers between devices, moments_over(): other = lax.ppermute(stats, axis, pairs)  8.36 us
  transfers between devices with their start and end apart: 21, of which 16 were waited for; matrix products, arithmetic and copies ran while one was open for 10% of the time, Pallas kernels for 0%

profile of v4, /device:TPU:2, one launch (start us, length us, event | category | flops | bytes accessed | tf_op | source)
XLA Modules:
  0.0 241.3 jit_solution(5971113797064399023)
XLA Ops:
  9.0 2.0 fusion.16
  13.7 2.3 collective-permute-start.2
  20.2 3.5 %collective-permute-done.3 = bf16[96,768]{1,0:T(8,128)(2,1)S(1)} collective-permute-done((bf16[96,768]{1,0:T(8,128)(2,1)S(1)}, bf16[96,768]{1,0:T(8,128)(2,1)S(1)}, u32[]{:S(2)}, u32[]{:S(2)}) %collective-permute-start.3) | collective-permute-done | bytes 147488 | tf_op jit(solution)/shard_map/ppermute | solution.py:76
  24.7 3.1 %collective-permute-start.5 = (bf16[384,768]{1,0:T(8,128)(2,1)S(1)}, bf16[384,768]{1,0:T(8,128)(2,1)S(1)}, u32[]{:S(2)}, u32[]{:S(2)}) collective-permute-start(bf16[384,768]{1,0:T(8,128)(2,1)S(1)} %pad_maximum_fusion.1), channel_id=1, source_target_pairs={{0,192},{8,200},{16,208},{24,216},{32,224},{40,232},{48,240},{56,2... | collective-permute-start | bytes 1769480 | tf_op jit(solution)/shard_map/ppermute | solution.py:76
  35.7 16.5 %collective-permute-done.5 = bf16[384,768]{1,0:T(8,128)(2,1)S(1)} collective-permute-done((bf16[384,768]{1,0:T(8,128)(2,1)S(1)}, bf16[384,768]{1,0:T(8,128)(2,1)S(1)}, u32[]{:S(2)}, u32[]{:S(2)}) %collective-permute-start.5) | collective-permute-done | bytes 589856 | tf_op jit(solution)/shard_map/ppermute | solution.py:76
  52.2 3.7 %collective-permute-done.7 = bf16[384,768]{1,0:T(8,128)(2,1)S(1)} collective-permute-done((bf16[384,768]{1,0:T(8,128)(2,1)S(1)}, bf16[384,768]{1,0:T(8,128)(2,1)S(1)}, u32[]{:S(2)}, u32[]{:S(2)}) %collective-permute-start.7) | collective-permute-done | bytes 589856 | tf_op jit(solution)/shard_map/ppermute | solution.py:76
  57.0 2.2 all-gather.4.cloned.1.call-done
  59.2 3.3 %fusion.5 = f32[1024,192]{0,1:T(8,128)S(1)} fusion(bf16[1024,1536]{1,0:T(8,128)(2,1)} %all-gather.4.cloned.1.call-done, bf16[1536,192]{0,1:T(8,128)(2,1)S(1)} %copy-done), kind=kOutput, calls=%fused_computation.27 | convolution fusion | flops 604569600 | bytes 4521984 | tf_op jit(solution)/shard_map/dot_general | solution.py:128
  64.0 3.1 %collective-permute-start.9 = (bf16[15,192]{0,1:T(8,128)(2,1)S(1)}, bf16[15,192]{0,1:T(8,128)(2,1)S(1)}, u32[]{:S(2)}, u32[]{:S(2)}) collective-permute-start(bf16[15,192]{0,1:T(8,128)(2,1)S(1)} %get-tuple-element.44), channel_id=1, source_target_pairs={{8,0},{16,8},{24,16},{32,24},{40,32},{48,40},{56,48},{64,56},{72,6... | collective-permute-start | bytes 17288 | tf_op jit(solution)/shard_map/ppermute | solution.py:17
  67.2 2.1 collective-permute-start.8
  69.3 3.3 %collective-permute-done.8 = bf16[15,192]{0,1:T(8,128)(2,1)S(1)} collective-permute-done((bf16[15,192]{0,1:T(8,128)(2,1)S(1)}, bf16[15,192]{0,1:T(8,128)(2,1)S(1)}, u32[]{:S(2)}, u32[]{:S(2)}) %collective-permute-start.8) | collective-permute-done | bytes 5792 | tf_op jit(solution)/shard_map/ppermute | solution.py:16
  72.9 5.3 %multiply_reduce_fusion.1 = (f32[192]{0:T(256)S(1)}, f32[1024,192]{0,1:T(8,128)S(1)}) fusion(f32[1024]{0:T(1024)S(1)} %get-tuple-element.30, f32[192]{0:T(256)S(1)} %bitcast.73, bf16[1039,192]{0,1:T(8,128)(2,1)S(1)} %constant_dynamic-update-slice_fusion, f32[192]{0:T(256)S(1)} %bitcast.74, f32[192]{0:T(256)S(1)} %bitcast.76, f32[192]{0:T(256)S(1)} %bitcast.77, ...), kind=kLoop, calls=%fused_computation.47 | loop fusion | flops 27328320 | bytes 7112320 | tf_op jit(solution)/shard_map/reduce_sum | solution.py:136
  80.9 3.6 %collective-permute-done.11 = f32[3,192]{1,0:T(4,128)S(1)} collective-permute-done((f32[3,192]{1,0:T(4,128)S(1)}, f32[3,192]{1,0:T(4,128)S(1)}, u32[]{:S(2)}, u32[]{:S(2)}) %collective-permute-start.11) | collective-permute-done | bytes 2336 | tf_op jit(solution)/shard_map/ppermute | solution.py:46
  86.3 3.5 %collective-permute-done.12 = f32[3,192]{1,0:T(4,128)S(1)} collective-permute-done((f32[3,192]{1,0:T(4,128)S(1)}, f32[3,192]{1,0:T(4,128)S(1)}, u32[]{:S(2)}, u32[]{:S(2)}) %collective-permute-start.12) | collective-permute-done | bytes 2336 | tf_op jit(solution)/shard_map/ppermute | solution.py:46
  89.8 2.9 %collective-permute-start.13 = (f32[3,192]{1,0:T(4,128)S(1)}, f32[3,192]{1,0:T(4,128)S(1)}, u32[]{:S(2)}, u32[]{:S(2)}) collective-permute-start(f32[3,192]{1,0:T(4,128)S(1)} %pad_maximum_fusion.6), channel_id=1, source_target_pairs={{0,64},{8,72},{16,80},{24,88},{32,96},{40,104},{48,112},{56,120},{... | collective-permute-start | bytes 6920 | tf_op jit(solution)/shard_map/ppermute | solution.py:46
  94.3 3.6 %collective-permute-start.14 = (f32[3,192]{1,0:T(4,128)S(1)}, f32[3,192]{1,0:T(4,128)S(1)}, u32[]{:S(2)}, u32[]{:S(2)}) collective-permute-start(f32[3,192]{1,0:T(4,128)S(1)} %pad_maximum_fusion.7), channel_id=1, source_target_pairs={{0,128},{8,136},{16,144},{24,152},{32,160},{40,168},{48,176},{56,1... | collective-permute-start | bytes 6920 | tf_op jit(solution)/shard_map/ppermute | solution.py:46
  99.6 2.3 copy_bitcast_fusion
  101.9 7.8 %all-to-all-start = ((bf16[8,128,192]{1,2,0:T(8,128)(2,1)}), bf16[8,128,192]{1,2,0:T(8,128)(2,1)}, u32[]{:S(2)}, u32[]{:S(2)}) async-start(bf16[8,128,192]{1,2,0:T(8,128)(2,1)} %copy_bitcast_fusion), calls=%async_computation | async-start | bytes 786432 | tf_op jit(solution)/shard_map/all_to_all | solution.py:146
  109.8 4.3 %broadcast_select_fusion = (bf16[1536,768]{1,0:T(8,128)(2,1)}, bf16[1536,768]{1,0:T(8,128)(2,1)}) fusion(bf16[1536,768]{1,0:T(8,128)(2,1)} %collective-permute-done.15, bf16[1536,768]{1,0:T(8,128)(2,1)S(1)} %pad_maximum_fusion, pred[]{:T(512)S(6)} %eq.117), kind=kLoop, calls=%fused_computation.5 | loop fusion | flops 2359296 | bytes 9437185 | tf_op jit(solution)/shard_map/jit(_where)/select_n | solution.py:101
  114.1 13.6 %all-to-all-done = bf16[8,128,192]{1,2,0:T(8,128)(2,1)} async-done(((bf16[8,128,192]{1,2,0:T(8,128)(2,1)}), bf16[8,128,192]{1,2,0:T(8,128)(2,1)}, u32[]{:S(2)}, u32[]{:S(2)}) %all-to-all-start) | async-done | bytes 393248 | tf_op jit(solution)/shard_map/all_to_all | solution.py:146
  127.7 3.3 %fusion = bf16[128,1536]{1,0:T(8,128)(2,1)S(1)} fusion(bf16[128,1536]{0,1:T(8,128)(2,1)} %bitcast.38, bf16[1536,1536]{1,0:T(8,128)(2,1)} %all-gather.6.cloned.1.call-done, bf16[128,1536]{1,0:T(8,128)(2,1)S(1)} %copy-done.2), kind=kOutput, calls=%fused_computation.3 | convolution fusion | flops 604569600 | bytes 5898240 | tf_op jit(solution)/shard_map/dot_general | solution.py:147
  132.7 43.6 %all-gather.8.cloned.1.call-done = bf16[1024,1536]{1,0:T(8,128)(2,1)} async-done(((bf16[128,1536]{1,0:T(8,128)(2,1)}), bf16[1024,1536]{1,0:T(8,128)(2,1)}) %all-gather.8.cloned.1.call-update) | async-done | bytes 3145744 | tf_op jit(solution)/shard_map/all_gather | solution.py:151
  176.3 11.0 %convolution_convert_fusion = bf16[1024,1536]{1,0:T(8,128)(2,1)} fusion(bf16[1536,768]{1,0:T(8,128)(2,1)} %get-tuple-element.14, bf16[1024,1536]{1,0:T(8,128)(2,1)} %all-gather.8.cloned.1.call-done, bf16[1536,768]{1,0:T(8,128)(2,1)} %get-tuple-element.13), kind=kOutput, calls=%fused_computation | convolution fusion | flops 4837343232 | bytes 11010048 | tf_op jit(solution)/shard_map/dot_general | solution.py:154
  187.3 45.6 %reduce-scatter.2.cloned.1.call-done = bf16[128,1536]{1,0:T(8,128)(2,1)} async-done(((bf16[1024,1536]{1,0:T(8,128)(2,1)}), bf16[128,1536]{1,0:T(8,128)(2,1)}) %reduce-scatter.2.cloned.1.call-update) | async-done | bytes 393232 | tf_op jit(solution)/shard_map/reduce_scatter | solution.py:157
  (155 shorter events, 29.8 us)
Async XLA Ops:
  6.5 52.6 %copy-start = (bf16[1536,192]{0,1:T(8,128)(2,1)S(1)}, bf16[1536,192]{0,1:T(8,128)(2,1)}, u32[]{:S(2)}) copy-start(bf16[1536,192]{0,1:T(8,128)(2,1)} %param.18) | copy-start | bytes 1769476
  6.5 52.6 %all-gather.4.cloned.1.call-start = ((), (), s32[]{:S(2)}) async-start(), calls=%async_computation.2 | async-start | bytes 3538944 | tf_op jit(solution)/shard_map/all_gather | solution.py:125
  11.1 116.6 %all-gather.6.cloned.1.call-start = ((), (), s32[]{:S(2)}) async-start(), calls=%async_computation.3 | async-start | bytes 5308416 | tf_op jit(solution)/shard_map/all_gather | solution.py:126
  11.1 1.6 collective-permute-start.1
  11.2 2.4 collective-permute-start
  13.7 6.6 %collective-permute-start.2 = (bf16[96,768]{1,0:T(8,128)(2,1)S(1)}, bf16[96,768]{1,0:T(8,128)(2,1)S(1)}, u32[]{:S(2)}, u32[]{:S(2)}) collective-permute-start(bf16[96,768]{1,0:T(8,128)(2,1)S(1)} %maximum_select_fusion), channel_id=1, source_target_pairs={{0,48},{8,56},{16,0},{24,8},{32,16},{40,24},{48,32},{56,40},{64,11... | collective-permute-start | bytes 442376 | tf_op jit(solution)/shard_map/ppermute | solution.py:76
  16.0 7.7 %collective-permute-start.3 = (bf16[96,768]{1,0:T(8,128)(2,1)S(1)}, bf16[96,768]{1,0:T(8,128)(2,1)S(1)}, u32[]{:S(2)}, u32[]{:S(2)}) collective-permute-start(bf16[96,768]{1,0:T(8,128)(2,1)S(1)} %maximum_select_fusion), channel_id=1, source_target_pairs={{0,32},{8,40},{16,48},{24,56},{32,0},{40,8},{48,16},{56,24},{64,96... | collective-permute-start | bytes 442376 | tf_op jit(solution)/shard_map/ppermute | solution.py:76
  16.7 7.9 %collective-permute-start.4 = (bf16[96,768]{1,0:T(8,128)(2,1)S(1)}, bf16[96,768]{1,0:T(8,128)(2,1)S(1)}, u32[]{:S(2)}, u32[]{:S(2)}) collective-permute-start(bf16[96,768]{1,0:T(8,128)(2,1)S(1)} %maximum_select_fusion), channel_id=1, source_target_pairs={{0,16},{8,24},{16,32},{24,40},{32,48},{40,56},{48,0},{56,8},{64,80... | collective-permute-start | bytes 442376 | tf_op jit(solution)/shard_map/ppermute | solution.py:76
  24.7 27.5 %collective-permute-start.5 = (bf16[384,768]{1,0:T(8,128)(2,1)S(1)}, bf16[384,768]{1,0:T(8,128)(2,1)S(1)}, u32[]{:S(2)}, u32[]{:S(2)}) collective-permute-start(bf16[384,768]{1,0:T(8,128)(2,1)S(1)} %pad_maximum_fusion.1), channel_id=1, source_target_pairs={{0,192},{8,200},{16,208},{24,216},{32,224},{40,232},{48,240},{56,2... | collective-permute-start | bytes 1769480 | tf_op jit(solution)/shard_map/ppermute | solution.py:76
  27.8 24.4 %collective-permute-start.6 = (bf16[384,768]{1,0:T(8,128)(2,1)S(1)}, bf16[384,768]{1,0:T(8,128)(2,1)S(1)}, u32[]{:S(2)}, u32[]{:S(2)}) collective-permute-start(bf16[384,768]{1,0:T(8,128)(2,1)S(1)} %pad_maximum_fusion.1), channel_id=1, source_target_pairs={{0,128},{8,136},{16,144},{24,152},{32,160},{40,168},{48,176},{56,1... | collective-permute-start | bytes 1769480 | tf_op jit(solution)/shard_map/ppermute | solution.py:76
  28.5 27.5 %collective-permute-start.7 = (bf16[384,768]{1,0:T(8,128)(2,1)S(1)}, bf16[384,768]{1,0:T(8,128)(2,1)S(1)}, u32[]{:S(2)}, u32[]{:S(2)}) collective-permute-start(bf16[384,768]{1,0:T(8,128)(2,1)S(1)} %pad_maximum_fusion.1), channel_id=1, source_target_pairs={{0,64},{8,72},{16,80},{24,88},{32,96},{40,104},{48,112},{56,120},{... | collective-permute-start | bytes 1769480 | tf_op jit(solution)/shard_map/ppermute | solution.py:76
  64.0 5.3 %collective-permute-start.9 = (bf16[15,192]{0,1:T(8,128)(2,1)S(1)}, bf16[15,192]{0,1:T(8,128)(2,1)S(1)}, u32[]{:S(2)}, u32[]{:S(2)}) collective-permute-start(bf16[15,192]{0,1:T(8,128)(2,1)S(1)} %get-tuple-element.44), channel_id=1, source_target_pairs={{8,0},{16,8},{24,16},{32,24},{40,32},{48,40},{56,48},{64,56},{72,6... | collective-permute-start | bytes 17288 | tf_op jit(solution)/shard_map/ppermute | solution.py:17
  67.2 5.4 %collective-permute-start.8 = (bf16[15,192]{0,1:T(8,128)(2,1)S(1)}, bf16[15,192]{0,1:T(8,128)(2,1)S(1)}, u32[]{:S(2)}, u32[]{:S(2)}) collective-permute-start(bf16[15,192]{0,1:T(8,128)(2,1)S(1)} %get-tuple-element.43), channel_id=1, source_target_pairs={{0,8},{8,16},{16,24},{24,32},{32,40},{40,48},{48,56},{56,64},{64,7... | collective-permute-start | bytes 17288 | tf_op jit(solution)/shard_map/ppermute | solution.py:16
  72.9 26.7 %copy-start.35 = (f32[192]{0:T(256)S(1)}, f32[192]{0:T(256)}, u32[]{:S(2)}) copy-start(f32[192]{0:T(256)} %param.21) | copy-start | bytes 2308
  72.9 26.7 %copy-start.36 = (f32[192]{0:T(256)S(1)}, f32[192]{0:T(256)}, u32[]{:S(2)}) copy-start(f32[192]{0:T(256)} %param.20) | copy-start | bytes 2308
  79.4 1.2 collective-permute-start.10
  80.8 3.7 %collective-permute-start.11 = (f32[3,192]{1,0:T(4,128)S(1)}, f32[3,192]{1,0:T(4,128)S(1)}, u32[]{:S(2)}, u32[]{:S(2)}) collective-permute-start(f32[3,192]{1,0:T(4,128)S(1)} %pad_maximum_fusion.4), channel_id=1, source_target_pairs={{0,16},{8,24},{16,0},{24,8},{32,48},{40,56},{48,32},{56,40},{64,80... | collective-permute-start | bytes 6920 | tf_op jit(solution)/shard_map/ppermute | solution.py:46
  84.5 5.2 %collective-permute-start.12 = (f32[3,192]{1,0:T(4,128)S(1)}, f32[3,192]{1,0:T(4,128)S(1)}, u32[]{:S(2)}, u32[]{:S(2)}) collective-permute-start(f32[3,192]{1,0:T(4,128)S(1)} %pad_maximum_fusion.5), channel_id=1, source_target_pairs={{0,32},{8,40},{16,48},{24,56},{32,0},{40,8},{48,16},{56,24},{64,96... | collective-permute-start | bytes 6920 | tf_op jit(solution)/shard_map/ppermute | solution.py:46
  86.3 23.5 %collective-permute-start.15 = (bf16[1536,768]{1,0:T(8,128)(2,1)S(1)}, bf16[1536,768]{1,0:T(8,128)(2,1)}, u32[]{:S(2)}, u32[]{:S(2)}) collective-permute-start(bf16[1536,768]{1,0:T(8,128)(2,1)S(1)} %pad_maximum_fusion), channel_id=1, source_target_pairs={{0,8},{8,0},{16,24},{24,16},{32,40},{40,32},{48,56},{56,48},{64,72... | collective-permute-start | bytes 7077896 | tf_op jit(solution)/shard_map/ppermute | solution.py:76
  89.8 4.5 %collective-permute-start.13 = (f32[3,192]{1,0:T(4,128)S(1)}, f32[3,192]{1,0:T(4,128)S(1)}, u32[]{:S(2)}, u32[]{:S(2)}) collective-permute-start(f32[3,192]{1,0:T(4,128)S(1)} %pad_maximum_fusion.6), channel_id=1, source_target_pairs={{0,64},{8,72},{16,80},{24,88},{32,96},{40,104},{48,112},{56,120},{... | collective-permute-start | bytes 6920 | tf_op jit(solution)/shard_map/ppermute | solution.py:46
  94.3 5.2 %collective-permute-start.14 = (f32[3,192]{1,0:T(4,128)S(1)}, f32[3,192]{1,0:T(4,128)S(1)}, u32[]{:S(2)}, u32[]{:S(2)}) collective-permute-start(f32[3,192]{1,0:T(4,128)S(1)} %pad_maximum_fusion.7), channel_id=1, source_target_pairs={{0,128},{8,136},{16,144},{24,152},{32,160},{40,168},{48,176},{56,1... | collective-permute-start | bytes 6920 | tf_op jit(solution)/shard_map/ppermute | solution.py:46
  101.9 25.7 %all-to-all-start = ((bf16[8,128,192]{1,2,0:T(8,128)(2,1)}), bf16[8,128,192]{1,2,0:T(8,128)(2,1)}, u32[]{:S(2)}, u32[]{:S(2)}) async-start(bf16[8,128,192]{1,2,0:T(8,128)(2,1)} %copy_bitcast_fusion), calls=%async_computation | async-start | bytes 786432 | tf_op jit(solution)/shard_map/all_to_all | solution.py:146
  109.7 66.6 %all-gather.8.cloned.1.call-start = ((), (), s32[]{:S(2)}) async-start(), calls=%async_computation.4 | async-start | bytes 3538944 | tf_op jit(solution)/shard_map/all_gather | solution.py:151
  132.4 100.5 %reduce-scatter.2.cloned.1.call-start = ((), (), s32[]{:S(2)}) async-start(), calls=%async_computation.5 | async-start | bytes 3538944 | tf_op jit(solution)/shard_map/reduce_scatter | solution.py:157
  (36 other events, 344.2 us)
Sparse Core Ops, SparseCore 0:
  11.2 47.9 all-gather.3
  60.9 66.6 all-gather.5
  132.5 43.7 all-gather.7
  187.5 45.3 reduce-scatter.1

commit v5 on v4

--- a/solution.py
+++ b/solution.py
@@ -121,9 +121,12 @@
     block = own_rows * lax.axis_size("tensor")
     positions = lax.axis_index("tm") * block + jnp.arange(block, dtype=jnp.int32)
     valid = ((frame_mask > 0) & (positions < total_length[0])).astype(jnp.float32)
-    normed = layer_norm(features, norm_gain).astype(jnp.bfloat16)
-    piece = lax.all_gather(normed, "tensor", axis=0, tiled=True)
-    out_whole = lax.all_gather(out_weight, "tensor", axis=0, tiled=True)
+    feature_block = lax.all_gather(features, "tensor", axis=0, tiled=True)
+    piece = layer_norm(feature_block, norm_gain).astype(jnp.bfloat16)
+    my_core = lax.axis_index("tm") % 2
+    cols = out_weight.shape[1] // 2
+    out_half = jnp.where(my_core == 0, out_weight[:, :cols], out_weight[:, cols:])
+    out_mine = lax.all_gather(out_half, "tensor", axis=0, tiled=True)
     value = jnp.dot(piece, value_weight, preferred_element_type=jnp.float32)
     gate = jnp.dot(piece, gate_weight, preferred_element_type=jnp.float32)
     glu = (value * jax.nn.sigmoid(gate) * valid[:, None]).astype(jnp.bfloat16)
@@ -143,12 +146,22 @@
     var = m2 / count
     scaled = centred * lax.rsqrt(var + 1e-05) * batch_gain + batch_bias
     swished = (scaled * jax.nn.sigmoid(scaled)).astype(jnp.bfloat16)
-    own_swished = lax.all_to_all(swished, "tensor", 0, 1, tiled=True)
-    conv_out = jnp.dot(own_swished, out_whole, preferred_element_type=jnp.float32)
-    mid = (features.astype(jnp.float32) + conv_out).astype(jnp.bfloat16)
-    mid, up_whole, down_t = lax.optimization_barrier((mid, up_whole, down_t))
-    feed_normed = layer_norm(mid, feed_gain).astype(jnp.bfloat16)
-    feed_block = lax.all_gather(feed_normed, "tensor", axis=0, tiled=True)
+    swished_all = lax.all_gather(swished.T, "tensor", axis=0, tiled=True)
+    out_other = lax.ppermute(out_mine, "tm", [(i, i ^ 1) for i in range(lax.axis_size("tm"))])
+    left = jnp.where(my_core == 0, out_mine, out_other)
+    right = jnp.where(my_core == 0, out_other, out_mine)
+    contract = (((0,), (0,)), ((), ()))
+    conv_out = jnp.concatenate(
+        [
+            lax.dot_general(swished_all, left, contract, preferred_element_type=jnp.float32),
+            lax.dot_general(swished_all, right, contract, preferred_element_type=jnp.float32),
+        ],
+        axis=1,
+    )
+    mid_block = (feature_block.astype(jnp.float32) + conv_out).astype(jnp.bfloat16)
+    mid_block, up_whole, down_t = lax.optimization_barrier((mid_block, up_whole, down_t))
+    feed_block = layer_norm(mid_block, feed_gain).astype(jnp.bfloat16)
+    mid = lax.dynamic_slice_in_dim(mid_block, lax.axis_index("tensor") * own_rows, own_rows, axis=0)
     pre = jnp.dot(feed_block, up_whole, preferred_element_type=jnp.float32)
     hidden = (pre * jax.nn.sigmoid(pre)).astype(jnp.bfloat16)
     partial_out = lax.dot_general(

time: 242 us -> 235 us (0.971)
  waiting for transfers between devices: 146 us -> 136 us
  starting transfers between devices: 31.8 us -> 23.5 us
  local copies, waits for them, and re-layouts: 5.56 us -> 11.2 us
  matrix products: 18.7 us -> 21.9 us
    unnamed x4 -> x5, waiting for transfers between devices: 0.07 us -> 46.7 us
    reduce_scatter x1 -> x0, waiting for transfers between devices: 45.6 us -> none  [shards(): lax.psum_scatter(partial_out.astype(jnp.bfloat16), 'tensor', scatter_dime...]
    all_to_all x1 -> x0, waiting for transfers between devices: 13.6 us -> none  [shards(): own_swished = lax.all_to_all(swished, 'tensor', 0, 1, tiled=True)]
    all_to_all x1 -> x0, starting transfers between devices: 7.78 us -> none  [shards(): own_swished = lax.all_to_all(swished, 'tensor', 0, 1, tiled=True)]
    dot_general x1 -> x2, matrix products: 3.29 us -> 8.31 us  [the longest x1 5.54 us: shards(): lax.dot_general(swished_all, right, contract, preferred_element_type=jnp....]
    unnamed x79 -> x89, local copies, waits for them, and re-layouts: 1.07 us -> 5.74 us
    ppermute x9, waiting for transfers between devices: 26.4 us -> 30.8 us  [shifted(): return lax.ppermute(value, axis, pairs)]
  transfers between devices with their start and end apart: 21 -> 21, of which waited for: 16 -> 15; matrix products, arithmetic and copies ran while one was open for 10% -> 12% of each run, Pallas kernels for 0% -> 0%
where the time goes in v5:
time: 235 us; the launch traced here: 234 us
  waiting for transfers between devices  136 us (58%)
  other arithmetic  25.2 us (11%)
  starting transfers between devices  23.5 us (10%)
  matrix products  21.9 us (9%)
  between operations  16.1 us (7%)
  local copies, waits for them, and re-layouts  11.2 us (5%)
    unnamed x5, waiting for transfers between devices  46.7 us
    all_gather x1, waiting for transfers between devices, shards(): swished_all = lax.all_gather(swished.T, 'tensor', axis=0, tiled=True)  33.7 us
    ppermute x9, waiting for transfers between devices, shifted(): return lax.ppermute(value, axis, pairs)  30.8 us
    all_gather x1, waiting for transfers between devices, shards(): feature_block = lax.all_gather(features, 'tensor', axis=0, tiled=True)  11.2 us
    ppermute x5, waiting for transfers between devices, moments_over(): other = lax.ppermute(stats, axis, pairs)  10.9 us
    dot_general x1, matrix products, shards(): lax.dot_general(hidden, down_t, (((1,), (1,)), ((), ())), preferred_eleme...  10.8 us
    ppermute x9, starting transfers between devices, shifted(): return lax.ppermute(value, axis, pairs)  10.2 us
    ppermute x5, starting transfers between devices, moments_over(): other = lax.ppermute(stats, axis, pairs)  8.15 us
  transfers between devices with their start and end apart: 21, of which 15 were waited for; matrix products, arithmetic and copies ran while one was open for 12% of the time, Pallas kernels for 0%

profile of v5, /device:TPU:2, one launch (start us, length us, event | category | flops | bytes accessed | tf_op | source)
XLA Modules:
  0.0 234.0 jit_solution(16796365921034903836)
XLA Ops:
  6.5 2.0 copy.17
  12.0 2.3 %collective-permute-start.2 = (bf16[96,768]{1,0:T(8,128)(2,1)S(1)}, bf16[96,768]{1,0:T(8,128)(2,1)S(1)}, u32[]{:S(2)}, u32[]{:S(2)}) collective-permute-start(bf16[96,768]{1,0:T(8,128)(2,1)S(1)} %maximum_select_fusion), channel_id=1, source_target_pairs={{0,48},{8,56},{16,0},{24,8},{32,16},{40,24},{48,32},{56,40},{64,11... | collective-permute-start | bytes 442376 | tf_op jit(solution)/shard_map/ppermute | solution.py:76
  19.6 2.5 %collective-permute-done.3 = bf16[96,768]{1,0:T(8,128)(2,1)S(1)} collective-permute-done((bf16[96,768]{1,0:T(8,128)(2,1)S(1)}, bf16[96,768]{1,0:T(8,128)(2,1)S(1)}, u32[]{:S(2)}, u32[]{:S(2)}) %collective-permute-start.3) | collective-permute-done | bytes 147488 | tf_op jit(solution)/shard_map/ppermute | solution.py:76
  23.1 3.1 %collective-permute-start.5 = (bf16[384,768]{1,0:T(8,128)(2,1)S(1)}, bf16[384,768]{1,0:T(8,128)(2,1)S(1)}, u32[]{:S(2)}, u32[]{:S(2)}) collective-permute-start(bf16[384,768]{1,0:T(8,128)(2,1)S(1)} %pad_maximum_fusion.1), channel_id=1, source_target_pairs={{0,192},{8,200},{16,208},{24,216},{32,224},{40,232},{48,240},{56,2... | collective-permute-start | bytes 1769480 | tf_op jit(solution)/shard_map/ppermute | solution.py:76
  34.1 16.5 %collective-permute-done.5 = bf16[384,768]{1,0:T(8,128)(2,1)S(1)} collective-permute-done((bf16[384,768]{1,0:T(8,128)(2,1)S(1)}, bf16[384,768]{1,0:T(8,128)(2,1)S(1)}, u32[]{:S(2)}, u32[]{:S(2)}) %collective-permute-start.5) | collective-permute-done | bytes 589856 | tf_op jit(solution)/shard_map/ppermute | solution.py:76
  50.6 3.7 %collective-permute-done.7 = bf16[384,768]{1,0:T(8,128)(2,1)S(1)} collective-permute-done((bf16[384,768]{1,0:T(8,128)(2,1)S(1)}, bf16[384,768]{1,0:T(8,128)(2,1)S(1)}, u32[]{:S(2)}, u32[]{:S(2)}) %collective-permute-start.7) | collective-permute-done | bytes 589856 | tf_op jit(solution)/shard_map/ppermute | solution.py:76
  55.3 11.2 %all-gather.4.cloned.1.call-done = bf16[1024,1536]{0,1:T(8,128)(2,1)} async-done(((bf16[128,1536]{0,1:T(8,128)(2,1)}), bf16[1024,1536]{0,1:T(8,128)(2,1)}) %all-gather.4.cloned.1.call-update) | async-done | bytes 3145744 | tf_op jit(solution)/shard_map/all_gather | solution.py:124
  66.5 2.6 %convert_reduce_fusion = f32[1024]{0:T(1024)S(1)} fusion(bf16[1024,1536]{0,1:T(8,128)(2,1)} %all-gather.4.cloned.1.call-done), kind=kLoop, calls=%fused_computation.2 | loop fusion | flops 3144704 | bytes 3149824 | tf_op jit(solution)/shard_map/reduce_sum | solution.py:24
  75.4 2.6 %collective-permute-start.8 = (bf16[15,192]{0,1:T(8,128)(2,1)S(1)}, bf16[15,192]{0,1:T(8,128)(2,1)S(1)}, u32[]{:S(2)}, u32[]{:S(2)}) collective-permute-start(bf16[15,192]{0,1:T(8,128)(2,1)S(1)} %get-tuple-element.43), channel_id=1, source_target_pairs={{0,8},{8,16},{16,24},{24,32},{32,40},{40,48},{48,56},{56,64},{64,7... | collective-permute-start | bytes 17288 | tf_op jit(solution)/shard_map/ppermute | solution.py:16
  78.0 2.8 %collective-permute-done.8 = bf16[15,192]{0,1:T(8,128)(2,1)S(1)} collective-permute-done((bf16[15,192]{0,1:T(8,128)(2,1)S(1)}, bf16[15,192]{0,1:T(8,128)(2,1)S(1)}, u32[]{:S(2)}, u32[]{:S(2)}) %collective-permute-start.8) | collective-permute-done | bytes 5792 | tf_op jit(solution)/shard_map/ppermute | solution.py:16
  81.1 5.3 %multiply_reduce_fusion.1 = (f32[192]{0:T(256)S(1)}, f32[1024,192]{0,1:T(8,128)S(1)}) fusion(f32[1024]{0:T(1024)S(1)} %get-tuple-element.30, f32[192]{0:T(256)S(1)} %bitcast.65, bf16[1039,192]{0,1:T(8,128)(2,1)S(1)} %constant_dynamic-update-slice_fusion, f32[192]{0:T(256)S(1)} %bitcast.66, f32[192]{0:T(256)S(1)} %bitcast.68, f32[192]{0:T(256)S(1)} %bitcast.69, ...), kind=kLoop, calls=%fused_computation.55 | loop fusion | flops 27328320 | bytes 7112320 | tf_op jit(solution)/shard_map/reduce_sum | solution.py:139
  89.1 3.6 %collective-permute-done.11 = f32[3,192]{1,0:T(4,128)S(1)} collective-permute-done((f32[3,192]{1,0:T(4,128)S(1)}, f32[3,192]{1,0:T(4,128)S(1)}, u32[]{:S(2)}, u32[]{:S(2)}) %collective-permute-start.11) | collective-permute-done | bytes 2336 | tf_op jit(solution)/shard_map/ppermute | solution.py:46
  92.7 2.2 collective-permute-start.12
  94.9 3.0 %collective-permute-done.12 = f32[3,192]{1,0:T(4,128)S(1)} collective-permute-done((f32[3,192]{1,0:T(4,128)S(1)}, f32[3,192]{1,0:T(4,128)S(1)}, u32[]{:S(2)}, u32[]{:S(2)}) %collective-permute-start.12) | collective-permute-done | bytes 2336 | tf_op jit(solution)/shard_map/ppermute | solution.py:46
  98.0 2.2 collective-permute-start.13
  101.9 3.6 %collective-permute-start.14 = (f32[3,192]{1,0:T(4,128)S(1)}, f32[3,192]{1,0:T(4,128)S(1)}, u32[]{:S(2)}, u32[]{:S(2)}) collective-permute-start(f32[3,192]{1,0:T(4,128)S(1)} %pad_maximum_fusion.7), channel_id=1, source_target_pairs={{0,128},{8,136},{16,144},{24,152},{32,160},{40,168},{48,176},{56,1... | collective-permute-start | bytes 6920 | tf_op jit(solution)/shard_map/ppermute | solution.py:46
  107.2 2.3 fusion.47
  110.1 6.2 %collective-permute-done.16 = bf16[1536,768]{1,0:T(8,128)(2,1)} collective-permute-done((bf16[1536,768]{1,0:T(8,128)(2,1)S(1)}, bf16[1536,768]{1,0:T(8,128)(2,1)}, u32[]{:S(2)}, u32[]{:S(2)}) %collective-permute-start.16) | collective-permute-done | bytes 2359328 | tf_op jit(solution)/shard_map/ppermute | solution.py:76
  116.4 4.1 %broadcast_select_fusion = (bf16[1536,768]{1,0:T(8,128)(2,1)}, bf16[1536,768]{1,0:T(8,128)(2,1)}) fusion(bf16[1536,768]{1,0:T(8,128)(2,1)} %collective-permute-done.16, bf16[1536,768]{1,0:T(8,128)(2,1)S(1)} %pad_maximum_fusion, pred[]{:T(512)S(6)} %eq.121), kind=kLoop, calls=%fused_computation.27 | loop fusion | flops 2359296 | bytes 9437185 | tf_op jit(solution)/shard_map/jit(_where)/select_n | solution.py:101
  120.5 33.7 %all-gather.6.cloned.1.call-done = bf16[1536,1024]{1,0:T(8,128)(2,1)} async-done(((bf16[192,1024]{1,0:T(8,128)(2,1)}), bf16[1536,1024]{1,0:T(8,128)(2,1)}) %all-gather.6.cloned.1.call-update) | async-done | bytes 3145744 | tf_op jit(solution)/shard_map/all_gather | solution.py:149
  154.3 5.5 %fusion.16 = f32[1024,768]{0,1:T(8,128)S(1)} fusion(bf16[1536,1024]{1,0:T(8,128)(2,1)} %all-gather.6.cloned.1.call-done, bf16[1536,768]{1,0:T(8,128)(2,1)} %collective-permute-done.15, bf16[1536,768]{1,0:T(8,128)(2,1)} %all-gather.8.cloned.1.call-done, pred[]{:T(512)S(6)} %eq.121), kind=kOutput, calls=%fused_computation.23 | convolution fusion | flops 2417098752 | bytes 11010049 | tf_op jit(solution)/shard_map/dot_general | solution.py:157
  159.8 2.8 %fusion.18 = f32[1024,768]{0,1:T(8,128)S(1)} fusion(bf16[1536,1024]{1,0:T(8,128)(2,1)S(1)} %copy-done.38, bf16[1536,768]{1,0:T(8,128)(2,1)S(1)} %copy-done.39, bf16[1536,768]{1,0:T(8,128)(2,1)} %collective-permute-done.15, pred[]{:T(512)S(6)} %eq.121), kind=kOutput, calls=%fused_computation.25 | convolution fusion | flops 2417098752 | bytes 11010049 | tf_op jit(solution)/shard_map/dot_general | solution.py:156
  166.7 10.8 %convolution_convert_fusion = bf16[1024,1536]{1,0:T(8,128)(2,1)} fusion(bf16[1536,768]{1,0:T(8,128)(2,1)S(1)} %copy-done.5, bf16[1536,768]{1,0:T(8,128)(2,1)} %get-tuple-element.13, bf16[1024,1536]{0,1:T(8,128)(2,1)} %copy-done.1, f32[1536]{0:T(1024)S(1)} %copy-done.42, f32[1024]{0:T(1024)S(1)} %add_rsqrt_fusion, f32[1024]{0:T(1024)S(1)} %broadcast_multiply_fusion), kind=kOutput, calls=%fused_computation.16 | convolution fusion | flops 4845207552 | bytes 11024384 | tf_op jit(solution)/shard_map/dot_general | solution.py:167
  177.5 46.6 %reduce-scatter.4.cloned.1.call-done = bf16[128,1536]{1,0:T(8,128)(2,1)} async-done(((bf16[1024,1536]{1,0:T(8,128)(2,1)}), bf16[128,1536]{1,0:T(8,128)(2,1)}) %reduce-scatter.4.cloned.1.call-update) | async-done | bytes 393232
  (167 shorter events, 36.4 us)
Async XLA Ops:
  6.5 63.7 %copy-start = (bf16[1536,192]{0,1:T(8,128)(2,1)S(1)}, bf16[1536,192]{0,1:T(8,128)(2,1)}, u32[]{:S(2)}) copy-start(bf16[1536,192]{0,1:T(8,128)(2,1)} %param.18) | copy-start | bytes 1769476
  6.5 60.0 %all-gather.4.cloned.1.call-start = ((), (), s32[]{:S(2)}) async-start(), calls=%async_computation.1 | async-start | bytes 3538944 | tf_op jit(solution)/shard_map/all_gather | solution.py:124
  8.6 101.1 %all-gather.8.cloned.1.call-start = ((), (), s32[]{:S(2)}) async-start(), calls=%async_computation.3 | async-start | bytes 2654208 | tf_op jit(solution)/shard_map/all_gather | solution.py:129
  8.6 1.6 collective-permute-start
  8.7 2.4 %collective-permute-start.1 = (bf16[48,768]{1,0:T(8,128)(2,1)}, bf16[48,768]{1,0:T(8,128)(2,1)S(1)}, u32[]{:S(2)}, u32[]{:S(2)}) collective-permute-start(bf16[48,768]{1,0:T(8,128)(2,1)} %bitcast.50), channel_id=1, source_target_pairs={{0,8},{8,0},{16,24},{24,16},{32,40},{40,32},{48,56},{56,48},{64,72... | collective-permute-start | bytes 221192 | tf_op jit(solution)/shard_map/ppermute | solution.py:76
  12.0 7.6 %collective-permute-start.2 = (bf16[96,768]{1,0:T(8,128)(2,1)S(1)}, bf16[96,768]{1,0:T(8,128)(2,1)S(1)}, u32[]{:S(2)}, u32[]{:S(2)}) collective-permute-start(bf16[96,768]{1,0:T(8,128)(2,1)S(1)} %maximum_select_fusion), channel_id=1, source_target_pairs={{0,48},{8,56},{16,0},{24,8},{32,16},{40,24},{48,32},{56,40},{64,11... | collective-permute-start | bytes 442376 | tf_op jit(solution)/shard_map/ppermute | solution.py:76
  14.4 7.7 %collective-permute-start.3 = (bf16[96,768]{1,0:T(8,128)(2,1)S(1)}, bf16[96,768]{1,0:T(8,128)(2,1)S(1)}, u32[]{:S(2)}, u32[]{:S(2)}) collective-permute-start(bf16[96,768]{1,0:T(8,128)(2,1)S(1)} %maximum_select_fusion), channel_id=1, source_target_pairs={{0,32},{8,40},{16,48},{24,56},{32,0},{40,8},{48,16},{56,24},{64,96... | collective-permute-start | bytes 442376 | tf_op jit(solution)/shard_map/ppermute | solution.py:76
  15.1 7.9 %collective-permute-start.4 = (bf16[96,768]{1,0:T(8,128)(2,1)S(1)}, bf16[96,768]{1,0:T(8,128)(2,1)S(1)}, u32[]{:S(2)}, u32[]{:S(2)}) collective-permute-start(bf16[96,768]{1,0:T(8,128)(2,1)S(1)} %maximum_select_fusion), channel_id=1, source_target_pairs={{0,16},{8,24},{16,32},{24,40},{32,48},{40,56},{48,0},{56,8},{64,80... | collective-permute-start | bytes 442376 | tf_op jit(solution)/shard_map/ppermute | solution.py:76
  18.7 135.6 %all-gather.6.cloned.1.call-start = ((), (), s32[]{:S(2)}) async-start(), calls=%async_computation.2 | async-start | bytes 3538944 | tf_op jit(solution)/shard_map/all_gather | solution.py:149
  23.1 27.5 %collective-permute-start.5 = (bf16[384,768]{1,0:T(8,128)(2,1)S(1)}, bf16[384,768]{1,0:T(8,128)(2,1)S(1)}, u32[]{:S(2)}, u32[]{:S(2)}) collective-permute-start(bf16[384,768]{1,0:T(8,128)(2,1)S(1)} %pad_maximum_fusion.1), channel_id=1, source_target_pairs={{0,192},{8,200},{16,208},{24,216},{32,224},{40,232},{48,240},{56,2... | collective-permute-start | bytes 1769480 | tf_op jit(solution)/shard_map/ppermute | solution.py:76
  26.2 24.4 %collective-permute-start.6 = (bf16[384,768]{1,0:T(8,128)(2,1)S(1)}, bf16[384,768]{1,0:T(8,128)(2,1)S(1)}, u32[]{:S(2)}, u32[]{:S(2)}) collective-permute-start(bf16[384,768]{1,0:T(8,128)(2,1)S(1)} %pad_maximum_fusion.1), channel_id=1, source_target_pairs={{0,128},{8,136},{16,144},{24,152},{32,160},{40,168},{48,176},{56,1... | collective-permute-start | bytes 1769480 | tf_op jit(solution)/shard_map/ppermute | solution.py:76
  26.8 27.5 %collective-permute-start.7 = (bf16[384,768]{1,0:T(8,128)(2,1)S(1)}, bf16[384,768]{1,0:T(8,128)(2,1)S(1)}, u32[]{:S(2)}, u32[]{:S(2)}) collective-permute-start(bf16[384,768]{1,0:T(8,128)(2,1)S(1)} %pad_maximum_fusion.1), channel_id=1, source_target_pairs={{0,64},{8,72},{16,80},{24,88},{32,96},{40,104},{48,112},{56,120},{... | collective-permute-start | bytes 1769480 | tf_op jit(solution)/shard_map/ppermute | solution.py:76
  73.4 4.6 %collective-permute-start.9 = (bf16[15,192]{0,1:T(8,128)(2,1)S(1)}, bf16[15,192]{0,1:T(8,128)(2,1)S(1)}, u32[]{:S(2)}, u32[]{:S(2)}) collective-permute-start(bf16[15,192]{0,1:T(8,128)(2,1)S(1)} %get-tuple-element.44), channel_id=1, source_target_pairs={{8,0},{16,8},{24,16},{32,24},{40,32},{48,40},{56,48},{64,56},{72,6... | collective-permute-start | bytes 17288 | tf_op jit(solution)/shard_map/ppermute | solution.py:17
  75.4 5.4 %collective-permute-start.8 = (bf16[15,192]{0,1:T(8,128)(2,1)S(1)}, bf16[15,192]{0,1:T(8,128)(2,1)S(1)}, u32[]{:S(2)}, u32[]{:S(2)}) collective-permute-start(bf16[15,192]{0,1:T(8,128)(2,1)S(1)} %get-tuple-element.43), channel_id=1, source_target_pairs={{0,8},{8,16},{16,24},{24,32},{32,40},{40,48},{48,56},{56,64},{64,7... | collective-permute-start | bytes 17288 | tf_op jit(solution)/shard_map/ppermute | solution.py:16
  81.1 26.1 %copy-start.36 = (f32[192]{0:T(256)S(1)}, f32[192]{0:T(256)}, u32[]{:S(2)}) copy-start(f32[192]{0:T(256)} %param.21) | copy-start | bytes 2308
  87.6 1.2 collective-permute-start.10
  89.0 3.7 %collective-permute-start.11 = (f32[3,192]{1,0:T(4,128)S(1)}, f32[3,192]{1,0:T(4,128)S(1)}, u32[]{:S(2)}, u32[]{:S(2)}) collective-permute-start(f32[3,192]{1,0:T(4,128)S(1)} %pad_maximum_fusion.4), channel_id=1, source_target_pairs={{0,16},{8,24},{16,0},{24,8},{32,48},{40,56},{48,32},{56,40},{64,80... | collective-permute-start | bytes 6920 | tf_op jit(solution)/shard_map/ppermute | solution.py:46
  92.7 5.2 %collective-permute-start.12 = (f32[3,192]{1,0:T(4,128)S(1)}, f32[3,192]{1,0:T(4,128)S(1)}, u32[]{:S(2)}, u32[]{:S(2)}) collective-permute-start(f32[3,192]{1,0:T(4,128)S(1)} %pad_maximum_fusion.5), channel_id=1, source_target_pairs={{0,32},{8,40},{16,48},{24,56},{32,0},{40,8},{48,16},{56,24},{64,96... | collective-permute-start | bytes 6920 | tf_op jit(solution)/shard_map/ppermute | solution.py:46
  98.0 3.8 %collective-permute-start.13 = (f32[3,192]{1,0:T(4,128)S(1)}, f32[3,192]{1,0:T(4,128)S(1)}, u32[]{:S(2)}, u32[]{:S(2)}) collective-permute-start(f32[3,192]{1,0:T(4,128)S(1)} %pad_maximum_fusion.6), channel_id=1, source_target_pairs={{0,64},{8,72},{16,80},{24,88},{32,96},{40,104},{48,112},{56,120},{... | collective-permute-start | bytes 6920 | tf_op jit(solution)/shard_map/ppermute | solution.py:46
  101.9 5.2 %collective-permute-start.14 = (f32[3,192]{1,0:T(4,128)S(1)}, f32[3,192]{1,0:T(4,128)S(1)}, u32[]{:S(2)}, u32[]{:S(2)}) collective-permute-start(f32[3,192]{1,0:T(4,128)S(1)} %pad_maximum_fusion.7), channel_id=1, source_target_pairs={{0,128},{8,136},{16,144},{24,152},{32,160},{40,168},{48,176},{56,1... | collective-permute-start | bytes 6920 | tf_op jit(solution)/shard_map/ppermute | solution.py:46
  109.5 114.7 %reduce-scatter.4.cloned.1.call-start = ((), (), s32[]{:S(2)}) async-start(), calls=%async_computation.4 | async-start | bytes 3538944
  109.5 6.8 %collective-permute-start.16 = (bf16[1536,768]{1,0:T(8,128)(2,1)S(1)}, bf16[1536,768]{1,0:T(8,128)(2,1)}, u32[]{:S(2)}, u32[]{:S(2)}) collective-permute-start(bf16[1536,768]{1,0:T(8,128)(2,1)S(1)} %pad_maximum_fusion), channel_id=1, source_target_pairs={{0,8},{8,0},{16,24},{24,16},{32,40},{40,32},{48,56},{56,48},{64,72... | collective-permute-start | bytes 7077896 | tf_op jit(solution)/shard_map/ppermute | solution.py:76
  109.7 10.9 %collective-permute-start.15 = (bf16[1536,768]{1,0:T(8,128)(2,1)}, bf16[1536,768]{1,0:T(8,128)(2,1)}, u32[]{:S(2)}, u32[]{:S(2)}) collective-permute-start(bf16[1536,768]{1,0:T(8,128)(2,1)} %all-gather.8.cloned.1.call-done), channel_id=1, source_target_pairs={{0,8},{8,0},{16,24},{24,16},{32,40},{40,32},{48,56},{56,48},{64,72... | collective-permute-start | bytes 7077896 | tf_op jit(solution)/shard_map/ppermute | solution.py:150
  120.5 39.3 %copy-start.39 = (bf16[1536,768]{1,0:T(8,128)(2,1)S(1)}, bf16[1536,768]{1,0:T(8,128)(2,1)}, u32[]{:S(2)}) copy-start(bf16[1536,768]{1,0:T(8,128)(2,1)} %all-gather.8.cloned.1.call-done) | copy-start | bytes 7077892
  (40 other events, 344.1 us)
Sparse Core Ops, SparseCore 0:
  9.1 57.3 all-gather.3
  68.3 40.3 all-gather.7
  110.5 43.7 all-gather.5
  177.6 46.4 reduce-scatter.3

commit v6 on v5

--- a/solution.py
+++ b/solution.py
@@ -1,6 +1,7 @@
 import jax
 import jax.numpy as jnp
 from jax import lax
+from jax.experimental.layout import Layout, with_layout_constraint
 from jax.sharding import PartitionSpec as P
 
 KERNEL = 31
@@ -122,6 +123,7 @@
     positions = lax.axis_index("tm") * block + jnp.arange(block, dtype=jnp.int32)
     valid = ((frame_mask > 0) & (positions < total_length[0])).astype(jnp.float32)
     feature_block = lax.all_gather(features, "tensor", axis=0, tiled=True)
+    feature_block = with_layout_constraint(feature_block, Layout(major_to_minor=(0, 1)))
     piece = layer_norm(feature_block, norm_gain).astype(jnp.bfloat16)
     my_core = lax.axis_index("tm") % 2
     cols = out_weight.shape[1] // 2
@@ -146,11 +148,11 @@
     var = m2 / count
     scaled = centred * lax.rsqrt(var + 1e-05) * batch_gain + batch_bias
     swished = (scaled * jax.nn.sigmoid(scaled)).astype(jnp.bfloat16)
-    swished_all = lax.all_gather(swished.T, "tensor", axis=0, tiled=True)
+    swished_all = lax.all_gather(swished, "tensor", axis=1, tiled=True)
     out_other = lax.ppermute(out_mine, "tm", [(i, i ^ 1) for i in range(lax.axis_size("tm"))])
     left = jnp.where(my_core == 0, out_mine, out_other)
     right = jnp.where(my_core == 0, out_other, out_mine)
-    contract = (((0,), (0,)), ((), ()))
+    contract = (((1,), (0,)), ((), ()))
     conv_out = jnp.concatenate(
         [
             lax.dot_general(swished_all, left, contract, preferred_element_type=jnp.float32),

time: 235 us -> 225 us (0.957)
  waiting for transfers between devices: 136 us -> 128 us
  local copies, waits for them, and re-layouts: 11.2 us -> 7.22 us
    reduce_scatter x0 -> x1, waiting for transfers between devices: none -> 46.7 us  [shards(): lax.psum_scatter(partial_out.astype(jnp.bfloat16), 'tensor', scatter_dime...]
    unnamed x5 -> x4, waiting for transfers between devices: 46.7 us -> 0.76 us
    all_gather x1, waiting for transfers between devices: 11.2 us -> 3.09 us  [shards(): feature_block = lax.all_gather(features, 'tensor', axis=0, tiled=True)]
    convert_element_type x0 -> x2, other arithmetic: none -> 3.3 us  [the longest x1 2.3 us: shards(): swished = (scaled * jax.nn.sigmoid(scaled)).astype(jnp.bfloat16)]
    unnamed x89 -> x87, local copies, waits for them, and re-layouts: 5.74 us -> 2.7 us
  transfers between devices with their start and end apart: 21 -> 21, of which waited for: 15 -> 15; matrix products, arithmetic and copies ran while one was open for 12% -> 13% of each run, Pallas kernels for 0% -> 0%
where the time goes in v6:
time: 225 us; the launch traced here: 224 us
  waiting for transfers between devices  128 us (57%)
  other arithmetic  26.5 us (12%)
  starting transfers between devices  25.3 us (11%)
  matrix products  21.3 us (9%)
  between operations  16.1 us (7%)
  local copies, waits for them, and re-layouts  7.22 us (3%)
    reduce_scatter x1, waiting for transfers between devices, shards(): lax.psum_scatter(partial_out.astype(jnp.bfloat16), 'tensor', scatter_dime...  46.7 us
    all_gather x1, waiting for transfers between devices, shards(): swished_all = lax.all_gather(swished, 'tensor', axis=1, tiled=True)  34.7 us
    ppermute x9, waiting for transfers between devices, shifted(): return lax.ppermute(value, axis, pairs)  28.7 us
    ppermute x5, waiting for transfers between devices, moments_over(): other = lax.ppermute(stats, axis, pairs)  10.6 us
    dot_general x1, matrix products, shards(): lax.dot_general(hidden, down_t, (((1,), (1,)), ((), ())), preferred_eleme...  10.5 us
    ppermute x9, starting transfers between devices, shifted(): return lax.ppermute(value, axis, pairs)  10.2 us
    ppermute x5, starting transfers between devices, moments_over(): other = lax.ppermute(stats, axis, pairs)  9.98 us
    dot_general x1, matrix products, shards(): lax.dot_general(swished_all, right, contract, preferred_element_type=jnp....  5.52 us
  transfers between devices with their start and end apart: 21, of which 15 were waited for; matrix products, arithmetic and copies ran while one was open for 13% of the time, Pallas kernels for 0%

profile of v6, /device:TPU:2, one launch (start us, length us, event | category | flops | bytes accessed | tf_op | source)
XLA Modules:
  0.0 224.1 jit_solution(17181508772518261467)
XLA Ops:
  10.7 2.3 %collective-permute-start.2 = (bf16[96,768]{1,0:T(8,128)(2,1)S(1)}, bf16[96,768]{1,0:T(8,128)(2,1)S(1)}, u32[]{:S(2)}, u32[]{:S(2)}) collective-permute-start(bf16[96,768]{1,0:T(8,128)(2,1)S(1)} %maximum_select_fusion), channel_id=1, source_target_pairs={{0,48},{8,56},{16,0},{24,8},{32,16},{40,24},{48,32},{56,40},{64,11... | collective-permute-start | bytes 442376 | tf_op jit(solution)/shard_map/ppermute | solution.py:77
  18.3 2.5 %collective-permute-done.3 = bf16[96,768]{1,0:T(8,128)(2,1)S(1)} collective-permute-done((bf16[96,768]{1,0:T(8,128)(2,1)S(1)}, bf16[96,768]{1,0:T(8,128)(2,1)S(1)}, u32[]{:S(2)}, u32[]{:S(2)}) %collective-permute-start.3) | collective-permute-done | bytes 147488 | tf_op jit(solution)/shard_map/ppermute | solution.py:77
  21.8 3.1 %collective-permute-start.5 = (bf16[384,768]{1,0:T(8,128)(2,1)S(1)}, bf16[384,768]{1,0:T(8,128)(2,1)S(1)}, u32[]{:S(2)}, u32[]{:S(2)}) collective-permute-start(bf16[384,768]{1,0:T(8,128)(2,1)S(1)} %pad_maximum_fusion.1), channel_id=1, source_target_pairs={{0,192},{8,200},{16,208},{24,216},{32,224},{40,232},{48,240},{56,2... | collective-permute-start | bytes 1769480 | tf_op jit(solution)/shard_map/ppermute | solution.py:77
  32.8 16.5 %collective-permute-done.5 = bf16[384,768]{1,0:T(8,128)(2,1)S(1)} collective-permute-done((bf16[384,768]{1,0:T(8,128)(2,1)S(1)}, bf16[384,768]{1,0:T(8,128)(2,1)S(1)}, u32[]{:S(2)}, u32[]{:S(2)}) %collective-permute-start.5) | collective-permute-done | bytes 589856 | tf_op jit(solution)/shard_map/ppermute | solution.py:77
  49.3 3.7 %collective-permute-done.7 = bf16[384,768]{1,0:T(8,128)(2,1)S(1)} collective-permute-done((bf16[384,768]{1,0:T(8,128)(2,1)S(1)}, bf16[384,768]{1,0:T(8,128)(2,1)S(1)}, u32[]{:S(2)}, u32[]{:S(2)}) %collective-permute-start.7) | collective-permute-done | bytes 589856 | tf_op jit(solution)/shard_map/ppermute | solution.py:77
  54.0 3.1 %all-gather.4.cloned.1.call-done = bf16[1024,1536]{1,0:T(8,128)(2,1)} async-done(((bf16[128,1536]{1,0:T(8,128)(2,1)}), bf16[1024,1536]{1,0:T(8,128)(2,1)}) %all-gather.4.cloned.1.call-update) | async-done | bytes 3145744 | tf_op jit(solution)/shard_map/all_gather | solution.py:125
  57.1 2.5 %convert_reduce_fusion = f32[1024]{0:T(1024)S(1)} fusion(bf16[1024,1536]{1,0:T(8,128)(2,1)} %all-gather.4.cloned.1.call-done), kind=kLoop, calls=%fused_computation.2 | loop fusion | flops 3144704 | bytes 3149824 | tf_op jit(solution)/shard_map/reduce_sum | solution.py:25
  64.8 2.3 %collective-permute-start.9 = (bf16[15,192]{0,1:T(8,128)(2,1)S(1)}, bf16[15,192]{0,1:T(8,128)(2,1)S(1)}, u32[]{:S(2)}, u32[]{:S(2)}) collective-permute-start(bf16[15,192]{0,1:T(8,128)(2,1)S(1)} %get-tuple-element.44), channel_id=1, source_target_pairs={{8,0},{16,8},{24,16},{32,24},{40,32},{48,40},{56,48},{64,56},{72,6... | collective-permute-start | bytes 17288 | tf_op jit(solution)/shard_map/ppermute | solution.py:18
  67.1 2.2 collective-permute-start.8
  69.4 3.2 %collective-permute-done.8 = bf16[15,192]{0,1:T(8,128)(2,1)S(1)} collective-permute-done((bf16[15,192]{0,1:T(8,128)(2,1)S(1)}, bf16[15,192]{0,1:T(8,128)(2,1)S(1)}, u32[]{:S(2)}, u32[]{:S(2)}) %collective-permute-start.8) | collective-permute-done | bytes 5792 | tf_op jit(solution)/shard_map/ppermute | solution.py:17
  72.8 5.3 %multiply_reduce_fusion.1 = (f32[192]{0:T(256)S(1)}, f32[1024,192]{0,1:T(8,128)S(1)}) fusion(f32[1024]{0:T(1024)S(1)} %get-tuple-element.30, f32[192]{0:T(256)S(1)} %bitcast.64, bf16[1039,192]{0,1:T(8,128)(2,1)S(1)} %constant_dynamic-update-slice_fusion, f32[192]{0:T(256)S(1)} %bitcast.65, f32[192]{0:T(256)S(1)} %bitcast.67, f32[192]{0:T(256)S(1)} %bitcast.68, ...), kind=kLoop, calls=%fused_computation.55 | loop fusion | flops 27328320 | bytes 7112320 | tf_op jit(solution)/shard_map/reduce_sum | solution.py:141
  80.8 3.6 %collective-permute-done.11 = f32[3,192]{1,0:T(4,128)S(1)} collective-permute-done((f32[3,192]{1,0:T(4,128)S(1)}, f32[3,192]{1,0:T(4,128)S(1)}, u32[]{:S(2)}, u32[]{:S(2)}) %collective-permute-start.11) | collective-permute-done | bytes 2336 | tf_op jit(solution)/shard_map/ppermute | solution.py:47
  84.5 2.5 %collective-permute-start.12 = (f32[3,192]{1,0:T(4,128)S(1)}, f32[3,192]{1,0:T(4,128)S(1)}, u32[]{:S(2)}, u32[]{:S(2)}) collective-permute-start(f32[3,192]{1,0:T(4,128)S(1)} %pad_maximum_fusion.5), channel_id=1, source_target_pairs={{0,32},{8,40},{16,48},{24,56},{32,0},{40,8},{48,16},{56,24},{64,96... | collective-permute-start | bytes 6920 | tf_op jit(solution)/shard_map/ppermute | solution.py:47
  87.0 2.7 %collective-permute-done.12 = f32[3,192]{1,0:T(4,128)S(1)} collective-permute-done((f32[3,192]{1,0:T(4,128)S(1)}, f32[3,192]{1,0:T(4,128)S(1)}, u32[]{:S(2)}, u32[]{:S(2)}) %collective-permute-start.12) | collective-permute-done | bytes 2336 | tf_op jit(solution)/shard_map/ppermute | solution.py:47
  89.7 3.7 %collective-permute-start.13 = (f32[3,192]{1,0:T(4,128)S(1)}, f32[3,192]{1,0:T(4,128)S(1)}, u32[]{:S(2)}, u32[]{:S(2)}) collective-permute-start(f32[3,192]{1,0:T(4,128)S(1)} %pad_maximum_fusion.6), channel_id=1, source_target_pairs={{0,64},{8,72},{16,80},{24,88},{32,96},{40,104},{48,112},{56,120},{... | collective-permute-start | bytes 6920 | tf_op jit(solution)/shard_map/ppermute | solution.py:47
  95.1 3.6 %collective-permute-start.14 = (f32[3,192]{1,0:T(4,128)S(1)}, f32[3,192]{1,0:T(4,128)S(1)}, u32[]{:S(2)}, u32[]{:S(2)}) collective-permute-start(f32[3,192]{1,0:T(4,128)S(1)} %pad_maximum_fusion.7), channel_id=1, source_target_pairs={{0,128},{8,136},{16,144},{24,152},{32,160},{40,168},{48,176},{56,1... | collective-permute-start | bytes 6920 | tf_op jit(solution)/shard_map/ppermute | solution.py:47
  100.4 2.3 %multiply_convert_fusion.1 = bf16[1024,192]{0,1:T(8,128)(2,1)} fusion(f32[1024,192]{0,1:T(8,128)} %copy-done.6, f32[192]{0:T(256)S(1)} %copy-done.39, f32[192]{0:T(256)S(1)} %copy-done.40, f32[192]{0:T(256)S(1)} %bitcast.86, f32[192]{0:T(256)S(1)} %bitcast.85), kind=kLoop, calls=%fused_computation.53 | loop fusion | flops 1769472 | bytes 1182720 | tf_op jit(solution)/shard_map/convert_element_type | solution.py:150
  103.3 4.2 %collective-permute-done.16 = bf16[1536,768]{1,0:T(8,128)(2,1)} collective-permute-done((bf16[1536,768]{1,0:T(8,128)(2,1)S(1)}, bf16[1536,768]{1,0:T(8,128)(2,1)}, u32[]{:S(2)}, u32[]{:S(2)}) %collective-permute-start.16) | collective-permute-done | bytes 2359328 | tf_op jit(solution)/shard_map/ppermute | solution.py:77
  107.5 4.1 %broadcast_select_fusion = (bf16[1536,768]{1,0:T(8,128)(2,1)}, bf16[1536,768]{1,0:T(8,128)(2,1)}) fusion(bf16[1536,768]{1,0:T(8,128)(2,1)} %collective-permute-done.16, bf16[1536,768]{1,0:T(8,128)(2,1)S(1)} %pad_maximum_fusion, pred[]{:T(512)S(6)} %eq.121), kind=kLoop, calls=%fused_computation.27 | loop fusion | flops 2359296 | bytes 9437185 | tf_op jit(solution)/shard_map/jit(_where)/select_n | solution.py:102
  111.6 34.7 %all-gather.6.cloned.1.call-done = bf16[1024,1536]{0,1:T(8,128)(2,1)} async-done(((bf16[1024,192]{0,1:T(8,128)(2,1)}), bf16[1024,1536]{0,1:T(8,128)(2,1)}) %all-gather.6.cloned.1.call-update) | async-done | bytes 3145744 | tf_op jit(solution)/shard_map/all_gather | solution.py:151
  146.3 5.5 %fusion.16 = f32[1024,768]{1,0:T(8,128)S(1)} fusion(bf16[1024,1536]{0,1:T(8,128)(2,1)} %all-gather.6.cloned.1.call-done, bf16[1536,768]{1,0:T(8,128)(2,1)} %collective-permute-done.15, bf16[1536,768]{1,0:T(8,128)(2,1)} %all-gather.8.cloned.1.call-done, pred[]{:T(512)S(6)} %eq.121), kind=kOutput, calls=%fused_computation.23 | convolution fusion | flops 2417098752 | bytes 11010049 | tf_op jit(solution)/shard_map/dot_general | solution.py:159
  151.9 2.9 %fusion.18 = f32[1024,768]{1,0:T(8,128)S(1)} fusion(bf16[1024,1536]{0,1:T(8,128)(2,1)S(1)} %copy-done.4, bf16[1536,768]{1,0:T(8,128)(2,1)S(1)} %copy-done.5, bf16[1536,768]{1,0:T(8,128)(2,1)} %collective-permute-done.15, pred[]{:T(512)S(6)} %eq.121), kind=kOutput, calls=%fused_computation.25 | convolution fusion | flops 2417098752 | bytes 11010049 | tf_op jit(solution)/shard_map/dot_general | solution.py:158
  158.4 10.5 %convolution_convert_fusion = bf16[1024,1536]{1,0:T(8,128)(2,1)} fusion(bf16[1536,768]{1,0:T(8,128)(2,1)S(1)} %copy-done.7, bf16[1536,768]{1,0:T(8,128)(2,1)} %get-tuple-element.13, bf16[1024,1536]{1,0:T(8,128)(2,1)} %copy-done.3, f32[1536]{0:T(1024)S(1)} %copy-done.42, f32[1024]{0:T(1024)S(1)} %add_rsqrt_fusion, f32[1024]{0:T(1024)S(1)} %broadcast_multiply_fusion), kind=kOutput, calls=%fused_computation.16 | convolution fusion | flops 4845207552 | bytes 11024384 | tf_op jit(solution)/shard_map/dot_general | solution.py:169
  168.9 46.7 %reduce-scatter.2.cloned.1.call-done = bf16[128,1536]{1,0:T(8,128)(2,1)} async-done(((bf16[1024,1536]{1,0:T(8,128)(2,1)}), bf16[128,1536]{1,0:T(8,128)(2,1)}) %reduce-scatter.2.cloned.1.call-update) | async-done | bytes 393232 | tf_op jit(solution)/shard_map/reduce_scatter | solution.py:172
  (165 shorter events, 34.2 us)
Async XLA Ops:
  6.5 55.4 %copy-start = (bf16[1536,192]{0,1:T(8,128)(2,1)S(1)}, bf16[1536,192]{0,1:T(8,128)(2,1)}, u32[]{:S(2)}) copy-start(bf16[1536,192]{0,1:T(8,128)(2,1)} %param.18) | copy-start | bytes 1769476
  6.5 50.6 %all-gather.4.cloned.1.call-start = ((), (), s32[]{:S(2)}) async-start(), calls=%async_computation.1 | async-start | bytes 3538944 | tf_op jit(solution)/shard_map/all_gather | solution.py:125
  7.3 95.6 %all-gather.8.cloned.1.call-start = ((), (), s32[]{:S(2)}) async-start(), calls=%async_computation.3 | async-start | bytes 2654208 | tf_op jit(solution)/shard_map/all_gather | solution.py:131
  7.3 1.6 collective-permute-start
  7.4 2.4 %collective-permute-start.1 = (bf16[48,768]{1,0:T(8,128)(2,1)}, bf16[48,768]{1,0:T(8,128)(2,1)S(1)}, u32[]{:S(2)}, u32[]{:S(2)}) collective-permute-start(bf16[48,768]{1,0:T(8,128)(2,1)} %bitcast.49), channel_id=1, source_target_pairs={{0,8},{8,0},{16,24},{24,16},{32,40},{40,32},{48,56},{56,48},{64,72... | collective-permute-start | bytes 221192 | tf_op jit(solution)/shard_map/ppermute | solution.py:77
  10.7 7.6 %collective-permute-start.2 = (bf16[96,768]{1,0:T(8,128)(2,1)S(1)}, bf16[96,768]{1,0:T(8,128)(2,1)S(1)}, u32[]{:S(2)}, u32[]{:S(2)}) collective-permute-start(bf16[96,768]{1,0:T(8,128)(2,1)S(1)} %maximum_select_fusion), channel_id=1, source_target_pairs={{0,48},{8,56},{16,0},{24,8},{32,16},{40,24},{48,32},{56,40},{64,11... | collective-permute-start | bytes 442376 | tf_op jit(solution)/shard_map/ppermute | solution.py:77
  13.1 7.7 %collective-permute-start.3 = (bf16[96,768]{1,0:T(8,128)(2,1)S(1)}, bf16[96,768]{1,0:T(8,128)(2,1)S(1)}, u32[]{:S(2)}, u32[]{:S(2)}) collective-permute-start(bf16[96,768]{1,0:T(8,128)(2,1)S(1)} %maximum_select_fusion), channel_id=1, source_target_pairs={{0,32},{8,40},{16,48},{24,56},{32,0},{40,8},{48,16},{56,24},{64,96... | collective-permute-start | bytes 442376 | tf_op jit(solution)/shard_map/ppermute | solution.py:77
  13.8 7.9 %collective-permute-start.4 = (bf16[96,768]{1,0:T(8,128)(2,1)S(1)}, bf16[96,768]{1,0:T(8,128)(2,1)S(1)}, u32[]{:S(2)}, u32[]{:S(2)}) collective-permute-start(bf16[96,768]{1,0:T(8,128)(2,1)S(1)} %maximum_select_fusion), channel_id=1, source_target_pairs={{0,16},{8,24},{16,32},{24,40},{32,48},{40,56},{48,0},{56,8},{64,80... | collective-permute-start | bytes 442376 | tf_op jit(solution)/shard_map/ppermute | solution.py:77
  17.4 128.9 %all-gather.6.cloned.1.call-start = ((), (), s32[]{:S(2)}) async-start(), calls=%async_computation.2 | async-start | bytes 3538944 | tf_op jit(solution)/shard_map/all_gather | solution.py:151
  21.8 27.5 %collective-permute-start.5 = (bf16[384,768]{1,0:T(8,128)(2,1)S(1)}, bf16[384,768]{1,0:T(8,128)(2,1)S(1)}, u32[]{:S(2)}, u32[]{:S(2)}) collective-permute-start(bf16[384,768]{1,0:T(8,128)(2,1)S(1)} %pad_maximum_fusion.1), channel_id=1, source_target_pairs={{0,192},{8,200},{16,208},{24,216},{32,224},{40,232},{48,240},{56,2... | collective-permute-start | bytes 1769480 | tf_op jit(solution)/shard_map/ppermute | solution.py:77
  24.9 24.4 %collective-permute-start.6 = (bf16[384,768]{1,0:T(8,128)(2,1)S(1)}, bf16[384,768]{1,0:T(8,128)(2,1)S(1)}, u32[]{:S(2)}, u32[]{:S(2)}) collective-permute-start(bf16[384,768]{1,0:T(8,128)(2,1)S(1)} %pad_maximum_fusion.1), channel_id=1, source_target_pairs={{0,128},{8,136},{16,144},{24,152},{32,160},{40,168},{48,176},{56,1... | collective-permute-start | bytes 1769480 | tf_op jit(solution)/shard_map/ppermute | solution.py:77
  25.5 27.5 %collective-permute-start.7 = (bf16[384,768]{1,0:T(8,128)(2,1)S(1)}, bf16[384,768]{1,0:T(8,128)(2,1)S(1)}, u32[]{:S(2)}, u32[]{:S(2)}) collective-permute-start(bf16[384,768]{1,0:T(8,128)(2,1)S(1)} %pad_maximum_fusion.1), channel_id=1, source_target_pairs={{0,64},{8,72},{16,80},{24,88},{32,96},{40,104},{48,112},{56,120},{... | collective-permute-start | bytes 1769480 | tf_op jit(solution)/shard_map/ppermute | solution.py:77
  64.8 4.6 %collective-permute-start.9 = (bf16[15,192]{0,1:T(8,128)(2,1)S(1)}, bf16[15,192]{0,1:T(8,128)(2,1)S(1)}, u32[]{:S(2)}, u32[]{:S(2)}) collective-permute-start(bf16[15,192]{0,1:T(8,128)(2,1)S(1)} %get-tuple-element.44), channel_id=1, source_target_pairs={{8,0},{16,8},{24,16},{32,24},{40,32},{48,40},{56,48},{64,56},{72,6... | collective-permute-start | bytes 17288 | tf_op jit(solution)/shard_map/ppermute | solution.py:18
  67.1 5.4 %collective-permute-start.8 = (bf16[15,192]{0,1:T(8,128)(2,1)S(1)}, bf16[15,192]{0,1:T(8,128)(2,1)S(1)}, u32[]{:S(2)}, u32[]{:S(2)}) collective-permute-start(bf16[15,192]{0,1:T(8,128)(2,1)S(1)} %get-tuple-element.43), channel_id=1, source_target_pairs={{0,8},{8,16},{16,24},{24,32},{32,40},{40,48},{48,56},{56,64},{64,7... | collective-permute-start | bytes 17288 | tf_op jit(solution)/shard_map/ppermute | solution.py:17
  72.8 27.5 %copy-start.39 = (f32[192]{0:T(256)S(1)}, f32[192]{0:T(256)}, u32[]{:S(2)}) copy-start(f32[192]{0:T(256)} %param.21) | copy-start | bytes 2308
  79.4 1.2 collective-permute-start.10
  80.7 3.7 %collective-permute-start.11 = (f32[3,192]{1,0:T(4,128)S(1)}, f32[3,192]{1,0:T(4,128)S(1)}, u32[]{:S(2)}, u32[]{:S(2)}) collective-permute-start(f32[3,192]{1,0:T(4,128)S(1)} %pad_maximum_fusion.4), channel_id=1, source_target_pairs={{0,16},{8,24},{16,0},{24,8},{32,48},{40,56},{48,32},{56,40},{64,80... | collective-permute-start | bytes 6920 | tf_op jit(solution)/shard_map/ppermute | solution.py:47
  84.5 5.2 %collective-permute-start.12 = (f32[3,192]{1,0:T(4,128)S(1)}, f32[3,192]{1,0:T(4,128)S(1)}, u32[]{:S(2)}, u32[]{:S(2)}) collective-permute-start(f32[3,192]{1,0:T(4,128)S(1)} %pad_maximum_fusion.5), channel_id=1, source_target_pairs={{0,32},{8,40},{16,48},{24,56},{32,0},{40,8},{48,16},{56,24},{64,96... | collective-permute-start | bytes 6920 | tf_op jit(solution)/shard_map/ppermute | solution.py:47
  89.7 5.3 %collective-permute-start.13 = (f32[3,192]{1,0:T(4,128)S(1)}, f32[3,192]{1,0:T(4,128)S(1)}, u32[]{:S(2)}, u32[]{:S(2)}) collective-permute-start(f32[3,192]{1,0:T(4,128)S(1)} %pad_maximum_fusion.6), channel_id=1, source_target_pairs={{0,64},{8,72},{16,80},{24,88},{32,96},{40,104},{48,112},{56,120},{... | collective-permute-start | bytes 6920 | tf_op jit(solution)/shard_map/ppermute | solution.py:47
  95.1 5.2 %collective-permute-start.14 = (f32[3,192]{1,0:T(4,128)S(1)}, f32[3,192]{1,0:T(4,128)S(1)}, u32[]{:S(2)}, u32[]{:S(2)}) collective-permute-start(f32[3,192]{1,0:T(4,128)S(1)} %pad_maximum_fusion.7), channel_id=1, source_target_pairs={{0,128},{8,136},{16,144},{24,152},{32,160},{40,168},{48,176},{56,1... | collective-permute-start | bytes 6920 | tf_op jit(solution)/shard_map/ppermute | solution.py:47
  102.7 112.9 %reduce-scatter.2.cloned.1.call-start = ((), (), s32[]{:S(2)}) async-start(), calls=%async_computation.4 | async-start | bytes 3538944 | tf_op jit(solution)/shard_map/reduce_scatter | solution.py:172
  102.7 4.8 %collective-permute-start.16 = (bf16[1536,768]{1,0:T(8,128)(2,1)S(1)}, bf16[1536,768]{1,0:T(8,128)(2,1)}, u32[]{:S(2)}, u32[]{:S(2)}) collective-permute-start(bf16[1536,768]{1,0:T(8,128)(2,1)S(1)} %pad_maximum_fusion), channel_id=1, source_target_pairs={{0,8},{8,0},{16,24},{24,16},{32,40},{40,32},{48,56},{56,48},{64,72... | collective-permute-start | bytes 7077896 | tf_op jit(solution)/shard_map/ppermute | solution.py:77
  102.9 8.8 %collective-permute-start.15 = (bf16[1536,768]{1,0:T(8,128)(2,1)}, bf16[1536,768]{1,0:T(8,128)(2,1)}, u32[]{:S(2)}, u32[]{:S(2)}) collective-permute-start(bf16[1536,768]{1,0:T(8,128)(2,1)} %all-gather.8.cloned.1.call-done), channel_id=1, source_target_pairs={{0,8},{8,0},{16,24},{24,16},{32,40},{40,32},{48,56},{56,48},{64,72... | collective-permute-start | bytes 7077896 | tf_op jit(solution)/shard_map/ppermute | solution.py:152
  111.6 40.2 %copy-start.5 = (bf16[1536,768]{1,0:T(8,128)(2,1)S(1)}, bf16[1536,768]{1,0:T(8,128)(2,1)}, u32[]{:S(2)}) copy-start(bf16[1536,768]{1,0:T(8,128)(2,1)} %all-gather.8.cloned.1.call-done) | copy-start | bytes 7077892
  (40 other events, 341.9 us)
Sparse Core Ops, SparseCore 0:
  9.1 47.9 all-gather.3
  58.9 40.1 all-gather.7
  102.8 43.4 all-gather.5
  169.0 46.5 reduce-scatter.1

commit v7 on v6

--- a/solution.py
+++ b/solution.py
@@ -101,6 +101,13 @@
     up_whole = jnp.where(my_c == 0, whole, swapped)
     down_whole = jnp.where(my_c == 0, swapped, whole)
     return up_whole, down_whole, tie
+
+
+def gather_by_all_to_all(up_piece, down_piece, axis):
+    size = lax.axis_size(axis)
+    sent = jnp.stack([up_piece, down_piece] * (size // 2))
+    got = lax.all_to_all(sent, axis, 0, 0, tiled=True)
+    return got.reshape(size * up_piece.shape[0], up_piece.shape[1])
 
 
 def shards(
@@ -132,7 +139,6 @@
     value = jnp.dot(piece, value_weight, preferred_element_type=jnp.float32)
     gate = jnp.dot(piece, gate_weight, preferred_element_type=jnp.float32)
     glu = (value * jax.nn.sigmoid(gate) * valid[:, None]).astype(jnp.bfloat16)
-    up_whole, down_t, glu = gather_torus(up_weight, down_weight.T, "tm", glu)
     padded = extended(glu, (("tm", 0),), KERNEL // 2)
     conv = jnp.zeros(glu.shape, jnp.float32)
     for tap in range(KERNEL):
@@ -149,7 +155,11 @@
     scaled = centred * lax.rsqrt(var + 1e-05) * batch_gain + batch_bias
     swished = (scaled * jax.nn.sigmoid(scaled)).astype(jnp.bfloat16)
     swished_all = lax.all_gather(swished, "tensor", axis=1, tiled=True)
-    out_other = lax.ppermute(out_mine, "tm", [(i, i ^ 1) for i in range(lax.axis_size("tm"))])
+    ff_mine = gather_by_all_to_all(up_weight, down_weight.T, "tm")
+    swap = [(i, i ^ 1) for i in range(lax.axis_size("tm"))]
+    out_other, ff_other = lax.ppermute(jnp.stack([out_mine, ff_mine]), "tm", swap)
+    up_whole = jnp.where(my_core == 0, ff_mine, ff_other)
+    down_t = jnp.where(my_core == 0, ff_other, ff_mine)
     left = jnp.where(my_core == 0, out_mine, out_other)
     right = jnp.where(my_core == 0, out_other, out_mine)
     contract = (((1,), (0,)), ((), ()))

time: 225 us -> 253 us (1.12)
  local copies, waits for them, and re-layouts: 7.22 us -> 32 us
  waiting for transfers between devices: 128 us -> 137 us
  starting transfers between devices: 25.3 us -> 22.5 us
    unnamed x87 -> x67, local copies, waits for them, and re-layouts: 2.7 us -> 28.7 us
    ppermute x10 -> x1, waiting for transfers between devices: 28.7 us -> 7.9 us  [shards(): lax.ppermute(jnp.stack([out_mine, ff_mine]), 'tm', swap)]
    all_gather x1, waiting for transfers between devices: 3.09 us -> 22.9 us  [shards(): feature_block = lax.all_gather(features, 'tensor', axis=0, tiled=True)]
    ppermute x5, waiting for transfers between devices: 10.6 us -> 28 us  [moments_over(): other = lax.ppermute(stats, axis, pairs)]
    ppermute x10 -> x1, starting transfers between devices: 10.7 us -> 0.09 us  [shards(): lax.ppermute(jnp.stack([out_mine, ff_mine]), 'tm', swap)]
    all_to_all x0 -> x1, starting transfers between devices: none -> 7.67 us  [gather_by_all_to_all(): got = lax.all_to_all(sent, axis, 0, 0, tiled=True)]
    select_n x7 -> x1, other arithmetic: 6.91 us -> 2.62 us  [shards(): down_t = jnp.where(my_core == 0, ff_other, ff_mine)]
    all_gather x1, waiting for transfers between devices: 34.7 us -> 31.7 us  [shards(): swished_all = lax.all_gather(swished, 'tensor', axis=1, tiled=True)]
  transfers between devices with their start and end apart: 21 -> 13, of which waited for: 15 -> 9; matrix products, arithmetic and copies ran while one was open for 13% -> 20% of each run, Pallas kernels for 0% -> 0%
where the time goes in v7:
time: 253 us; the launch traced here: 252 us
  waiting for transfers between devices  137 us (54%)
  local copies, waits for them, and re-layouts  32 us (13%)
  other arithmetic  24.3 us (10%)
  starting transfers between devices  22.5 us (9%)
  matrix products  21.3 us (8%)
  between operations  15.4 us (6%)
    reduce_scatter x1, waiting for transfers between devices, shards(): lax.psum_scatter(partial_out.astype(jnp.bfloat16), 'tensor', scatter_dime...  45.3 us
    all_gather x1, waiting for transfers between devices, shards(): swished_all = lax.all_gather(swished, 'tensor', axis=1, tiled=True)  31.7 us
    unnamed x67, local copies, waits for them, and re-layouts  28.7 us
    ppermute x5, waiting for transfers between devices, moments_over(): other = lax.ppermute(stats, axis, pairs)  28 us
    all_gather x1, waiting for transfers between devices, shards(): feature_block = lax.all_gather(features, 'tensor', axis=0, tiled=True)  22.9 us
    dot_general x1, matrix products, shards(): lax.dot_general(hidden, down_t, (((1,), (1,)), ((), ())), preferred_eleme...  10.5 us
    ppermute x5, starting transfers between devices, moments_over(): other = lax.ppermute(stats, axis, pairs)  10.3 us
    ppermute x1, waiting for transfers between devices, shards(): lax.ppermute(jnp.stack([out_mine, ff_mine]), 'tm', swap)  7.9 us
  transfers between devices with their start and end apart: 13, of which 9 were waited for; matrix products, arithmetic and copies ran while one was open for 20% of the time, Pallas kernels for 0%

profile of v7, /device:TPU:2, one launch (start us, length us, event | category | flops | bytes accessed | tf_op | source)
XLA Modules:
  0.0 252.3 jit_solution(16429452655850499776)
XLA Ops:
  7.3 1.8 slice_select_fusion
  34.2 22.9 %all-gather.4.cloned.1.call-done = bf16[1024,1536]{1,0:T(8,128)(2,1)} async-done(((bf16[128,1536]{1,0:T(8,128)(2,1)}), bf16[1024,1536]{1,0:T(8,128)(2,1)}) %all-gather.4.cloned.1.call-update) | async-done | bytes 3145744 | tf_op jit(solution)/shard_map/all_gather | solution.py:132
  57.1 2.5 convert_reduce_fusion
  64.5 1.9 collective-permute-start.1
  66.4 2.4 collective-permute-start
  71.8 5.6 %multiply_reduce_fusion.1 = (f32[192]{0:T(256)S(1)}, f32[1024,192]{0,1:T(8,128)S(1)}) fusion(f32[1024]{0:T(1024)S(1)} %get-tuple-element.26, f32[192]{0:T(256)S(1)} %bitcast.136, bf16[15,192]{0,1:T(8,128)(2,1)S(1)} %collective-permute-done.1, bf16[1024,192]{0,1:T(8,128)(2,1)S(1)} %fusion.30, f32[192]{0:T(256)S(1)} %bitcast.137, f32[192]{0:T(256)S(1)} %bitcast.108, ...), kind=kLoop, calls=%fused_computation.71 | loop fusion | flops 36175680 | bytes 1219840 | tf_op jit(solution)/shard_map/reduce_sum | solution.py:147
  81.8 2.4 collective-permute-done.3
  84.3 4.0 %collective-permute-start.4 = (f32[3,192]{1,0:T(4,128)S(1)}, f32[3,192]{1,0:T(4,128)S(1)}, u32[]{:S(2)}, u32[]{:S(2)}) collective-permute-start(f32[3,192]{1,0:T(4,128)S(1)} %pad_maximum_fusion.5), channel_id=1, source_target_pairs={{0,32},{8,40},{16,48},{24,56},{32,0},{40,8},{48,16},{56,24},{64,96... | collective-permute-start | bytes 6920 | tf_op jit(solution)/shard_map/ppermute | solution.py:47
  89.0 7.7 %all-to-all-start = ((bf16[32,48,768]{2,1,0:T(8,128)(2,1)}), bf16[32,48,768]{2,1,0:T(8,128)(2,1)S(1)}, u32[]{:S(2)}, u32[]{:S(2)}) async-start(bf16[32,48,768]{2,1,0:T(8,128)(2,1)} %bitcast_dynamic-update-slice_fusion.15), calls=%async_computation | async-start | bytes 4718592 | tf_op jit(solution)/shard_map/all_to_all | solution.py:109
  96.8 1.6 collective-permute-start.5
  98.4 22.8 %collective-permute-done.5 = f32[3,192]{1,0:T(4,128)S(1)} collective-permute-done((f32[3,192]{1,0:T(4,128)S(1)}, f32[3,192]{1,0:T(4,128)S(1)}, u32[]{:S(2)}, u32[]{:S(2)}) %collective-permute-start.5) | collective-permute-done | bytes 2336 | tf_op jit(solution)/shard_map/ppermute | solution.py:47
  121.2 3.1 %collective-permute-start.6 = (f32[3,192]{1,0:T(4,128)S(1)}, f32[3,192]{1,0:T(4,128)S(1)}, u32[]{:S(2)}, u32[]{:S(2)}) collective-permute-start(f32[3,192]{1,0:T(4,128)S(1)} %pad_maximum_fusion.7), channel_id=1, source_target_pairs={{0,128},{8,136},{16,144},{24,152},{32,160},{40,168},{48,176},{56,1... | collective-permute-start | bytes 6920 | tf_op jit(solution)/shard_map/ppermute | solution.py:47
  124.3 2.5 %collective-permute-done.6 = f32[3,192]{1,0:T(4,128)S(1)} collective-permute-done((f32[3,192]{1,0:T(4,128)S(1)}, f32[3,192]{1,0:T(4,128)S(1)}, u32[]{:S(2)}, u32[]{:S(2)}) %collective-permute-start.6) | collective-permute-done | bytes 2336 | tf_op jit(solution)/shard_map/ppermute | solution.py:47
  126.9 2.3 multiply_convert_fusion.1
  129.3 2.1 pad_maximum_fusion
  131.5 7.9 %collective-permute-done.7 = bf16[2,1536,768]{2,1,0:T(8,128)(2,1)S(1)} collective-permute-done((bf16[2,1536,768]{2,1,0:T(8,128)(2,1)S(1)}, bf16[2,1536,768]{2,1,0:T(8,128)(2,1)S(1)}, u32[]{:S(2)}, u32[]{:S(2)}) %collective-permute-start.7) | collective-permute-done | bytes 4718624 | tf_op jit(solution)/shard_map/ppermute | solution.py:160
  139.4 2.1 copy-done.9
  141.6 2.6 %bitcast_select_fusion = (bf16[1536,768]{1,0:T(8,128)(2,1)}, bf16[1536,768]{1,0:T(8,128)(2,1)}) fusion(bf16[32,48,768]{2,1,0:T(8,128)(2,1)S(1)} %all-to-all-done, pred[]{:T(512)S(6)} %eq.29, bf16[2,1536,768]{2,1,0:T(8,128)(2,1)S(1)} %collective-permute-done.7), kind=kLoop, calls=%fused_computation.25 | loop fusion | flops 2359296 | bytes 9437185 | tf_op jit(solution)/shard_map/jit(_where)/select_n | solution.py:162
  144.2 31.7 %all-gather.6.cloned.1.call-done = bf16[1024,1536]{0,1:T(8,128)(2,1)} async-done(((bf16[1024,192]{0,1:T(8,128)(2,1)}), bf16[1024,1536]{0,1:T(8,128)(2,1)}) %all-gather.6.cloned.1.call-update) | async-done | bytes 3145744 | tf_op jit(solution)/shard_map/all_gather | solution.py:157
  175.9 5.5 %fusion.16 = f32[1024,768]{1,0:T(8,128)S(1)} fusion(bf16[1024,1536]{0,1:T(8,128)(2,1)} %all-gather.6.cloned.1.call-done, bf16[1536,768]{1,0:T(8,128)(2,1)} %all-gather.8.cloned.1.call-done, pred[]{:T(512)S(6)} %eq.29, bf16[2,1536,768]{2,1,0:T(8,128)(2,1)} %copy-done.9), kind=kOutput, calls=%fused_computation.27 | convolution fusion | flops 2417098752 | bytes 11010049 | tf_op jit(solution)/shard_map/dot_general | solution.py:169
  181.5 2.9 %fusion.18 = f32[1024,768]{1,0:T(8,128)S(1)} fusion(bf16[1024,1536]{0,1:T(8,128)(2,1)S(1)} %copy-done.15, bf16[1536,768]{1,0:T(8,128)(2,1)S(1)} %copy-done.7, pred[]{:T(512)S(6)} %eq.29, bf16[2,1536,768]{2,1,0:T(8,128)(2,1)S(1)} %copy-done.10), kind=kOutput, calls=%fused_computation.29 | convolution fusion | flops 2417098752 | bytes 11010049 | tf_op jit(solution)/shard_map/dot_general | solution.py:168
  187.9 10.5 %convolution_convert_fusion = bf16[1024,1536]{1,0:T(8,128)(2,1)} fusion(bf16[1536,768]{1,0:T(8,128)(2,1)S(1)} %copy-done.8, bf16[1536,768]{1,0:T(8,128)(2,1)} %get-tuple-element.9, bf16[1024,1536]{1,0:T(8,128)(2,1)} %copy-done.3, f32[1536]{0:T(1024)S(1)} %copy-done.17, f32[1024]{0:T(1024)S(1)} %add_rsqrt_fusion, f32[1024]{0:T(1024)S(1)} %broadcast_multiply_fusion), kind=kOutput, calls=%fused_computation.17 | convolution fusion | flops 4845207552 | bytes 11024384 | tf_op jit(solution)/shard_map/dot_general | solution.py:179
  198.4 45.3 %reduce-scatter.2.cloned.1.call-done = bf16[128,1536]{1,0:T(8,128)(2,1)} async-done(((bf16[1024,1536]{1,0:T(8,128)(2,1)}), bf16[128,1536]{1,0:T(8,128)(2,1)}) %reduce-scatter.2.cloned.1.call-update) | async-done | bytes 393232 | tf_op jit(solution)/shard_map/reduce_scatter | solution.py:182
  243.8 2.0 add_convert_fusion
  (122 shorter events, 40.8 us)
Async XLA Ops:
  6.5 55.4 %copy-start = (bf16[1536,192]{0,1:T(8,128)(2,1)S(1)}, bf16[1536,192]{0,1:T(8,128)(2,1)}, u32[]{:S(2)}) copy-start(bf16[1536,192]{0,1:T(8,128)(2,1)} %param.18) | copy-start | bytes 1769476
  6.5 12.5 %copy-start.4 = (bf16[48,768]{1,0:T(8,128)(2,1)S(1)}, bf16[48,768]{1,0:T(8,128)(2,1)}, u32[]{:S(2)}) copy-start(bf16[48,768]{1,0:T(8,128)(2,1)} %param.24) | copy-start | bytes 221188
  6.5 11.9 %copy-start.5 = (bf16[768,48]{0,1:T(8,128)(2,1)S(1)}, bf16[768,48]{0,1:T(8,128)(2,1)}, u32[]{:S(2)}) copy-start(bf16[768,48]{0,1:T(8,128)(2,1)} %param.25) | copy-start | bytes 221188
  6.5 50.6 %all-gather.4.cloned.1.call-start = ((), (), s32[]{:S(2)}) async-start(), calls=%async_computation.2 | async-start | bytes 3538944 | tf_op jit(solution)/shard_map/all_gather | solution.py:132
  7.3 122.0 %all-gather.8.cloned.1.call-start = ((), (), s32[]{:S(2)}) async-start(), calls=%async_computation.4 | async-start | bytes 2654208 | tf_op jit(solution)/shard_map/all_gather | solution.py:138
  9.1 24.5 %copy-start.12 = (s32[1024]{0:T(1024)S(1)}, s32[1024]{0:T(1024)}, u32[]{:S(2)}) copy-start(s32[1024]{0:T(1024)} %param.14) | copy-start | bytes 12292
  57.1 2.8 %copy-start.1 = (bf16[1024,1536]{1,0:T(8,128)(2,1)S(1)}, bf16[1024,1536]{1,0:T(8,128)(2,1)}, u32[]{:S(2)}) copy-start(bf16[1024,1536]{1,0:T(8,128)(2,1)} %all-gather.4.cloned.1.call-done) | copy-start | bytes 9437188
  64.5 7.0 %collective-permute-start.1 = (bf16[15,192]{0,1:T(8,128)(2,1)S(1)}, bf16[15,192]{0,1:T(8,128)(2,1)S(1)}, u32[]{:S(2)}, u32[]{:S(2)}) collective-permute-start(bf16[15,192]{0,1:T(8,128)(2,1)S(1)} %get-tuple-element.32), channel_id=1, source_target_pairs={{8,0},{16,8},{24,16},{32,24},{40,32},{48,40},{56,48},{64,56},{72,6... | collective-permute-start | bytes 17288 | tf_op jit(solution)/shard_map/ppermute | solution.py:18
  66.4 5.4 %collective-permute-start = (bf16[15,192]{0,1:T(8,128)(2,1)S(1)}, bf16[15,192]{0,1:T(8,128)(2,1)S(1)}, u32[]{:S(2)}, u32[]{:S(2)}) collective-permute-start(bf16[15,192]{0,1:T(8,128)(2,1)S(1)} %get-tuple-element.31), channel_id=1, source_target_pairs={{0,8},{8,16},{16,24},{24,32},{32,40},{40,48},{48,56},{56,64},{64,7... | collective-permute-start | bytes 17288 | tf_op jit(solution)/shard_map/ppermute | solution.py:17
  78.6 1.7 collective-permute-start.2
  80.4 3.9 %collective-permute-start.3 = (f32[3,192]{1,0:T(4,128)S(1)}, f32[3,192]{1,0:T(4,128)S(1)}, u32[]{:S(2)}, u32[]{:S(2)}) collective-permute-start(f32[3,192]{1,0:T(4,128)S(1)} %pad_maximum_fusion.4), channel_id=1, source_target_pairs={{0,16},{8,24},{16,0},{24,8},{32,48},{40,56},{48,32},{56,40},{64,80... | collective-permute-start | bytes 6920 | tf_op jit(solution)/shard_map/ppermute | solution.py:47
  84.3 12.4 %collective-permute-start.4 = (f32[3,192]{1,0:T(4,128)S(1)}, f32[3,192]{1,0:T(4,128)S(1)}, u32[]{:S(2)}, u32[]{:S(2)}) collective-permute-start(f32[3,192]{1,0:T(4,128)S(1)} %pad_maximum_fusion.5), channel_id=1, source_target_pairs={{0,32},{8,40},{16,48},{24,56},{32,0},{40,8},{48,16},{56,24},{64,96... | collective-permute-start | bytes 6920 | tf_op jit(solution)/shard_map/ppermute | solution.py:47
  89.0 37.9 %copy-start.13 = (f32[192]{0:T(256)S(1)}, f32[192]{0:T(256)}, u32[]{:S(2)}) copy-start(f32[192]{0:T(256)} %param.21) | copy-start | bytes 2308
  89.0 37.9 %copy-start.14 = (f32[192]{0:T(256)S(1)}, f32[192]{0:T(256)}, u32[]{:S(2)}) copy-start(f32[192]{0:T(256)} %param.20) | copy-start | bytes 2308
  89.0 40.3 %all-to-all-start = ((bf16[32,48,768]{2,1,0:T(8,128)(2,1)}), bf16[32,48,768]{2,1,0:T(8,128)(2,1)S(1)}, u32[]{:S(2)}, u32[]{:S(2)}) async-start(bf16[32,48,768]{2,1,0:T(8,128)(2,1)} %bitcast_dynamic-update-slice_fusion.15), calls=%async_computation | async-start | bytes 4718592 | tf_op jit(solution)/shard_map/all_to_all | solution.py:109
  96.7 79.3 %all-gather.6.cloned.1.call-start = ((), (), s32[]{:S(2)}) async-start(), calls=%async_computation.3 | async-start | bytes 3538944 | tf_op jit(solution)/shard_map/all_gather | solution.py:157
  96.8 24.4 %collective-permute-start.5 = (f32[3,192]{1,0:T(4,128)S(1)}, f32[3,192]{1,0:T(4,128)S(1)}, u32[]{:S(2)}, u32[]{:S(2)}) collective-permute-start(f32[3,192]{1,0:T(4,128)S(1)} %pad_maximum_fusion.6), channel_id=1, source_target_pairs={{0,64},{8,72},{16,80},{24,88},{32,96},{40,104},{48,112},{56,120},{... | collective-permute-start | bytes 6920 | tf_op jit(solution)/shard_map/ppermute | solution.py:47
  121.2 5.6 %collective-permute-start.6 = (f32[3,192]{1,0:T(4,128)S(1)}, f32[3,192]{1,0:T(4,128)S(1)}, u32[]{:S(2)}, u32[]{:S(2)}) collective-permute-start(f32[3,192]{1,0:T(4,128)S(1)} %pad_maximum_fusion.7), channel_id=1, source_target_pairs={{0,128},{8,136},{16,144},{24,152},{32,160},{40,168},{48,176},{56,1... | collective-permute-start | bytes 6920 | tf_op jit(solution)/shard_map/ppermute | solution.py:47
  129.2 114.6 %reduce-scatter.2.cloned.1.call-start = ((), (), s32[]{:S(2)}) async-start(), calls=%async_computation.5 | async-start | bytes 3538944 | tf_op jit(solution)/shard_map/reduce_scatter | solution.py:182
  131.4 8.0 %collective-permute-start.7 = (bf16[2,1536,768]{2,1,0:T(8,128)(2,1)S(1)}, bf16[2,1536,768]{2,1,0:T(8,128)(2,1)S(1)}, u32[]{:S(2)}, u32[]{:S(2)}) collective-permute-start(bf16[2,1536,768]{2,1,0:T(8,128)(2,1)S(1)} %pad_maximum_fusion), channel_id=1, source_target_pairs={{0,8},{8,0},{16,24},{24,16},{32,40},{40,32},{48,56},{56,48},{64,72... | collective-permute-start | bytes 14155784 | tf_op jit(solution)/shard_map/ppermute | solution.py:160
  144.2 37.3 %copy-start.7 = (bf16[1536,768]{1,0:T(8,128)(2,1)S(1)}, bf16[1536,768]{1,0:T(8,128)(2,1)}, u32[]{:S(2)}) copy-start(bf16[1536,768]{1,0:T(8,128)(2,1)} %all-gather.8.cloned.1.call-done) | copy-start | bytes 7077892
  175.9 5.5 %copy-start.10 = (bf16[2,1536,768]{2,1,0:T(8,128)(2,1)S(1)}, bf16[2,1536,768]{2,1,0:T(8,128)(2,1)}, u32[]{:S(2)}) copy-start(bf16[2,1536,768]{2,1,0:T(8,128)(2,1)} %copy-done.9) | copy-start | bytes 14155780
  175.9 5.5 %copy-start.15 = (bf16[1024,1536]{0,1:T(8,128)(2,1)S(1)}, bf16[1024,1536]{0,1:T(8,128)(2,1)}, u32[]{:S(2)}) copy-start(bf16[1024,1536]{0,1:T(8,128)(2,1)} %all-gather.6.cloned.1.call-done) | copy-start | bytes 9437188
  181.5 2.9 %copy-start.2 = (bf16[1024,1536]{1,0:T(8,128)(2,1)S(1)}, bf16[1024,1536]{1,0:T(8,128)(2,1)}, u32[]{:S(2)}) copy-start(bf16[1024,1536]{1,0:T(8,128)(2,1)} %all-gather.4.cloned.1.call-done) | copy-start | bytes 9437188
  (7 other events, 11.8 us)
Sparse Core Ops, SparseCore 0:
  9.2 47.9 all-gather.3
  58.9 40.1 all-gather.7
  129.3 46.5 all-gather.5
  198.6 45.1 reduce-scatter.1

commit v8 on v7

--- a/solution.py
+++ b/solution.py
@@ -139,6 +139,8 @@
     value = jnp.dot(piece, value_weight, preferred_element_type=jnp.float32)
     gate = jnp.dot(piece, gate_weight, preferred_element_type=jnp.float32)
     glu = (value * jax.nn.sigmoid(gate) * valid[:, None]).astype(jnp.bfloat16)
+    ff_mine = gather_by_all_to_all(up_weight, down_weight.T, "tm")
+    ff_mine, glu = lax.optimization_barrier((ff_mine, glu))
     padded = extended(glu, (("tm", 0),), KERNEL // 2)
     conv = jnp.zeros(glu.shape, jnp.float32)
     for tap in range(KERNEL):
@@ -155,7 +157,6 @@
     scaled = centred * lax.rsqrt(var + 1e-05) * batch_gain + batch_bias
     swished = (scaled * jax.nn.sigmoid(scaled)).astype(jnp.bfloat16)
     swished_all = lax.all_gather(swished, "tensor", axis=1, tiled=True)
-    ff_mine = gather_by_all_to_all(up_weight, down_weight.T, "tm")
     swap = [(i, i ^ 1) for i in range(lax.axis_size("tm"))]
     out_other, ff_other = lax.ppermute(jnp.stack([out_mine, ff_mine]), "tm", swap)
     up_whole = jnp.where(my_core == 0, ff_mine, ff_other)

time: 253 us -> 240 us (0.949)
  waiting for transfers between devices: 137 us -> 120 us
  local copies, waits for them, and re-layouts: 32 us -> 39.2 us
    all_gather x1, waiting for transfers between devices: 22.9 us -> 4.26 us  [shards(): feature_block = lax.all_gather(features, 'tensor', axis=0, tiled=True)]
    ppermute x5, waiting for transfers between devices: 28 us -> 11.5 us  [moments_over(): other = lax.ppermute(stats, axis, pairs)]
    all_to_all x1, waiting for transfers between devices: 0.01 us -> 13.2 us  [gather_by_all_to_all(): got = lax.all_to_all(sent, axis, 0, 0, tiled=True)]
    unnamed x67 -> x70, local copies, waits for them, and re-layouts: 28.7 us -> 35.8 us
    ppermute x1, waiting for transfers between devices: 0.32 us -> 3.77 us  [extended(): before = lax.ppermute(last, axis, up)]
  transfers between devices with their start and end apart: 13 -> 13, of which waited for: 9 -> 11; matrix products, arithmetic and copies ran while one was open for 20% -> 23% of each run, Pallas kernels for 0% -> 0%
where the time goes in v8:
time: 240 us; the launch traced here: 239 us
  waiting for transfers between devices  120 us (50%)
  local copies, waits for them, and re-layouts  39.2 us (16%)
  other arithmetic  22.8 us (10%)
  matrix products  21.3 us (9%)
  starting transfers between devices  20.8 us (9%)
  between operations  15.5 us (6%)
    reduce_scatter x1, waiting for transfers between devices, shards(): lax.psum_scatter(partial_out.astype(jnp.bfloat16), 'tensor', scatter_dime...  45.6 us
    unnamed x70, local copies, waits for them, and re-layouts  35.8 us
    all_gather x1, waiting for transfers between devices, shards(): swished_all = lax.all_gather(swished, 'tensor', axis=1, tiled=True)  32.5 us
    all_to_all x1, waiting for transfers between devices, gather_by_all_to_all(): got = lax.all_to_all(sent, axis, 0, 0, tiled=True)  13.2 us
    ppermute x5, waiting for transfers between devices, moments_over(): other = lax.ppermute(stats, axis, pairs)  11.5 us
    dot_general x1, matrix products, shards(): lax.dot_general(hidden, down_t, (((1,), (1,)), ((), ())), preferred_eleme...  10.5 us
    ppermute x5, starting transfers between devices, moments_over(): other = lax.ppermute(stats, axis, pairs)  8.49 us
    ppermute x1, waiting for transfers between devices, shards(): lax.ppermute(jnp.stack([out_mine, ff_mine]), 'tm', swap)  7.9 us
  transfers between devices with their start and end apart: 13, of which 11 were waited for; matrix products, arithmetic and copies ran while one was open for 23% of the time, Pallas kernels for 0%

profile of v8, /device:TPU:2, one launch (start us, length us, event | category | flops | bytes accessed | tf_op | source)
XLA Modules:
  0.0 239.2 jit_solution(4305412734782823477)
XLA Ops:
  39.0 7.8 %all-to-all-start = ((bf16[32,48,768]{2,1,0:T(8,128)(2,1)}), bf16[32,48,768]{2,1,0:T(8,128)(2,1)S(1)}, u32[]{:S(2)}, u32[]{:S(2)}) async-start(bf16[32,48,768]{2,1,0:T(8,128)(2,1)} %bitcast_dynamic-update-slice_fusion.15), calls=%async_computation | async-start | bytes 4718592 | tf_op jit(solution)/shard_map/all_to_all | solution.py:109
  52.9 4.3 %all-gather.4.cloned.1.call-done = bf16[1024,1536]{1,0:T(8,128)(2,1)} async-done(((bf16[128,1536]{1,0:T(8,128)(2,1)}), bf16[1024,1536]{1,0:T(8,128)(2,1)}) %all-gather.4.cloned.1.call-update) | async-done | bytes 3145744 | tf_op jit(solution)/shard_map/all_gather | solution.py:132
  57.1 2.5 %convert_reduce_fusion = f32[1024]{0:T(1024)S(1)} fusion(bf16[1024,1536]{1,0:T(8,128)(2,1)} %all-gather.4.cloned.1.call-done), kind=kLoop, calls=%fused_computation.2 | loop fusion | flops 3144704 | bytes 3149824 | tf_op jit(solution)/shard_map/reduce_sum | solution.py:25
  64.4 13.2 %all-to-all-done = bf16[32,48,768]{2,1,0:T(8,128)(2,1)S(1)} async-done(((bf16[32,48,768]{2,1,0:T(8,128)(2,1)}), bf16[32,48,768]{2,1,0:T(8,128)(2,1)S(1)}, u32[]{:S(2)}, u32[]{:S(2)}) %all-to-all-start) | async-done | bytes 2359328 | tf_op jit(solution)/shard_map/all_to_all | solution.py:109
  77.7 1.9 collective-permute-start.1
  79.7 2.4 %collective-permute-start = (bf16[15,192]{0,1:T(8,128)(2,1)S(1)}, bf16[15,192]{0,1:T(8,128)(2,1)S(1)}, u32[]{:S(2)}, u32[]{:S(2)}) collective-permute-start(bf16[15,192]{0,1:T(8,128)(2,1)S(1)} %get-tuple-element.35), channel_id=1, source_target_pairs={{0,8},{8,16},{16,24},{24,32},{32,40},{40,48},{48,56},{56,64},{64,7... | collective-permute-start | bytes 17288 | tf_op jit(solution)/shard_map/ppermute | solution.py:17
  82.1 3.8 %collective-permute-done = bf16[15,192]{0,1:T(8,128)(2,1)S(1)} collective-permute-done((bf16[15,192]{0,1:T(8,128)(2,1)S(1)}, bf16[15,192]{0,1:T(8,128)(2,1)S(1)}, u32[]{:S(2)}, u32[]{:S(2)}) %collective-permute-start) | collective-permute-done | bytes 5792 | tf_op jit(solution)/shard_map/ppermute | solution.py:17
  85.9 5.3 %multiply_reduce_fusion.1 = (f32[192]{0:T(256)S(1)}, f32[1024,192]{0,1:T(8,128)S(1)}) fusion(f32[1024]{0:T(1024)S(1)} %get-tuple-element.30, f32[192]{0:T(256)S(1)} %bitcast.116, bf16[1039,192]{0,1:T(8,128)(2,1)S(1)} %constant_dynamic-update-slice_fusion, f32[192]{0:T(256)S(1)} %bitcast.117, f32[192]{0:T(256)S(1)} %bitcast.119, f32[192]{0:T(256)S(1)} %bitcast.120, ...), kind=kLoop, calls=%fused_computation.57 | loop fusion | flops 27328320 | bytes 7112320 | tf_op jit(solution)/shard_map/reduce_sum | solution.py:149
  94.1 3.6 %collective-permute-done.3 = f32[3,192]{1,0:T(4,128)S(1)} collective-permute-done((f32[3,192]{1,0:T(4,128)S(1)}, f32[3,192]{1,0:T(4,128)S(1)}, u32[]{:S(2)}, u32[]{:S(2)}) %collective-permute-start.3) | collective-permute-done | bytes 2336 | tf_op jit(solution)/shard_map/ppermute | solution.py:47
  97.7 1.8 collective-permute-start.4
  99.5 3.4 %collective-permute-done.4 = f32[3,192]{1,0:T(4,128)S(1)} collective-permute-done((f32[3,192]{1,0:T(4,128)S(1)}, f32[3,192]{1,0:T(4,128)S(1)}, u32[]{:S(2)}, u32[]{:S(2)}) %collective-permute-start.4) | collective-permute-done | bytes 2336 | tf_op jit(solution)/shard_map/ppermute | solution.py:47
  103.0 2.9 %collective-permute-start.5 = (f32[3,192]{1,0:T(4,128)S(1)}, f32[3,192]{1,0:T(4,128)S(1)}, u32[]{:S(2)}, u32[]{:S(2)}) collective-permute-start(f32[3,192]{1,0:T(4,128)S(1)} %pad_maximum_fusion.5), channel_id=1, source_target_pairs={{0,64},{8,72},{16,80},{24,88},{32,96},{40,104},{48,112},{56,120},{... | collective-permute-start | bytes 6920 | tf_op jit(solution)/shard_map/ppermute | solution.py:47
  107.6 3.5 %collective-permute-start.6 = (f32[3,192]{1,0:T(4,128)S(1)}, f32[3,192]{1,0:T(4,128)S(1)}, u32[]{:S(2)}, u32[]{:S(2)}) collective-permute-start(f32[3,192]{1,0:T(4,128)S(1)} %pad_maximum_fusion.6), channel_id=1, source_target_pairs={{0,128},{8,136},{16,144},{24,152},{32,160},{40,168},{48,176},{56,1... | collective-permute-start | bytes 6920 | tf_op jit(solution)/shard_map/ppermute | solution.py:47
  112.8 2.3 multiply_convert_fusion.1
  115.2 2.1 pad_maximum_fusion
  117.4 7.9 %collective-permute-done.7 = bf16[2,1536,768]{2,1,0:T(8,128)(2,1)S(1)} collective-permute-done((bf16[2,1536,768]{2,1,0:T(8,128)(2,1)S(1)}, bf16[2,1536,768]{2,1,0:T(8,128)(2,1)S(1)}, u32[]{:S(2)}, u32[]{:S(2)}) %collective-permute-start.7) | collective-permute-done | bytes 4718624 | tf_op jit(solution)/shard_map/ppermute | solution.py:161
  125.3 2.1 copy-done.9
  127.5 2.5 %broadcast_select_fusion = (bf16[1536,768]{1,0:T(8,128)(2,1)}, bf16[1536,768]{1,0:T(8,128)(2,1)}) fusion(bf16[1536,768]{1,0:T(8,128)(2,1)S(1)} %bitcast.100, pred[]{:T(512)S(6)} %eq.29, bf16[2,1536,768]{2,1,0:T(8,128)(2,1)S(1)} %collective-permute-done.7), kind=kLoop, calls=%fused_computation.29 | loop fusion | flops 2359296 | bytes 9437185 | tf_op jit(solution)/shard_map/jit(_where)/select_n | solution.py:163
  130.0 32.5 %all-gather.6.cloned.1.call-done = bf16[1024,1536]{0,1:T(8,128)(2,1)} async-done(((bf16[1024,192]{0,1:T(8,128)(2,1)}), bf16[1024,1536]{0,1:T(8,128)(2,1)}) %all-gather.6.cloned.1.call-update) | async-done | bytes 3145744 | tf_op jit(solution)/shard_map/all_gather | solution.py:159
  162.5 5.5 %fusion.16 = f32[1024,768]{1,0:T(8,128)S(1)} fusion(bf16[1024,1536]{0,1:T(8,128)(2,1)} %all-gather.6.cloned.1.call-done, bf16[1536,768]{1,0:T(8,128)(2,1)} %all-gather.8.cloned.1.call-done, pred[]{:T(512)S(6)} %eq.29, bf16[2,1536,768]{2,1,0:T(8,128)(2,1)} %copy-done.9), kind=kOutput, calls=%fused_computation.25 | convolution fusion | flops 2417098752 | bytes 11010049 | tf_op jit(solution)/shard_map/dot_general | solution.py:170
  168.1 2.9 %fusion.18 = f32[1024,768]{1,0:T(8,128)S(1)} fusion(bf16[1024,1536]{0,1:T(8,128)(2,1)S(1)} %copy-done.16, bf16[1536,768]{1,0:T(8,128)(2,1)S(1)} %copy-done.7, pred[]{:T(512)S(6)} %eq.29, bf16[2,1536,768]{2,1,0:T(8,128)(2,1)S(1)} %copy-done.10), kind=kOutput, calls=%fused_computation.27 | convolution fusion | flops 2417098752 | bytes 11010049 | tf_op jit(solution)/shard_map/dot_general | solution.py:169
  174.5 10.5 %convolution_convert_fusion = bf16[1024,1536]{1,0:T(8,128)(2,1)} fusion(bf16[1536,768]{1,0:T(8,128)(2,1)S(1)} %copy-done.8, bf16[1536,768]{1,0:T(8,128)(2,1)} %get-tuple-element.13, bf16[1024,1536]{1,0:T(8,128)(2,1)} %copy-done.3, f32[1536]{0:T(1024)S(1)} %copy-done.18, f32[1024]{0:T(1024)S(1)} %add_rsqrt_fusion, f32[1024]{0:T(1024)S(1)} %broadcast_multiply_fusion), kind=kOutput, calls=%fused_computation.17 | convolution fusion | flops 4845207552 | bytes 11024384 | tf_op jit(solution)/shard_map/dot_general | solution.py:180
  185.0 45.6 %reduce-scatter.2.cloned.1.call-done = bf16[128,1536]{1,0:T(8,128)(2,1)} async-done(((bf16[1024,1536]{1,0:T(8,128)(2,1)}), bf16[128,1536]{1,0:T(8,128)(2,1)}) %reduce-scatter.2.cloned.1.call-update) | async-done | bytes 393232 | tf_op jit(solution)/shard_map/reduce_scatter | solution.py:183
  230.7 2.0 add_convert_fusion
  (126 shorter events, 51.4 us)
Async XLA Ops:
  6.5 55.4 %copy-start = (bf16[1536,192]{0,1:T(8,128)(2,1)S(1)}, bf16[1536,192]{0,1:T(8,128)(2,1)}, u32[]{:S(2)}) copy-start(bf16[1536,192]{0,1:T(8,128)(2,1)} %param.18) | copy-start | bytes 1769476
  6.5 21.1 %copy-start.4 = (bf16[48,768]{1,0:T(8,128)(2,1)S(1)}, bf16[48,768]{1,0:T(8,128)(2,1)}, u32[]{:S(2)}) copy-start(bf16[48,768]{1,0:T(8,128)(2,1)} %param.24) | copy-start | bytes 221188
  6.5 20.5 %copy-start.5 = (bf16[768,48]{0,1:T(8,128)(2,1)S(1)}, bf16[768,48]{0,1:T(8,128)(2,1)}, u32[]{:S(2)}) copy-start(bf16[768,48]{0,1:T(8,128)(2,1)} %param.25) | copy-start | bytes 221188
  6.5 50.6 %all-gather.4.cloned.1.call-start = ((), (), s32[]{:S(2)}) async-start(), calls=%async_computation.2 | async-start | bytes 3538944 | tf_op jit(solution)/shard_map/all_gather | solution.py:132
  39.0 7.8 %copy-start.11 = (bf16[192,1536]{1,0:T(8,128)(2,1)S(1)}, bf16[192,1536]{1,0:T(8,128)(2,1)}, u32[]{:S(2)}) copy-start(bf16[192,1536]{1,0:T(8,128)(2,1)} %param.22) | copy-start | bytes 1769476
  39.0 11.3 %copy-start.13 = (s32[1024]{0:T(1024)S(1)}, s32[1024]{0:T(1024)}, u32[]{:S(2)}) copy-start(s32[1024]{0:T(1024)} %param.14) | copy-start | bytes 12292
  39.0 38.6 %all-to-all-start = ((bf16[32,48,768]{2,1,0:T(8,128)(2,1)}), bf16[32,48,768]{2,1,0:T(8,128)(2,1)S(1)}, u32[]{:S(2)}, u32[]{:S(2)}) async-start(bf16[32,48,768]{2,1,0:T(8,128)(2,1)} %bitcast_dynamic-update-slice_fusion.15), calls=%async_computation | async-start | bytes 4718592 | tf_op jit(solution)/shard_map/all_to_all | solution.py:109
  46.8 68.5 %all-gather.8.cloned.1.call-start = ((), (), s32[]{:S(2)}) async-start(), calls=%async_computation.4 | async-start | bytes 2654208 | tf_op jit(solution)/shard_map/all_gather | solution.py:138
  47.6 114.9 %all-gather.6.cloned.1.call-start = ((), (), s32[]{:S(2)}) async-start(), calls=%async_computation.3 | async-start | bytes 3538944 | tf_op jit(solution)/shard_map/all_gather | solution.py:159
  77.7 4.4 %collective-permute-start.1 = (bf16[15,192]{0,1:T(8,128)(2,1)S(1)}, bf16[15,192]{0,1:T(8,128)(2,1)S(1)}, u32[]{:S(2)}, u32[]{:S(2)}) collective-permute-start(bf16[15,192]{0,1:T(8,128)(2,1)S(1)} %get-tuple-element.36), channel_id=1, source_target_pairs={{8,0},{16,8},{24,16},{32,24},{40,32},{48,40},{56,48},{64,56},{72,6... | collective-permute-start | bytes 17288 | tf_op jit(solution)/shard_map/ppermute | solution.py:18
  79.7 6.2 %collective-permute-start = (bf16[15,192]{0,1:T(8,128)(2,1)S(1)}, bf16[15,192]{0,1:T(8,128)(2,1)S(1)}, u32[]{:S(2)}, u32[]{:S(2)}) collective-permute-start(bf16[15,192]{0,1:T(8,128)(2,1)S(1)} %get-tuple-element.35), channel_id=1, source_target_pairs={{0,8},{8,16},{16,24},{24,32},{32,40},{40,48},{48,56},{56,64},{64,7... | collective-permute-start | bytes 17288 | tf_op jit(solution)/shard_map/ppermute | solution.py:17
  85.9 26.9 %copy-start.14 = (f32[192]{0:T(256)S(1)}, f32[192]{0:T(256)}, u32[]{:S(2)}) copy-start(f32[192]{0:T(256)} %param.21) | copy-start | bytes 2308
  85.9 26.9 %copy-start.15 = (f32[192]{0:T(256)S(1)}, f32[192]{0:T(256)}, u32[]{:S(2)}) copy-start(f32[192]{0:T(256)} %param.20) | copy-start | bytes 2308
  92.5 1.2 collective-permute-start.2
  93.8 3.9 %collective-permute-start.3 = (f32[3,192]{1,0:T(4,128)S(1)}, f32[3,192]{1,0:T(4,128)S(1)}, u32[]{:S(2)}, u32[]{:S(2)}) collective-permute-start(f32[3,192]{1,0:T(4,128)S(1)} %pad_maximum_fusion.3), channel_id=1, source_target_pairs={{0,16},{8,24},{16,0},{24,8},{32,48},{40,56},{48,32},{56,40},{64,80... | collective-permute-start | bytes 6920 | tf_op jit(solution)/shard_map/ppermute | solution.py:47
  97.7 5.2 %collective-permute-start.4 = (f32[3,192]{1,0:T(4,128)S(1)}, f32[3,192]{1,0:T(4,128)S(1)}, u32[]{:S(2)}, u32[]{:S(2)}) collective-permute-start(f32[3,192]{1,0:T(4,128)S(1)} %pad_maximum_fusion.4), channel_id=1, source_target_pairs={{0,32},{8,40},{16,48},{24,56},{32,0},{40,8},{48,16},{56,24},{64,96... | collective-permute-start | bytes 6920 | tf_op jit(solution)/shard_map/ppermute | solution.py:47
  103.0 4.5 %collective-permute-start.5 = (f32[3,192]{1,0:T(4,128)S(1)}, f32[3,192]{1,0:T(4,128)S(1)}, u32[]{:S(2)}, u32[]{:S(2)}) collective-permute-start(f32[3,192]{1,0:T(4,128)S(1)} %pad_maximum_fusion.5), channel_id=1, source_target_pairs={{0,64},{8,72},{16,80},{24,88},{32,96},{40,104},{48,112},{56,120},{... | collective-permute-start | bytes 6920 | tf_op jit(solution)/shard_map/ppermute | solution.py:47
  107.6 5.2 %collective-permute-start.6 = (f32[3,192]{1,0:T(4,128)S(1)}, f32[3,192]{1,0:T(4,128)S(1)}, u32[]{:S(2)}, u32[]{:S(2)}) collective-permute-start(f32[3,192]{1,0:T(4,128)S(1)} %pad_maximum_fusion.6), channel_id=1, source_target_pairs={{0,128},{8,136},{16,144},{24,152},{32,160},{40,168},{48,176},{56,1... | collective-permute-start | bytes 6920 | tf_op jit(solution)/shard_map/ppermute | solution.py:47
  115.2 115.5 %reduce-scatter.2.cloned.1.call-start = ((), (), s32[]{:S(2)}) async-start(), calls=%async_computation.5 | async-start | bytes 3538944 | tf_op jit(solution)/shard_map/reduce_scatter | solution.py:183
  117.3 8.0 %collective-permute-start.7 = (bf16[2,1536,768]{2,1,0:T(8,128)(2,1)S(1)}, bf16[2,1536,768]{2,1,0:T(8,128)(2,1)S(1)}, u32[]{:S(2)}, u32[]{:S(2)}) collective-permute-start(bf16[2,1536,768]{2,1,0:T(8,128)(2,1)S(1)} %pad_maximum_fusion), channel_id=1, source_target_pairs={{0,8},{8,0},{16,24},{24,16},{32,40},{40,32},{48,56},{56,48},{64,72... | collective-permute-start | bytes 14155784 | tf_op jit(solution)/shard_map/ppermute | solution.py:161
  130.0 38.1 %copy-start.7 = (bf16[1536,768]{1,0:T(8,128)(2,1)S(1)}, bf16[1536,768]{1,0:T(8,128)(2,1)}, u32[]{:S(2)}) copy-start(bf16[1536,768]{1,0:T(8,128)(2,1)} %all-gather.8.cloned.1.call-done) | copy-start | bytes 7077892
  162.5 5.5 %copy-start.10 = (bf16[2,1536,768]{2,1,0:T(8,128)(2,1)S(1)}, bf16[2,1536,768]{2,1,0:T(8,128)(2,1)}, u32[]{:S(2)}) copy-start(bf16[2,1536,768]{2,1,0:T(8,128)(2,1)} %copy-done.9) | copy-start | bytes 14155780
  162.5 5.5 %copy-start.16 = (bf16[1024,1536]{0,1:T(8,128)(2,1)S(1)}, bf16[1024,1536]{0,1:T(8,128)(2,1)}, u32[]{:S(2)}) copy-start(bf16[1024,1536]{0,1:T(8,128)(2,1)} %all-gather.6.cloned.1.call-done) | copy-start | bytes 9437188
  168.1 2.9 %copy-start.2 = (bf16[1024,1536]{1,0:T(8,128)(2,1)S(1)}, bf16[1024,1536]{1,0:T(8,128)(2,1)}, u32[]{:S(2)}) copy-start(bf16[1024,1536]{1,0:T(8,128)(2,1)} %all-gather.4.cloned.1.call-done) | copy-start | bytes 9437188
  (8 other events, 14.7 us)
Sparse Core Ops, SparseCore 0:
  9.2 47.9 all-gather.3
  58.9 40.1 all-gather.7
  115.3 47.1 all-gather.5
  185.1 45.4 reduce-scatter.1

commit v9 on v6

--- a/solution.py
+++ b/solution.py
@@ -133,7 +133,18 @@
     gate = jnp.dot(piece, gate_weight, preferred_element_type=jnp.float32)
     glu = (value * jax.nn.sigmoid(gate) * valid[:, None]).astype(jnp.bfloat16)
     up_whole, down_t, glu = gather_torus(up_weight, down_weight.T, "tm", glu)
-    padded = extended(glu, (("tm", 0),), KERNEL // 2)
+    reach = KERNEL // 2
+    edges = jnp.concatenate([piece[:reach], piece[block - reach :]], axis=0)
+    edge_valid = jnp.concatenate([valid[:reach], valid[block - reach :]], axis=0)
+    edge_value = jnp.dot(edges, value_weight, preferred_element_type=jnp.float32)
+    edge_gate = jnp.dot(edges, gate_weight, preferred_element_type=jnp.float32)
+    edge_glu = (edge_value * jax.nn.sigmoid(edge_gate) * edge_valid[:, None]).astype(jnp.bfloat16)
+    devices = lax.axis_size("tm")
+    up = [(i, (i + 1) % devices) for i in range(devices - 1)]
+    down = [(j, i) for i, j in up]
+    before = lax.ppermute(edge_glu[reach:], "tm", up)
+    after = lax.ppermute(edge_glu[:reach], "tm", down)
+    padded = jnp.concatenate([before, glu, after], axis=0)
     conv = jnp.zeros(glu.shape, jnp.float32)
     for tap in range(KERNEL):
         conv = conv + padded[tap : tap + block].astype(jnp.float32) * depth_kernel[tap]

time: 225 us -> 228 us (1.013)
  other arithmetic: 26.5 us -> 30 us
  transfers between devices with their start and end apart: 21 -> 21, of which waited for: 15 -> 15; matrix products, arithmetic and copies ran while one was open for 13% -> 15% of each run, Pallas kernels for 0% -> 0%
where the time goes in v9:
time: 228 us; the launch traced here: 227 us
  waiting for transfers between devices  127 us (56%)
  other arithmetic  30 us (13%)
  starting transfers between devices  24.6 us (11%)
  matrix products  21.8 us (10%)
  between operations  15.9 us (7%)
  local copies, waits for them, and re-layouts  7.4 us (3%)
    reduce_scatter x1, waiting for transfers between devices, shards(): lax.psum_scatter(partial_out.astype(jnp.bfloat16), 'tensor', scatter_dime...  46.9 us
    all_gather x1, waiting for transfers between devices, shards(): swished_all = lax.all_gather(swished, 'tensor', axis=1, tiled=True)  36.2 us
    ppermute x9, waiting for transfers between devices, shifted(): return lax.ppermute(value, axis, pairs)  29.2 us
    ppermute x5, waiting for transfers between devices, moments_over(): other = lax.ppermute(stats, axis, pairs)  11.1 us
    dot_general x1, matrix products, shards(): lax.dot_general(hidden, down_t, (((1,), (1,)), ((), ())), preferred_eleme...  10.5 us
    ppermute x9, starting transfers between devices, shifted(): return lax.ppermute(value, axis, pairs)  10.2 us
    ppermute x5, starting transfers between devices, moments_over(): other = lax.ppermute(stats, axis, pairs)  7.87 us
    reduce_sum x1, other arithmetic, shards(): local_sum = jnp.sum(conv * valid[:, None], axis=0)  6.3 us
  transfers between devices with their start and end apart: 21, of which 15 were waited for; matrix products, arithmetic and copies ran while one was open for 15% of the time, Pallas kernels for 0%

profile of v9, /device:TPU:2, one launch (start us, length us, event | category | flops | bytes accessed | tf_op | source)
XLA Modules:
  0.0 226.9 jit_solution(1958063453259780921)
XLA Ops:
  7.9 1.8 slice_select_fusion
  12.5 2.3 %collective-permute-start.3 = (bf16[96,768]{1,0:T(8,128)(2,1)S(1)}, bf16[96,768]{1,0:T(8,128)(2,1)S(1)}, u32[]{:S(2)}, u32[]{:S(2)}) collective-permute-start(bf16[96,768]{1,0:T(8,128)(2,1)S(1)} %maximum_select_fusion), channel_id=1, source_target_pairs={{0,48},{8,56},{16,0},{24,8},{32,16},{40,24},{48,32},{56,40},{64,11... | collective-permute-start | bytes 442376 | tf_op jit(solution)/shard_map/ppermute | solution.py:77
  15.5 1.8 collective-permute-start.5
  19.0 3.5 %collective-permute-done.4 = bf16[96,768]{1,0:T(8,128)(2,1)S(1)} collective-permute-done((bf16[96,768]{1,0:T(8,128)(2,1)S(1)}, bf16[96,768]{1,0:T(8,128)(2,1)S(1)}, u32[]{:S(2)}, u32[]{:S(2)}) %collective-permute-start.4) | collective-permute-done | bytes 147488 | tf_op jit(solution)/shard_map/ppermute | solution.py:77
  23.5 3.1 %collective-permute-start.6 = (bf16[384,768]{1,0:T(8,128)(2,1)S(1)}, bf16[384,768]{1,0:T(8,128)(2,1)S(1)}, u32[]{:S(2)}, u32[]{:S(2)}) collective-permute-start(bf16[384,768]{1,0:T(8,128)(2,1)S(1)} %pad_maximum_fusion.1), channel_id=1, source_target_pairs={{0,192},{8,200},{16,208},{24,216},{32,224},{40,232},{48,240},{56,2... | collective-permute-start | bytes 1769480 | tf_op jit(solution)/shard_map/ppermute | solution.py:77
  34.4 16.5 %collective-permute-done.6 = bf16[384,768]{1,0:T(8,128)(2,1)S(1)} collective-permute-done((bf16[384,768]{1,0:T(8,128)(2,1)S(1)}, bf16[384,768]{1,0:T(8,128)(2,1)S(1)}, u32[]{:S(2)}, u32[]{:S(2)}) %collective-permute-start.6) | collective-permute-done | bytes 589856 | tf_op jit(solution)/shard_map/ppermute | solution.py:77
  50.9 3.7 %collective-permute-done.8 = bf16[384,768]{1,0:T(8,128)(2,1)S(1)} collective-permute-done((bf16[384,768]{1,0:T(8,128)(2,1)S(1)}, bf16[384,768]{1,0:T(8,128)(2,1)S(1)}, u32[]{:S(2)}, u32[]{:S(2)}) %collective-permute-start.8) | collective-permute-done | bytes 589856 | tf_op jit(solution)/shard_map/ppermute | solution.py:77
  57.1 2.5 %convert_reduce_fusion = f32[1024]{0:T(1024)S(1)} fusion(bf16[1024,1536]{1,0:T(8,128)(2,1)} %all-gather.4.cloned.1.call-done), kind=kLoop, calls=%fused_computation.2 | loop fusion | flops 3144704 | bytes 3149824 | tf_op jit(solution)/shard_map/reduce_sum | solution.py:25
  63.9 3.9 %collective-permute-start.9 = (bf16[15,192]{1,0:T(8,128)(2,1)S(1)}, bf16[15,192]{1,0:T(8,128)(2,1)S(1)}, u32[]{:S(2)}, u32[]{:S(2)}) collective-permute-start(bf16[15,192]{1,0:T(8,128)(2,1)S(1)} %get-tuple-element.81), channel_id=1, source_target_pairs={{8,0},{16,8},{24,16},{32,24},{40,32},{48,40},{56,48},{64,56},{72,6... | collective-permute-start | bytes 17288 | tf_op jit(solution)/shard_map/ppermute | solution.py:146
  68.0 2.1 collective-permute-start
  73.3 6.3 %multiply_reduce_fusion.1 = (f32[192]{0:T(256)S(1)}, f32[1024,192]{0,1:T(8,128)S(1)}) fusion(f32[1024]{0:T(1024)S(1)} %get-tuple-element.30, f32[192]{0:T(256)S(1)} %bitcast.66, bf16[15,192]{0,1:T(8,128)(2,1)S(1)} %copy.15, bf16[1024,192]{0,1:T(8,128)(2,1)S(1)} %fusion.30, f32[192]{0:T(256)S(1)} %bitcast.67, f32[192]{0:T(256)S(1)} %bitcast.69, ...), kind=kLoop, calls=%fused_computation.76 | loop fusion | flops 36175680 | bytes 1219840 | tf_op jit(solution)/shard_map/reduce_sum | solution.py:152
  83.8 3.4 %collective-permute-done.11 = f32[3,192]{1,0:T(4,128)S(1)} collective-permute-done((f32[3,192]{1,0:T(4,128)S(1)}, f32[3,192]{1,0:T(4,128)S(1)}, u32[]{:S(2)}, u32[]{:S(2)}) %collective-permute-start.11) | collective-permute-done | bytes 2336 | tf_op jit(solution)/shard_map/ppermute | solution.py:47
  89.0 3.4 %collective-permute-done.12 = f32[3,192]{1,0:T(4,128)S(1)} collective-permute-done((f32[3,192]{1,0:T(4,128)S(1)}, f32[3,192]{1,0:T(4,128)S(1)}, u32[]{:S(2)}, u32[]{:S(2)}) %collective-permute-start.12) | collective-permute-done | bytes 2336 | tf_op jit(solution)/shard_map/ppermute | solution.py:47
  92.5 2.1 collective-permute-start.13
  96.2 3.6 %collective-permute-start.14 = (f32[3,192]{1,0:T(4,128)S(1)}, f32[3,192]{1,0:T(4,128)S(1)}, u32[]{:S(2)}, u32[]{:S(2)}) collective-permute-start(f32[3,192]{1,0:T(4,128)S(1)} %pad_maximum_fusion.11), channel_id=1, source_target_pairs={{0,128},{8,136},{16,144},{24,152},{32,160},{40,168},{48,176},{56,1... | collective-permute-start | bytes 6920 | tf_op jit(solution)/shard_map/ppermute | solution.py:47
  101.5 2.3 %multiply_convert_fusion.1 = bf16[1024,192]{0,1:T(8,128)(2,1)} fusion(f32[1024,192]{0,1:T(8,128)} %copy-done.6, f32[192]{0:T(256)} %param.21, f32[192]{0:T(256)} %param.20, f32[192]{0:T(256)S(1)} %bitcast.88, f32[192]{0:T(256)S(1)} %bitcast.87), kind=kLoop, calls=%fused_computation.74 | loop fusion | flops 1769472 | bytes 1182720 | tf_op jit(solution)/shard_map/convert_element_type | solution.py:161
  104.5 4.2 %collective-permute-done.16 = bf16[1536,768]{1,0:T(8,128)(2,1)} collective-permute-done((bf16[1536,768]{1,0:T(8,128)(2,1)S(1)}, bf16[1536,768]{1,0:T(8,128)(2,1)}, u32[]{:S(2)}, u32[]{:S(2)}) %collective-permute-start.16) | collective-permute-done | bytes 2359328 | tf_op jit(solution)/shard_map/ppermute | solution.py:77
  108.7 4.1 %broadcast_select_fusion = (bf16[1536,768]{1,0:T(8,128)(2,1)}, bf16[1536,768]{1,0:T(8,128)(2,1)}) fusion(bf16[1536,768]{1,0:T(8,128)(2,1)} %collective-permute-done.16, bf16[1536,768]{1,0:T(8,128)(2,1)S(1)} %pad_maximum_fusion, pred[]{:T(512)S(6)} %eq.121), kind=kLoop, calls=%fused_computation.27 | loop fusion | flops 2359296 | bytes 9437185 | tf_op jit(solution)/shard_map/jit(_where)/select_n | solution.py:102
  112.8 36.2 %all-gather.6.cloned.1.call-done = bf16[1024,1536]{0,1:T(8,128)(2,1)} async-done(((bf16[1024,192]{0,1:T(8,128)(2,1)}), bf16[1024,1536]{0,1:T(8,128)(2,1)}) %all-gather.6.cloned.1.call-update) | async-done | bytes 3145744 | tf_op jit(solution)/shard_map/all_gather | solution.py:162
  149.0 5.5 %fusion.16 = f32[1024,768]{1,0:T(8,128)S(1)} fusion(bf16[1024,1536]{0,1:T(8,128)(2,1)} %all-gather.6.cloned.1.call-done, bf16[1536,768]{1,0:T(8,128)(2,1)} %collective-permute-done.15, bf16[1536,768]{1,0:T(8,128)(2,1)} %all-gather.8.cloned.1.call-done, pred[]{:T(512)S(6)} %eq.121), kind=kOutput, calls=%fused_computation.23 | convolution fusion | flops 2417098752 | bytes 11010049 | tf_op jit(solution)/shard_map/dot_general | solution.py:170
  154.5 2.9 %fusion.18 = f32[1024,768]{1,0:T(8,128)S(1)} fusion(bf16[1024,1536]{0,1:T(8,128)(2,1)S(1)} %copy-done.4, bf16[1536,768]{1,0:T(8,128)(2,1)S(1)} %copy-done.5, bf16[1536,768]{1,0:T(8,128)(2,1)} %collective-permute-done.15, pred[]{:T(512)S(6)} %eq.121), kind=kOutput, calls=%fused_computation.25 | convolution fusion | flops 2417098752 | bytes 11010049 | tf_op jit(solution)/shard_map/dot_general | solution.py:169
  161.0 10.5 %convolution_convert_fusion = bf16[1024,1536]{1,0:T(8,128)(2,1)} fusion(bf16[1536,768]{1,0:T(8,128)(2,1)S(1)} %copy-done.7, bf16[1536,768]{1,0:T(8,128)(2,1)} %get-tuple-element.13, bf16[1024,1536]{1,0:T(8,128)(2,1)} %copy-done.3, f32[1536]{0:T(1024)S(1)} %copy-done.33, f32[1024]{0:T(1024)S(1)} %add_rsqrt_fusion, f32[1024]{0:T(1024)S(1)} %broadcast_multiply_fusion), kind=kOutput, calls=%fused_computation.16 | convolution fusion | flops 4845207552 | bytes 11024384 | tf_op jit(solution)/shard_map/dot_general | solution.py:180
  171.5 46.9 %reduce-scatter.2.cloned.1.call-done = bf16[128,1536]{1,0:T(8,128)(2,1)} async-done(((bf16[1024,1536]{1,0:T(8,128)(2,1)}), bf16[128,1536]{1,0:T(8,128)(2,1)}) %reduce-scatter.2.cloned.1.call-update) | async-done | bytes 393232 | tf_op jit(solution)/shard_map/reduce_scatter | solution.py:183
  218.4 2.0 add_convert_fusion
  (152 shorter events, 36.5 us)
Async XLA Ops:
  6.5 55.4 %copy-start = (bf16[1536,192]{0,1:T(8,128)(2,1)S(1)}, bf16[1536,192]{0,1:T(8,128)(2,1)}, u32[]{:S(2)}) copy-start(bf16[1536,192]{0,1:T(8,128)(2,1)} %param.18) | copy-start | bytes 1769476
  6.5 50.6 %all-gather.4.cloned.1.call-start = ((), (), s32[]{:S(2)}) async-start(), calls=%async_computation.1 | async-start | bytes 3538944 | tf_op jit(solution)/shard_map/all_gather | solution.py:125
  7.3 96.8 %all-gather.8.cloned.1.call-start = ((), (), s32[]{:S(2)}) async-start(), calls=%async_computation.3 | async-start | bytes 2654208 | tf_op jit(solution)/shard_map/all_gather | solution.py:131
  7.3 3.3 %collective-permute-start.1 = (bf16[48,768]{1,0:T(8,128)(2,1)}, bf16[48,768]{1,0:T(8,128)(2,1)S(1)}, u32[]{:S(2)}, u32[]{:S(2)}) collective-permute-start(bf16[48,768]{1,0:T(8,128)(2,1)} %param.24), channel_id=1, source_target_pairs={{0,8},{8,0},{16,24},{24,16},{32,40},{40,32},{48,56},{56,48},{64,72... | collective-permute-start | bytes 221192 | tf_op jit(solution)/shard_map/ppermute | solution.py:77
  7.4 4.1 %collective-permute-start.2 = (bf16[48,768]{1,0:T(8,128)(2,1)}, bf16[48,768]{1,0:T(8,128)(2,1)S(1)}, u32[]{:S(2)}, u32[]{:S(2)}) collective-permute-start(bf16[48,768]{1,0:T(8,128)(2,1)} %bitcast.51), channel_id=1, source_target_pairs={{0,8},{8,0},{16,24},{24,16},{32,40},{40,32},{48,56},{56,48},{64,72... | collective-permute-start | bytes 221192 | tf_op jit(solution)/shard_map/ppermute | solution.py:77
  9.7 139.2 %all-gather.6.cloned.1.call-start = ((), (), s32[]{:S(2)}) async-start(), calls=%async_computation.2 | async-start | bytes 3538944 | tf_op jit(solution)/shard_map/all_gather | solution.py:162
  12.5 6.6 %collective-permute-start.3 = (bf16[96,768]{1,0:T(8,128)(2,1)S(1)}, bf16[96,768]{1,0:T(8,128)(2,1)S(1)}, u32[]{:S(2)}, u32[]{:S(2)}) collective-permute-start(bf16[96,768]{1,0:T(8,128)(2,1)S(1)} %maximum_select_fusion), channel_id=1, source_target_pairs={{0,48},{8,56},{16,0},{24,8},{32,16},{40,24},{48,32},{56,40},{64,11... | collective-permute-start | bytes 442376 | tf_op jit(solution)/shard_map/ppermute | solution.py:77
  14.8 7.7 %collective-permute-start.4 = (bf16[96,768]{1,0:T(8,128)(2,1)S(1)}, bf16[96,768]{1,0:T(8,128)(2,1)S(1)}, u32[]{:S(2)}, u32[]{:S(2)}) collective-permute-start(bf16[96,768]{1,0:T(8,128)(2,1)S(1)} %maximum_select_fusion), channel_id=1, source_target_pairs={{0,32},{8,40},{16,48},{24,56},{32,0},{40,8},{48,16},{56,24},{64,96... | collective-permute-start | bytes 442376 | tf_op jit(solution)/shard_map/ppermute | solution.py:77
  15.5 7.8 %collective-permute-start.5 = (bf16[96,768]{1,0:T(8,128)(2,1)S(1)}, bf16[96,768]{1,0:T(8,128)(2,1)S(1)}, u32[]{:S(2)}, u32[]{:S(2)}) collective-permute-start(bf16[96,768]{1,0:T(8,128)(2,1)S(1)} %maximum_select_fusion), channel_id=1, source_target_pairs={{0,16},{8,24},{16,32},{24,40},{32,48},{40,56},{48,0},{56,8},{64,80... | collective-permute-start | bytes 442376 | tf_op jit(solution)/shard_map/ppermute | solution.py:77
  23.5 27.4 %collective-permute-start.6 = (bf16[384,768]{1,0:T(8,128)(2,1)S(1)}, bf16[384,768]{1,0:T(8,128)(2,1)S(1)}, u32[]{:S(2)}, u32[]{:S(2)}) collective-permute-start(bf16[384,768]{1,0:T(8,128)(2,1)S(1)} %pad_maximum_fusion.1), channel_id=1, source_target_pairs={{0,192},{8,200},{16,208},{24,216},{32,224},{40,232},{48,240},{56,2... | collective-permute-start | bytes 1769480 | tf_op jit(solution)/shard_map/ppermute | solution.py:77
  26.6 24.3 %collective-permute-start.7 = (bf16[384,768]{1,0:T(8,128)(2,1)S(1)}, bf16[384,768]{1,0:T(8,128)(2,1)S(1)}, u32[]{:S(2)}, u32[]{:S(2)}) collective-permute-start(bf16[384,768]{1,0:T(8,128)(2,1)S(1)} %pad_maximum_fusion.1), channel_id=1, source_target_pairs={{0,128},{8,136},{16,144},{24,152},{32,160},{40,168},{48,176},{56,1... | collective-permute-start | bytes 1769480 | tf_op jit(solution)/shard_map/ppermute | solution.py:77
  27.2 27.4 %collective-permute-start.8 = (bf16[384,768]{1,0:T(8,128)(2,1)S(1)}, bf16[384,768]{1,0:T(8,128)(2,1)S(1)}, u32[]{:S(2)}, u32[]{:S(2)}) collective-permute-start(bf16[384,768]{1,0:T(8,128)(2,1)S(1)} %pad_maximum_fusion.1), channel_id=1, source_target_pairs={{0,64},{8,72},{16,80},{24,88},{32,96},{40,104},{48,112},{56,120},{... | collective-permute-start | bytes 1769480 | tf_op jit(solution)/shard_map/ppermute | solution.py:77
  63.9 7.4 %collective-permute-start.9 = (bf16[15,192]{1,0:T(8,128)(2,1)S(1)}, bf16[15,192]{1,0:T(8,128)(2,1)S(1)}, u32[]{:S(2)}, u32[]{:S(2)}) collective-permute-start(bf16[15,192]{1,0:T(8,128)(2,1)S(1)} %get-tuple-element.81), channel_id=1, source_target_pairs={{8,0},{16,8},{24,16},{32,24},{40,32},{48,40},{56,48},{64,56},{72,6... | collective-permute-start | bytes 17288 | tf_op jit(solution)/shard_map/ppermute | solution.py:146
  68.0 5.0 %collective-permute-start = (bf16[15,192]{1,0:T(8,128)(2,1)S(1)}, bf16[15,192]{1,0:T(8,128)(2,1)S(1)}, u32[]{:S(2)}, u32[]{:S(2)}) collective-permute-start(bf16[15,192]{1,0:T(8,128)(2,1)S(1)} %get-tuple-element.80), channel_id=1, source_target_pairs={{0,8},{8,16},{16,24},{24,32},{32,40},{40,48},{48,56},{56,64},{64,7... | collective-permute-start | bytes 17288 | tf_op jit(solution)/shard_map/ppermute | solution.py:145
  81.5 1.2 collective-permute-start.10
  83.4 3.7 %collective-permute-start.11 = (f32[3,192]{1,0:T(4,128)S(1)}, f32[3,192]{1,0:T(4,128)S(1)}, u32[]{:S(2)}, u32[]{:S(2)}) collective-permute-start(f32[3,192]{1,0:T(4,128)S(1)} %pad_maximum_fusion.8), channel_id=1, source_target_pairs={{0,16},{8,24},{16,0},{24,8},{32,48},{40,56},{48,32},{56,40},{64,80... | collective-permute-start | bytes 6920 | tf_op jit(solution)/shard_map/ppermute | solution.py:47
  87.2 5.2 %collective-permute-start.12 = (f32[3,192]{1,0:T(4,128)S(1)}, f32[3,192]{1,0:T(4,128)S(1)}, u32[]{:S(2)}, u32[]{:S(2)}) collective-permute-start(f32[3,192]{1,0:T(4,128)S(1)} %pad_maximum_fusion.9), channel_id=1, source_target_pairs={{0,32},{8,40},{16,48},{24,56},{32,0},{40,8},{48,16},{56,24},{64,96... | collective-permute-start | bytes 6920 | tf_op jit(solution)/shard_map/ppermute | solution.py:47
  92.5 3.7 %collective-permute-start.13 = (f32[3,192]{1,0:T(4,128)S(1)}, f32[3,192]{1,0:T(4,128)S(1)}, u32[]{:S(2)}, u32[]{:S(2)}) collective-permute-start(f32[3,192]{1,0:T(4,128)S(1)} %pad_maximum_fusion.10), channel_id=1, source_target_pairs={{0,64},{8,72},{16,80},{24,88},{32,96},{40,104},{48,112},{56,120},{... | collective-permute-start | bytes 6920 | tf_op jit(solution)/shard_map/ppermute | solution.py:47
  96.2 5.2 %collective-permute-start.14 = (f32[3,192]{1,0:T(4,128)S(1)}, f32[3,192]{1,0:T(4,128)S(1)}, u32[]{:S(2)}, u32[]{:S(2)}) collective-permute-start(f32[3,192]{1,0:T(4,128)S(1)} %pad_maximum_fusion.11), channel_id=1, source_target_pairs={{0,128},{8,136},{16,144},{24,152},{32,160},{40,168},{48,176},{56,1... | collective-permute-start | bytes 6920 | tf_op jit(solution)/shard_map/ppermute | solution.py:47
  103.9 114.6 %reduce-scatter.2.cloned.1.call-start = ((), (), s32[]{:S(2)}) async-start(), calls=%async_computation.4 | async-start | bytes 3538944 | tf_op jit(solution)/shard_map/reduce_scatter | solution.py:183
  103.9 4.8 %collective-permute-start.16 = (bf16[1536,768]{1,0:T(8,128)(2,1)S(1)}, bf16[1536,768]{1,0:T(8,128)(2,1)}, u32[]{:S(2)}, u32[]{:S(2)}) collective-permute-start(bf16[1536,768]{1,0:T(8,128)(2,1)S(1)} %pad_maximum_fusion), channel_id=1, source_target_pairs={{0,8},{8,0},{16,24},{24,16},{32,40},{40,32},{48,56},{56,48},{64,72... | collective-permute-start | bytes 7077896 | tf_op jit(solution)/shard_map/ppermute | solution.py:77
  104.0 8.8 %collective-permute-start.15 = (bf16[1536,768]{1,0:T(8,128)(2,1)}, bf16[1536,768]{1,0:T(8,128)(2,1)}, u32[]{:S(2)}, u32[]{:S(2)}) collective-permute-start(bf16[1536,768]{1,0:T(8,128)(2,1)} %all-gather.8.cloned.1.call-done), channel_id=1, source_target_pairs={{0,8},{8,0},{16,24},{24,16},{32,40},{40,32},{48,56},{56,48},{64,72... | collective-permute-start | bytes 7077896 | tf_op jit(solution)/shard_map/ppermute | solution.py:163
  112.8 41.7 %copy-start.5 = (bf16[1536,768]{1,0:T(8,128)(2,1)S(1)}, bf16[1536,768]{1,0:T(8,128)(2,1)}, u32[]{:S(2)}) copy-start(bf16[1536,768]{1,0:T(8,128)(2,1)} %all-gather.8.cloned.1.call-done) | copy-start | bytes 7077892
  149.0 5.5 %copy-start.4 = (bf16[1024,1536]{0,1:T(8,128)(2,1)S(1)}, bf16[1024,1536]{0,1:T(8,128)(2,1)}, u32[]{:S(2)}) copy-start(bf16[1024,1536]{0,1:T(8,128)(2,1)} %all-gather.6.cloned.1.call-done) | copy-start | bytes 9437188
  (31 other events, 138.8 us)
Sparse Core Ops, SparseCore 0:
  9.1 47.9 all-gather.3
  58.9 40.2 all-gather.7
  104.0 44.9 all-gather.5
  171.6 46.7 reduce-scatter.1

commit v10 on v7

--- a/solution.py
+++ b/solution.py
@@ -88,7 +88,8 @@
         return picks
 
     partner = lambda y, x, c: (y, x, 1 - c)
-    other_up, other_down = shifted((up_piece, down_piece), partner)
+    other = shifted(jnp.stack([up_piece, down_piece]), partner)
+    other_up, other_down = other[0], other[1]
     pair_up = jnp.concatenate(ordered(up_piece, [other_up], my_c, cores), axis=0)
     pair_down = jnp.concatenate(ordered(down_piece, [other_down], my_c, cores), axis=0)
     pair = jnp.where(my_c == 0, pair_up, pair_down)
@@ -97,17 +98,7 @@
     got = [shifted(row, lambda y, x, c, d=d: ((y + d) % ys, x, c)) for d in range(1, ys)]
     whole = jnp.concatenate(ordered(row, got, my_y, ys), axis=0)
     whole, tie = lax.optimization_barrier((whole, tie))
-    swapped = shifted(whole, partner)
-    up_whole = jnp.where(my_c == 0, whole, swapped)
-    down_whole = jnp.where(my_c == 0, swapped, whole)
-    return up_whole, down_whole, tie
-
-
-def gather_by_all_to_all(up_piece, down_piece, axis):
-    size = lax.axis_size(axis)
-    sent = jnp.stack([up_piece, down_piece] * (size // 2))
-    got = lax.all_to_all(sent, axis, 0, 0, tiled=True)
-    return got.reshape(size * up_piece.shape[0], up_piece.shape[1])
+    return whole, tie
 
 
 def shards(
@@ -139,6 +130,7 @@
     value = jnp.dot(piece, value_weight, preferred_element_type=jnp.float32)
     gate = jnp.dot(piece, gate_weight, preferred_element_type=jnp.float32)
     glu = (value * jax.nn.sigmoid(gate) * valid[:, None]).astype(jnp.bfloat16)
+    ff_mine, glu = gather_torus(up_weight, down_weight.T, "tm", glu)
     padded = extended(glu, (("tm", 0),), KERNEL // 2)
     conv = jnp.zeros(glu.shape, jnp.float32)
     for tap in range(KERNEL):
@@ -155,7 +147,6 @@
     scaled = centred * lax.rsqrt(var + 1e-05) * batch_gain + batch_bias
     swished = (scaled * jax.nn.sigmoid(scaled)).astype(jnp.bfloat16)
     swished_all = lax.all_gather(swished, "tensor", axis=1, tiled=True)
-    ff_mine = gather_by_all_to_all(up_weight, down_weight.T, "tm")
     swap = [(i, i ^ 1) for i in range(lax.axis_size("tm"))]
     out_other, ff_other = lax.ppermute(jnp.stack([out_mine, ff_mine]), "tm", swap)
     up_whole = jnp.where(my_core == 0, ff_mine, ff_other)

time: 253 us -> 224 us (0.89)
  local copies, waits for them, and re-layouts: 32 us -> 9.36 us
  waiting for transfers between devices: 137 us -> 125 us
  other arithmetic: 24.3 us -> 26.9 us
    ppermute x0 -> x7, waiting for transfers between devices: none -> 25.2 us  [shifted(): return lax.ppermute(value, axis, pairs)]
    unnamed x67 -> x91, local copies, waits for them, and re-layouts: 28.7 us -> 4.94 us
    all_gather x1, waiting for transfers between devices: 22.9 us -> 3.15 us  [shards(): feature_block = lax.all_gather(features, 'tensor', axis=0, tiled=True)]
    ppermute x5, waiting for transfers between devices: 28 us -> 10.5 us  [moments_over(): other = lax.ppermute(stats, axis, pairs)]
    ppermute x0 -> x7, starting transfers between devices: none -> 9.62 us  [shifted(): return lax.ppermute(value, axis, pairs)]
    all_to_all x1 -> x0, starting transfers between devices: 7.67 us -> none  [gather_by_all_to_all(): got = lax.all_to_all(sent, axis, 0, 0, tiled=True)]
    all_gather x1, waiting for transfers between devices: 31.7 us -> 28.5 us  [shards(): swished_all = lax.all_gather(swished, 'tensor', axis=1, tiled=True)]
    ppermute x1, waiting for transfers between devices: 0.32 us -> 3.13 us  [extended(): before = lax.ppermute(last, axis, up)]
  transfers between devices with their start and end apart: 13 -> 19, of which waited for: 9 -> 15; matrix products, arithmetic and copies ran while one was open for 20% -> 13% of each run, Pallas kernels for 0% -> 0%
where the time goes in v10:
time: 224 us; the launch traced here: 223 us
  waiting for transfers between devices  125 us (56%)
  other arithmetic  26.9 us (12%)
  starting transfers between devices  24.6 us (11%)
  matrix products  21.3 us (10%)
  between operations  16.1 us (7%)
  local copies, waits for them, and re-layouts  9.36 us (4%)
    reduce_scatter x1, waiting for transfers between devices, shards(): lax.psum_scatter(partial_out.astype(jnp.bfloat16), 'tensor', scatter_dime...  45.6 us
    all_gather x1, waiting for transfers between devices, shards(): swished_all = lax.all_gather(swished, 'tensor', axis=1, tiled=True)  28.5 us
    ppermute x7, waiting for transfers between devices, shifted(): return lax.ppermute(value, axis, pairs)  25.2 us
    ppermute x5, waiting for transfers between devices, moments_over(): other = lax.ppermute(stats, axis, pairs)  10.5 us
    dot_general x1, matrix products, shards(): lax.dot_general(hidden, down_t, (((1,), (1,)), ((), ())), preferred_eleme...  10.5 us
    ppermute x5, starting transfers between devices, moments_over(): other = lax.ppermute(stats, axis, pairs)  10.1 us
    ppermute x7, starting transfers between devices, shifted(): return lax.ppermute(value, axis, pairs)  9.62 us
    ppermute x1, waiting for transfers between devices, shards(): lax.ppermute(jnp.stack([out_mine, ff_mine]), 'tm', swap)  7.9 us
  transfers between devices with their start and end apart: 19, of which 15 were waited for; matrix products, arithmetic and copies ran while one was open for 13% of the time, Pallas kernels for 0%

profile of v10, /device:TPU:2, one launch (start us, length us, event | category | flops | bytes accessed | tf_op | source)
XLA Modules:
  0.0 222.9 jit_solution(9574126894193071066)
XLA Ops:
  10.7 2.3 %collective-permute-start.1 = (bf16[96,768]{1,0:T(8,128)(2,1)S(1)}, bf16[96,768]{1,0:T(8,128)(2,1)S(1)}, u32[]{:S(2)}, u32[]{:S(2)}) collective-permute-start(bf16[96,768]{1,0:T(8,128)(2,1)S(1)} %maximum_select_fusion), channel_id=1, source_target_pairs={{0,48},{8,56},{16,0},{24,8},{32,16},{40,24},{48,32},{56,40},{64,11... | collective-permute-start | bytes 442376 | tf_op jit(solution)/shard_map/ppermute | solution.py:77
  18.3 2.5 %collective-permute-done.2 = bf16[96,768]{1,0:T(8,128)(2,1)S(1)} collective-permute-done((bf16[96,768]{1,0:T(8,128)(2,1)S(1)}, bf16[96,768]{1,0:T(8,128)(2,1)S(1)}, u32[]{:S(2)}, u32[]{:S(2)}) %collective-permute-start.2) | collective-permute-done | bytes 147488 | tf_op jit(solution)/shard_map/ppermute | solution.py:77
  21.8 3.1 %collective-permute-start.4 = (bf16[384,768]{1,0:T(8,128)(2,1)S(1)}, bf16[384,768]{1,0:T(8,128)(2,1)S(1)}, u32[]{:S(2)}, u32[]{:S(2)}) collective-permute-start(bf16[384,768]{1,0:T(8,128)(2,1)S(1)} %pad_maximum_fusion.2), channel_id=1, source_target_pairs={{0,192},{8,200},{16,208},{24,216},{32,224},{40,232},{48,240},{56,2... | collective-permute-start | bytes 1769480 | tf_op jit(solution)/shard_map/ppermute | solution.py:77
  32.4 16.8 %collective-permute-done.4 = bf16[384,768]{1,0:T(8,128)(2,1)S(1)} collective-permute-done((bf16[384,768]{1,0:T(8,128)(2,1)S(1)}, bf16[384,768]{1,0:T(8,128)(2,1)S(1)}, u32[]{:S(2)}, u32[]{:S(2)}) %collective-permute-start.4) | collective-permute-done | bytes 589856 | tf_op jit(solution)/shard_map/ppermute | solution.py:77
  49.2 3.7 %collective-permute-done.6 = bf16[384,768]{1,0:T(8,128)(2,1)S(1)} collective-permute-done((bf16[384,768]{1,0:T(8,128)(2,1)S(1)}, bf16[384,768]{1,0:T(8,128)(2,1)S(1)}, u32[]{:S(2)}, u32[]{:S(2)}) %collective-permute-start.6) | collective-permute-done | bytes 589856 | tf_op jit(solution)/shard_map/ppermute | solution.py:77
  54.0 3.1 %all-gather.4.cloned.1.call-done = bf16[1024,1536]{1,0:T(8,128)(2,1)} async-done(((bf16[128,1536]{1,0:T(8,128)(2,1)}), bf16[1024,1536]{1,0:T(8,128)(2,1)}) %all-gather.4.cloned.1.call-update) | async-done | bytes 3145744 | tf_op jit(solution)/shard_map/all_gather | solution.py:123
  57.1 2.5 %convert_reduce_fusion = f32[1024]{0:T(1024)S(1)} fusion(bf16[1024,1536]{1,0:T(8,128)(2,1)} %all-gather.4.cloned.1.call-done), kind=kLoop, calls=%fused_computation.2 | loop fusion | flops 3144704 | bytes 3149824 | tf_op jit(solution)/shard_map/reduce_sum | solution.py:25
  64.8 2.3 %collective-permute-start.8 = (bf16[15,192]{0,1:T(8,128)(2,1)S(1)}, bf16[15,192]{0,1:T(8,128)(2,1)S(1)}, u32[]{:S(2)}, u32[]{:S(2)}) collective-permute-start(bf16[15,192]{0,1:T(8,128)(2,1)S(1)} %get-tuple-element.44), channel_id=1, source_target_pairs={{8,0},{16,8},{24,16},{32,24},{40,32},{48,40},{56,48},{64,56},{72,6... | collective-permute-start | bytes 17288 | tf_op jit(solution)/shard_map/ppermute | solution.py:18
  67.1 2.2 %collective-permute-start.7 = (bf16[15,192]{0,1:T(8,128)(2,1)S(1)}, bf16[15,192]{0,1:T(8,128)(2,1)S(1)}, u32[]{:S(2)}, u32[]{:S(2)}) collective-permute-start(bf16[15,192]{0,1:T(8,128)(2,1)S(1)} %get-tuple-element.43), channel_id=1, source_target_pairs={{0,8},{8,16},{16,24},{24,32},{32,40},{40,48},{48,56},{56,64},{64,7... | collective-permute-start | bytes 17288 | tf_op jit(solution)/shard_map/ppermute | solution.py:17
  69.4 3.1 %collective-permute-done.7 = bf16[15,192]{0,1:T(8,128)(2,1)S(1)} collective-permute-done((bf16[15,192]{0,1:T(8,128)(2,1)S(1)}, bf16[15,192]{0,1:T(8,128)(2,1)S(1)}, u32[]{:S(2)}, u32[]{:S(2)}) %collective-permute-start.7) | collective-permute-done | bytes 5792 | tf_op jit(solution)/shard_map/ppermute | solution.py:17
  72.8 5.3 %multiply_reduce_fusion.1 = (f32[192]{0:T(256)S(1)}, f32[1024,192]{0,1:T(8,128)S(1)}) fusion(f32[1024]{0:T(1024)S(1)} %get-tuple-element.30, f32[192]{0:T(256)S(1)} %bitcast.98, bf16[1039,192]{0,1:T(8,128)(2,1)S(1)} %constant_dynamic-update-slice_fusion, f32[192]{0:T(256)S(1)} %bitcast.99, f32[192]{0:T(256)S(1)} %bitcast.101, f32[192]{0:T(256)S(1)} %bitcast.102, ...), kind=kLoop, calls=%fused_computation.58 | loop fusion | flops 27328320 | bytes 7112320 | tf_op jit(solution)/shard_map/reduce_sum | solution.py:139
  80.8 3.6 %collective-permute-done.10 = f32[3,192]{1,0:T(4,128)S(1)} collective-permute-done((f32[3,192]{1,0:T(4,128)S(1)}, f32[3,192]{1,0:T(4,128)S(1)}, u32[]{:S(2)}, u32[]{:S(2)}) %collective-permute-start.10) | collective-permute-done | bytes 2336 | tf_op jit(solution)/shard_map/ppermute | solution.py:47
  84.5 2.6 %collective-permute-start.11 = (f32[3,192]{1,0:T(4,128)S(1)}, f32[3,192]{1,0:T(4,128)S(1)}, u32[]{:S(2)}, u32[]{:S(2)}) collective-permute-start(f32[3,192]{1,0:T(4,128)S(1)} %pad_maximum_fusion.7), channel_id=1, source_target_pairs={{0,32},{8,40},{16,48},{24,56},{32,0},{40,8},{48,16},{56,24},{64,96... | collective-permute-start | bytes 6920 | tf_op jit(solution)/shard_map/ppermute | solution.py:47
  87.1 2.6 %collective-permute-done.11 = f32[3,192]{1,0:T(4,128)S(1)} collective-permute-done((f32[3,192]{1,0:T(4,128)S(1)}, f32[3,192]{1,0:T(4,128)S(1)}, u32[]{:S(2)}, u32[]{:S(2)}) %collective-permute-start.11) | collective-permute-done | bytes 2336 | tf_op jit(solution)/shard_map/ppermute | solution.py:47
  89.7 3.7 %collective-permute-start.12 = (f32[3,192]{1,0:T(4,128)S(1)}, f32[3,192]{1,0:T(4,128)S(1)}, u32[]{:S(2)}, u32[]{:S(2)}) collective-permute-start(f32[3,192]{1,0:T(4,128)S(1)} %pad_maximum_fusion.8), channel_id=1, source_target_pairs={{0,64},{8,72},{16,80},{24,88},{32,96},{40,104},{48,112},{56,120},{... | collective-permute-start | bytes 6920 | tf_op jit(solution)/shard_map/ppermute | solution.py:47
  95.1 3.6 %collective-permute-start.13 = (f32[3,192]{1,0:T(4,128)S(1)}, f32[3,192]{1,0:T(4,128)S(1)}, u32[]{:S(2)}, u32[]{:S(2)}) collective-permute-start(f32[3,192]{1,0:T(4,128)S(1)} %pad_maximum_fusion.9), channel_id=1, source_target_pairs={{0,128},{8,136},{16,144},{24,152},{32,160},{40,168},{48,176},{56,1... | collective-permute-start | bytes 6920 | tf_op jit(solution)/shard_map/ppermute | solution.py:47
  100.4 2.3 %multiply_convert_fusion.1 = bf16[1024,192]{0,1:T(8,128)(2,1)} fusion(f32[1024,192]{0,1:T(8,128)} %copy-done.4, f32[192]{0:T(256)S(1)} %copy-done.40, f32[192]{0:T(256)S(1)} %copy-done.41, f32[192]{0:T(256)S(1)} %bitcast.120, f32[192]{0:T(256)S(1)} %bitcast.119), kind=kLoop, calls=%fused_computation.56 | loop fusion | flops 1769472 | bytes 1182720 | tf_op jit(solution)/shard_map/convert_element_type | solution.py:148
  105.2 7.9 %collective-permute-done.14 = bf16[2,1536,768]{2,1,0:T(8,128)(2,1)S(1)} collective-permute-done((bf16[2,1536,768]{2,1,0:T(8,128)(2,1)S(1)}, bf16[2,1536,768]{2,1,0:T(8,128)(2,1)S(1)}, u32[]{:S(2)}, u32[]{:S(2)}) %collective-permute-start.14) | collective-permute-done | bytes 4718624 | tf_op jit(solution)/shard_map/ppermute | solution.py:151
  115.3 2.5 %broadcast_select_fusion = (bf16[1536,768]{1,0:T(8,128)(2,1)}, bf16[1536,768]{1,0:T(8,128)(2,1)}) fusion(bf16[1536,768]{1,0:T(8,128)(2,1)S(1)} %pad_maximum_fusion.1, pred[]{:T(512)S(6)} %eq.121, bf16[2,1536,768]{2,1,0:T(8,128)(2,1)S(1)} %collective-permute-done.14), kind=kLoop, calls=%fused_computation.30 | loop fusion | flops 2359296 | bytes 9437185 | tf_op jit(solution)/shard_map/jit(_where)/select_n | solution.py:153
  117.8 28.5 %all-gather.6.cloned.1.call-done = bf16[1024,1536]{0,1:T(8,128)(2,1)} async-done(((bf16[1024,192]{0,1:T(8,128)(2,1)}), bf16[1024,1536]{0,1:T(8,128)(2,1)}) %all-gather.6.cloned.1.call-update) | async-done | bytes 3145744 | tf_op jit(solution)/shard_map/all_gather | solution.py:149
  146.3 5.5 %fusion.16 = f32[1024,768]{1,0:T(8,128)S(1)} fusion(bf16[1024,1536]{0,1:T(8,128)(2,1)} %all-gather.6.cloned.1.call-done, bf16[1536,768]{1,0:T(8,128)(2,1)} %all-gather.8.cloned.1.call-done, pred[]{:T(512)S(6)} %eq.121, bf16[2,1536,768]{2,1,0:T(8,128)(2,1)} %copy-done.7), kind=kOutput, calls=%fused_computation.26 | convolution fusion | flops 2417098752 | bytes 11010049 | tf_op jit(solution)/shard_map/dot_general | solution.py:160
  151.9 2.9 %fusion.18 = f32[1024,768]{1,0:T(8,128)S(1)} fusion(bf16[1024,1536]{0,1:T(8,128)(2,1)S(1)} %copy-done.42, bf16[1536,768]{1,0:T(8,128)(2,1)S(1)} %copy-done.5, pred[]{:T(512)S(6)} %eq.121, bf16[2,1536,768]{2,1,0:T(8,128)(2,1)S(1)} %copy-done.8), kind=kOutput, calls=%fused_computation.28 | convolution fusion | flops 2417098752 | bytes 11010049 | tf_op jit(solution)/shard_map/dot_general | solution.py:159
  158.3 10.5 %convolution_convert_fusion = bf16[1024,1536]{1,0:T(8,128)(2,1)} fusion(bf16[1536,768]{1,0:T(8,128)(2,1)S(1)} %copy-done.6, bf16[1536,768]{1,0:T(8,128)(2,1)} %get-tuple-element.13, bf16[1024,1536]{1,0:T(8,128)(2,1)} %copy-done.3, f32[1536]{0:T(1024)S(1)} %copy-done.44, f32[1024]{0:T(1024)S(1)} %add_rsqrt_fusion, f32[1024]{0:T(1024)S(1)} %broadcast_multiply_fusion), kind=kOutput, calls=%fused_computation.17 | convolution fusion | flops 4845207552 | bytes 11024384 | tf_op jit(solution)/shard_map/dot_general | solution.py:170
  168.8 45.6 %reduce-scatter.2.cloned.1.call-done = bf16[128,1536]{1,0:T(8,128)(2,1)} async-done(((bf16[1024,1536]{1,0:T(8,128)(2,1)}), bf16[128,1536]{1,0:T(8,128)(2,1)}) %reduce-scatter.2.cloned.1.call-update) | async-done | bytes 393232 | tf_op jit(solution)/shard_map/reduce_scatter | solution.py:173
  (166 shorter events, 38.1 us)
Async XLA Ops:
  6.5 55.4 %copy-start = (bf16[1536,192]{0,1:T(8,128)(2,1)S(1)}, bf16[1536,192]{0,1:T(8,128)(2,1)}, u32[]{:S(2)}) copy-start(bf16[1536,192]{0,1:T(8,128)(2,1)} %param.18) | copy-start | bytes 1769476
  6.5 19.9 %copy-start.38 = (s32[1024]{0:T(1024)S(1)}, s32[1024]{0:T(1024)}, u32[]{:S(2)}) copy-start(s32[1024]{0:T(1024)} %param.14) | copy-start | bytes 12292
  6.5 50.6 %all-gather.4.cloned.1.call-start = ((), (), s32[]{:S(2)}) async-start(), calls=%async_computation.1 | async-start | bytes 3538944 | tf_op jit(solution)/shard_map/all_gather | solution.py:123
  7.3 95.6 %all-gather.8.cloned.1.call-start = ((), (), s32[]{:S(2)}) async-start(), calls=%async_computation.3 | async-start | bytes 2654208 | tf_op jit(solution)/shard_map/all_gather | solution.py:129
  8.2 1.5 collective-permute-start
  10.7 7.6 %collective-permute-start.1 = (bf16[96,768]{1,0:T(8,128)(2,1)S(1)}, bf16[96,768]{1,0:T(8,128)(2,1)S(1)}, u32[]{:S(2)}, u32[]{:S(2)}) collective-permute-start(bf16[96,768]{1,0:T(8,128)(2,1)S(1)} %maximum_select_fusion), channel_id=1, source_target_pairs={{0,48},{8,56},{16,0},{24,8},{32,16},{40,24},{48,32},{56,40},{64,11... | collective-permute-start | bytes 442376 | tf_op jit(solution)/shard_map/ppermute | solution.py:77
  13.0 7.7 %collective-permute-start.2 = (bf16[96,768]{1,0:T(8,128)(2,1)S(1)}, bf16[96,768]{1,0:T(8,128)(2,1)S(1)}, u32[]{:S(2)}, u32[]{:S(2)}) collective-permute-start(bf16[96,768]{1,0:T(8,128)(2,1)S(1)} %maximum_select_fusion), channel_id=1, source_target_pairs={{0,32},{8,40},{16,48},{24,56},{32,0},{40,8},{48,16},{56,24},{64,96... | collective-permute-start | bytes 442376 | tf_op jit(solution)/shard_map/ppermute | solution.py:77
  13.7 7.9 %collective-permute-start.3 = (bf16[96,768]{1,0:T(8,128)(2,1)S(1)}, bf16[96,768]{1,0:T(8,128)(2,1)S(1)}, u32[]{:S(2)}, u32[]{:S(2)}) collective-permute-start(bf16[96,768]{1,0:T(8,128)(2,1)S(1)} %maximum_select_fusion), channel_id=1, source_target_pairs={{0,16},{8,24},{16,32},{24,40},{32,48},{40,56},{48,0},{56,8},{64,80... | collective-permute-start | bytes 442376 | tf_op jit(solution)/shard_map/ppermute | solution.py:77
  17.4 128.9 %all-gather.6.cloned.1.call-start = ((), (), s32[]{:S(2)}) async-start(), calls=%async_computation.2 | async-start | bytes 3538944 | tf_op jit(solution)/shard_map/all_gather | solution.py:149
  21.8 27.5 %collective-permute-start.4 = (bf16[384,768]{1,0:T(8,128)(2,1)S(1)}, bf16[384,768]{1,0:T(8,128)(2,1)S(1)}, u32[]{:S(2)}, u32[]{:S(2)}) collective-permute-start(bf16[384,768]{1,0:T(8,128)(2,1)S(1)} %pad_maximum_fusion.2), channel_id=1, source_target_pairs={{0,192},{8,200},{16,208},{24,216},{32,224},{40,232},{48,240},{56,2... | collective-permute-start | bytes 1769480 | tf_op jit(solution)/shard_map/ppermute | solution.py:77
  24.8 24.4 %collective-permute-start.5 = (bf16[384,768]{1,0:T(8,128)(2,1)S(1)}, bf16[384,768]{1,0:T(8,128)(2,1)S(1)}, u32[]{:S(2)}, u32[]{:S(2)}) collective-permute-start(bf16[384,768]{1,0:T(8,128)(2,1)S(1)} %pad_maximum_fusion.2), channel_id=1, source_target_pairs={{0,128},{8,136},{16,144},{24,152},{32,160},{40,168},{48,176},{56,1... | collective-permute-start | bytes 1769480 | tf_op jit(solution)/shard_map/ppermute | solution.py:77
  25.5 27.5 %collective-permute-start.6 = (bf16[384,768]{1,0:T(8,128)(2,1)S(1)}, bf16[384,768]{1,0:T(8,128)(2,1)S(1)}, u32[]{:S(2)}, u32[]{:S(2)}) collective-permute-start(bf16[384,768]{1,0:T(8,128)(2,1)S(1)} %pad_maximum_fusion.2), channel_id=1, source_target_pairs={{0,64},{8,72},{16,80},{24,88},{32,96},{40,104},{48,112},{56,120},{... | collective-permute-start | bytes 1769480 | tf_op jit(solution)/shard_map/ppermute | solution.py:77
  64.8 4.6 %collective-permute-start.8 = (bf16[15,192]{0,1:T(8,128)(2,1)S(1)}, bf16[15,192]{0,1:T(8,128)(2,1)S(1)}, u32[]{:S(2)}, u32[]{:S(2)}) collective-permute-start(bf16[15,192]{0,1:T(8,128)(2,1)S(1)} %get-tuple-element.44), channel_id=1, source_target_pairs={{8,0},{16,8},{24,16},{32,24},{40,32},{48,40},{56,48},{64,56},{72,6... | collective-permute-start | bytes 17288 | tf_op jit(solution)/shard_map/ppermute | solution.py:18
  67.1 5.4 %collective-permute-start.7 = (bf16[15,192]{0,1:T(8,128)(2,1)S(1)}, bf16[15,192]{0,1:T(8,128)(2,1)S(1)}, u32[]{:S(2)}, u32[]{:S(2)}) collective-permute-start(bf16[15,192]{0,1:T(8,128)(2,1)S(1)} %get-tuple-element.43), channel_id=1, source_target_pairs={{0,8},{8,16},{16,24},{24,32},{32,40},{40,48},{48,56},{56,64},{64,7... | collective-permute-start | bytes 17288 | tf_op jit(solution)/shard_map/ppermute | solution.py:17
  72.8 27.6 %copy-start.40 = (f32[192]{0:T(256)S(1)}, f32[192]{0:T(256)}, u32[]{:S(2)}) copy-start(f32[192]{0:T(256)} %param.21) | copy-start | bytes 2308
  72.8 27.6 %copy-start.41 = (f32[192]{0:T(256)S(1)}, f32[192]{0:T(256)}, u32[]{:S(2)}) copy-start(f32[192]{0:T(256)} %param.20) | copy-start | bytes 2308
  79.4 1.2 collective-permute-start.9
  80.7 3.7 %collective-permute-start.10 = (f32[3,192]{1,0:T(4,128)S(1)}, f32[3,192]{1,0:T(4,128)S(1)}, u32[]{:S(2)}, u32[]{:S(2)}) collective-permute-start(f32[3,192]{1,0:T(4,128)S(1)} %pad_maximum_fusion.6), channel_id=1, source_target_pairs={{0,16},{8,24},{16,0},{24,8},{32,48},{40,56},{48,32},{56,40},{64,80... | collective-permute-start | bytes 6920 | tf_op jit(solution)/shard_map/ppermute | solution.py:47
  84.5 5.2 %collective-permute-start.11 = (f32[3,192]{1,0:T(4,128)S(1)}, f32[3,192]{1,0:T(4,128)S(1)}, u32[]{:S(2)}, u32[]{:S(2)}) collective-permute-start(f32[3,192]{1,0:T(4,128)S(1)} %pad_maximum_fusion.7), channel_id=1, source_target_pairs={{0,32},{8,40},{16,48},{24,56},{32,0},{40,8},{48,16},{56,24},{64,96... | collective-permute-start | bytes 6920 | tf_op jit(solution)/shard_map/ppermute | solution.py:47
  89.7 5.3 %collective-permute-start.12 = (f32[3,192]{1,0:T(4,128)S(1)}, f32[3,192]{1,0:T(4,128)S(1)}, u32[]{:S(2)}, u32[]{:S(2)}) collective-permute-start(f32[3,192]{1,0:T(4,128)S(1)} %pad_maximum_fusion.8), channel_id=1, source_target_pairs={{0,64},{8,72},{16,80},{24,88},{32,96},{40,104},{48,112},{56,120},{... | collective-permute-start | bytes 6920 | tf_op jit(solution)/shard_map/ppermute | solution.py:47
  95.1 5.2 %collective-permute-start.13 = (f32[3,192]{1,0:T(4,128)S(1)}, f32[3,192]{1,0:T(4,128)S(1)}, u32[]{:S(2)}, u32[]{:S(2)}) collective-permute-start(f32[3,192]{1,0:T(4,128)S(1)} %pad_maximum_fusion.9), channel_id=1, source_target_pairs={{0,128},{8,136},{16,144},{24,152},{32,160},{40,168},{48,176},{56,1... | collective-permute-start | bytes 6920 | tf_op jit(solution)/shard_map/ppermute | solution.py:47
  102.8 111.7 %reduce-scatter.2.cloned.1.call-start = ((), (), s32[]{:S(2)}) async-start(), calls=%async_computation.4 | async-start | bytes 3538944 | tf_op jit(solution)/shard_map/reduce_scatter | solution.py:173
  104.9 8.2 %collective-permute-start.14 = (bf16[2,1536,768]{2,1,0:T(8,128)(2,1)S(1)}, bf16[2,1536,768]{2,1,0:T(8,128)(2,1)S(1)}, u32[]{:S(2)}, u32[]{:S(2)}) collective-permute-start(bf16[2,1536,768]{2,1,0:T(8,128)(2,1)S(1)} %pad_maximum_fusion), channel_id=1, source_target_pairs={{0,8},{8,0},{16,24},{24,16},{32,40},{40,32},{48,56},{56,48},{64,72... | collective-permute-start | bytes 14155784 | tf_op jit(solution)/shard_map/ppermute | solution.py:151
  117.8 34.0 %copy-start.5 = (bf16[1536,768]{1,0:T(8,128)(2,1)S(1)}, bf16[1536,768]{1,0:T(8,128)(2,1)}, u32[]{:S(2)}) copy-start(bf16[1536,768]{1,0:T(8,128)(2,1)} %all-gather.8.cloned.1.call-done) | copy-start | bytes 7077892
  (40 other events, 301.0 us)
Sparse Core Ops, SparseCore 0:
  9.1 47.9 all-gather.3
  58.9 40.3 all-gather.7
  102.9 43.3 all-gather.5
  169.0 45.4 reduce-scatter.1

commit v11 on v10

--- a/solution.py
+++ b/solution.py
@@ -93,10 +93,21 @@
     pair_up = jnp.concatenate(ordered(up_piece, [other_up], my_c, cores), axis=0)
     pair_down = jnp.concatenate(ordered(down_piece, [other_down], my_c, cores), axis=0)
     pair = jnp.where(my_c == 0, pair_up, pair_down)
-    got = [shifted(pair, lambda y, x, c, d=d: (y, (x + d) % xs, c)) for d in range(1, xs)]
-    row = jnp.concatenate(ordered(pair, got, my_x, xs), axis=0)
-    got = [shifted(row, lambda y, x, c, d=d: ((y + d) % ys, x, c)) for d in range(1, ys)]
-    whole = jnp.concatenate(ordered(row, got, my_y, ys), axis=0)
+    def doubled(value, mine, count, move):
+        step = 1
+        while step < count:
+            other = shifted(value, lambda y, x, c, s=step: move(y, x, c, s))
+            low = (mine & step) == 0
+            value = jnp.where(
+                low,
+                jnp.concatenate([value, other], axis=0),
+                jnp.concatenate([other, value], axis=0),
+            )
+            step *= 2
+        return value
+
+    row = doubled(pair, my_x, xs, lambda y, x, c, s: (y, x ^ s, c))
+    whole = doubled(row, my_y, ys, lambda y, x, c, s: (y ^ s, x, c))
     whole, tie = lax.optimization_barrier((whole, tie))
     return whole, tie
 

time: 224 us -> 240 us (1.071)
  waiting for transfers between devices: 125 us -> 150 us
  starting transfers between devices: 24.6 us -> 16.8 us
    ppermute x7 -> x5, waiting for transfers between devices: 25.2 us -> 46.5 us  [shifted(): return lax.ppermute(value, axis, pairs)]
    ppermute x5, starting transfers between devices: 10.1 us -> 4.82 us  [moments_over(): other = lax.ppermute(stats, axis, pairs)]
    ppermute x5, waiting for transfers between devices: 10.5 us -> 14.1 us  [moments_over(): other = lax.ppermute(stats, axis, pairs)]
    select_n x0 -> x4, other arithmetic: none -> 3.45 us  [doubled(): jnp.where(low, jnp.concatenate([value, other], axis=0), jnp.concatenate([...]
    all_gather x1, waiting for transfers between devices: 28.5 us -> 31.8 us  [shards(): swished_all = lax.all_gather(swished, 'tensor', axis=1, tiled=True)]
    all_gather x1, waiting for transfers between devices: 3.15 us -> 0.02 us  [shards(): feature_block = lax.all_gather(features, 'tensor', axis=0, tiled=True)]
    ppermute x7 -> x5, starting transfers between devices: 9.62 us -> 7.04 us  [shifted(): return lax.ppermute(value, axis, pairs)]
    unnamed x91 -> x37, local copies, waits for them, and re-layouts: 4.94 us -> 4.79 us
  transfers between devices with their start and end apart: 19 -> 17, of which waited for: 15 -> 14; matrix products, arithmetic and copies ran while one was open for 13% -> 12% of each run, Pallas kernels for 0% -> 0%
where the time goes in v11:
time: 240 us; the launch traced here: 239 us
  waiting for transfers between devices  150 us (62%)
  other arithmetic  28.2 us (12%)
  matrix products  21.3 us (9%)
  starting transfers between devices  16.8 us (7%)
  between operations  15.6 us (6%)
  local copies, waits for them, and re-layouts  7.53 us (3%)
    ppermute x5, waiting for transfers between devices, shifted(): return lax.ppermute(value, axis, pairs)  46.5 us
    reduce_scatter x1, waiting for transfers between devices, shards(): lax.psum_scatter(partial_out.astype(jnp.bfloat16), 'tensor', scatter_dime...  45.8 us
    all_gather x1, waiting for transfers between devices, shards(): swished_all = lax.all_gather(swished, 'tensor', axis=1, tiled=True)  31.8 us
    ppermute x5, waiting for transfers between devices, moments_over(): other = lax.ppermute(stats, axis, pairs)  14.1 us
    dot_general x1, matrix products, shards(): lax.dot_general(hidden, down_t, (((1,), (1,)), ((), ())), preferred_eleme...  10.5 us
    ppermute x1, waiting for transfers between devices, shards(): lax.ppermute(jnp.stack([out_mine, ff_mine]), 'tm', swap)  7.9 us
    ppermute x5, starting transfers between devices, shifted(): return lax.ppermute(value, axis, pairs)  7.04 us
    dot_general x1, matrix products, shards(): lax.dot_general(swished_all, right, contract, preferred_element_type=jnp....  5.51 us
  transfers between devices with their start and end apart: 17, of which 14 were waited for; matrix products, arithmetic and copies ran while one was open for 12% of the time, Pallas kernels for 0%

profile of v11, /device:TPU:2, one launch (start us, length us, event | category | flops | bytes accessed | tf_op | source)
XLA Modules:
  0.0 239.1 jit_solution(16008081435770825312)
XLA Ops:
  10.7 2.4 collective-permute-start.1
  13.1 4.2 %collective-permute-done.1 = bf16[96,768]{1,0:T(8,128)(2,1)S(1)} collective-permute-done((bf16[96,768]{1,0:T(8,128)(2,1)S(1)}, bf16[96,768]{1,0:T(8,128)(2,1)S(1)}, u32[]{:S(2)}, u32[]{:S(2)}) %collective-permute-start.1) | collective-permute-done | bytes 147488 | tf_op jit(solution)/shard_map/ppermute | solution.py:77
  19.0 8.5 %collective-permute-done.2 = bf16[192,768]{1,0:T(8,128)(2,1)S(1)} collective-permute-done((bf16[192,768]{1,0:T(8,128)(2,1)S(1)}, bf16[192,768]{1,0:T(8,128)(2,1)S(1)}, u32[]{:S(2)}, u32[]{:S(2)}) %collective-permute-start.2) | collective-permute-done | bytes 294944 | tf_op jit(solution)/shard_map/ppermute | solution.py:77
  28.4 13.2 %collective-permute-done.3 = bf16[384,768]{1,0:T(8,128)(2,1)S(1)} collective-permute-done((bf16[384,768]{1,0:T(8,128)(2,1)S(1)}, bf16[384,768]{1,0:T(8,128)(2,1)S(1)}, u32[]{:S(2)}, u32[]{:S(2)}) %collective-permute-start.3) | collective-permute-done | bytes 589856 | tf_op jit(solution)/shard_map/ppermute | solution.py:77
  50.3 19.3 %collective-permute-done.4 = bf16[768,768]{1,0:T(8,128)(2,1)} collective-permute-done((bf16[768,768]{1,0:T(8,128)(2,1)S(1)}, bf16[768,768]{1,0:T(8,128)(2,1)}, u32[]{:S(2)}, u32[]{:S(2)}) %collective-permute-start.4) | collective-permute-done | bytes 1179680 | tf_op jit(solution)/shard_map/ppermute | solution.py:77
  69.6 2.8 %maximum_select_fusion = bf16[1536,768]{1,0:T(8,128)(2,1)S(1)} fusion(bf16[768,768]{1,0:T(8,128)(2,1)} %collective-permute-done.4, bf16[768,768]{1,0:T(8,128)(2,1)} %copy-done.5, pred[]{:T(512)S(6)} %eq.51), kind=kLoop, calls=%fused_computation.25 | loop fusion | flops 10616832 | bytes 4718593 | tf_op jit(solution)/shard_map/jit(_where)/select_n | solution.py:101
  72.4 2.5 %convert_reduce_fusion = f32[1024]{0:T(1024)S(1)} fusion(bf16[1024,1536]{1,0:T(8,128)(2,1)} %all-gather.4.cloned.1.call-done), kind=kLoop, calls=%fused_computation.2 | loop fusion | flops 3144704 | bytes 3149824 | tf_op jit(solution)/shard_map/reduce_sum | solution.py:25
  81.8 2.6 %collective-permute-start.5 = (bf16[15,192]{0,1:T(8,128)(2,1)S(1)}, bf16[15,192]{0,1:T(8,128)(2,1)S(1)}, u32[]{:S(2)}, u32[]{:S(2)}) collective-permute-start(bf16[15,192]{0,1:T(8,128)(2,1)S(1)} %get-tuple-element.35), channel_id=1, source_target_pairs={{0,8},{8,16},{16,24},{24,32},{32,40},{40,48},{48,56},{56,64},{64,7... | collective-permute-start | bytes 17288 | tf_op jit(solution)/shard_map/ppermute | solution.py:17
  84.4 2.8 %collective-permute-done.5 = bf16[15,192]{0,1:T(8,128)(2,1)S(1)} collective-permute-done((bf16[15,192]{0,1:T(8,128)(2,1)S(1)}, bf16[15,192]{0,1:T(8,128)(2,1)S(1)}, u32[]{:S(2)}, u32[]{:S(2)}) %collective-permute-start.5) | collective-permute-done | bytes 5792 | tf_op jit(solution)/shard_map/ppermute | solution.py:17
  87.2 5.3 %multiply_reduce_fusion.1 = (f32[192]{0:T(256)S(1)}, f32[1024,192]{0,1:T(8,128)S(1)}) fusion(f32[1024]{0:T(1024)S(1)} %get-tuple-element.30, f32[192]{0:T(256)S(1)} %bitcast.98, bf16[1039,192]{0,1:T(8,128)(2,1)S(1)} %constant_dynamic-update-slice_fusion, f32[192]{0:T(256)S(1)} %bitcast.99, f32[192]{0:T(256)S(1)} %bitcast.101, f32[192]{0:T(256)S(1)} %bitcast.102, ...), kind=kLoop, calls=%fused_computation.59 | loop fusion | flops 27328320 | bytes 7112320 | tf_op jit(solution)/shard_map/reduce_sum | solution.py:150
  95.2 3.6 %collective-permute-done.8 = f32[3,192]{1,0:T(4,128)S(1)} collective-permute-done((f32[3,192]{1,0:T(4,128)S(1)}, f32[3,192]{1,0:T(4,128)S(1)}, u32[]{:S(2)}, u32[]{:S(2)}) %collective-permute-start.8) | collective-permute-done | bytes 2336 | tf_op jit(solution)/shard_map/ppermute | solution.py:47
  99.7 4.3 %collective-permute-done.9 = f32[3,192]{1,0:T(4,128)S(1)} collective-permute-done((f32[3,192]{1,0:T(4,128)S(1)}, f32[3,192]{1,0:T(4,128)S(1)}, u32[]{:S(2)}, u32[]{:S(2)}) %collective-permute-start.9) | collective-permute-done | bytes 2336 | tf_op jit(solution)/shard_map/ppermute | solution.py:47
  105.6 2.2 collective-permute-done.10
  107.9 2.4 collective-permute-start.11
  110.2 2.8 %collective-permute-done.11 = f32[3,192]{1,0:T(4,128)S(1)} collective-permute-done((f32[3,192]{1,0:T(4,128)S(1)}, f32[3,192]{1,0:T(4,128)S(1)}, u32[]{:S(2)}, u32[]{:S(2)}) %collective-permute-start.11) | collective-permute-done | bytes 2336 | tf_op jit(solution)/shard_map/ppermute | solution.py:47
  113.1 2.3 multiply_convert_fusion.1
  118.0 7.9 %collective-permute-done.12 = bf16[2,1536,768]{2,1,0:T(8,128)(2,1)S(1)} collective-permute-done((bf16[2,1536,768]{2,1,0:T(8,128)(2,1)S(1)}, bf16[2,1536,768]{2,1,0:T(8,128)(2,1)S(1)}, u32[]{:S(2)}, u32[]{:S(2)}) %collective-permute-start.12) | collective-permute-done | bytes 4718624 | tf_op jit(solution)/shard_map/ppermute | solution.py:162
  125.9 2.1 copy-done.8
  128.0 2.5 %broadcast_select_fusion = (bf16[1536,768]{1,0:T(8,128)(2,1)}, bf16[1536,768]{1,0:T(8,128)(2,1)}) fusion(bf16[1536,768]{1,0:T(8,128)(2,1)S(1)} %maximum_select_fusion, pred[]{:T(512)S(6)} %eq.55, bf16[2,1536,768]{2,1,0:T(8,128)(2,1)S(1)} %collective-permute-done.12), kind=kLoop, calls=%fused_computation.30 | loop fusion | flops 2359296 | bytes 9437185 | tf_op jit(solution)/shard_map/jit(_where)/select_n | solution.py:164
  130.5 31.8 %all-gather.6.cloned.1.call-done = bf16[1024,1536]{0,1:T(8,128)(2,1)} async-done(((bf16[1024,192]{0,1:T(8,128)(2,1)}), bf16[1024,1536]{0,1:T(8,128)(2,1)}) %all-gather.6.cloned.1.call-update) | async-done | bytes 3145744 | tf_op jit(solution)/shard_map/all_gather | solution.py:160
  162.3 5.5 %fusion.16 = f32[1024,768]{1,0:T(8,128)S(1)} fusion(bf16[1024,1536]{0,1:T(8,128)(2,1)} %all-gather.6.cloned.1.call-done, bf16[1536,768]{1,0:T(8,128)(2,1)} %all-gather.8.cloned.1.call-done, pred[]{:T(512)S(6)} %eq.55, bf16[2,1536,768]{2,1,0:T(8,128)(2,1)} %copy-done.8), kind=kOutput, calls=%fused_computation.26 | convolution fusion | flops 2417098752 | bytes 11010049 | tf_op jit(solution)/shard_map/dot_general | solution.py:171
  167.9 2.9 %fusion.18 = f32[1024,768]{1,0:T(8,128)S(1)} fusion(bf16[1024,1536]{0,1:T(8,128)(2,1)S(1)} %copy-done.15, bf16[1536,768]{1,0:T(8,128)(2,1)S(1)} %copy-done.6, pred[]{:T(512)S(6)} %eq.55, bf16[2,1536,768]{2,1,0:T(8,128)(2,1)S(1)} %copy-done.9), kind=kOutput, calls=%fused_computation.28 | convolution fusion | flops 2417098752 | bytes 11010049 | tf_op jit(solution)/shard_map/dot_general | solution.py:170
  174.3 10.5 %convolution_convert_fusion = bf16[1024,1536]{1,0:T(8,128)(2,1)} fusion(bf16[1536,768]{1,0:T(8,128)(2,1)S(1)} %copy-done.7, bf16[1536,768]{1,0:T(8,128)(2,1)} %get-tuple-element.13, bf16[1024,1536]{1,0:T(8,128)(2,1)} %copy-done.3, f32[1536]{0:T(1024)S(1)} %copy-done.17, f32[1024]{0:T(1024)S(1)} %add_rsqrt_fusion, f32[1024]{0:T(1024)S(1)} %broadcast_multiply_fusion), kind=kOutput, calls=%fused_computation.17 | convolution fusion | flops 4845207552 | bytes 11024384 | tf_op jit(solution)/shard_map/dot_general | solution.py:181
  184.9 45.8 %reduce-scatter.2.cloned.1.call-done = bf16[128,1536]{1,0:T(8,128)(2,1)} async-done(((bf16[1024,1536]{1,0:T(8,128)(2,1)}), bf16[128,1536]{1,0:T(8,128)(2,1)}) %reduce-scatter.2.cloned.1.call-update) | async-done | bytes 393232 | tf_op jit(solution)/shard_map/reduce_scatter | solution.py:184
  (107 shorter events, 33.4 us)
Async XLA Ops:
  6.5 70.7 %copy-start = (bf16[1536,192]{0,1:T(8,128)(2,1)S(1)}, bf16[1536,192]{0,1:T(8,128)(2,1)}, u32[]{:S(2)}) copy-start(bf16[1536,192]{0,1:T(8,128)(2,1)} %param.18) | copy-start | bytes 1769476
  6.5 37.7 %copy-start.10 = (bf16[192,1536]{1,0:T(8,128)(2,1)S(1)}, bf16[192,1536]{1,0:T(8,128)(2,1)}, u32[]{:S(2)}) copy-start(bf16[192,1536]{1,0:T(8,128)(2,1)} %param.22) | copy-start | bytes 1769476
  6.5 65.9 %all-gather.4.cloned.1.call-start = ((), (), s32[]{:S(2)}) async-start(), calls=%async_computation.1 | async-start | bytes 3538944 | tf_op jit(solution)/shard_map/all_gather | solution.py:134
  7.3 108.3 %all-gather.8.cloned.1.call-start = ((), (), s32[]{:S(2)}) async-start(), calls=%async_computation.3 | async-start | bytes 2654208 | tf_op jit(solution)/shard_map/all_gather | solution.py:140
  8.2 1.5 collective-permute-start
  8.4 37.3 %copy-start.12 = (s32[1024]{0:T(1024)S(1)}, s32[1024]{0:T(1024)}, u32[]{:S(2)}) copy-start(s32[1024]{0:T(1024)} %param.14) | copy-start | bytes 12292
  10.7 6.5 %collective-permute-start.1 = (bf16[96,768]{1,0:T(8,128)(2,1)S(1)}, bf16[96,768]{1,0:T(8,128)(2,1)S(1)}, u32[]{:S(2)}, u32[]{:S(2)}) collective-permute-start(bf16[96,768]{1,0:T(8,128)(2,1)S(1)} %maximum_select_fusion.4), channel_id=1, source_target_pairs={{0,16},{8,24},{16,0},{24,8},{32,48},{40,56},{48,32},{56,40},{64,80... | collective-permute-start | bytes 442376 | tf_op jit(solution)/shard_map/ppermute | solution.py:77
  17.3 10.1 %collective-permute-start.2 = (bf16[192,768]{1,0:T(8,128)(2,1)S(1)}, bf16[192,768]{1,0:T(8,128)(2,1)S(1)}, u32[]{:S(2)}, u32[]{:S(2)}) collective-permute-start(bf16[192,768]{1,0:T(8,128)(2,1)S(1)} %maximum_select_fusion.3), channel_id=1, source_target_pairs={{0,32},{8,40},{16,48},{24,56},{32,0},{40,8},{48,16},{56,24},{64,96... | collective-permute-start | bytes 884744 | tf_op jit(solution)/shard_map/ppermute | solution.py:77
  27.6 14.1 %collective-permute-start.3 = (bf16[384,768]{1,0:T(8,128)(2,1)S(1)}, bf16[384,768]{1,0:T(8,128)(2,1)S(1)}, u32[]{:S(2)}, u32[]{:S(2)}) collective-permute-start(bf16[384,768]{1,0:T(8,128)(2,1)S(1)} %maximum_select_fusion.2), channel_id=1, source_target_pairs={{0,64},{8,72},{16,80},{24,88},{32,96},{40,104},{48,112},{56,120},{... | collective-permute-start | bytes 1769480 | tf_op jit(solution)/shard_map/ppermute | solution.py:77
  42.1 8.2 %copy-start.5 = (bf16[768,768]{1,0:T(8,128)(2,1)}, bf16[768,768]{1,0:T(8,128)(2,1)S(1)}, u32[]{:S(2)}) copy-start(bf16[768,768]{1,0:T(8,128)(2,1)S(1)} %maximum_select_fusion.1) | copy-start | bytes 3538948
  42.1 27.5 %collective-permute-start.4 = (bf16[768,768]{1,0:T(8,128)(2,1)S(1)}, bf16[768,768]{1,0:T(8,128)(2,1)}, u32[]{:S(2)}, u32[]{:S(2)}) collective-permute-start(bf16[768,768]{1,0:T(8,128)(2,1)S(1)} %maximum_select_fusion.1), channel_id=1, source_target_pairs={{0,128},{8,136},{16,144},{24,152},{32,160},{40,168},{48,176},{56,1... | collective-permute-start | bytes 3538952 | tf_op jit(solution)/shard_map/ppermute | solution.py:77
  45.0 117.3 %all-gather.6.cloned.1.call-start = ((), (), s32[]{:S(2)}) async-start(), calls=%async_computation.2 | async-start | bytes 3538944 | tf_op jit(solution)/shard_map/all_gather | solution.py:160
  79.8 4.6 %collective-permute-start.6 = (bf16[15,192]{0,1:T(8,128)(2,1)S(1)}, bf16[15,192]{0,1:T(8,128)(2,1)S(1)}, u32[]{:S(2)}, u32[]{:S(2)}) collective-permute-start(bf16[15,192]{0,1:T(8,128)(2,1)S(1)} %get-tuple-element.36), channel_id=1, source_target_pairs={{8,0},{16,8},{24,16},{32,24},{40,32},{48,40},{56,48},{64,56},{72,6... | collective-permute-start | bytes 17288 | tf_op jit(solution)/shard_map/ppermute | solution.py:18
  81.8 5.4 %collective-permute-start.5 = (bf16[15,192]{0,1:T(8,128)(2,1)S(1)}, bf16[15,192]{0,1:T(8,128)(2,1)S(1)}, u32[]{:S(2)}, u32[]{:S(2)}) collective-permute-start(bf16[15,192]{0,1:T(8,128)(2,1)S(1)} %get-tuple-element.35), channel_id=1, source_target_pairs={{0,8},{8,16},{16,24},{24,32},{32,40},{40,48},{48,56},{56,64},{64,7... | collective-permute-start | bytes 17288 | tf_op jit(solution)/shard_map/ppermute | solution.py:17
  87.2 25.9 %copy-start.13 = (f32[192]{0:T(256)S(1)}, f32[192]{0:T(256)}, u32[]{:S(2)}) copy-start(f32[192]{0:T(256)} %param.21) | copy-start | bytes 2308
  87.2 26.0 %copy-start.14 = (f32[192]{0:T(256)S(1)}, f32[192]{0:T(256)}, u32[]{:S(2)}) copy-start(f32[192]{0:T(256)} %param.20) | copy-start | bytes 2308
  93.7 1.2 collective-permute-start.7
  95.1 3.7 %collective-permute-start.8 = (f32[3,192]{1,0:T(4,128)S(1)}, f32[3,192]{1,0:T(4,128)S(1)}, u32[]{:S(2)}, u32[]{:S(2)}) collective-permute-start(f32[3,192]{1,0:T(4,128)S(1)} %pad_maximum_fusion.4), channel_id=1, source_target_pairs={{0,16},{8,24},{16,0},{24,8},{32,48},{40,56},{48,32},{56,40},{64,80... | collective-permute-start | bytes 6920 | tf_op jit(solution)/shard_map/ppermute | solution.py:47
  98.8 5.2 %collective-permute-start.9 = (f32[3,192]{1,0:T(4,128)S(1)}, f32[3,192]{1,0:T(4,128)S(1)}, u32[]{:S(2)}, u32[]{:S(2)}) collective-permute-start(f32[3,192]{1,0:T(4,128)S(1)} %pad_maximum_fusion.5), channel_id=1, source_target_pairs={{0,32},{8,40},{16,48},{24,56},{32,0},{40,8},{48,16},{56,24},{64,96... | collective-permute-start | bytes 6920 | tf_op jit(solution)/shard_map/ppermute | solution.py:47
  104.1 3.7 %collective-permute-start.10 = (f32[3,192]{1,0:T(4,128)S(1)}, f32[3,192]{1,0:T(4,128)S(1)}, u32[]{:S(2)}, u32[]{:S(2)}) collective-permute-start(f32[3,192]{1,0:T(4,128)S(1)} %pad_maximum_fusion.6), channel_id=1, source_target_pairs={{0,64},{8,72},{16,80},{24,88},{32,96},{40,104},{48,112},{56,120},{... | collective-permute-start | bytes 6920 | tf_op jit(solution)/shard_map/ppermute | solution.py:47
  107.9 5.2 %collective-permute-start.11 = (f32[3,192]{1,0:T(4,128)S(1)}, f32[3,192]{1,0:T(4,128)S(1)}, u32[]{:S(2)}, u32[]{:S(2)}) collective-permute-start(f32[3,192]{1,0:T(4,128)S(1)} %pad_maximum_fusion.7), channel_id=1, source_target_pairs={{0,128},{8,136},{16,144},{24,152},{32,160},{40,168},{48,176},{56,1... | collective-permute-start | bytes 6920 | tf_op jit(solution)/shard_map/ppermute | solution.py:47
  115.5 115.2 %reduce-scatter.2.cloned.1.call-start = ((), (), s32[]{:S(2)}) async-start(), calls=%async_computation.4 | async-start | bytes 3538944 | tf_op jit(solution)/shard_map/reduce_scatter | solution.py:184
  117.6 8.2 %collective-permute-start.12 = (bf16[2,1536,768]{2,1,0:T(8,128)(2,1)S(1)}, bf16[2,1536,768]{2,1,0:T(8,128)(2,1)S(1)}, u32[]{:S(2)}, u32[]{:S(2)}) collective-permute-start(bf16[2,1536,768]{2,1,0:T(8,128)(2,1)S(1)} %pad_maximum_fusion), channel_id=1, source_target_pairs={{0,8},{8,0},{16,24},{24,16},{32,40},{40,32},{48,56},{56,48},{64,72... | collective-permute-start | bytes 14155784 | tf_op jit(solution)/shard_map/ppermute | solution.py:162
  130.5 37.4 %copy-start.6 = (bf16[1536,768]{1,0:T(8,128)(2,1)S(1)}, bf16[1536,768]{1,0:T(8,128)(2,1)}, u32[]{:S(2)}) copy-start(bf16[1536,768]{1,0:T(8,128)(2,1)} %all-gather.8.cloned.1.call-done) | copy-start | bytes 7077892
  (11 other events, 32.3 us)
Sparse Core Ops, SparseCore 0:
  9.1 47.9 all-gather.3
  58.9 39.9 all-gather.7
  115.6 46.6 all-gather.5
  185.0 45.5 reduce-scatter.1

commit v12 on v10

--- a/solution.py
+++ b/solution.py
@@ -99,6 +99,22 @@
     whole = jnp.concatenate(ordered(row, got, my_y, ys), axis=0)
     whole, tie = lax.optimization_barrier((whole, tie))
     return whole, tie
+
+
+def gather_tensor(values, axis):
+    size = lax.axis_size(axis)
+    me = lax.axis_index(axis)
+    step = 1
+    while step < size:
+        other = lax.ppermute(values, axis, [(i, i ^ step) for i in range(size)])
+        mine_low = (me & step) == 0
+        values = jnp.where(
+            mine_low,
+            jnp.concatenate([values, other], axis=-1),
+            jnp.concatenate([other, values], axis=-1),
+        )
+        step *= 2
+    return values
 
 
 def shards(
@@ -122,7 +138,13 @@
     valid = ((frame_mask > 0) & (positions < total_length[0])).astype(jnp.float32)
     feature_block = lax.all_gather(features, "tensor", axis=0, tiled=True)
     feature_block = with_layout_constraint(feature_block, Layout(major_to_minor=(0, 1)))
-    piece = layer_norm(feature_block, norm_gain).astype(jnp.bfloat16)
+    own = features.astype(jnp.float32)
+    centre = jnp.mean(own, axis=-1)
+    spread = jnp.mean(jnp.square(own - centre[:, None]), axis=-1)
+    rows = gather_tensor(jnp.stack([centre, lax.rsqrt(spread + 1e-05)]), "tensor")
+    piece = (
+        (feature_block.astype(jnp.float32) - rows[0][:, None]) * rows[1][:, None] * norm_gain
+    ).astype(jnp.bfloat16)
     my_core = lax.axis_index("tm") % 2
     cols = out_weight.shape[1] // 2
     out_half = jnp.where(my_core == 0, out_weight[:, :cols], out_weight[:, cols:])

time: 224 us -> 228 us (1.018)
  starting transfers between devices: 24.6 us -> 32 us
  waiting for transfers between devices: 125 us -> 120 us
    ppermute x0 -> x3, starting transfers between devices: none -> 11.7 us  [gather_tensor(): other = lax.ppermute(values, axis, [(i, i ^ step) for i in range(size)])]
    ppermute x7, waiting for transfers between devices: 25.2 us -> 16.9 us  [shifted(): return lax.ppermute(value, axis, pairs)]
    ppermute x5, starting transfers between devices: 10.1 us -> 2.91 us  [moments_over(): other = lax.ppermute(stats, axis, pairs)]
    ppermute x5, waiting for transfers between devices: 10.5 us -> 16 us  [moments_over(): other = lax.ppermute(stats, axis, pairs)]
    all_gather x1, waiting for transfers between devices: 3.15 us -> 0.02 us  [shards(): feature_block = lax.all_gather(features, 'tensor', axis=0, tiled=True)]
    ppermute x1, starting transfers between devices: 2.27 us -> 5.2 us  [extended(): after = lax.ppermute(initial, axis, down)]
    reduce_sum x2 -> x1, other arithmetic: 3 us -> 0.48 us  [layer_norm(): centre = jnp.mean(values, axis=-1, keepdims=True)]
    reduce_sum x0 -> x2, other arithmetic: none -> 2.38 us  [the longest x1 1.25 us: shards(): spread = jnp.mean(jnp.square(own - centre[:, None]), axis=-1)]
  transfers between devices with their start and end apart: 19 -> 22, of which waited for: 15 -> 12; matrix products, arithmetic and copies ran while one was open for 13% -> 14% of each run, Pallas kernels for 0% -> 0%
where the time goes in v12:
time: 228 us; the launch traced here: 227 us
  waiting for transfers between devices  120 us (53%)
  starting transfers between devices  32 us (14%)
  other arithmetic  28.5 us (12%)
  matrix products  21.2 us (9%)
  between operations  16.1 us (7%)
  local copies, waits for them, and re-layouts  9.72 us (4%)
    reduce_scatter x1, waiting for transfers between devices, shards(): lax.psum_scatter(partial_out.astype(jnp.bfloat16), 'tensor', scatter_dime...  45.8 us
    all_gather x1, waiting for transfers between devices, shards(): swished_all = lax.all_gather(swished, 'tensor', axis=1, tiled=True)  29.2 us
    ppermute x7, waiting for transfers between devices, shifted(): return lax.ppermute(value, axis, pairs)  16.9 us
    ppermute x5, waiting for transfers between devices, moments_over(): other = lax.ppermute(stats, axis, pairs)  16 us
    ppermute x3, starting transfers between devices, gather_tensor(): other = lax.ppermute(values, axis, [(i, i ^ step) for i in range(size)])  11.7 us
    dot_general x1, matrix products, shards(): lax.dot_general(hidden, down_t, (((1,), (1,)), ((), ())), preferred_eleme...  10.5 us
    ppermute x7, starting transfers between devices, shifted(): return lax.ppermute(value, axis, pairs)  9.62 us
    ppermute x1, waiting for transfers between devices, shards(): lax.ppermute(jnp.stack([out_mine, ff_mine]), 'tm', swap)  7.9 us
  transfers between devices with their start and end apart: 22, of which 12 were waited for; matrix products, arithmetic and copies ran while one was open for 14% of the time, Pallas kernels for 0%

profile of v12, /device:TPU:2, one launch (start us, length us, event | category | flops | bytes accessed | tf_op | source)
XLA Modules:
  0.0 227.5 jit_solution(17104513509629966805)
XLA Ops:
  18.0 2.4 %collective-permute-start.2 = (bf16[96,768]{1,0:T(8,128)(2,1)S(1)}, bf16[96,768]{1,0:T(8,128)(2,1)S(1)}, u32[]{:S(2)}, u32[]{:S(2)}) collective-permute-start(bf16[96,768]{1,0:T(8,128)(2,1)S(1)} %maximum_select_fusion), channel_id=1, source_target_pairs={{0,32},{8,40},{16,48},{24,56},{32,0},{40,8},{48,16},{56,24},{64,96... | collective-permute-start | bytes 442376 | tf_op jit(solution)/shard_map/ppermute | solution.py:77
  24.6 3.4 %collective-permute-start.8 = (f32[2,256]{1,0:T(2,128)S(1)}, f32[2,256]{1,0:T(2,128)S(1)}, u32[]{:S(2)}, u32[]{:S(2)}) collective-permute-start(f32[2,256]{1,0:T(2,128)S(1)} %maximum_select_fusion.3), channel_id=1, source_target_pairs={{0,2},{1,3},{2,0},{3,1},{4,6},{5,7},{6,4},{7,5},{8,10},{9,11},{10,... | collective-permute-start | bytes 6152 | tf_op jit(solution)/shard_map/ppermute | solution.py:109
  28.5 3.1 %collective-permute-start.4 = (bf16[384,768]{1,0:T(8,128)(2,1)S(1)}, bf16[384,768]{1,0:T(8,128)(2,1)S(1)}, u32[]{:S(2)}, u32[]{:S(2)}) collective-permute-start(bf16[384,768]{1,0:T(8,128)(2,1)S(1)} %pad_maximum_fusion.2), channel_id=1, source_target_pairs={{0,192},{8,200},{16,208},{24,216},{32,224},{40,232},{48,240},{56,2... | collective-permute-start | bytes 1769480 | tf_op jit(solution)/shard_map/ppermute | solution.py:77
  33.2 6.4 %collective-permute-start.9 = (f32[2,512]{1,0:T(2,128)S(1)}, f32[2,512]{1,0:T(2,128)}, u32[]{:S(2)}, u32[]{:S(2)}) collective-permute-start(f32[2,512]{1,0:T(2,128)S(1)} %maximum_select_fusion.2), channel_id=1, source_target_pairs={{0,4},{1,5},{2,6},{3,7},{4,0},{5,1},{6,2},{7,3},{8,12},{9,13},{10,... | collective-permute-start | bytes 12296 | tf_op jit(solution)/shard_map/ppermute | solution.py:109
  43.4 12.7 %collective-permute-done.4 = bf16[384,768]{1,0:T(8,128)(2,1)S(1)} collective-permute-done((bf16[384,768]{1,0:T(8,128)(2,1)S(1)}, bf16[384,768]{1,0:T(8,128)(2,1)S(1)}, u32[]{:S(2)}, u32[]{:S(2)}) %collective-permute-start.4) | collective-permute-done | bytes 589856 | tf_op jit(solution)/shard_map/ppermute | solution.py:77
  56.2 3.7 %collective-permute-done.6 = bf16[384,768]{1,0:T(8,128)(2,1)S(1)} collective-permute-done((bf16[384,768]{1,0:T(8,128)(2,1)S(1)}, bf16[384,768]{1,0:T(8,128)(2,1)S(1)}, u32[]{:S(2)}, u32[]{:S(2)}) %collective-permute-start.6) | collective-permute-done | bytes 589856 | tf_op jit(solution)/shard_map/ppermute | solution.py:77
  61.4 2.9 %fusion.7 = bf16[1024,1536]{1,0:T(8,128)(2,1)S(1)} fusion(bf16[1024,1536]{1,0:T(8,128)(2,1)} %all-gather.4.cloned.1.call-done, f32[1536]{0:T(1024)S(1)} %copy-done.8, f32[1024]{0:T(1024)S(1)} %bitcast.91, f32[1024]{0:T(1024)S(1)} %bitcast.90), kind=kLoop, calls=%fused_computation.11 | loop fusion | flops 7864320 | bytes 6305792 | tf_op jit(solution)/shard_map/convert_element_type | solution.py:147
  67.2 5.2 %collective-permute-start.11 = (bf16[15,192]{0,1:T(8,128)(2,1)S(1)}, bf16[15,192]{0,1:T(8,128)(2,1)S(1)}, u32[]{:S(2)}, u32[]{:S(2)}) collective-permute-start(bf16[15,192]{0,1:T(8,128)(2,1)S(1)} %get-tuple-element.44), channel_id=1, source_target_pairs={{8,0},{16,8},{24,16},{32,24},{40,32},{48,40},{56,48},{64,56},{72,6... | collective-permute-start | bytes 17288 | tf_op jit(solution)/shard_map/ppermute | solution.py:18
  72.4 2.1 collective-permute-start.10
  74.6 3.3 %collective-permute-done.10 = bf16[15,192]{0,1:T(8,128)(2,1)S(1)} collective-permute-done((bf16[15,192]{0,1:T(8,128)(2,1)S(1)}, bf16[15,192]{0,1:T(8,128)(2,1)S(1)}, u32[]{:S(2)}, u32[]{:S(2)}) %collective-permute-start.10) | collective-permute-done | bytes 5792 | tf_op jit(solution)/shard_map/ppermute | solution.py:17
  78.1 5.3 %multiply_reduce_fusion.1 = (f32[192]{0:T(256)S(1)}, f32[1024,192]{0,1:T(8,128)S(1)}) fusion(f32[1024]{0:T(1024)S(1)} %get-tuple-element.30, f32[192]{0:T(256)S(1)} %bitcast.125, bf16[1039,192]{0,1:T(8,128)(2,1)S(1)} %constant_dynamic-update-slice_fusion, f32[192]{0:T(256)S(1)} %bitcast.126, f32[192]{0:T(256)S(1)} %bitcast.97, f32[192]{0:T(256)S(1)} %bitcast.98, ...), kind=kLoop, calls=%fused_computation.59 | loop fusion | flops 27328320 | bytes 7112320 | tf_op jit(solution)/shard_map/reduce_sum | solution.py:161
  86.2 3.6 %collective-permute-done.13 = f32[3,192]{1,0:T(4,128)S(1)} collective-permute-done((f32[3,192]{1,0:T(4,128)S(1)}, f32[3,192]{1,0:T(4,128)S(1)}, u32[]{:S(2)}, u32[]{:S(2)}) %collective-permute-start.13) | collective-permute-done | bytes 2336 | tf_op jit(solution)/shard_map/ppermute | solution.py:47
  90.1 4.9 %collective-permute-done.14 = f32[3,192]{1,0:T(4,128)S(1)} collective-permute-done((f32[3,192]{1,0:T(4,128)S(1)}, f32[3,192]{1,0:T(4,128)S(1)}, u32[]{:S(2)}, u32[]{:S(2)}) %collective-permute-start.14) | collective-permute-done | bytes 2336 | tf_op jit(solution)/shard_map/ppermute | solution.py:47
  96.4 2.4 %collective-permute-done.15 = f32[3,192]{1,0:T(4,128)S(1)} collective-permute-done((f32[3,192]{1,0:T(4,128)S(1)}, f32[3,192]{1,0:T(4,128)S(1)}, u32[]{:S(2)}, u32[]{:S(2)}) %collective-permute-start.15) | collective-permute-done | bytes 2336 | tf_op jit(solution)/shard_map/ppermute | solution.py:47
  100.1 4.0 %collective-permute-done.16 = f32[3,192]{1,0:T(4,128)S(1)} collective-permute-done((f32[3,192]{1,0:T(4,128)S(1)}, f32[3,192]{1,0:T(4,128)S(1)}, u32[]{:S(2)}, u32[]{:S(2)}) %collective-permute-start.16) | collective-permute-done | bytes 2336 | tf_op jit(solution)/shard_map/ppermute | solution.py:47
  104.1 2.3 %multiply_convert_fusion.1 = bf16[1024,192]{0,1:T(8,128)(2,1)} fusion(f32[1024,192]{0,1:T(8,128)} %copy-done.3, f32[192]{0:T(256)S(1)} %copy-done.41, f32[192]{0:T(256)S(1)} %copy-done.42, f32[192]{0:T(256)S(1)} %bitcast.128, f32[192]{0:T(256)S(1)} %bitcast.127), kind=kLoop, calls=%fused_computation.57 | loop fusion | flops 1769472 | bytes 1182720 | tf_op jit(solution)/shard_map/convert_element_type | solution.py:170
  108.9 7.9 %collective-permute-done.17 = bf16[2,1536,768]{2,1,0:T(8,128)(2,1)S(1)} collective-permute-done((bf16[2,1536,768]{2,1,0:T(8,128)(2,1)S(1)}, bf16[2,1536,768]{2,1,0:T(8,128)(2,1)S(1)}, u32[]{:S(2)}, u32[]{:S(2)}) %collective-permute-start.17) | collective-permute-done | bytes 4718624 | tf_op jit(solution)/shard_map/ppermute | solution.py:173
  116.8 2.2 copy-done.6
  119.0 2.5 %broadcast_select_fusion = (bf16[1536,768]{1,0:T(8,128)(2,1)}, bf16[1536,768]{1,0:T(8,128)(2,1)}) fusion(bf16[1536,768]{1,0:T(8,128)(2,1)S(1)} %pad_maximum_fusion.1, pred[]{:T(512)S(6)} %eq.130, bf16[2,1536,768]{2,1,0:T(8,128)(2,1)S(1)} %collective-permute-done.17), kind=kLoop, calls=%fused_computation.27 | loop fusion | flops 2359296 | bytes 9437185 | tf_op jit(solution)/shard_map/jit(_where)/select_n | solution.py:175
  121.5 29.2 %all-gather.6.cloned.1.call-done = bf16[1024,1536]{0,1:T(8,128)(2,1)} async-done(((bf16[1024,192]{0,1:T(8,128)(2,1)}), bf16[1024,1536]{0,1:T(8,128)(2,1)}) %all-gather.6.cloned.1.call-update) | async-done | bytes 3145744 | tf_op jit(solution)/shard_map/all_gather | solution.py:171
  150.7 5.5 %fusion.14 = f32[1024,768]{1,0:T(8,128)S(1)} fusion(bf16[1024,1536]{0,1:T(8,128)(2,1)} %all-gather.6.cloned.1.call-done, bf16[1536,768]{1,0:T(8,128)(2,1)} %all-gather.8.cloned.1.call-done, pred[]{:T(512)S(6)} %eq.130, bf16[2,1536,768]{2,1,0:T(8,128)(2,1)} %copy-done.6), kind=kOutput, calls=%fused_computation.23 | convolution fusion | flops 2417098752 | bytes 11010049 | tf_op jit(solution)/shard_map/dot_general | solution.py:182
  156.3 2.9 %fusion.16 = f32[1024,768]{1,0:T(8,128)S(1)} fusion(bf16[1024,1536]{0,1:T(8,128)(2,1)S(1)} %copy-done.43, bf16[1536,768]{1,0:T(8,128)(2,1)S(1)} %copy-done.4, pred[]{:T(512)S(6)} %eq.130, bf16[2,1536,768]{2,1,0:T(8,128)(2,1)S(1)} %copy-done.7), kind=kOutput, calls=%fused_computation.25 | convolution fusion | flops 2417098752 | bytes 11010049 | tf_op jit(solution)/shard_map/dot_general | solution.py:181
  162.7 10.5 %convolution_convert_fusion = bf16[1024,1536]{1,0:T(8,128)(2,1)} fusion(bf16[1536,768]{1,0:T(8,128)(2,1)S(1)} %copy-done.5, bf16[1536,768]{1,0:T(8,128)(2,1)} %get-tuple-element.13, bf16[1024,1536]{1,0:T(8,128)(2,1)} %copy-done.1, f32[1536]{0:T(1024)S(1)} %copy-done.45, f32[1024]{0:T(1024)S(1)} %add_rsqrt_fusion, f32[1024]{0:T(1024)S(1)} %broadcast_multiply_fusion), kind=kOutput, calls=%fused_computation.14 | convolution fusion | flops 4845207552 | bytes 11024384 | tf_op jit(solution)/shard_map/dot_general | solution.py:192
  173.2 45.8 %reduce-scatter.2.cloned.1.call-done = bf16[128,1536]{1,0:T(8,128)(2,1)} async-done(((bf16[1024,1536]{1,0:T(8,128)(2,1)}), bf16[128,1536]{1,0:T(8,128)(2,1)}) %reduce-scatter.2.cloned.1.call-update) | async-done | bytes 393232 | tf_op jit(solution)/shard_map/reduce_scatter | solution.py:195
  (179 shorter events, 37.4 us)
Async XLA Ops:
  6.5 57.8 %copy-start = (bf16[1536,192]{0,1:T(8,128)(2,1)S(1)}, bf16[1536,192]{0,1:T(8,128)(2,1)}, u32[]{:S(2)}) copy-start(bf16[1536,192]{0,1:T(8,128)(2,1)} %param.18) | copy-start | bytes 1769476
  6.5 54.4 %all-gather.4.cloned.1.call-start = ((), (), s32[]{:S(2)}) async-start(), calls=%async_computation.1 | async-start | bytes 3538944 | tf_op jit(solution)/shard_map/all_gather | solution.py:139
  7.3 99.3 %all-gather.8.cloned.1.call-start = ((), (), s32[]{:S(2)}) async-start(), calls=%async_computation.3 | async-start | bytes 2654208 | tf_op jit(solution)/shard_map/all_gather | solution.py:151
  8.2 8.1 %collective-permute-start = (bf16[2,48,768]{2,1,0:T(8,128)(2,1)S(1)}, bf16[2,48,768]{2,1,0:T(8,128)(2,1)S(1)}, u32[]{:S(2)}, u32[]{:S(2)}) collective-permute-start(bf16[2,48,768]{2,1,0:T(8,128)(2,1)S(1)} %pad_maximum_fusion.4), channel_id=1, source_target_pairs={{0,8},{8,0},{16,24},{24,16},{32,40},{40,32},{48,56},{56,48},{64,72... | collective-permute-start | bytes 442376 | tf_op jit(solution)/shard_map/ppermute | solution.py:77
  10.8 13.8 %collective-permute-start.7 = (f32[2,128]{1,0:T(2,128)S(1)}, f32[2,128]{1,0:T(2,128)S(1)}, u32[]{:S(2)}, u32[]{:S(2)}) collective-permute-start(f32[2,128]{1,0:T(2,128)S(1)} %pad_maximum_fusion.10), channel_id=1, source_target_pairs={{0,1},{1,0},{2,3},{3,2},{4,5},{5,4},{6,7},{7,6},{8,9},{9,8},{10,11... | collective-permute-start | bytes 3080 | tf_op jit(solution)/shard_map/ppermute | solution.py:109
  14.6 136.1 %all-gather.6.cloned.1.call-start = ((), (), s32[]{:S(2)}) async-start(), calls=%async_computation.2 | async-start | bytes 3538944 | tf_op jit(solution)/shard_map/all_gather | solution.py:171
  17.4 10.6 %collective-permute-start.1 = (bf16[96,768]{1,0:T(8,128)(2,1)S(1)}, bf16[96,768]{1,0:T(8,128)(2,1)S(1)}, u32[]{:S(2)}, u32[]{:S(2)}) collective-permute-start(bf16[96,768]{1,0:T(8,128)(2,1)S(1)} %maximum_select_fusion), channel_id=1, source_target_pairs={{0,48},{8,56},{16,0},{24,8},{32,16},{40,24},{48,32},{56,40},{64,11... | collective-permute-start | bytes 442376 | tf_op jit(solution)/shard_map/ppermute | solution.py:77
  18.0 10.0 %collective-permute-start.2 = (bf16[96,768]{1,0:T(8,128)(2,1)S(1)}, bf16[96,768]{1,0:T(8,128)(2,1)S(1)}, u32[]{:S(2)}, u32[]{:S(2)}) collective-permute-start(bf16[96,768]{1,0:T(8,128)(2,1)S(1)} %maximum_select_fusion), channel_id=1, source_target_pairs={{0,32},{8,40},{16,48},{24,56},{32,0},{40,8},{48,16},{56,24},{64,96... | collective-permute-start | bytes 442376 | tf_op jit(solution)/shard_map/ppermute | solution.py:77
  20.4 8.0 %collective-permute-start.3 = (bf16[96,768]{1,0:T(8,128)(2,1)S(1)}, bf16[96,768]{1,0:T(8,128)(2,1)S(1)}, u32[]{:S(2)}, u32[]{:S(2)}) collective-permute-start(bf16[96,768]{1,0:T(8,128)(2,1)S(1)} %maximum_select_fusion), channel_id=1, source_target_pairs={{0,16},{8,24},{16,32},{24,40},{32,48},{40,56},{48,0},{56,8},{64,80... | collective-permute-start | bytes 442376 | tf_op jit(solution)/shard_map/ppermute | solution.py:77
  24.6 8.6 %collective-permute-start.8 = (f32[2,256]{1,0:T(2,128)S(1)}, f32[2,256]{1,0:T(2,128)S(1)}, u32[]{:S(2)}, u32[]{:S(2)}) collective-permute-start(f32[2,256]{1,0:T(2,128)S(1)} %maximum_select_fusion.3), channel_id=1, source_target_pairs={{0,2},{1,3},{2,0},{3,1},{4,6},{5,7},{6,4},{7,5},{8,10},{9,11},{10,... | collective-permute-start | bytes 6152 | tf_op jit(solution)/shard_map/ppermute | solution.py:109
  28.5 27.7 %collective-permute-start.4 = (bf16[384,768]{1,0:T(8,128)(2,1)S(1)}, bf16[384,768]{1,0:T(8,128)(2,1)S(1)}, u32[]{:S(2)}, u32[]{:S(2)}) collective-permute-start(bf16[384,768]{1,0:T(8,128)(2,1)S(1)} %pad_maximum_fusion.2), channel_id=1, source_target_pairs={{0,192},{8,200},{16,208},{24,216},{32,224},{40,232},{48,240},{56,2... | collective-permute-start | bytes 1769480 | tf_op jit(solution)/shard_map/ppermute | solution.py:77
  31.6 24.6 %collective-permute-start.5 = (bf16[384,768]{1,0:T(8,128)(2,1)S(1)}, bf16[384,768]{1,0:T(8,128)(2,1)S(1)}, u32[]{:S(2)}, u32[]{:S(2)}) collective-permute-start(bf16[384,768]{1,0:T(8,128)(2,1)S(1)} %pad_maximum_fusion.2), channel_id=1, source_target_pairs={{0,128},{8,136},{16,144},{24,152},{32,160},{40,168},{48,176},{56,1... | collective-permute-start | bytes 1769480 | tf_op jit(solution)/shard_map/ppermute | solution.py:77
  32.2 27.7 %collective-permute-start.6 = (bf16[384,768]{1,0:T(8,128)(2,1)S(1)}, bf16[384,768]{1,0:T(8,128)(2,1)S(1)}, u32[]{:S(2)}, u32[]{:S(2)}) collective-permute-start(bf16[384,768]{1,0:T(8,128)(2,1)S(1)} %pad_maximum_fusion.2), channel_id=1, source_target_pairs={{0,64},{8,72},{16,80},{24,88},{32,96},{40,104},{48,112},{56,120},{... | collective-permute-start | bytes 1769480 | tf_op jit(solution)/shard_map/ppermute | solution.py:77
  33.2 9.5 %collective-permute-start.9 = (f32[2,512]{1,0:T(2,128)S(1)}, f32[2,512]{1,0:T(2,128)}, u32[]{:S(2)}, u32[]{:S(2)}) collective-permute-start(f32[2,512]{1,0:T(2,128)S(1)} %maximum_select_fusion.2), channel_id=1, source_target_pairs={{0,4},{1,5},{2,6},{3,7},{4,0},{5,1},{6,2},{7,3},{8,12},{9,13},{10,... | collective-permute-start | bytes 12296 | tf_op jit(solution)/shard_map/ppermute | solution.py:109
  67.2 7.4 %collective-permute-start.11 = (bf16[15,192]{0,1:T(8,128)(2,1)S(1)}, bf16[15,192]{0,1:T(8,128)(2,1)S(1)}, u32[]{:S(2)}, u32[]{:S(2)}) collective-permute-start(bf16[15,192]{0,1:T(8,128)(2,1)S(1)} %get-tuple-element.44), channel_id=1, source_target_pairs={{8,0},{16,8},{24,16},{32,24},{40,32},{48,40},{56,48},{64,56},{72,6... | collective-permute-start | bytes 17288 | tf_op jit(solution)/shard_map/ppermute | solution.py:18
  72.4 5.4 %collective-permute-start.10 = (bf16[15,192]{0,1:T(8,128)(2,1)S(1)}, bf16[15,192]{0,1:T(8,128)(2,1)S(1)}, u32[]{:S(2)}, u32[]{:S(2)}) collective-permute-start(bf16[15,192]{0,1:T(8,128)(2,1)S(1)} %get-tuple-element.43), channel_id=1, source_target_pairs={{0,8},{8,16},{16,24},{24,32},{32,40},{40,48},{48,56},{56,64},{64,7... | collective-permute-start | bytes 17288 | tf_op jit(solution)/shard_map/ppermute | solution.py:17
  84.7 1.2 collective-permute-start.12
  86.1 3.7 %collective-permute-start.13 = (f32[3,192]{1,0:T(4,128)S(1)}, f32[3,192]{1,0:T(4,128)S(1)}, u32[]{:S(2)}, u32[]{:S(2)}) collective-permute-start(f32[3,192]{1,0:T(4,128)S(1)} %pad_maximum_fusion.6), channel_id=1, source_target_pairs={{0,16},{8,24},{16,0},{24,8},{32,48},{40,56},{48,32},{56,40},{64,80... | collective-permute-start | bytes 6920 | tf_op jit(solution)/shard_map/ppermute | solution.py:47
  89.8 5.2 %collective-permute-start.14 = (f32[3,192]{1,0:T(4,128)S(1)}, f32[3,192]{1,0:T(4,128)S(1)}, u32[]{:S(2)}, u32[]{:S(2)}) collective-permute-start(f32[3,192]{1,0:T(4,128)S(1)} %pad_maximum_fusion.7), channel_id=1, source_target_pairs={{0,32},{8,40},{16,48},{24,56},{32,0},{40,8},{48,16},{56,24},{64,96... | collective-permute-start | bytes 6920 | tf_op jit(solution)/shard_map/ppermute | solution.py:47
  95.1 3.7 %collective-permute-start.15 = (f32[3,192]{1,0:T(4,128)S(1)}, f32[3,192]{1,0:T(4,128)S(1)}, u32[]{:S(2)}, u32[]{:S(2)}) collective-permute-start(f32[3,192]{1,0:T(4,128)S(1)} %pad_maximum_fusion.8), channel_id=1, source_target_pairs={{0,64},{8,72},{16,80},{24,88},{32,96},{40,104},{48,112},{56,120},{... | collective-permute-start | bytes 6920 | tf_op jit(solution)/shard_map/ppermute | solution.py:47
  98.9 5.2 %collective-permute-start.16 = (f32[3,192]{1,0:T(4,128)S(1)}, f32[3,192]{1,0:T(4,128)S(1)}, u32[]{:S(2)}, u32[]{:S(2)}) collective-permute-start(f32[3,192]{1,0:T(4,128)S(1)} %pad_maximum_fusion.9), channel_id=1, source_target_pairs={{0,128},{8,136},{16,144},{24,152},{32,160},{40,168},{48,176},{56,1... | collective-permute-start | bytes 6920 | tf_op jit(solution)/shard_map/ppermute | solution.py:47
  106.5 112.5 %reduce-scatter.2.cloned.1.call-start = ((), (), s32[]{:S(2)}) async-start(), calls=%async_computation.4 | async-start | bytes 3538944 | tf_op jit(solution)/shard_map/reduce_scatter | solution.py:195
  108.6 8.2 %collective-permute-start.17 = (bf16[2,1536,768]{2,1,0:T(8,128)(2,1)S(1)}, bf16[2,1536,768]{2,1,0:T(8,128)(2,1)S(1)}, u32[]{:S(2)}, u32[]{:S(2)}) collective-permute-start(bf16[2,1536,768]{2,1,0:T(8,128)(2,1)S(1)} %pad_maximum_fusion), channel_id=1, source_target_pairs={{0,8},{8,0},{16,24},{24,16},{32,40},{40,32},{48,56},{56,48},{64,72... | collective-permute-start | bytes 14155784 | tf_op jit(solution)/shard_map/ppermute | solution.py:173
  121.5 34.7 %copy-start.4 = (bf16[1536,768]{1,0:T(8,128)(2,1)S(1)}, bf16[1536,768]{1,0:T(8,128)(2,1)}, u32[]{:S(2)}) copy-start(bf16[1536,768]{1,0:T(8,128)(2,1)} %all-gather.8.cloned.1.call-done) | copy-start | bytes 7077892
  (44 other events, 484.1 us)
Sparse Core Ops, SparseCore 0:
  9.1 48.0 all-gather.3
  59.1 40.2 all-gather.7
  106.6 44.0 all-gather.5
  173.3 45.5 reduce-scatter.1

commit v13 on v10

--- a/solution.py
+++ b/solution.py
@@ -166,7 +166,7 @@
     feed_block = layer_norm(mid_block, feed_gain).astype(jnp.bfloat16)
     mid = lax.dynamic_slice_in_dim(mid_block, lax.axis_index("tensor") * own_rows, own_rows, axis=0)
     pre = jnp.dot(feed_block, up_whole, preferred_element_type=jnp.float32)
-    hidden = (pre * jax.nn.sigmoid(pre)).astype(jnp.bfloat16)
+    hidden = lax.optimization_barrier((pre * jax.nn.sigmoid(pre)).astype(jnp.bfloat16))
     partial_out = lax.dot_general(
         hidden, down_t, (((1,), (1,)), ((), ())), preferred_element_type=jnp.float32
     )

time: 224 us -> 220 us (0.982)
  matrix products: 21.3 us -> 18.1 us
    dot_general x1, matrix products: 10.5 us -> 4.08 us  [shards(): lax.dot_general(hidden, down_t, (((1,), (1,)), ((), ())), preferred_eleme...]
    dot_general x0 -> x1, matrix products: none -> 3.21 us  [shards(): pre = jnp.dot(feed_block, up_whole, preferred_element_type=jnp.float32)]
    unnamed x91 -> x93, local copies, waits for them, and re-layouts: 4.94 us -> 4.93 us
where the time goes in v13:
time: 220 us
  waiting for transfers between devices  125 us (57%)
  other arithmetic  26.9 us (12%)
  starting transfers between devices  24.6 us (11%)
  matrix products  18.1 us (8%)
  between operations  16.1 us (7%)
  local copies, waits for them, and re-layouts  9.38 us (4%)
    reduce_scatter x1, waiting for transfers between devices, shards(): lax.psum_scatter(partial_out.astype(jnp.bfloat16), 'tensor', scatter_dime...  45.4 us
    all_gather x1, waiting for transfers between devices, shards(): swished_all = lax.all_gather(swished, 'tensor', axis=1, tiled=True)  28.5 us
    ppermute x7, waiting for transfers between devices, shifted(): return lax.ppermute(value, axis, pairs)  25.1 us
    ppermute x5, waiting for transfers between devices, moments_over(): other = lax.ppermute(stats, axis, pairs)  10.5 us
    ppermute x5, starting transfers between devices, moments_over(): other = lax.ppermute(stats, axis, pairs)  10.1 us
    ppermute x7, starting transfers between devices, shifted(): return lax.ppermute(value, axis, pairs)  9.62 us
    ppermute x1, waiting for transfers between devices, shards(): lax.ppermute(jnp.stack([out_mine, ff_mine]), 'tm', swap)  7.9 us
    dot_general x1, matrix products, shards(): lax.dot_general(swished_all, right, contract, preferred_element_type=jnp....  5.52 us
  transfers between devices with their start and end apart: 19, of which 15 were waited for; matrix products, arithmetic and copies ran while one was open for 13% of the time, Pallas kernels for 0%

profile of v13, /device:TPU:2, one launch (start us, length us, event | category | flops | bytes accessed | tf_op | source)
XLA Modules:
  0.0 219.6 jit_solution(14638422563003680207)
XLA Ops:
  10.7 2.3 %collective-permute-start.1 = (bf16[96,768]{1,0:T(8,128)(2,1)S(1)}, bf16[96,768]{1,0:T(8,128)(2,1)S(1)}, u32[]{:S(2)}, u32[]{:S(2)}) collective-permute-start(bf16[96,768]{1,0:T(8,128)(2,1)S(1)} %maximum_select_fusion), channel_id=1, source_target_pairs={{0,48},{8,56},{16,0},{24,8},{32,16},{40,24},{48,32},{56,40},{64,11... | collective-permute-start | bytes 442376 | tf_op jit(solution)/shard_map/ppermute | solution.py:77
  18.3 2.5 %collective-permute-done.2 = bf16[96,768]{1,0:T(8,128)(2,1)S(1)} collective-permute-done((bf16[96,768]{1,0:T(8,128)(2,1)S(1)}, bf16[96,768]{1,0:T(8,128)(2,1)S(1)}, u32[]{:S(2)}, u32[]{:S(2)}) %collective-permute-start.2) | collective-permute-done | bytes 147488 | tf_op jit(solution)/shard_map/ppermute | solution.py:77
  21.8 3.1 %collective-permute-start.4 = (bf16[384,768]{1,0:T(8,128)(2,1)S(1)}, bf16[384,768]{1,0:T(8,128)(2,1)S(1)}, u32[]{:S(2)}, u32[]{:S(2)}) collective-permute-start(bf16[384,768]{1,0:T(8,128)(2,1)S(1)} %pad_maximum_fusion.2), channel_id=1, source_target_pairs={{0,192},{8,200},{16,208},{24,216},{32,224},{40,232},{48,240},{56,2... | collective-permute-start | bytes 1769480 | tf_op jit(solution)/shard_map/ppermute | solution.py:77
  32.5 16.7 %collective-permute-done.4 = bf16[384,768]{1,0:T(8,128)(2,1)S(1)} collective-permute-done((bf16[384,768]{1,0:T(8,128)(2,1)S(1)}, bf16[384,768]{1,0:T(8,128)(2,1)S(1)}, u32[]{:S(2)}, u32[]{:S(2)}) %collective-permute-start.4) | collective-permute-done | bytes 589856 | tf_op jit(solution)/shard_map/ppermute | solution.py:77
  49.2 3.7 %collective-permute-done.6 = bf16[384,768]{1,0:T(8,128)(2,1)S(1)} collective-permute-done((bf16[384,768]{1,0:T(8,128)(2,1)S(1)}, bf16[384,768]{1,0:T(8,128)(2,1)S(1)}, u32[]{:S(2)}, u32[]{:S(2)}) %collective-permute-start.6) | collective-permute-done | bytes 589856 | tf_op jit(solution)/shard_map/ppermute | solution.py:77
  54.0 3.1 %all-gather.4.cloned.1.call-done = bf16[1024,1536]{1,0:T(8,128)(2,1)} async-done(((bf16[128,1536]{1,0:T(8,128)(2,1)}), bf16[1024,1536]{1,0:T(8,128)(2,1)}) %all-gather.4.cloned.1.call-update) | async-done | bytes 3145744 | tf_op jit(solution)/shard_map/all_gather | solution.py:123
  57.1 2.5 %convert_reduce_fusion = f32[1024]{0:T(1024)S(1)} fusion(bf16[1024,1536]{1,0:T(8,128)(2,1)} %all-gather.4.cloned.1.call-done), kind=kLoop, calls=%fused_computation.2 | loop fusion | flops 3144704 | bytes 3149824 | tf_op jit(solution)/shard_map/reduce_sum | solution.py:25
  64.8 2.3 %collective-permute-start.8 = (bf16[15,192]{0,1:T(8,128)(2,1)S(1)}, bf16[15,192]{0,1:T(8,128)(2,1)S(1)}, u32[]{:S(2)}, u32[]{:S(2)}) collective-permute-start(bf16[15,192]{0,1:T(8,128)(2,1)S(1)} %get-tuple-element.44), channel_id=1, source_target_pairs={{8,0},{16,8},{24,16},{32,24},{40,32},{48,40},{56,48},{64,56},{72,6... | collective-permute-start | bytes 17288 | tf_op jit(solution)/shard_map/ppermute | solution.py:18
  69.4 3.1 %collective-permute-done.7 = bf16[15,192]{0,1:T(8,128)(2,1)S(1)} collective-permute-done((bf16[15,192]{0,1:T(8,128)(2,1)S(1)}, bf16[15,192]{0,1:T(8,128)(2,1)S(1)}, u32[]{:S(2)}, u32[]{:S(2)}) %collective-permute-start.7) | collective-permute-done | bytes 5792 | tf_op jit(solution)/shard_map/ppermute | solution.py:17
  72.8 5.3 %multiply_reduce_fusion.1 = (f32[192]{0:T(256)S(1)}, f32[1024,192]{0,1:T(8,128)S(1)}) fusion(f32[1024]{0:T(1024)S(1)} %get-tuple-element.30, f32[192]{0:T(256)S(1)} %bitcast.99, bf16[1039,192]{0,1:T(8,128)(2,1)S(1)} %constant_dynamic-update-slice_fusion, f32[192]{0:T(256)S(1)} %bitcast.100, f32[192]{0:T(256)S(1)} %bitcast.102, f32[192]{0:T(256)S(1)} %bitcast.103, ...), kind=kLoop, calls=%fused_computation.58 | loop fusion | flops 27328320 | bytes 7112320 | tf_op jit(solution)/shard_map/reduce_sum | solution.py:139
  80.8 3.6 %collective-permute-done.10 = f32[3,192]{1,0:T(4,128)S(1)} collective-permute-done((f32[3,192]{1,0:T(4,128)S(1)}, f32[3,192]{1,0:T(4,128)S(1)}, u32[]{:S(2)}, u32[]{:S(2)}) %collective-permute-start.10) | collective-permute-done | bytes 2336 | tf_op jit(solution)/shard_map/ppermute | solution.py:47
  84.5 2.6 %collective-permute-start.11 = (f32[3,192]{1,0:T(4,128)S(1)}, f32[3,192]{1,0:T(4,128)S(1)}, u32[]{:S(2)}, u32[]{:S(2)}) collective-permute-start(f32[3,192]{1,0:T(4,128)S(1)} %pad_maximum_fusion.7), channel_id=1, source_target_pairs={{0,32},{8,40},{16,48},{24,56},{32,0},{40,8},{48,16},{56,24},{64,96... | collective-permute-start | bytes 6920 | tf_op jit(solution)/shard_map/ppermute | solution.py:47
  87.1 2.6 %collective-permute-done.11 = f32[3,192]{1,0:T(4,128)S(1)} collective-permute-done((f32[3,192]{1,0:T(4,128)S(1)}, f32[3,192]{1,0:T(4,128)S(1)}, u32[]{:S(2)}, u32[]{:S(2)}) %collective-permute-start.11) | collective-permute-done | bytes 2336 | tf_op jit(solution)/shard_map/ppermute | solution.py:47
  89.7 3.7 %collective-permute-start.12 = (f32[3,192]{1,0:T(4,128)S(1)}, f32[3,192]{1,0:T(4,128)S(1)}, u32[]{:S(2)}, u32[]{:S(2)}) collective-permute-start(f32[3,192]{1,0:T(4,128)S(1)} %pad_maximum_fusion.8), channel_id=1, source_target_pairs={{0,64},{8,72},{16,80},{24,88},{32,96},{40,104},{48,112},{56,120},{... | collective-permute-start | bytes 6920 | tf_op jit(solution)/shard_map/ppermute | solution.py:47
  95.1 3.6 %collective-permute-start.13 = (f32[3,192]{1,0:T(4,128)S(1)}, f32[3,192]{1,0:T(4,128)S(1)}, u32[]{:S(2)}, u32[]{:S(2)}) collective-permute-start(f32[3,192]{1,0:T(4,128)S(1)} %pad_maximum_fusion.9), channel_id=1, source_target_pairs={{0,128},{8,136},{16,144},{24,152},{32,160},{40,168},{48,176},{56,1... | collective-permute-start | bytes 6920 | tf_op jit(solution)/shard_map/ppermute | solution.py:47
  100.4 2.3 %multiply_convert_fusion.1 = bf16[1024,192]{0,1:T(8,128)(2,1)} fusion(f32[1024,192]{0,1:T(8,128)} %copy-done.4, f32[192]{0:T(256)S(1)} %copy-done.41, f32[192]{0:T(256)S(1)} %copy-done.42, f32[192]{0:T(256)S(1)} %bitcast.121, f32[192]{0:T(256)S(1)} %bitcast.120), kind=kLoop, calls=%fused_computation.56 | loop fusion | flops 1769472 | bytes 1182720 | tf_op jit(solution)/shard_map/convert_element_type | solution.py:148
  105.2 7.9 %collective-permute-done.14 = bf16[2,1536,768]{2,1,0:T(8,128)(2,1)S(1)} collective-permute-done((bf16[2,1536,768]{2,1,0:T(8,128)(2,1)S(1)}, bf16[2,1536,768]{2,1,0:T(8,128)(2,1)S(1)}, u32[]{:S(2)}, u32[]{:S(2)}) %collective-permute-start.14) | collective-permute-done | bytes 4718624 | tf_op jit(solution)/shard_map/ppermute | solution.py:151
  115.3 2.4 %broadcast_select_fusion = (bf16[1536,768]{1,0:T(8,128)(2,1)}, bf16[1536,768]{1,0:T(8,128)(2,1)}) fusion(bf16[1536,768]{1,0:T(8,128)(2,1)S(1)} %pad_maximum_fusion.1, pred[]{:T(512)S(6)} %eq.121, bf16[2,1536,768]{2,1,0:T(8,128)(2,1)S(1)} %collective-permute-done.14), kind=kLoop, calls=%fused_computation.30 | loop fusion | flops 2359296 | bytes 9437185 | tf_op jit(solution)/shard_map/jit(_where)/select_n | solution.py:153
  117.8 28.5 %all-gather.6.cloned.1.call-done = bf16[1024,1536]{0,1:T(8,128)(2,1)} async-done(((bf16[1024,192]{0,1:T(8,128)(2,1)}), bf16[1024,1536]{0,1:T(8,128)(2,1)}) %all-gather.6.cloned.1.call-update) | async-done | bytes 3145744 | tf_op jit(solution)/shard_map/all_gather | solution.py:149
  146.3 5.5 %fusion.16 = f32[1024,768]{1,0:T(8,128)S(1)} fusion(bf16[1024,1536]{0,1:T(8,128)(2,1)} %all-gather.6.cloned.1.call-done, bf16[1536,768]{1,0:T(8,128)(2,1)} %all-gather.8.cloned.1.call-done, pred[]{:T(512)S(6)} %eq.121, bf16[2,1536,768]{2,1,0:T(8,128)(2,1)} %copy-done.8), kind=kOutput, calls=%fused_computation.26 | convolution fusion | flops 2417098752 | bytes 11010049 | tf_op jit(solution)/shard_map/dot_general | solution.py:160
  151.9 2.9 %fusion.18 = f32[1024,768]{1,0:T(8,128)S(1)} fusion(bf16[1024,1536]{0,1:T(8,128)(2,1)S(1)} %copy-done.43, bf16[1536,768]{1,0:T(8,128)(2,1)S(1)} %copy-done.5, pred[]{:T(512)S(6)} %eq.121, bf16[2,1536,768]{2,1,0:T(8,128)(2,1)S(1)} %copy-done.9), kind=kOutput, calls=%fused_computation.28 | convolution fusion | flops 2417098752 | bytes 11010049 | tf_op jit(solution)/shard_map/dot_general | solution.py:159
  158.3 3.2 %multiply_convert_fusion = bf16[1024,768]{1,0:T(8,128)(2,1)S(1)} fusion(bf16[1536,768]{1,0:T(8,128)(2,1)S(1)} %copy-done.7, bf16[1024,1536]{1,0:T(8,128)(2,1)S(1)} %fusion.10, f32[1536]{0:T(1024)S(1)} %copy-done.45, f32[1024]{0:T(1024)S(1)} %add_rsqrt_fusion, f32[1024]{0:T(1024)S(1)} %broadcast_multiply_fusion), kind=kOutput, calls=%fused_computation.19 | convolution fusion | flops 2427715584 | bytes 7092224 | tf_op jit(solution)/shard_map/dot_general | solution.py:168
  161.6 4.1 %convolution_convert_fusion = bf16[1024,1536]{1,0:T(8,128)(2,1)} fusion(bf16[1024,768]{1,0:T(8,128)(2,1)S(1)} %multiply_convert_fusion, bf16[1536,768]{1,0:T(8,128)(2,1)S(1)} %copy-done.6), kind=kOutput, calls=%fused_computation.17 | convolution fusion | flops 2417491968 | bytes 7077888 | tf_op jit(solution)/shard_map/dot_general | solution.py:170
  165.7 45.4 %reduce-scatter.2.cloned.1.call-done = bf16[128,1536]{1,0:T(8,128)(2,1)} async-done(((bf16[1024,1536]{1,0:T(8,128)(2,1)}), bf16[128,1536]{1,0:T(8,128)(2,1)}) %reduce-scatter.2.cloned.1.call-update) | async-done | bytes 393232 | tf_op jit(solution)/shard_map/reduce_scatter | solution.py:173
  (169 shorter events, 40.4 us)
Async XLA Ops:
  6.5 55.4 %copy-start = (bf16[1536,192]{0,1:T(8,128)(2,1)S(1)}, bf16[1536,192]{0,1:T(8,128)(2,1)}, u32[]{:S(2)}) copy-start(bf16[1536,192]{0,1:T(8,128)(2,1)} %param.18) | copy-start | bytes 1769476
  6.5 19.9 %copy-start.39 = (s32[1024]{0:T(1024)S(1)}, s32[1024]{0:T(1024)}, u32[]{:S(2)}) copy-start(s32[1024]{0:T(1024)} %param.14) | copy-start | bytes 12292
  6.5 50.6 %all-gather.4.cloned.1.call-start = ((), (), s32[]{:S(2)}) async-start(), calls=%async_computation.1 | async-start | bytes 3538944 | tf_op jit(solution)/shard_map/all_gather | solution.py:123
  7.3 95.6 %all-gather.8.cloned.1.call-start = ((), (), s32[]{:S(2)}) async-start(), calls=%async_computation.3 | async-start | bytes 2654208 | tf_op jit(solution)/shard_map/all_gather | solution.py:129
  8.2 1.5 collective-permute-start
  10.7 7.6 %collective-permute-start.1 = (bf16[96,768]{1,0:T(8,128)(2,1)S(1)}, bf16[96,768]{1,0:T(8,128)(2,1)S(1)}, u32[]{:S(2)}, u32[]{:S(2)}) collective-permute-start(bf16[96,768]{1,0:T(8,128)(2,1)S(1)} %maximum_select_fusion), channel_id=1, source_target_pairs={{0,48},{8,56},{16,0},{24,8},{32,16},{40,24},{48,32},{56,40},{64,11... | collective-permute-start | bytes 442376 | tf_op jit(solution)/shard_map/ppermute | solution.py:77
  13.0 7.7 %collective-permute-start.2 = (bf16[96,768]{1,0:T(8,128)(2,1)S(1)}, bf16[96,768]{1,0:T(8,128)(2,1)S(1)}, u32[]{:S(2)}, u32[]{:S(2)}) collective-permute-start(bf16[96,768]{1,0:T(8,128)(2,1)S(1)} %maximum_select_fusion), channel_id=1, source_target_pairs={{0,32},{8,40},{16,48},{24,56},{32,0},{40,8},{48,16},{56,24},{64,96... | collective-permute-start | bytes 442376 | tf_op jit(solution)/shard_map/ppermute | solution.py:77
  13.7 7.9 %collective-permute-start.3 = (bf16[96,768]{1,0:T(8,128)(2,1)S(1)}, bf16[96,768]{1,0:T(8,128)(2,1)S(1)}, u32[]{:S(2)}, u32[]{:S(2)}) collective-permute-start(bf16[96,768]{1,0:T(8,128)(2,1)S(1)} %maximum_select_fusion), channel_id=1, source_target_pairs={{0,16},{8,24},{16,32},{24,40},{32,48},{40,56},{48,0},{56,8},{64,80... | collective-permute-start | bytes 442376 | tf_op jit(solution)/shard_map/ppermute | solution.py:77
  17.4 128.9 %all-gather.6.cloned.1.call-start = ((), (), s32[]{:S(2)}) async-start(), calls=%async_computation.2 | async-start | bytes 3538944 | tf_op jit(solution)/shard_map/all_gather | solution.py:149
  21.8 27.5 %collective-permute-start.4 = (bf16[384,768]{1,0:T(8,128)(2,1)S(1)}, bf16[384,768]{1,0:T(8,128)(2,1)S(1)}, u32[]{:S(2)}, u32[]{:S(2)}) collective-permute-start(bf16[384,768]{1,0:T(8,128)(2,1)S(1)} %pad_maximum_fusion.2), channel_id=1, source_target_pairs={{0,192},{8,200},{16,208},{24,216},{32,224},{40,232},{48,240},{56,2... | collective-permute-start | bytes 1769480 | tf_op jit(solution)/shard_map/ppermute | solution.py:77
  24.8 24.4 %collective-permute-start.5 = (bf16[384,768]{1,0:T(8,128)(2,1)S(1)}, bf16[384,768]{1,0:T(8,128)(2,1)S(1)}, u32[]{:S(2)}, u32[]{:S(2)}) collective-permute-start(bf16[384,768]{1,0:T(8,128)(2,1)S(1)} %pad_maximum_fusion.2), channel_id=1, source_target_pairs={{0,128},{8,136},{16,144},{24,152},{32,160},{40,168},{48,176},{56,1... | collective-permute-start | bytes 1769480 | tf_op jit(solution)/shard_map/ppermute | solution.py:77
  25.5 27.5 %collective-permute-start.6 = (bf16[384,768]{1,0:T(8,128)(2,1)S(1)}, bf16[384,768]{1,0:T(8,128)(2,1)S(1)}, u32[]{:S(2)}, u32[]{:S(2)}) collective-permute-start(bf16[384,768]{1,0:T(8,128)(2,1)S(1)} %pad_maximum_fusion.2), channel_id=1, source_target_pairs={{0,64},{8,72},{16,80},{24,88},{32,96},{40,104},{48,112},{56,120},{... | collective-permute-start | bytes 1769480 | tf_op jit(solution)/shard_map/ppermute | solution.py:77
  64.8 4.6 %collective-permute-start.8 = (bf16[15,192]{0,1:T(8,128)(2,1)S(1)}, bf16[15,192]{0,1:T(8,128)(2,1)S(1)}, u32[]{:S(2)}, u32[]{:S(2)}) collective-permute-start(bf16[15,192]{0,1:T(8,128)(2,1)S(1)} %get-tuple-element.44), channel_id=1, source_target_pairs={{8,0},{16,8},{24,16},{32,24},{40,32},{48,40},{56,48},{64,56},{72,6... | collective-permute-start | bytes 17288 | tf_op jit(solution)/shard_map/ppermute | solution.py:18
  67.1 5.4 %collective-permute-start.7 = (bf16[15,192]{0,1:T(8,128)(2,1)S(1)}, bf16[15,192]{0,1:T(8,128)(2,1)S(1)}, u32[]{:S(2)}, u32[]{:S(2)}) collective-permute-start(bf16[15,192]{0,1:T(8,128)(2,1)S(1)} %get-tuple-element.43), channel_id=1, source_target_pairs={{0,8},{8,16},{16,24},{24,32},{32,40},{40,48},{48,56},{56,64},{64,7... | collective-permute-start | bytes 17288 | tf_op jit(solution)/shard_map/ppermute | solution.py:17
  72.8 27.6 %copy-start.41 = (f32[192]{0:T(256)S(1)}, f32[192]{0:T(256)}, u32[]{:S(2)}) copy-start(f32[192]{0:T(256)} %param.21) | copy-start | bytes 2308
  72.8 27.6 %copy-start.42 = (f32[192]{0:T(256)S(1)}, f32[192]{0:T(256)}, u32[]{:S(2)}) copy-start(f32[192]{0:T(256)} %param.20) | copy-start | bytes 2308
  79.4 1.2 collective-permute-start.9
  80.7 3.7 %collective-permute-start.10 = (f32[3,192]{1,0:T(4,128)S(1)}, f32[3,192]{1,0:T(4,128)S(1)}, u32[]{:S(2)}, u32[]{:S(2)}) collective-permute-start(f32[3,192]{1,0:T(4,128)S(1)} %pad_maximum_fusion.6), channel_id=1, source_target_pairs={{0,16},{8,24},{16,0},{24,8},{32,48},{40,56},{48,32},{56,40},{64,80... | collective-permute-start | bytes 6920 | tf_op jit(solution)/shard_map/ppermute | solution.py:47
  84.5 5.2 %collective-permute-start.11 = (f32[3,192]{1,0:T(4,128)S(1)}, f32[3,192]{1,0:T(4,128)S(1)}, u32[]{:S(2)}, u32[]{:S(2)}) collective-permute-start(f32[3,192]{1,0:T(4,128)S(1)} %pad_maximum_fusion.7), channel_id=1, source_target_pairs={{0,32},{8,40},{16,48},{24,56},{32,0},{40,8},{48,16},{56,24},{64,96... | collective-permute-start | bytes 6920 | tf_op jit(solution)/shard_map/ppermute | solution.py:47
  89.7 5.3 %collective-permute-start.12 = (f32[3,192]{1,0:T(4,128)S(1)}, f32[3,192]{1,0:T(4,128)S(1)}, u32[]{:S(2)}, u32[]{:S(2)}) collective-permute-start(f32[3,192]{1,0:T(4,128)S(1)} %pad_maximum_fusion.8), channel_id=1, source_target_pairs={{0,64},{8,72},{16,80},{24,88},{32,96},{40,104},{48,112},{56,120},{... | collective-permute-start | bytes 6920 | tf_op jit(solution)/shard_map/ppermute | solution.py:47
  95.1 5.2 %collective-permute-start.13 = (f32[3,192]{1,0:T(4,128)S(1)}, f32[3,192]{1,0:T(4,128)S(1)}, u32[]{:S(2)}, u32[]{:S(2)}) collective-permute-start(f32[3,192]{1,0:T(4,128)S(1)} %pad_maximum_fusion.9), channel_id=1, source_target_pairs={{0,128},{8,136},{16,144},{24,152},{32,160},{40,168},{48,176},{56,1... | collective-permute-start | bytes 6920 | tf_op jit(solution)/shard_map/ppermute | solution.py:47
  102.7 108.3 %reduce-scatter.2.cloned.1.call-start = ((), (), s32[]{:S(2)}) async-start(), calls=%async_computation.4 | async-start | bytes 3538944 | tf_op jit(solution)/shard_map/reduce_scatter | solution.py:173
  104.9 8.2 %collective-permute-start.14 = (bf16[2,1536,768]{2,1,0:T(8,128)(2,1)S(1)}, bf16[2,1536,768]{2,1,0:T(8,128)(2,1)S(1)}, u32[]{:S(2)}, u32[]{:S(2)}) collective-permute-start(bf16[2,1536,768]{2,1,0:T(8,128)(2,1)S(1)} %pad_maximum_fusion), channel_id=1, source_target_pairs={{0,8},{8,0},{16,24},{24,16},{32,40},{40,32},{48,56},{56,48},{64,72... | collective-permute-start | bytes 14155784 | tf_op jit(solution)/shard_map/ppermute | solution.py:151
  117.8 34.1 %copy-start.5 = (bf16[1536,768]{1,0:T(8,128)(2,1)S(1)}, bf16[1536,768]{1,0:T(8,128)(2,1)}, u32[]{:S(2)}) copy-start(bf16[1536,768]{1,0:T(8,128)(2,1)} %all-gather.8.cloned.1.call-done) | copy-start | bytes 7077892
  (41 other events, 304.2 us)
Sparse Core Ops, SparseCore 0:
  9.1 47.9 all-gather.3
  58.9 40.3 all-gather.7
  102.9 43.3 all-gather.5
  165.8 45.2 reduce-scatter.1

commit v14 on v13

--- a/solution.py
+++ b/solution.py
@@ -135,6 +135,7 @@
     conv = jnp.zeros(glu.shape, jnp.float32)
     for tap in range(KERNEL):
         conv = conv + padded[tap : tap + block].astype(jnp.float32) * depth_kernel[tap]
+    conv = lax.optimization_barrier(conv)
     count_local = jnp.sum(valid)
     local_sum = jnp.sum(conv * valid[:, None], axis=0)
     local_mean = jnp.where(count_local > 0, local_sum / jnp.maximum(count_local, 1.0), 0.0)

time: 220 us -> 220 us (level)
    add x0 -> x1, other arithmetic: none -> 5.51 us  [shards(): conv + padded[tap:tap + block].astype(jnp.float32) * depth_kernel[tap]]
    reduce_sum x1, other arithmetic: 5.32 us -> 0.13 us  [shards(): local_sum = jnp.sum(conv * valid[:, None], axis=0)]
  transfers between devices with their start and end apart: 19 -> 19, of which waited for: 15 -> 15; matrix products, arithmetic and copies ran while one was open for 13% -> 14% of each run, Pallas kernels for 0% -> 0%
where the time goes in v14:
time: 220 us
  waiting for transfers between devices  125 us (57%)
  other arithmetic  27.2 us (12%)
  starting transfers between devices  24.6 us (11%)
  matrix products  18.1 us (8%)
  between operations  16.1 us (7%)
  local copies, waits for them, and re-layouts  9.21 us (4%)
    reduce_scatter x1, waiting for transfers between devices, shards(): lax.psum_scatter(partial_out.astype(jnp.bfloat16), 'tensor', scatter_dime...  45.5 us
    all_gather x1, waiting for transfers between devices, shards(): swished_all = lax.all_gather(swished, 'tensor', axis=1, tiled=True)  28.5 us
    ppermute x7, waiting for transfers between devices, shifted(): return lax.ppermute(value, axis, pairs)  25.2 us
    ppermute x5, waiting for transfers between devices, moments_over(): other = lax.ppermute(stats, axis, pairs)  10.5 us
    ppermute x5, starting transfers between devices, moments_over(): other = lax.ppermute(stats, axis, pairs)  10.1 us
    ppermute x7, starting transfers between devices, shifted(): return lax.ppermute(value, axis, pairs)  9.62 us
    ppermute x1, waiting for transfers between devices, shards(): lax.ppermute(jnp.stack([out_mine, ff_mine]), 'tm', swap)  7.9 us
    dot_general x1, matrix products, shards(): lax.dot_general(swished_all, right, contract, preferred_element_type=jnp....  5.52 us
  transfers between devices with their start and end apart: 19, of which 15 were waited for; matrix products, arithmetic and copies ran while one was open for 14% of the time, Pallas kernels for 0%

profile of v14, /device:TPU:2, one launch (start us, length us, event | category | flops | bytes accessed | tf_op | source)
XLA Modules:
  0.0 219.8 jit_solution(1169917828150465457)
XLA Ops:
  10.7 2.3 %collective-permute-start.1 = (bf16[96,768]{1,0:T(8,128)(2,1)S(1)}, bf16[96,768]{1,0:T(8,128)(2,1)S(1)}, u32[]{:S(2)}, u32[]{:S(2)}) collective-permute-start(bf16[96,768]{1,0:T(8,128)(2,1)S(1)} %maximum_select_fusion), channel_id=1, source_target_pairs={{0,48},{8,56},{16,0},{24,8},{32,16},{40,24},{48,32},{56,40},{64,11... | collective-permute-start | bytes 442376 | tf_op jit(solution)/shard_map/ppermute | solution.py:77
  18.3 2.5 %collective-permute-done.2 = bf16[96,768]{1,0:T(8,128)(2,1)S(1)} collective-permute-done((bf16[96,768]{1,0:T(8,128)(2,1)S(1)}, bf16[96,768]{1,0:T(8,128)(2,1)S(1)}, u32[]{:S(2)}, u32[]{:S(2)}) %collective-permute-start.2) | collective-permute-done | bytes 147488 | tf_op jit(solution)/shard_map/ppermute | solution.py:77
  21.8 3.1 %collective-permute-start.4 = (bf16[384,768]{1,0:T(8,128)(2,1)S(1)}, bf16[384,768]{1,0:T(8,128)(2,1)S(1)}, u32[]{:S(2)}, u32[]{:S(2)}) collective-permute-start(bf16[384,768]{1,0:T(8,128)(2,1)S(1)} %pad_maximum_fusion.2), channel_id=1, source_target_pairs={{0,192},{8,200},{16,208},{24,216},{32,224},{40,232},{48,240},{56,2... | collective-permute-start | bytes 1769480 | tf_op jit(solution)/shard_map/ppermute | solution.py:77
  32.4 16.8 %collective-permute-done.4 = bf16[384,768]{1,0:T(8,128)(2,1)S(1)} collective-permute-done((bf16[384,768]{1,0:T(8,128)(2,1)S(1)}, bf16[384,768]{1,0:T(8,128)(2,1)S(1)}, u32[]{:S(2)}, u32[]{:S(2)}) %collective-permute-start.4) | collective-permute-done | bytes 589856 | tf_op jit(solution)/shard_map/ppermute | solution.py:77
  49.2 3.7 %collective-permute-done.6 = bf16[384,768]{1,0:T(8,128)(2,1)S(1)} collective-permute-done((bf16[384,768]{1,0:T(8,128)(2,1)S(1)}, bf16[384,768]{1,0:T(8,128)(2,1)S(1)}, u32[]{:S(2)}, u32[]{:S(2)}) %collective-permute-start.6) | collective-permute-done | bytes 589856 | tf_op jit(solution)/shard_map/ppermute | solution.py:77
  54.0 3.1 %all-gather.4.cloned.1.call-done = bf16[1024,1536]{1,0:T(8,128)(2,1)} async-done(((bf16[128,1536]{1,0:T(8,128)(2,1)}), bf16[1024,1536]{1,0:T(8,128)(2,1)}) %all-gather.4.cloned.1.call-update) | async-done | bytes 3145744 | tf_op jit(solution)/shard_map/all_gather | solution.py:123
  57.1 2.5 %convert_reduce_fusion = f32[1024]{0:T(1024)S(1)} fusion(bf16[1024,1536]{1,0:T(8,128)(2,1)} %all-gather.4.cloned.1.call-done), kind=kLoop, calls=%fused_computation.2 | loop fusion | flops 3144704 | bytes 3149824 | tf_op jit(solution)/shard_map/reduce_sum | solution.py:25
  64.8 2.3 %collective-permute-start.8 = (bf16[15,192]{0,1:T(8,128)(2,1)S(1)}, bf16[15,192]{0,1:T(8,128)(2,1)S(1)}, u32[]{:S(2)}, u32[]{:S(2)}) collective-permute-start(bf16[15,192]{0,1:T(8,128)(2,1)S(1)} %get-tuple-element.41), channel_id=1, source_target_pairs={{8,0},{16,8},{24,16},{32,24},{40,32},{48,40},{56,48},{64,56},{72,6... | collective-permute-start | bytes 17288 | tf_op jit(solution)/shard_map/ppermute | solution.py:18
  69.4 3.1 %collective-permute-done.7 = bf16[15,192]{0,1:T(8,128)(2,1)S(1)} collective-permute-done((bf16[15,192]{0,1:T(8,128)(2,1)S(1)}, bf16[15,192]{0,1:T(8,128)(2,1)S(1)}, u32[]{:S(2)}, u32[]{:S(2)}) %collective-permute-start.7) | collective-permute-done | bytes 5792 | tf_op jit(solution)/shard_map/ppermute | solution.py:17
  72.8 5.5 %multiply_add_fusion = f32[1024,192]{0,1:T(8,128)S(1)} fusion(bf16[1024,192]{0,1:T(8,128)(2,1)S(1)} %fusion.28, bf16[15,192]{0,1:T(8,128)(2,1)S(1)} %collective-permute-done.7, bf16[1039,192]{0,1:T(8,128)(2,1)S(1)} %constant_dynamic-update-slice_fusion, f32[192]{0:T(256)S(1)} %bitcast.99, f32[192]{0:T(256)S(1)} %bitcast.100, f32[192]{0:T(256)S(1)} %bitcast.102, ...), kind=kLoop, calls=%fused_computation.59 | loop fusion | flops 26935296 | bytes 7107456 | tf_op jit(solution)/shard_map/add | solution.py:137
  81.0 3.6 %collective-permute-done.10 = f32[3,192]{1,0:T(4,128)S(1)} collective-permute-done((f32[3,192]{1,0:T(4,128)S(1)}, f32[3,192]{1,0:T(4,128)S(1)}, u32[]{:S(2)}, u32[]{:S(2)}) %collective-permute-start.10) | collective-permute-done | bytes 2336 | tf_op jit(solution)/shard_map/ppermute | solution.py:47
  84.7 2.6 %collective-permute-start.11 = (f32[3,192]{1,0:T(4,128)S(1)}, f32[3,192]{1,0:T(4,128)S(1)}, u32[]{:S(2)}, u32[]{:S(2)}) collective-permute-start(f32[3,192]{1,0:T(4,128)S(1)} %pad_maximum_fusion.7), channel_id=1, source_target_pairs={{0,32},{8,40},{16,48},{24,56},{32,0},{40,8},{48,16},{56,24},{64,96... | collective-permute-start | bytes 6920 | tf_op jit(solution)/shard_map/ppermute | solution.py:47
  87.3 2.6 %collective-permute-done.11 = f32[3,192]{1,0:T(4,128)S(1)} collective-permute-done((f32[3,192]{1,0:T(4,128)S(1)}, f32[3,192]{1,0:T(4,128)S(1)}, u32[]{:S(2)}, u32[]{:S(2)}) %collective-permute-start.11) | collective-permute-done | bytes 2336 | tf_op jit(solution)/shard_map/ppermute | solution.py:47
  89.9 3.7 %collective-permute-start.12 = (f32[3,192]{1,0:T(4,128)S(1)}, f32[3,192]{1,0:T(4,128)S(1)}, u32[]{:S(2)}, u32[]{:S(2)}) collective-permute-start(f32[3,192]{1,0:T(4,128)S(1)} %pad_maximum_fusion.8), channel_id=1, source_target_pairs={{0,64},{8,72},{16,80},{24,88},{32,96},{40,104},{48,112},{56,120},{... | collective-permute-start | bytes 6920 | tf_op jit(solution)/shard_map/ppermute | solution.py:47
  95.3 3.6 %collective-permute-start.13 = (f32[3,192]{1,0:T(4,128)S(1)}, f32[3,192]{1,0:T(4,128)S(1)}, u32[]{:S(2)}, u32[]{:S(2)}) collective-permute-start(f32[3,192]{1,0:T(4,128)S(1)} %pad_maximum_fusion.9), channel_id=1, source_target_pairs={{0,128},{8,136},{16,144},{24,152},{32,160},{40,168},{48,176},{56,1... | collective-permute-start | bytes 6920 | tf_op jit(solution)/shard_map/ppermute | solution.py:47
  100.6 2.3 %multiply_convert_fusion.1 = bf16[1024,192]{0,1:T(8,128)(2,1)} fusion(f32[1024,192]{0,1:T(8,128)} %copy-done.4, f32[192]{0:T(256)S(1)} %copy-done.41, f32[192]{0:T(256)S(1)} %copy-done.42, f32[192]{0:T(256)S(1)} %bitcast.121, f32[192]{0:T(256)S(1)} %bitcast.120), kind=kLoop, calls=%fused_computation.56 | loop fusion | flops 1769472 | bytes 1182720 | tf_op jit(solution)/shard_map/convert_element_type | solution.py:149
  105.4 7.9 %collective-permute-done.14 = bf16[2,1536,768]{2,1,0:T(8,128)(2,1)S(1)} collective-permute-done((bf16[2,1536,768]{2,1,0:T(8,128)(2,1)S(1)}, bf16[2,1536,768]{2,1,0:T(8,128)(2,1)S(1)}, u32[]{:S(2)}, u32[]{:S(2)}) %collective-permute-start.14) | collective-permute-done | bytes 4718624 | tf_op jit(solution)/shard_map/ppermute | solution.py:152
  115.5 2.4 %broadcast_select_fusion = (bf16[1536,768]{1,0:T(8,128)(2,1)}, bf16[1536,768]{1,0:T(8,128)(2,1)}) fusion(bf16[1536,768]{1,0:T(8,128)(2,1)S(1)} %pad_maximum_fusion.1, pred[]{:T(512)S(6)} %eq.121, bf16[2,1536,768]{2,1,0:T(8,128)(2,1)S(1)} %collective-permute-done.14), kind=kLoop, calls=%fused_computation.30 | loop fusion | flops 2359296 | bytes 9437185 | tf_op jit(solution)/shard_map/jit(_where)/select_n | solution.py:154
  118.0 28.5 %all-gather.6.cloned.1.call-done = bf16[1024,1536]{0,1:T(8,128)(2,1)} async-done(((bf16[1024,192]{0,1:T(8,128)(2,1)}), bf16[1024,1536]{0,1:T(8,128)(2,1)}) %all-gather.6.cloned.1.call-update) | async-done | bytes 3145744 | tf_op jit(solution)/shard_map/all_gather | solution.py:150
  146.5 5.5 %fusion.16 = f32[1024,768]{1,0:T(8,128)S(1)} fusion(bf16[1024,1536]{0,1:T(8,128)(2,1)} %all-gather.6.cloned.1.call-done, bf16[1536,768]{1,0:T(8,128)(2,1)} %all-gather.8.cloned.1.call-done, pred[]{:T(512)S(6)} %eq.121, bf16[2,1536,768]{2,1,0:T(8,128)(2,1)} %copy-done.8), kind=kOutput, calls=%fused_computation.26 | convolution fusion | flops 2417098752 | bytes 11010049 | tf_op jit(solution)/shard_map/dot_general | solution.py:161
  152.0 2.9 %fusion.18 = f32[1024,768]{1,0:T(8,128)S(1)} fusion(bf16[1024,1536]{0,1:T(8,128)(2,1)S(1)} %copy-done.43, bf16[1536,768]{1,0:T(8,128)(2,1)S(1)} %copy-done.5, pred[]{:T(512)S(6)} %eq.121, bf16[2,1536,768]{2,1,0:T(8,128)(2,1)S(1)} %copy-done.9), kind=kOutput, calls=%fused_computation.28 | convolution fusion | flops 2417098752 | bytes 11010049 | tf_op jit(solution)/shard_map/dot_general | solution.py:160
  158.5 3.2 %multiply_convert_fusion = bf16[1024,768]{1,0:T(8,128)(2,1)S(1)} fusion(bf16[1536,768]{1,0:T(8,128)(2,1)S(1)} %copy-done.7, bf16[1024,1536]{1,0:T(8,128)(2,1)S(1)} %fusion.10, f32[1536]{0:T(1024)S(1)} %copy-done.45, f32[1024]{0:T(1024)S(1)} %add_rsqrt_fusion, f32[1024]{0:T(1024)S(1)} %broadcast_multiply_fusion), kind=kOutput, calls=%fused_computation.19 | convolution fusion | flops 2427715584 | bytes 7092224 | tf_op jit(solution)/shard_map/dot_general | solution.py:169
  161.7 4.1 %convolution_convert_fusion = bf16[1024,1536]{1,0:T(8,128)(2,1)} fusion(bf16[1024,768]{1,0:T(8,128)(2,1)S(1)} %multiply_convert_fusion, bf16[1536,768]{1,0:T(8,128)(2,1)S(1)} %copy-done.6), kind=kOutput, calls=%fused_computation.17 | convolution fusion | flops 2417491968 | bytes 7077888 | tf_op jit(solution)/shard_map/dot_general | solution.py:171
  165.8 45.5 %reduce-scatter.2.cloned.1.call-done = bf16[128,1536]{1,0:T(8,128)(2,1)} async-done(((bf16[1024,1536]{1,0:T(8,128)(2,1)}), bf16[128,1536]{1,0:T(8,128)(2,1)}) %reduce-scatter.2.cloned.1.call-update) | async-done | bytes 393232 | tf_op jit(solution)/shard_map/reduce_scatter | solution.py:174
  (170 shorter events, 40.3 us)
Async XLA Ops:
  6.5 55.4 %copy-start = (bf16[1536,192]{0,1:T(8,128)(2,1)S(1)}, bf16[1536,192]{0,1:T(8,128)(2,1)}, u32[]{:S(2)}) copy-start(bf16[1536,192]{0,1:T(8,128)(2,1)} %param.18) | copy-start | bytes 1769476
  6.5 19.9 %copy-start.39 = (s32[1024]{0:T(1024)S(1)}, s32[1024]{0:T(1024)}, u32[]{:S(2)}) copy-start(s32[1024]{0:T(1024)} %param.14) | copy-start | bytes 12292
  6.5 50.6 %all-gather.4.cloned.1.call-start = ((), (), s32[]{:S(2)}) async-start(), calls=%async_computation.1 | async-start | bytes 3538944 | tf_op jit(solution)/shard_map/all_gather | solution.py:123
  7.3 95.8 %all-gather.8.cloned.1.call-start = ((), (), s32[]{:S(2)}) async-start(), calls=%async_computation.3 | async-start | bytes 2654208 | tf_op jit(solution)/shard_map/all_gather | solution.py:129
  8.2 1.5 collective-permute-start
  10.7 7.6 %collective-permute-start.1 = (bf16[96,768]{1,0:T(8,128)(2,1)S(1)}, bf16[96,768]{1,0:T(8,128)(2,1)S(1)}, u32[]{:S(2)}, u32[]{:S(2)}) collective-permute-start(bf16[96,768]{1,0:T(8,128)(2,1)S(1)} %maximum_select_fusion), channel_id=1, source_target_pairs={{0,48},{8,56},{16,0},{24,8},{32,16},{40,24},{48,32},{56,40},{64,11... | collective-permute-start | bytes 442376 | tf_op jit(solution)/shard_map/ppermute | solution.py:77
  13.0 7.7 %collective-permute-start.2 = (bf16[96,768]{1,0:T(8,128)(2,1)S(1)}, bf16[96,768]{1,0:T(8,128)(2,1)S(1)}, u32[]{:S(2)}, u32[]{:S(2)}) collective-permute-start(bf16[96,768]{1,0:T(8,128)(2,1)S(1)} %maximum_select_fusion), channel_id=1, source_target_pairs={{0,32},{8,40},{16,48},{24,56},{32,0},{40,8},{48,16},{56,24},{64,96... | collective-permute-start | bytes 442376 | tf_op jit(solution)/shard_map/ppermute | solution.py:77
  13.7 7.9 %collective-permute-start.3 = (bf16[96,768]{1,0:T(8,128)(2,1)S(1)}, bf16[96,768]{1,0:T(8,128)(2,1)S(1)}, u32[]{:S(2)}, u32[]{:S(2)}) collective-permute-start(bf16[96,768]{1,0:T(8,128)(2,1)S(1)} %maximum_select_fusion), channel_id=1, source_target_pairs={{0,16},{8,24},{16,32},{24,40},{32,48},{40,56},{48,0},{56,8},{64,80... | collective-permute-start | bytes 442376 | tf_op jit(solution)/shard_map/ppermute | solution.py:77
  17.4 129.1 %all-gather.6.cloned.1.call-start = ((), (), s32[]{:S(2)}) async-start(), calls=%async_computation.2 | async-start | bytes 3538944 | tf_op jit(solution)/shard_map/all_gather | solution.py:150
  21.8 27.5 %collective-permute-start.4 = (bf16[384,768]{1,0:T(8,128)(2,1)S(1)}, bf16[384,768]{1,0:T(8,128)(2,1)S(1)}, u32[]{:S(2)}, u32[]{:S(2)}) collective-permute-start(bf16[384,768]{1,0:T(8,128)(2,1)S(1)} %pad_maximum_fusion.2), channel_id=1, source_target_pairs={{0,192},{8,200},{16,208},{24,216},{32,224},{40,232},{48,240},{56,2... | collective-permute-start | bytes 1769480 | tf_op jit(solution)/shard_map/ppermute | solution.py:77
  24.8 24.4 %collective-permute-start.5 = (bf16[384,768]{1,0:T(8,128)(2,1)S(1)}, bf16[384,768]{1,0:T(8,128)(2,1)S(1)}, u32[]{:S(2)}, u32[]{:S(2)}) collective-permute-start(bf16[384,768]{1,0:T(8,128)(2,1)S(1)} %pad_maximum_fusion.2), channel_id=1, source_target_pairs={{0,128},{8,136},{16,144},{24,152},{32,160},{40,168},{48,176},{56,1... | collective-permute-start | bytes 1769480 | tf_op jit(solution)/shard_map/ppermute | solution.py:77
  25.5 27.5 %collective-permute-start.6 = (bf16[384,768]{1,0:T(8,128)(2,1)S(1)}, bf16[384,768]{1,0:T(8,128)(2,1)S(1)}, u32[]{:S(2)}, u32[]{:S(2)}) collective-permute-start(bf16[384,768]{1,0:T(8,128)(2,1)S(1)} %pad_maximum_fusion.2), channel_id=1, source_target_pairs={{0,64},{8,72},{16,80},{24,88},{32,96},{40,104},{48,112},{56,120},{... | collective-permute-start | bytes 1769480 | tf_op jit(solution)/shard_map/ppermute | solution.py:77
  64.8 4.6 %collective-permute-start.8 = (bf16[15,192]{0,1:T(8,128)(2,1)S(1)}, bf16[15,192]{0,1:T(8,128)(2,1)S(1)}, u32[]{:S(2)}, u32[]{:S(2)}) collective-permute-start(bf16[15,192]{0,1:T(8,128)(2,1)S(1)} %get-tuple-element.41), channel_id=1, source_target_pairs={{8,0},{16,8},{24,16},{32,24},{40,32},{48,40},{56,48},{64,56},{72,6... | collective-permute-start | bytes 17288 | tf_op jit(solution)/shard_map/ppermute | solution.py:18
  67.1 5.4 %collective-permute-start.7 = (bf16[15,192]{0,1:T(8,128)(2,1)S(1)}, bf16[15,192]{0,1:T(8,128)(2,1)S(1)}, u32[]{:S(2)}, u32[]{:S(2)}) collective-permute-start(bf16[15,192]{0,1:T(8,128)(2,1)S(1)} %get-tuple-element.42), channel_id=1, source_target_pairs={{0,8},{8,16},{16,24},{24,32},{32,40},{40,48},{48,56},{56,64},{64,7... | collective-permute-start | bytes 17288 | tf_op jit(solution)/shard_map/ppermute | solution.py:17
  72.8 27.8 %copy-start.41 = (f32[192]{0:T(256)S(1)}, f32[192]{0:T(256)}, u32[]{:S(2)}) copy-start(f32[192]{0:T(256)} %param.21) | copy-start | bytes 2308
  72.8 27.8 %copy-start.42 = (f32[192]{0:T(256)S(1)}, f32[192]{0:T(256)}, u32[]{:S(2)}) copy-start(f32[192]{0:T(256)} %param.20) | copy-start | bytes 2308
  79.6 1.2 collective-permute-start.9
  80.9 3.7 %collective-permute-start.10 = (f32[3,192]{1,0:T(4,128)S(1)}, f32[3,192]{1,0:T(4,128)S(1)}, u32[]{:S(2)}, u32[]{:S(2)}) collective-permute-start(f32[3,192]{1,0:T(4,128)S(1)} %pad_maximum_fusion.6), channel_id=1, source_target_pairs={{0,16},{8,24},{16,0},{24,8},{32,48},{40,56},{48,32},{56,40},{64,80... | collective-permute-start | bytes 6920 | tf_op jit(solution)/shard_map/ppermute | solution.py:47
  84.7 5.2 %collective-permute-start.11 = (f32[3,192]{1,0:T(4,128)S(1)}, f32[3,192]{1,0:T(4,128)S(1)}, u32[]{:S(2)}, u32[]{:S(2)}) collective-permute-start(f32[3,192]{1,0:T(4,128)S(1)} %pad_maximum_fusion.7), channel_id=1, source_target_pairs={{0,32},{8,40},{16,48},{24,56},{32,0},{40,8},{48,16},{56,24},{64,96... | collective-permute-start | bytes 6920 | tf_op jit(solution)/shard_map/ppermute | solution.py:47
  89.9 5.3 %collective-permute-start.12 = (f32[3,192]{1,0:T(4,128)S(1)}, f32[3,192]{1,0:T(4,128)S(1)}, u32[]{:S(2)}, u32[]{:S(2)}) collective-permute-start(f32[3,192]{1,0:T(4,128)S(1)} %pad_maximum_fusion.8), channel_id=1, source_target_pairs={{0,64},{8,72},{16,80},{24,88},{32,96},{40,104},{48,112},{56,120},{... | collective-permute-start | bytes 6920 | tf_op jit(solution)/shard_map/ppermute | solution.py:47
  95.3 5.2 %collective-permute-start.13 = (f32[3,192]{1,0:T(4,128)S(1)}, f32[3,192]{1,0:T(4,128)S(1)}, u32[]{:S(2)}, u32[]{:S(2)}) collective-permute-start(f32[3,192]{1,0:T(4,128)S(1)} %pad_maximum_fusion.9), channel_id=1, source_target_pairs={{0,128},{8,136},{16,144},{24,152},{32,160},{40,168},{48,176},{56,1... | collective-permute-start | bytes 6920 | tf_op jit(solution)/shard_map/ppermute | solution.py:47
  102.9 108.4 %reduce-scatter.2.cloned.1.call-start = ((), (), s32[]{:S(2)}) async-start(), calls=%async_computation.4 | async-start | bytes 3538944 | tf_op jit(solution)/shard_map/reduce_scatter | solution.py:174
  105.1 8.2 %collective-permute-start.14 = (bf16[2,1536,768]{2,1,0:T(8,128)(2,1)S(1)}, bf16[2,1536,768]{2,1,0:T(8,128)(2,1)S(1)}, u32[]{:S(2)}, u32[]{:S(2)}) collective-permute-start(bf16[2,1536,768]{2,1,0:T(8,128)(2,1)S(1)} %pad_maximum_fusion), channel_id=1, source_target_pairs={{0,8},{8,0},{16,24},{24,16},{32,40},{40,32},{48,56},{56,48},{64,72... | collective-permute-start | bytes 14155784 | tf_op jit(solution)/shard_map/ppermute | solution.py:152
  118.0 34.0 %copy-start.5 = (bf16[1536,768]{1,0:T(8,128)(2,1)S(1)}, bf16[1536,768]{1,0:T(8,128)(2,1)}, u32[]{:S(2)}) copy-start(bf16[1536,768]{1,0:T(8,128)(2,1)} %all-gather.8.cloned.1.call-done) | copy-start | bytes 7077892
  (41 other events, 304.4 us)
Sparse Core Ops, SparseCore 0:
  9.1 47.9 all-gather.3
  58.9 40.3 all-gather.7
  103.1 43.3 all-gather.5
  165.9 45.3 reduce-scatter.1

commit v15 on v13

--- a/solution.py
+++ b/solution.py
@@ -129,6 +129,7 @@
     out_mine = lax.all_gather(out_half, "tensor", axis=0, tiled=True)
     value = jnp.dot(piece, value_weight, preferred_element_type=jnp.float32)
     gate = jnp.dot(piece, gate_weight, preferred_element_type=jnp.float32)
+    value, gate = lax.optimization_barrier((value, gate))
     glu = (value * jax.nn.sigmoid(gate) * valid[:, None]).astype(jnp.bfloat16)
     ff_mine, glu = gather_torus(up_weight, down_weight.T, "tm", glu)
     padded = extended(glu, (("tm", 0),), KERNEL // 2)

time: 220 us -> 220 us (level)
  transfers between devices with their start and end apart: 19 -> 19, of which waited for: 15 -> 15; matrix products, arithmetic and copies ran while one was open for 13% -> 14% of each run, Pallas kernels for 0% -> 0%
where the time goes in v15:
time: 220 us
  waiting for transfers between devices  125 us (57%)
  other arithmetic  27.1 us (12%)
  starting transfers between devices  24.6 us (11%)
  matrix products  18 us (8%)
  between operations  16.1 us (7%)
  local copies, waits for them, and re-layouts  9.38 us (4%)
    reduce_scatter x1, waiting for transfers between devices, shards(): lax.psum_scatter(partial_out.astype(jnp.bfloat16), 'tensor', scatter_dime...  45.6 us
    all_gather x1, waiting for transfers between devices, shards(): swished_all = lax.all_gather(swished, 'tensor', axis=1, tiled=True)  28.5 us
    ppermute x7, waiting for transfers between devices, shifted(): return lax.ppermute(value, axis, pairs)  25.1 us
    ppermute x5, waiting for transfers between devices, moments_over(): other = lax.ppermute(stats, axis, pairs)  10.5 us
    ppermute x5, starting transfers between devices, moments_over(): other = lax.ppermute(stats, axis, pairs)  10.1 us
    ppermute x7, starting transfers between devices, shifted(): return lax.ppermute(value, axis, pairs)  9.62 us
    ppermute x1, waiting for transfers between devices, shards(): lax.ppermute(jnp.stack([out_mine, ff_mine]), 'tm', swap)  7.9 us
    dot_general x1, matrix products, shards(): lax.dot_general(swished_all, right, contract, preferred_element_type=jnp....  5.51 us
  transfers between devices with their start and end apart: 19, of which 15 were waited for; matrix products, arithmetic and copies ran while one was open for 14% of the time, Pallas kernels for 0%

profile of v15, /device:TPU:2, one launch (start us, length us, event | category | flops | bytes accessed | tf_op | source)
XLA Modules:
  0.0 219.9 jit_solution(7799935963796820756)
XLA Ops:
  10.7 2.3 %collective-permute-start.1 = (bf16[96,768]{1,0:T(8,128)(2,1)S(1)}, bf16[96,768]{1,0:T(8,128)(2,1)S(1)}, u32[]{:S(2)}, u32[]{:S(2)}) collective-permute-start(bf16[96,768]{1,0:T(8,128)(2,1)S(1)} %maximum_select_fusion), channel_id=1, source_target_pairs={{0,48},{8,56},{16,0},{24,8},{32,16},{40,24},{48,32},{56,40},{64,11... | collective-permute-start | bytes 442376 | tf_op jit(solution)/shard_map/ppermute | solution.py:77
  18.3 2.5 %collective-permute-done.2 = bf16[96,768]{1,0:T(8,128)(2,1)S(1)} collective-permute-done((bf16[96,768]{1,0:T(8,128)(2,1)S(1)}, bf16[96,768]{1,0:T(8,128)(2,1)S(1)}, u32[]{:S(2)}, u32[]{:S(2)}) %collective-permute-start.2) | collective-permute-done | bytes 147488 | tf_op jit(solution)/shard_map/ppermute | solution.py:77
  21.8 3.1 %collective-permute-start.4 = (bf16[384,768]{1,0:T(8,128)(2,1)S(1)}, bf16[384,768]{1,0:T(8,128)(2,1)S(1)}, u32[]{:S(2)}, u32[]{:S(2)}) collective-permute-start(bf16[384,768]{1,0:T(8,128)(2,1)S(1)} %pad_maximum_fusion.2), channel_id=1, source_target_pairs={{0,192},{8,200},{16,208},{24,216},{32,224},{40,232},{48,240},{56,2... | collective-permute-start | bytes 1769480 | tf_op jit(solution)/shard_map/ppermute | solution.py:77
  32.5 16.7 %collective-permute-done.4 = bf16[384,768]{1,0:T(8,128)(2,1)S(1)} collective-permute-done((bf16[384,768]{1,0:T(8,128)(2,1)S(1)}, bf16[384,768]{1,0:T(8,128)(2,1)S(1)}, u32[]{:S(2)}, u32[]{:S(2)}) %collective-permute-start.4) | collective-permute-done | bytes 589856 | tf_op jit(solution)/shard_map/ppermute | solution.py:77
  49.2 3.7 %collective-permute-done.6 = bf16[384,768]{1,0:T(8,128)(2,1)S(1)} collective-permute-done((bf16[384,768]{1,0:T(8,128)(2,1)S(1)}, bf16[384,768]{1,0:T(8,128)(2,1)S(1)}, u32[]{:S(2)}, u32[]{:S(2)}) %collective-permute-start.6) | collective-permute-done | bytes 589856 | tf_op jit(solution)/shard_map/ppermute | solution.py:77
  54.0 3.1 %all-gather.4.cloned.1.call-done = bf16[1024,1536]{1,0:T(8,128)(2,1)} async-done(((bf16[128,1536]{1,0:T(8,128)(2,1)}), bf16[1024,1536]{1,0:T(8,128)(2,1)}) %all-gather.4.cloned.1.call-update) | async-done | bytes 3145744 | tf_op jit(solution)/shard_map/all_gather | solution.py:123
  57.1 2.5 %convert_reduce_fusion = f32[1024]{0:T(1024)S(1)} fusion(bf16[1024,1536]{1,0:T(8,128)(2,1)} %all-gather.4.cloned.1.call-done), kind=kLoop, calls=%fused_computation.2 | loop fusion | flops 3144704 | bytes 3149824 | tf_op jit(solution)/shard_map/reduce_sum | solution.py:25
  64.9 2.3 %collective-permute-start.8 = (bf16[15,192]{0,1:T(8,128)(2,1)S(1)}, bf16[15,192]{0,1:T(8,128)(2,1)S(1)}, u32[]{:S(2)}, u32[]{:S(2)}) collective-permute-start(bf16[15,192]{0,1:T(8,128)(2,1)S(1)} %get-tuple-element.48), channel_id=1, source_target_pairs={{8,0},{16,8},{24,16},{32,24},{40,32},{48,40},{56,48},{64,56},{72,6... | collective-permute-start | bytes 17288 | tf_op jit(solution)/shard_map/ppermute | solution.py:18
  69.5 3.1 %collective-permute-done.7 = bf16[15,192]{0,1:T(8,128)(2,1)S(1)} collective-permute-done((bf16[15,192]{0,1:T(8,128)(2,1)S(1)}, bf16[15,192]{0,1:T(8,128)(2,1)S(1)}, u32[]{:S(2)}, u32[]{:S(2)}) %collective-permute-start.7) | collective-permute-done | bytes 5792 | tf_op jit(solution)/shard_map/ppermute | solution.py:17
  72.9 5.3 %multiply_reduce_fusion.1 = (f32[192]{0:T(256)S(1)}, f32[1024,192]{0,1:T(8,128)S(1)}) fusion(f32[1024]{0:T(1024)S(1)} %get-tuple-element.34, f32[192]{0:T(256)S(1)} %bitcast.99, bf16[1039,192]{0,1:T(8,128)(2,1)S(1)} %constant_dynamic-update-slice_fusion, f32[192]{0:T(256)S(1)} %bitcast.100, f32[192]{0:T(256)S(1)} %bitcast.102, f32[192]{0:T(256)S(1)} %bitcast.103, ...), kind=kLoop, calls=%fused_computation.51 | loop fusion | flops 27328320 | bytes 7112320 | tf_op jit(solution)/shard_map/reduce_sum | solution.py:140
  81.0 3.6 %collective-permute-done.10 = f32[3,192]{1,0:T(4,128)S(1)} collective-permute-done((f32[3,192]{1,0:T(4,128)S(1)}, f32[3,192]{1,0:T(4,128)S(1)}, u32[]{:S(2)}, u32[]{:S(2)}) %collective-permute-start.10) | collective-permute-done | bytes 2336 | tf_op jit(solution)/shard_map/ppermute | solution.py:47
  84.6 2.6 %collective-permute-start.11 = (f32[3,192]{1,0:T(4,128)S(1)}, f32[3,192]{1,0:T(4,128)S(1)}, u32[]{:S(2)}, u32[]{:S(2)}) collective-permute-start(f32[3,192]{1,0:T(4,128)S(1)} %pad_maximum_fusion.7), channel_id=1, source_target_pairs={{0,32},{8,40},{16,48},{24,56},{32,0},{40,8},{48,16},{56,24},{64,96... | collective-permute-start | bytes 6920 | tf_op jit(solution)/shard_map/ppermute | solution.py:47
  87.2 2.6 %collective-permute-done.11 = f32[3,192]{1,0:T(4,128)S(1)} collective-permute-done((f32[3,192]{1,0:T(4,128)S(1)}, f32[3,192]{1,0:T(4,128)S(1)}, u32[]{:S(2)}, u32[]{:S(2)}) %collective-permute-start.11) | collective-permute-done | bytes 2336 | tf_op jit(solution)/shard_map/ppermute | solution.py:47
  89.9 3.7 %collective-permute-start.12 = (f32[3,192]{1,0:T(4,128)S(1)}, f32[3,192]{1,0:T(4,128)S(1)}, u32[]{:S(2)}, u32[]{:S(2)}) collective-permute-start(f32[3,192]{1,0:T(4,128)S(1)} %pad_maximum_fusion.8), channel_id=1, source_target_pairs={{0,64},{8,72},{16,80},{24,88},{32,96},{40,104},{48,112},{56,120},{... | collective-permute-start | bytes 6920 | tf_op jit(solution)/shard_map/ppermute | solution.py:47
  95.3 3.6 %collective-permute-start.13 = (f32[3,192]{1,0:T(4,128)S(1)}, f32[3,192]{1,0:T(4,128)S(1)}, u32[]{:S(2)}, u32[]{:S(2)}) collective-permute-start(f32[3,192]{1,0:T(4,128)S(1)} %pad_maximum_fusion.9), channel_id=1, source_target_pairs={{0,128},{8,136},{16,144},{24,152},{32,160},{40,168},{48,176},{56,1... | collective-permute-start | bytes 6920 | tf_op jit(solution)/shard_map/ppermute | solution.py:47
  100.6 2.3 %multiply_convert_fusion.1 = bf16[1024,192]{0,1:T(8,128)(2,1)} fusion(f32[1024,192]{0,1:T(8,128)} %copy-done.4, f32[192]{0:T(256)S(1)} %copy-done.41, f32[192]{0:T(256)S(1)} %copy-done.42, f32[192]{0:T(256)S(1)} %bitcast.121, f32[192]{0:T(256)S(1)} %bitcast.120), kind=kLoop, calls=%fused_computation.49 | loop fusion | flops 1769472 | bytes 1182720 | tf_op jit(solution)/shard_map/convert_element_type | solution.py:149
  105.4 7.9 %collective-permute-done.14 = bf16[2,1536,768]{2,1,0:T(8,128)(2,1)S(1)} collective-permute-done((bf16[2,1536,768]{2,1,0:T(8,128)(2,1)S(1)}, bf16[2,1536,768]{2,1,0:T(8,128)(2,1)S(1)}, u32[]{:S(2)}, u32[]{:S(2)}) %collective-permute-start.14) | collective-permute-done | bytes 4718624 | tf_op jit(solution)/shard_map/ppermute | solution.py:152
  115.5 2.4 %broadcast_select_fusion = (bf16[1536,768]{1,0:T(8,128)(2,1)}, bf16[1536,768]{1,0:T(8,128)(2,1)}) fusion(bf16[1536,768]{1,0:T(8,128)(2,1)S(1)} %pad_maximum_fusion.1, pred[]{:T(512)S(6)} %eq.121, bf16[2,1536,768]{2,1,0:T(8,128)(2,1)S(1)} %collective-permute-done.14), kind=kLoop, calls=%fused_computation.30 | loop fusion | flops 2359296 | bytes 9437185 | tf_op jit(solution)/shard_map/jit(_where)/select_n | solution.py:154
  117.9 28.5 %all-gather.6.cloned.1.call-done = bf16[1024,1536]{0,1:T(8,128)(2,1)} async-done(((bf16[1024,192]{0,1:T(8,128)(2,1)}), bf16[1024,1536]{0,1:T(8,128)(2,1)}) %all-gather.6.cloned.1.call-update) | async-done | bytes 3145744 | tf_op jit(solution)/shard_map/all_gather | solution.py:150
  146.4 5.5 %fusion.16 = f32[1024,768]{1,0:T(8,128)S(1)} fusion(bf16[1024,1536]{0,1:T(8,128)(2,1)} %all-gather.6.cloned.1.call-done, bf16[1536,768]{1,0:T(8,128)(2,1)} %all-gather.8.cloned.1.call-done, pred[]{:T(512)S(6)} %eq.121, bf16[2,1536,768]{2,1,0:T(8,128)(2,1)} %copy-done.8), kind=kOutput, calls=%fused_computation.26 | convolution fusion | flops 2417098752 | bytes 11010049 | tf_op jit(solution)/shard_map/dot_general | solution.py:161
  152.0 2.9 %fusion.18 = f32[1024,768]{1,0:T(8,128)S(1)} fusion(bf16[1024,1536]{0,1:T(8,128)(2,1)S(1)} %copy-done.43, bf16[1536,768]{1,0:T(8,128)(2,1)S(1)} %copy-done.5, pred[]{:T(512)S(6)} %eq.121, bf16[2,1536,768]{2,1,0:T(8,128)(2,1)S(1)} %copy-done.9), kind=kOutput, calls=%fused_computation.28 | convolution fusion | flops 2417098752 | bytes 11010049 | tf_op jit(solution)/shard_map/dot_general | solution.py:160
  158.5 3.2 %multiply_convert_fusion = bf16[1024,768]{1,0:T(8,128)(2,1)S(1)} fusion(bf16[1536,768]{1,0:T(8,128)(2,1)S(1)} %copy-done.7, bf16[1024,1536]{1,0:T(8,128)(2,1)S(1)} %fusion.10, f32[1536]{0:T(1024)S(1)} %copy-done.45, f32[1024]{0:T(1024)S(1)} %add_rsqrt_fusion, f32[1024]{0:T(1024)S(1)} %broadcast_multiply_fusion), kind=kOutput, calls=%fused_computation.19 | convolution fusion | flops 2427715584 | bytes 7092224 | tf_op jit(solution)/shard_map/dot_general | solution.py:169
  161.7 4.1 %convolution_convert_fusion = bf16[1024,1536]{1,0:T(8,128)(2,1)} fusion(bf16[1024,768]{1,0:T(8,128)(2,1)S(1)} %multiply_convert_fusion, bf16[1536,768]{1,0:T(8,128)(2,1)S(1)} %copy-done.6), kind=kOutput, calls=%fused_computation.17 | convolution fusion | flops 2417491968 | bytes 7077888 | tf_op jit(solution)/shard_map/dot_general | solution.py:171
  165.8 45.6 %reduce-scatter.2.cloned.1.call-done = bf16[128,1536]{1,0:T(8,128)(2,1)} async-done(((bf16[1024,1536]{1,0:T(8,128)(2,1)}), bf16[128,1536]{1,0:T(8,128)(2,1)}) %reduce-scatter.2.cloned.1.call-update) | async-done | bytes 393232 | tf_op jit(solution)/shard_map/reduce_scatter | solution.py:174
  (170 shorter events, 40.5 us)
Async XLA Ops:
  6.5 55.4 %copy-start = (bf16[1536,192]{0,1:T(8,128)(2,1)S(1)}, bf16[1536,192]{0,1:T(8,128)(2,1)}, u32[]{:S(2)}) copy-start(bf16[1536,192]{0,1:T(8,128)(2,1)} %param.17) | copy-start | bytes 1769476
  6.5 19.9 %copy-start.39 = (s32[1024]{0:T(1024)S(1)}, s32[1024]{0:T(1024)}, u32[]{:S(2)}) copy-start(s32[1024]{0:T(1024)} %param.14) | copy-start | bytes 12292
  6.5 50.6 %all-gather.4.cloned.1.call-start = ((), (), s32[]{:S(2)}) async-start(), calls=%async_computation.1 | async-start | bytes 3538944 | tf_op jit(solution)/shard_map/all_gather | solution.py:123
  7.3 95.7 %all-gather.8.cloned.1.call-start = ((), (), s32[]{:S(2)}) async-start(), calls=%async_computation.3 | async-start | bytes 2654208 | tf_op jit(solution)/shard_map/all_gather | solution.py:129
  8.2 1.5 collective-permute-start
  10.7 7.6 %collective-permute-start.1 = (bf16[96,768]{1,0:T(8,128)(2,1)S(1)}, bf16[96,768]{1,0:T(8,128)(2,1)S(1)}, u32[]{:S(2)}, u32[]{:S(2)}) collective-permute-start(bf16[96,768]{1,0:T(8,128)(2,1)S(1)} %maximum_select_fusion), channel_id=1, source_target_pairs={{0,48},{8,56},{16,0},{24,8},{32,16},{40,24},{48,32},{56,40},{64,11... | collective-permute-start | bytes 442376 | tf_op jit(solution)/shard_map/ppermute | solution.py:77
  13.0 7.7 %collective-permute-start.2 = (bf16[96,768]{1,0:T(8,128)(2,1)S(1)}, bf16[96,768]{1,0:T(8,128)(2,1)S(1)}, u32[]{:S(2)}, u32[]{:S(2)}) collective-permute-start(bf16[96,768]{1,0:T(8,128)(2,1)S(1)} %maximum_select_fusion), channel_id=1, source_target_pairs={{0,32},{8,40},{16,48},{24,56},{32,0},{40,8},{48,16},{56,24},{64,96... | collective-permute-start | bytes 442376 | tf_op jit(solution)/shard_map/ppermute | solution.py:77
  13.7 7.9 %collective-permute-start.3 = (bf16[96,768]{1,0:T(8,128)(2,1)S(1)}, bf16[96,768]{1,0:T(8,128)(2,1)S(1)}, u32[]{:S(2)}, u32[]{:S(2)}) collective-permute-start(bf16[96,768]{1,0:T(8,128)(2,1)S(1)} %maximum_select_fusion), channel_id=1, source_target_pairs={{0,16},{8,24},{16,32},{24,40},{32,48},{40,56},{48,0},{56,8},{64,80... | collective-permute-start | bytes 442376 | tf_op jit(solution)/shard_map/ppermute | solution.py:77
  17.4 129.1 %all-gather.6.cloned.1.call-start = ((), (), s32[]{:S(2)}) async-start(), calls=%async_computation.2 | async-start | bytes 3538944 | tf_op jit(solution)/shard_map/all_gather | solution.py:150
  21.8 27.5 %collective-permute-start.4 = (bf16[384,768]{1,0:T(8,128)(2,1)S(1)}, bf16[384,768]{1,0:T(8,128)(2,1)S(1)}, u32[]{:S(2)}, u32[]{:S(2)}) collective-permute-start(bf16[384,768]{1,0:T(8,128)(2,1)S(1)} %pad_maximum_fusion.2), channel_id=1, source_target_pairs={{0,192},{8,200},{16,208},{24,216},{32,224},{40,232},{48,240},{56,2... | collective-permute-start | bytes 1769480 | tf_op jit(solution)/shard_map/ppermute | solution.py:77
  24.8 24.4 %collective-permute-start.5 = (bf16[384,768]{1,0:T(8,128)(2,1)S(1)}, bf16[384,768]{1,0:T(8,128)(2,1)S(1)}, u32[]{:S(2)}, u32[]{:S(2)}) collective-permute-start(bf16[384,768]{1,0:T(8,128)(2,1)S(1)} %pad_maximum_fusion.2), channel_id=1, source_target_pairs={{0,128},{8,136},{16,144},{24,152},{32,160},{40,168},{48,176},{56,1... | collective-permute-start | bytes 1769480 | tf_op jit(solution)/shard_map/ppermute | solution.py:77
  25.5 27.5 %collective-permute-start.6 = (bf16[384,768]{1,0:T(8,128)(2,1)S(1)}, bf16[384,768]{1,0:T(8,128)(2,1)S(1)}, u32[]{:S(2)}, u32[]{:S(2)}) collective-permute-start(bf16[384,768]{1,0:T(8,128)(2,1)S(1)} %pad_maximum_fusion.2), channel_id=1, source_target_pairs={{0,64},{8,72},{16,80},{24,88},{32,96},{40,104},{48,112},{56,120},{... | collective-permute-start | bytes 1769480 | tf_op jit(solution)/shard_map/ppermute | solution.py:77
  64.9 4.6 %collective-permute-start.8 = (bf16[15,192]{0,1:T(8,128)(2,1)S(1)}, bf16[15,192]{0,1:T(8,128)(2,1)S(1)}, u32[]{:S(2)}, u32[]{:S(2)}) collective-permute-start(bf16[15,192]{0,1:T(8,128)(2,1)S(1)} %get-tuple-element.48), channel_id=1, source_target_pairs={{8,0},{16,8},{24,16},{32,24},{40,32},{48,40},{56,48},{64,56},{72,6... | collective-permute-start | bytes 17288 | tf_op jit(solution)/shard_map/ppermute | solution.py:18
  67.2 5.4 %collective-permute-start.7 = (bf16[15,192]{0,1:T(8,128)(2,1)S(1)}, bf16[15,192]{0,1:T(8,128)(2,1)S(1)}, u32[]{:S(2)}, u32[]{:S(2)}) collective-permute-start(bf16[15,192]{0,1:T(8,128)(2,1)S(1)} %get-tuple-element.47), channel_id=1, source_target_pairs={{0,8},{8,16},{16,24},{24,32},{32,40},{40,48},{48,56},{56,64},{64,7... | collective-permute-start | bytes 17288 | tf_op jit(solution)/shard_map/ppermute | solution.py:17
  72.9 27.6 %copy-start.41 = (f32[192]{0:T(256)S(1)}, f32[192]{0:T(256)}, u32[]{:S(2)}) copy-start(f32[192]{0:T(256)} %param.21) | copy-start | bytes 2308
  72.9 27.6 %copy-start.42 = (f32[192]{0:T(256)S(1)}, f32[192]{0:T(256)}, u32[]{:S(2)}) copy-start(f32[192]{0:T(256)} %param.20) | copy-start | bytes 2308
  79.5 1.2 collective-permute-start.9
  80.9 3.7 %collective-permute-start.10 = (f32[3,192]{1,0:T(4,128)S(1)}, f32[3,192]{1,0:T(4,128)S(1)}, u32[]{:S(2)}, u32[]{:S(2)}) collective-permute-start(f32[3,192]{1,0:T(4,128)S(1)} %pad_maximum_fusion.6), channel_id=1, source_target_pairs={{0,16},{8,24},{16,0},{24,8},{32,48},{40,56},{48,32},{56,40},{64,80... | collective-permute-start | bytes 6920 | tf_op jit(solution)/shard_map/ppermute | solution.py:47
  84.6 5.2 %collective-permute-start.11 = (f32[3,192]{1,0:T(4,128)S(1)}, f32[3,192]{1,0:T(4,128)S(1)}, u32[]{:S(2)}, u32[]{:S(2)}) collective-permute-start(f32[3,192]{1,0:T(4,128)S(1)} %pad_maximum_fusion.7), channel_id=1, source_target_pairs={{0,32},{8,40},{16,48},{24,56},{32,0},{40,8},{48,16},{56,24},{64,96... | collective-permute-start | bytes 6920 | tf_op jit(solution)/shard_map/ppermute | solution.py:47
  89.9 5.3 %collective-permute-start.12 = (f32[3,192]{1,0:T(4,128)S(1)}, f32[3,192]{1,0:T(4,128)S(1)}, u32[]{:S(2)}, u32[]{:S(2)}) collective-permute-start(f32[3,192]{1,0:T(4,128)S(1)} %pad_maximum_fusion.8), channel_id=1, source_target_pairs={{0,64},{8,72},{16,80},{24,88},{32,96},{40,104},{48,112},{56,120},{... | collective-permute-start | bytes 6920 | tf_op jit(solution)/shard_map/ppermute | solution.py:47
  95.3 5.2 %collective-permute-start.13 = (f32[3,192]{1,0:T(4,128)S(1)}, f32[3,192]{1,0:T(4,128)S(1)}, u32[]{:S(2)}, u32[]{:S(2)}) collective-permute-start(f32[3,192]{1,0:T(4,128)S(1)} %pad_maximum_fusion.9), channel_id=1, source_target_pairs={{0,128},{8,136},{16,144},{24,152},{32,160},{40,168},{48,176},{56,1... | collective-permute-start | bytes 6920 | tf_op jit(solution)/shard_map/ppermute | solution.py:47
  102.9 108.5 %reduce-scatter.2.cloned.1.call-start = ((), (), s32[]{:S(2)}) async-start(), calls=%async_computation.4 | async-start | bytes 3538944 | tf_op jit(solution)/shard_map/reduce_scatter | solution.py:174
  105.1 8.2 %collective-permute-start.14 = (bf16[2,1536,768]{2,1,0:T(8,128)(2,1)S(1)}, bf16[2,1536,768]{2,1,0:T(8,128)(2,1)S(1)}, u32[]{:S(2)}, u32[]{:S(2)}) collective-permute-start(bf16[2,1536,768]{2,1,0:T(8,128)(2,1)S(1)} %pad_maximum_fusion), channel_id=1, source_target_pairs={{0,8},{8,0},{16,24},{24,16},{32,40},{40,32},{48,56},{56,48},{64,72... | collective-permute-start | bytes 14155784 | tf_op jit(solution)/shard_map/ppermute | solution.py:152
  117.9 34.1 %copy-start.5 = (bf16[1536,768]{1,0:T(8,128)(2,1)S(1)}, bf16[1536,768]{1,0:T(8,128)(2,1)}, u32[]{:S(2)}) copy-start(bf16[1536,768]{1,0:T(8,128)(2,1)} %all-gather.8.cloned.1.call-done) | copy-start | bytes 7077892
  (41 other events, 310.2 us)
Sparse Core Ops, SparseCore 0:
  9.1 47.9 all-gather.3
  58.9 40.1 all-gather.7
  103.0 43.3 all-gather.5
  165.9 45.4 reduce-scatter.1
